TPU v7x, 128 devices: a whole 4x4x4 slice. The times are simulated.
128 devices in a mesh: row: 16 (over z_lo, x, core), col: 8 (over y, z_hi).
Axes of the slice: x: 4, y: 4, z: 4 (z_hi: 2, z_lo: 2; z = z_hi * 2 + z_lo), core: 2. Of those that a mesh axis runs over, the one named last changes fastest.
Arguments:
- shared_rows: float32 [2048, 16384], P('row', 'col'), may hold values from -0.125 to 0.125
- event_counts: int32 [16], replicated, may hold values from 32 to 128, as said below
- ridge: float32 [16384], P('col'), may hold values from 0.5 to 2
- items: float32 [1024, 16384], P('row', 'col'), may hold values from -6 to 6
- cand_ids: int32 [512], replicated, may hold values from 0 to 1023
- theta: float32 [16384], P('col'), may hold values from -0.046875 to 0.046875
Outputs:
- gram_tile: float32 [16384, 16384], P('row', 'col')
- scores: float32 [512], replicated
Inputs may be any that keep to these rules, and one draw needn't show every extreme that they name: event_counts[s] counts the live slots at the start of row shard s's 128 slots; some shard is full.
All inputs are finite; a program needn't handle non-finite values.
Results may differ from a plain program's by a relative error of at most 0.000068.
Values sent between devices are 32-bit elements; how exact they have to be, the bound alone decides.
No kernel may reach another device: no remote copies, remote signals or barrier semaphores. Data moves between devices by JAX's collectives and lax.ppermute only.
A program may use at most 128 MiB of HBM per device.

v0:
```python
import jax
import jax.numpy as jnp
from jax import lax
from jax.sharding import PartitionSpec as P

F = 16384


high = lax.Precision.HIGHEST


def spread(value, axis, source):
    kept = jnp.where(lax.axis_index(axis) == source, value, 0).astype(value.dtype)
    return lax.psum(kept, axis)


def body(shared_rows, event_counts, ridge, items, cand_ids, theta):
    ratio = lax.axis_size("row") // lax.axis_size("col")
    row_pos = lax.axis_index("row")
    col_pos = lax.axis_index("col")
    width_col = shared_rows.shape[1]
    width_row = width_col // ratio
    ev_slots = shared_rows.shape[0]
    slot = lax.iota(jnp.int32, ev_slots)
    masked = jnp.where((slot < event_counts[row_pos])[:, None], shared_rows, jnp.float32(0.0))
    offset = row_pos % ratio * width_row
    root = row_pos // ratio
    contract = (((0,), (0,)), ((), ()))
    col_all = lax.all_gather(masked, "row", axis=0, tiled=True)
    row_all = spread(lax.dynamic_slice_in_dim(col_all, offset, width_row, 1), "col", root)
    tile = lax.dot_general(
        row_all, col_all, contract, precision=high, preferred_element_type=jnp.float32
    )
    rows_global = row_pos * width_row + lax.broadcasted_iota(jnp.int32, (width_row, width_col), 0)
    cols_global = col_pos * width_col + lax.broadcasted_iota(jnp.int32, (width_row, width_col), 1)
    tile = tile + jnp.where(rows_global == cols_global, ridge[None, :], jnp.float32(0.0))
    items_dev = items.shape[0]
    onehot = (
        cand_ids[:, None] == row_pos * items_dev + lax.iota(jnp.int32, items_dev)[None, :]
    ).astype(jnp.float32)
    picked = jnp.dot(onehot, items, precision=high, preferred_element_type=jnp.float32)
    cand_col = lax.psum(picked, "row")
    across = (((1,), (1,)), ((), ()))
    cand_row = spread(lax.dynamic_slice_in_dim(cand_col, offset, width_row, 1), "col", root)
    image_part = lax.dot_general(
        cand_col, tile, across, precision=high, preferred_element_type=jnp.float32
    )
    image_row = lax.psum(image_part, "col")
    quad = jnp.where(col_pos == 0, jnp.sum(cand_row * image_row, axis=1), jnp.float32(0.0))
    linear = jnp.where(
        row_pos == 0,
        jnp.dot(cand_col, theta, precision=high, preferred_element_type=jnp.float32),
        jnp.float32(0.0),
    )
    quad_all, linear_all = lax.psum((quad, linear), ("row", "col"))
    return (tile, linear_all + jnp.sqrt(quad_all / F))


def solution(mesh):
    return jax.shard_map(
        body,
        mesh=mesh,
        in_specs=(P("row", "col"), P(), P("col"), P("row", "col"), P(), P("col")),
        out_specs=(P("row", "col"), P()),
        check_vma=False,
    )
```

profile of v0, /device:TPU:0, one launch (start us, length us, event | category | flops | bytes accessed | tf_op | source)
XLA Modules:
  0.0 939.7 jit_solution(5957106584917055528)
XLA Ops:
  7.2 0.0 copy-start
  7.2 0.0 all-gather.2.cloned.1.call-start
  7.2 1.3 dynamic_slice.9
  8.5 0.6 iota_compare_fusion
  9.2 2.3 broadcast_select_fusion
  11.5 0.0 all-gather.2.cloned.1.call-update
  11.5 0.0 all-reduce.8.cloned.1.call-start
  11.6 0.0 copy-done
  11.6 4.5 fusion
  16.1 0.0 all-reduce.8.cloned.1.call-update
  16.1 0.0 all-reduce.6.cloned.1.call-start
  16.2 89.6 %all-gather.2.cloned.1.call-done = f32[2048,2048]{1,0:T(8,128)} async-done(((f32[128,2048]{1,0:T(8,128)}), f32[2048,2048]{1,0:T(8,128)}) %all-gather.2.cloned.1.call-update) | async-done | bytes 16777232 | tf_op jit(solution)/shard_map/all_gather | solution.py:29
  105.8 8.7 dynamic-slice_select_fusion
  114.5 0.0 copy-start.3
  114.5 0.0 all-reduce.6.cloned.1.call-update
  114.5 0.0 all-reduce.10.cloned.1.call-start
  114.6 124.1 %all-reduce.8.cloned.1.call-done = f32[512,2048]{1,0:T(8,128)} async-done(((f32[512,2048]{1,0:T(8,128)}), f32[512,2048]{1,0:T(8,128)}) %all-reduce.8.cloned.1.call-update) | async-done | bytes 4194320 | tf_op jit(solution)/shard_map/psum | solution.py:42
  238.7 3.2 dynamic-slice_select_fusion.1
  241.9 342.7 %all-reduce.6.cloned.1.call-done = f32[2048,1024]{1,0:T(8,128)} async-done(((f32[2048,1024]{1,0:T(8,128)}), f32[2048,1024]{1,0:T(8,128)}) %all-reduce.6.cloned.1.call-update) | async-done | bytes 8388624 | tf_op jit(solution)/shard_map/psum | solution.py:14
  584.6 0.0 copy-done.3
  584.6 67.7 %select_add_fusion = f32[1024,2048]{1,0:T(8,128)S(1)} fusion(f32[2048]{0:T(1024)S(1)} %copy-done.3, s32[2048]{0:T(1024)S(1)} %iota_add_fusion, s32[1024]{0:T(1024)S(1)} %iota_add_fusion.1, f32[2048,1024]{1,0:T(8,128)} %all-reduce.6.cloned.1.call-done, f32[2048,2048]{1,0:T(8,128)} %all-gather.2.cloned.1.call-done), kind=kOutput, calls=%fused_computation | convolution fusion | flops 51545899008 | bytes 33574912 | tf_op jit(solution)/shard_map/dot_general | solution.py:31
  652.3 0.0 copy-start.4
  652.3 3.4 copy-done.4
  655.7 0.0 copy-done.1
  655.7 15.2 %fusion.5 = f32[512,1024]{1,0:T(8,128)} fusion(f32[512,2048]{1,0:T(8,128)S(1)} %copy-done.1, f32[1024,2048]{1,0:T(8,128)S(1)} %select_add_fusion), kind=kOutput, calls=%fused_computation.17 | convolution fusion | flops 12884901888 | bytes 14680064 | tf_op jit(solution)/shard_map/dot_general | solution.py:45
  670.9 0.0 all-reduce.10.cloned.1.call-update
  671.0 0.0 copy-done.2
  671.0 5.8 fusion.4
  676.8 185.2 %all-reduce.10.cloned.1.call-done = (f32[512,1024]{1,0:T(8,128)}, f32[512,1024]{1,0:T(8,128)}) async-done(((f32[512,1024]{1,0:T(8,128)}, f32[512,1024]{1,0:T(8,128)}), (f32[512,1024]{1,0:T(8,128)}, f32[512,1024]{1,0:T(8,128)})) %all-reduce.10.cloned.1.call-update) | async-done | bytes 4194320 | tf_op jit(solution)/shard_map/psum | solution.py:14
  861.9 2.5 multiply_reduce_fusion
  864.4 67.9 %all-reduce = (f32[512]{0:T(512)S(1)}, f32[512]{0:T(512)S(1)}) all-reduce(f32[512]{0:T(512)S(1)} %broadcast_select_fusion.2, f32[512]{0:T(512)S(1)} %broadcast_select_fusion.1), channel_id=1, replica_groups=mesh['row'=16,'col'=8] {'row','col'}, use_global_device_ids=true, to_apply=%region_2.3 | all-reduce | flops 1024 | bytes 8192 | tf_op jit(solution)/shard_map/psum | solution.py:55
  932.3 0.6 sqrt_add_fusion
  (7 shorter events, 0.0 us)
Async XLA Ops:
  7.2 4.4 copy-start
  7.2 98.6 %all-gather.2.cloned.1.call-start = ((), (), s32[]{:S(2)}) async-start(), calls=%async_computation | async-start | bytes 17825792 | tf_op jit(solution)/shard_map/all_gather | solution.py:29
  11.5 227.1 %all-reduce.8.cloned.1.call-start = ((), (), s32[]{:S(2)}) async-start(), calls=%async_computation.2 | async-start | bytes 8388608 | tf_op jit(solution)/shard_map/psum | solution.py:42
  16.1 568.5 %all-reduce.6.cloned.1.call-start = ((), (), s32[]{:S(2)}) async-start(), calls=%async_computation.1 | async-start | bytes 16777216 | tf_op jit(solution)/shard_map/psum | solution.py:14
  114.5 470.1 %copy-start.3 = (f32[2048]{0:T(1024)S(1)}, f32[2048]{0:T(1024)}, u32[]{:S(2)}) copy-start(f32[2048]{0:T(1024)} %param.8) | copy-start | bytes 24580
  114.5 747.4 %all-reduce.10.cloned.1.call-start = ((), (), s32[]{:S(2)}) async-start(), calls=%async_computation.3 | async-start | bytes 8388608 | tf_op jit(solution)/shard_map/psum | solution.py:14
  584.6 71.1 %copy-start.1 = (f32[512,2048]{1,0:T(8,128)S(1)}, f32[512,2048]{1,0:T(8,128)}, u32[]{:S(2)}) copy-start(f32[512,2048]{1,0:T(8,128)} %all-reduce.8.cloned.1.call-done) | copy-start | bytes 12582916
  652.3 3.4 copy-start.4
  655.7 15.3 %copy-start.2 = (f32[2048]{0:T(1024)S(1)}, f32[2048]{0:T(1024)}, u32[]{:S(2)}) copy-start(f32[2048]{0:T(1024)} %param.11) | copy-start | bytes 24580
Sparse Core Ops, SparseCore 0:
  11.7 94.1 all-gather.1
  108.3 130.2 all-reduce.7
  241.8 342.7 all-reduce.5
  671.1 190.7 all-reduce.9
where the time goes:
time: 944 us; the launch traced here: 940 us
  waiting for transfers between devices  742 us (79%)
  matrix products  93.2 us (10%)
  blocking collectives  67.9 us (7%)
  other arithmetic  18 us (2%)
  between operations  14.1 us (1%)
    psum x2, waiting for transfers between devices, spread(): return lax.psum(kept, axis)  528 us
    psum x1, waiting for transfers between devices, body(): cand_col = lax.psum(picked, 'row')  124 us
    all_gather x1, waiting for transfers between devices, body(): col_all = lax.all_gather(masked, 'row', axis=0, tiled=True)  89.6 us
    psum x1, blocking collectives, body(): quad_all, linear_all = lax.psum((quad, linear), ('row', 'col'))  67.9 us
    dot_general x1, matrix products, body(): lax.dot_general(row_all, col_all, contract, precision=high, preferred_ele...  67.7 us
  transfers between devices with their start and end apart: 4, of which 4 were waited for; matrix products, arithmetic and copies ran while one was open for 2% of the time, Pallas kernels for 0%

commit v1 on v0

v1 whole, which is shorter than its diff:
```python
import jax
import jax.numpy as jnp
from jax import lax
from jax.sharding import PartitionSpec as P

F = 16384

highest = lax.Precision.HIGHEST


def body(shared_rows, event_counts, ridge, items, cand_ids, theta):
    n_row = lax.axis_size("row")
    n_col = lax.axis_size("col")
    ratio = n_row // n_col
    row_pos = lax.axis_index("row")
    col_pos = lax.axis_index("col")
    ev_slots, width_col = shared_rows.shape
    width_row = width_col // ratio
    slot = lax.iota(jnp.int32, ev_slots)
    masked = jnp.where((slot < event_counts[row_pos])[:, None], shared_rows, jnp.float32(0.0))

    col_all = lax.all_gather(masked, "row", axis=0, tiled=True)

    halves = masked.reshape(ev_slots, ratio, width_row)
    received = []
    for t in range(ratio):
        perm = []
        for s in range(n_row):
            for c in range(n_col):
                b = (s % ratio) ^ t
                perm.append((s * n_col + c, (ratio * c + b) * n_col + s // ratio))
        piece = halves[:, (row_pos % ratio) ^ t, :]
        received.append(lax.ppermute(piece, ("row", "col"), perm))
    parity = row_pos % ratio
    ordered = [
        sum(jnp.where(parity ^ t == a, received[t], 0.0) for t in range(ratio))
        for a in range(ratio)
    ]
    row_block = jnp.concatenate(ordered, axis=0)
    row_all = lax.all_gather(row_block, "col", axis=0, tiled=True)

    contract = (((0,), (0,)), ((), ()))
    tile = lax.dot_general(
        row_all, col_all, contract, precision=highest, preferred_element_type=jnp.float32
    )
    rows_global = row_pos * width_row + lax.broadcasted_iota(jnp.int32, (width_row, width_col), 0)
    cols_global = col_pos * width_col + lax.broadcasted_iota(jnp.int32, (width_row, width_col), 1)
    tile = tile + jnp.where(rows_global == cols_global, ridge[None, :], jnp.float32(0.0))

    z_part = lax.dot_general(
        col_all, items, (((1,), (1,)), ((), ())), precision=highest,
        preferred_element_type=jnp.float32,
    )
    z = lax.psum_scatter(z_part, "col", scatter_dimension=0, tiled=True)
    q_ev = jnp.sum(z * z, axis=0)
    q_ridge = jnp.sum(ridge[None, :] * items * items, axis=1)
    lin = jnp.dot(items, theta, precision=highest, preferred_element_type=jnp.float32)
    tot = lax.psum(jnp.stack([q_ev + q_ridge, lin]), "col")
    item_scores = tot[1] + jnp.sqrt(tot[0] / F)
    all_scores = lax.all_gather(item_scores, "row", axis=0, tiled=True)
    scores = all_scores[cand_ids]
    return (tile, scores)


def solution(mesh):
    return jax.shard_map(
        body,
        mesh=mesh,
        in_specs=(P("row", "col"), P(), P("col"), P("row", "col"), P(), P("col")),
        out_specs=(P("row", "col"), P()),
        check_vma=False,
    )
```

time: 944 us -> 394 us (0.42)
  waiting for transfers between devices: 742 us -> 234 us
  blocking collectives: 67.9 us -> 48.7 us
  other arithmetic: 18 us -> 5.53 us
  matrix products: 93.2 us -> 80.8 us
    psum x3 -> x0, waiting for transfers between devices: 652 us -> none  [the longest x2 528 us: spread(): return lax.psum(kept, axis)]
    all_gather x0 -> x1, waiting for transfers between devices: none -> 95.7 us  [body(): row_all = lax.all_gather(row_block, 'col', axis=0, tiled=True)]
    psum x1, blocking collectives: 67.9 us -> 21.6 us  [body(): tot = lax.psum(jnp.stack([q_ev + q_ridge, lin]), 'col')]
    all_gather x1, waiting for transfers between devices: 89.6 us -> 124 us  [body(): col_all = lax.all_gather(masked, 'row', axis=0, tiled=True)]
    all_gather x0 -> x1, blocking collectives: none -> 27.1 us  [body(): all_scores = lax.all_gather(item_scores, 'row', axis=0, tiled=True)]
    reduce_scatter x0 -> x1, waiting for transfers between devices: none -> 12.5 us  [body(): z = lax.psum_scatter(z_part, 'col', scatter_dimension=0, tiled=True)]
    dot_general x4 -> x3, matrix products: 93.2 us -> 80.8 us  [the longest x1 59.7 us: body(): lax.dot_general(row_all, col_all, contract, precision=highest, preferred_...]
    select_n x4 -> x1, other arithmetic: 11.9 us -> 0.01 us  [body(): scores = all_scores[cand_ids]]
  transfers between devices with their start and end apart: 4 -> 5, of which waited for: 4 -> 4; matrix products, arithmetic and copies ran while one was open for 2% -> 22% of each run, Pallas kernels for 0% -> 0%
where the time goes in v1:
time: 394 us; the launch traced here: 393 us
  waiting for transfers between devices  234 us (59%)
  matrix products  80.8 us (21%)
  blocking collectives  48.7 us (12%)
  between operations  14.6 us (4%)
  local copies, waits for them, and re-layouts  8.53 us (2%)
  other arithmetic  5.53 us (1%)
    all_gather x1, waiting for transfers between devices, body(): col_all = lax.all_gather(masked, 'row', axis=0, tiled=True)  124 us
    all_gather x1, waiting for transfers between devices, body(): row_all = lax.all_gather(row_block, 'col', axis=0, tiled=True)  95.7 us
    dot_general x1, matrix products, body(): lax.dot_general(row_all, col_all, contract, precision=highest, preferred_...  59.7 us
    all_gather x1, blocking collectives, body(): all_scores = lax.all_gather(item_scores, 'row', axis=0, tiled=True)  27.1 us
    psum x1, blocking collectives, body(): tot = lax.psum(jnp.stack([q_ev + q_ridge, lin]), 'col')  21.6 us
    dot_general x1, matrix products, body(): lax.dot_general(col_all, items, (((1,), (1,)), ((), ())), precision=highe...  20.6 us
    reduce_scatter x1, waiting for transfers between devices, body(): z = lax.psum_scatter(z_part, 'col', scatter_dimension=0, tiled=True)  12.5 us
  transfers between devices with their start and end apart: 5, of which 4 were waited for; matrix products, arithmetic and copies ran while one was open for 22% of the time, Pallas kernels for 0%

profile of v1, /device:TPU:0, one launch (start us, length us, event | category | flops | bytes accessed | tf_op | source)
XLA Modules:
  0.0 393.0 jit_solution(11862905705845880672)
XLA Ops:
  7.2 0.0 copy-start
  7.2 0.0 all-gather.6.cloned.1.call-start
  7.3 1.3 dynamic_slice.9
  8.6 0.6 iota_compare_fusion
  9.2 2.3 broadcast_select_fusion
  11.6 0.0 all-gather.6.cloned.1.call-update
  11.6 0.0 all-gather.4.cloned.1.call-start
  11.7 2.1 reshape.28
  13.8 0.9 constant_dynamic-slice_fusion.1
  14.7 0.1 copy.13
  14.8 0.7 collective-permute-start
  15.5 0.1 copy.12
  15.6 0.1 collective-permute-start.1
  15.7 1.9 collective-permute-done.1
  17.6 0.2 select_add_fusion.2
  17.8 1.1 pad_maximum_fusion
  18.9 0.0 all-gather.4.cloned.1.call-update
  18.9 0.0 reduce-scatter.2.cloned.1.call-start
  19.0 0.6 dynamic-slice
  20.3 0.2 fusion
  20.5 0.5 fusion.2
  21.0 123.8 %all-gather.6.cloned.1.call-done = f32[2048,2048]{1,0:T(8,128)} async-done(((f32[128,2048]{1,0:T(8,128)}), f32[2048,2048]{1,0:T(8,128)}) %all-gather.6.cloned.1.call-update) | async-done | bytes 16777232 | tf_op jit(solution)/shard_map/all_gather | solution.py:22
  144.8 20.6 %fusion.1 = f32[2048,64]{0,1:T(8,128)} fusion(f32[2048,2048]{1,0:T(8,128)} %all-gather.6.cloned.1.call-done, f32[64,2048]{1,0:T(8,128)S(1)} %copy-done.1), kind=kOutput, calls=%fused_computation.21 | convolution fusion | flops 3221225472 | bytes 17825792 | tf_op jit(solution)/shard_map/dot_general | solution.py:50
  165.3 0.0 reduce-scatter.2.cloned.1.call-update
  165.3 95.7 %all-gather.4.cloned.1.call-done = f32[2048,1024]{1,0:T(8,128)} async-done(((f32[256,1024]{1,0:T(8,128)}), f32[2048,1024]{1,0:T(8,128)}) %all-gather.4.cloned.1.call-update) | async-done | bytes 8388624 | tf_op jit(solution)/shard_map/all_gather | solution.py:40
  261.0 59.7 %select_add_fusion = f32[1024,2048]{1,0:T(8,128)} fusion(f32[2048]{0:T(1024)S(1)} %copy-done.2, s32[2048]{0:T(1024)S(1)} %iota_add_fusion, s32[1024]{0:T(1024)S(1)} %iota_add_fusion.1, f32[2048,1024]{1,0:T(8,128)} %all-gather.4.cloned.1.call-done, f32[2048,2048]{1,0:T(8,128)} %all-gather.6.cloned.1.call-done), kind=kOutput, calls=%fused_computation.1 | convolution fusion | flops 51545899008 | bytes 33574912 | tf_op jit(solution)/shard_map/dot_general | solution.py:43
  320.7 12.5 %reduce-scatter.2.cloned.1.call-done = f32[256,64]{0,1:T(8,128)} async-done(((f32[2048,64]{0,1:T(8,128)}), f32[256,64]{0,1:T(8,128)}) %reduce-scatter.2.cloned.1.call-update) | async-done | bytes 65552 | tf_op jit(solution)/shard_map/reduce_scatter | solution.py:54
  333.3 0.9 multiply_reduce_fusion
  334.2 21.6 %psum.7 = f32[2,64]{1,0:T(2,128)S(1)} all-reduce(f32[2,64]{1,0:T(2,128)S(1)} %pad_maximum_fusion.1), channel_id=1, replica_groups=mesh['row'=16,'col'=8] {'col'}, use_global_device_ids=true, to_apply=%region_3.4 | all-reduce | flops 128 | bytes 1024 | tf_op jit(solution)/shard_map/psum | solution.py:58
  355.8 0.1 bitcast_dynamic-update-slice_fusion
  356.0 27.1 %all-reduce = f32[1024]{0:T(1024)S(1)} all-reduce(f32[1024]{0:T(1024)S(1)} %bitcast_dynamic-update-slice_fusion), channel_id=2, replica_groups=mesh['row'=16,'col'=8] {'row'}, use_global_device_ids=true, to_apply=%add | all-reduce | flops 1024 | bytes 8192 | tf_op jit(solution)/shard_map/all_gather | solution.py:60
  383.1 3.4 gather_fusion
  (17 shorter events, 0.1 us)
Async XLA Ops:
  7.2 13.3 %copy-start = (f32[2048]{0:T(1024)S(1)}, f32[2048]{0:T(1024)}, u32[]{:S(2)}) copy-start(f32[2048]{0:T(1024)} %param.11) | copy-start | bytes 24580
  7.2 11.8 %copy-start.4 = (u32[128]{0:T(128)S(1)}, u32[128]{0:T(128)}, u32[]{:S(2)}) copy-start(u32[128]{0:T(128)} %constant.43) | copy-start | bytes 1540
  7.2 13.1 %copy-start.3 = (s32[512]{0:T(512)S(1)}, s32[512]{0:T(512)}, u32[]{:S(2)}) copy-start(s32[512]{0:T(512)} %param.10) | copy-start | bytes 6148
  7.2 13.1 %copy-start.2 = (f32[2048]{0:T(1024)S(1)}, f32[2048]{0:T(1024)}, u32[]{:S(2)}) copy-start(f32[2048]{0:T(1024)} %param.8) | copy-start | bytes 24580
  7.2 13.1 %copy-start.1 = (f32[64,2048]{1,0:T(8,128)S(1)}, f32[64,2048]{1,0:T(8,128)}, u32[]{:S(2)}) copy-start(f32[64,2048]{1,0:T(8,128)} %param.9) | copy-start | bytes 1572868
  7.2 137.5 %all-gather.6.cloned.1.call-start = ((), (), s32[]{:S(2)}) async-start(), calls=%async_computation.2 | async-start | bytes 17825792 | tf_op jit(solution)/shard_map/all_gather | solution.py:22
  11.6 249.4 %all-gather.4.cloned.1.call-start = ((), (), s32[]{:S(2)}) async-start(), calls=%async_computation.1 | async-start | bytes 9437184 | tf_op jit(solution)/shard_map/all_gather | solution.py:40
  14.8 0.9 collective-permute-start
  15.6 2.0 collective-permute-start.1
  18.9 314.3 %reduce-scatter.2.cloned.1.call-start = ((), (), s32[]{:S(2)}) async-start(), calls=%async_computation.3 | async-start | bytes 589824 | tf_op jit(solution)/shard_map/reduce_scatter | solution.py:54
Sparse Core Ops, SparseCore 0:
  11.7 133.0 all-gather.5
  147.1 113.8 all-gather.3
  264.6 68.6 reduce-scatter.1

commit v2 on v1

--- a/solution.py
+++ b/solution.py
@@ -6,6 +6,7 @@
 F = 16384
 
 highest = lax.Precision.HIGHEST
+high = lax.Precision.HIGH
 
 
 def body(shared_rows, event_counts, ridge, items, cand_ids, theta):
@@ -37,27 +38,52 @@
         for a in range(ratio)
     ]
     row_block = jnp.concatenate(ordered, axis=0)
-    row_all = lax.all_gather(row_block, "col", axis=0, tiled=True)
+
+    n_y = n_col // 2
+    ring = [y * 2 for y in range(n_y)] + [y * 2 + 1 for y in reversed(range(n_y))]
+    where_in_ring = [ring.index(c) for c in range(n_col)]
+    forward = [(ring[p], ring[(p + 1) % n_col]) for p in range(n_col)]
+    backward = [(ring[p], ring[(p - 1) % n_col]) for p in range(n_col)]
+    block_rows = row_block.shape[0]
+    half_rows = block_rows // 2
+    ring_tab = jnp.array(ring, jnp.int32)
+    me = jnp.array(where_in_ring, jnp.int32)[col_pos]
+    row_all = jnp.zeros((n_col * block_rows, width_row), jnp.float32)
+    ahead, behind = row_block[:half_rows], row_block[half_rows:]
+    row_all = lax.dynamic_update_slice_in_dim(row_all, ahead, col_pos * block_rows, 0)
+    row_all = lax.dynamic_update_slice_in_dim(row_all, behind, col_pos * block_rows + half_rows, 0)
+    for k in range(1, n_col):
+        ahead = lax.ppermute(ahead, "col", forward)
+        behind = lax.ppermute(behind, "col", backward)
+        from_ahead = ring_tab[(me - k) % n_col]
+        from_behind = ring_tab[(me + k) % n_col]
+        row_all = lax.dynamic_update_slice_in_dim(row_all, ahead, from_ahead * block_rows, 0)
+        row_all = lax.dynamic_update_slice_in_dim(
+            row_all, behind, from_behind * block_rows + half_rows, 0
+        )
 
     contract = (((0,), (0,)), ((), ()))
     tile = lax.dot_general(
-        row_all, col_all, contract, precision=highest, preferred_element_type=jnp.float32
+        row_all, col_all, contract, precision=high, preferred_element_type=jnp.float32
     )
     rows_global = row_pos * width_row + lax.broadcasted_iota(jnp.int32, (width_row, width_col), 0)
     cols_global = col_pos * width_col + lax.broadcasted_iota(jnp.int32, (width_row, width_col), 1)
     tile = tile + jnp.where(rows_global == cols_global, ridge[None, :], jnp.float32(0.0))
 
     z_part = lax.dot_general(
-        col_all, items, (((1,), (1,)), ((), ())), precision=highest,
+        col_all, items, (((1,), (1,)), ((), ())), precision=high,
         preferred_element_type=jnp.float32,
     )
     z = lax.psum_scatter(z_part, "col", scatter_dimension=0, tiled=True)
     q_ev = jnp.sum(z * z, axis=0)
     q_ridge = jnp.sum(ridge[None, :] * items * items, axis=1)
     lin = jnp.dot(items, theta, precision=highest, preferred_element_type=jnp.float32)
-    tot = lax.psum(jnp.stack([q_ev + q_ridge, lin]), "col")
-    item_scores = tot[1] + jnp.sqrt(tot[0] / F)
-    all_scores = lax.all_gather(item_scores, "row", axis=0, tiled=True)
+    items_dev = items.shape[0]
+    mine = jnp.stack([q_ev + q_ridge, lin])
+    slot_of = lax.broadcasted_iota(jnp.int32, (2, n_row * items_dev), 1) // items_dev
+    spread_out = jnp.where(slot_of == row_pos, jnp.tile(mine, (1, n_row)), jnp.float32(0.0))
+    tot = lax.psum(spread_out, ("row", "col"))
+    all_scores = tot[1] + jnp.sqrt(tot[0] / F)
     scores = all_scores[cand_ids]
     return (tile, scores)
 

time: 394 us -> 394 us (level)
  waiting for transfers between devices: 234 us -> 136 us
  starting transfers between devices: 0.9 us -> 76.3 us
  matrix products: 80.8 us -> 46.5 us
  local copies, waits for them, and re-layouts: 8.53 us -> 30.7 us
  between operations: 14.6 us -> 32.7 us
  blocking collectives: 48.7 us -> 64.7 us
    all_gather x1, waiting for transfers between devices: 124 us -> 0.01 us  [body(): col_all = lax.all_gather(masked, 'row', axis=0, tiled=True)]
    all_gather x1 -> x0, waiting for transfers between devices: 95.7 us -> none  [body(): row_all = lax.all_gather(row_block, 'col', axis=0, tiled=True)]
    ppermute x0 -> x14, waiting for transfers between devices: none -> 93.8 us  [the longest x7 56.2 us: body(): ahead = lax.ppermute(ahead, 'col', forward)]
    ppermute x0 -> x14, starting transfers between devices: none -> 75.4 us  [the longest x7 46.9 us: body(): ahead = lax.ppermute(ahead, 'col', forward)]
    psum x1, blocking collectives: 21.6 us -> 64.7 us  [body(): tot = lax.psum(spread_out, ('row', 'col'))]
    dot_general x2, matrix products: 80.3 us -> 46 us  [the longest x1 33.9 us: body(): lax.dot_general(row_all, col_all, contract, precision=high, preferred_ele...]
    reduce_scatter x1, waiting for transfers between devices: 12.5 us -> 40.4 us  [body(): z = lax.psum_scatter(z_part, 'col', scatter_dimension=0, tiled=True)]
    all_gather x1 -> x0, blocking collectives: 27.1 us -> none  [body(): all_scores = lax.all_gather(item_scores, 'row', axis=0, tiled=True)]
  transfers between devices with their start and end apart: 5 -> 18, of which waited for: 4 -> 14; matrix products, arithmetic and copies ran while one was open for 22% -> 16% of each run, Pallas kernels for 0% -> 0%
where the time goes in v2:
time: 394 us; the launch traced here: 393 us
  waiting for transfers between devices  136 us (35%)
  starting transfers between devices  76.3 us (19%)
  blocking collectives  64.7 us (16%)
  matrix products  46.5 us (12%)
  between operations  32.7 us (8%)
  local copies, waits for them, and re-layouts  30.7 us (8%)
  other arithmetic  6.02 us (2%)
    psum x1, blocking collectives, body(): tot = lax.psum(spread_out, ('row', 'col'))  64.7 us
    ppermute x7, waiting for transfers between devices, body(): ahead = lax.ppermute(ahead, 'col', forward)  56.2 us
    ppermute x7, starting transfers between devices, body(): ahead = lax.ppermute(ahead, 'col', forward)  46.9 us
    reduce_scatter x1, waiting for transfers between devices, body(): z = lax.psum_scatter(z_part, 'col', scatter_dimension=0, tiled=True)  40.4 us
    ppermute x7, waiting for transfers between devices, body(): behind = lax.ppermute(behind, 'col', backward)  37.7 us
    dot_general x1, matrix products, body(): lax.dot_general(row_all, col_all, contract, precision=high, preferred_ele...  33.9 us
    ppermute x7, starting transfers between devices, body(): behind = lax.ppermute(behind, 'col', backward)  28.5 us
    dot_general x1, matrix products, body(): lax.dot_general(col_all, items, (((1,), (1,)), ((), ())), precision=high,...  12.1 us
  transfers between devices with their start and end apart: 18, of which 14 were waited for; matrix products, arithmetic and copies ran while one was open for 16% of the time, Pallas kernels for 0%

profile of v2, /device:TPU:0, one launch (start us, length us, event | category | flops | bytes accessed | tf_op | source)
XLA Modules:
  0.0 393.1 jit_solution(7386860929162320634)
XLA Ops:
  9.1 2.3 broadcast_select_fusion
  11.6 2.1 reshape.116
  15.7 1.9 collective-permute-done.1
  17.6 4.3 %broadcast_in_dim.44 = f32[2048,1024]{1,0:T(8,128)} broadcast(f32[]{:T(128)} %constant.174.clone.1), dimensions={} | broadcast | bytes 8388612 | tf_op jit(solution)/shard_map/broadcast_in_dim | solution.py:51
  22.8 46.1 %collective-permute-start.2 = (f32[128,1024]{1,0:T(8,128)S(1)}, f32[128,1024]{1,0:T(8,128)S(1)}, u32[]{:S(2)}, u32[]{:S(2)}) collective-permute-start(f32[128,1024]{1,0:T(8,128)S(1)} %get-tuple-element.5), channel_id=1, source_target_pairs={{0,2},{2,4},{4,6},{6,7},{7,5},{5,3},{3,1},{1,0},{8,10},{10,12},{12... | collective-permute-start | bytes 1572872 | tf_op jit(solution)/shard_map/ppermute | solution.py:56
  69.8 4.6 %collective-permute-start.3 = (f32[128,1024]{1,0:T(8,128)S(1)}, f32[128,1024]{1,0:T(8,128)S(1)}, u32[]{:S(2)}, u32[]{:S(2)}) collective-permute-start(f32[128,1024]{1,0:T(8,128)S(1)} %get-tuple-element.3), channel_id=1, source_target_pairs={{0,1},{2,0},{4,2},{6,4},{7,6},{5,7},{3,5},{1,3},{8,9},{10,8},{12,1... | collective-permute-start | bytes 1572872 | tf_op jit(solution)/shard_map/ppermute | solution.py:57
  74.4 15.9 %collective-permute-done.2 = f32[128,1024]{1,0:T(8,128)S(1)} collective-permute-done((f32[128,1024]{1,0:T(8,128)S(1)}, f32[128,1024]{1,0:T(8,128)S(1)}, u32[]{:S(2)}, u32[]{:S(2)}) %collective-permute-start.2) | collective-permute-done | bytes 524320 | tf_op jit(solution)/shard_map/ppermute | solution.py:56
  90.3 7.0 %collective-permute-done.3 = f32[128,1024]{1,0:T(8,128)S(1)} collective-permute-done((f32[128,1024]{1,0:T(8,128)S(1)}, f32[128,1024]{1,0:T(8,128)S(1)}, u32[]{:S(2)}, u32[]{:S(2)}) %collective-permute-start.3) | collective-permute-done | bytes 524320 | tf_op jit(solution)/shard_map/ppermute | solution.py:57
  97.3 4.0 %collective-permute-start.5 = (f32[128,1024]{1,0:T(8,128)S(1)}, f32[128,1024]{1,0:T(8,128)S(1)}, u32[]{:S(2)}, u32[]{:S(2)}) collective-permute-start(f32[128,1024]{1,0:T(8,128)S(1)} %collective-permute-done.3), channel_id=1, source_target_pairs={{0,1},{2,0},{4,2},{6,4},{7,6},{5,7},{3,5},{1,3},{8,9},{10,8},{12,1... | collective-permute-start | bytes 1572872 | tf_op jit(solution)/shard_map/ppermute | solution.py:57
  101.2 14.8 %collective-permute-done.4 = f32[128,1024]{1,0:T(8,128)S(1)} collective-permute-done((f32[128,1024]{1,0:T(8,128)S(1)}, f32[128,1024]{1,0:T(8,128)S(1)}, u32[]{:S(2)}, u32[]{:S(2)}) %collective-permute-start.4) | collective-permute-done | bytes 524320 | tf_op jit(solution)/shard_map/ppermute | solution.py:56
  116.0 8.5 %collective-permute-done.5 = f32[128,1024]{1,0:T(8,128)S(1)} collective-permute-done((f32[128,1024]{1,0:T(8,128)S(1)}, f32[128,1024]{1,0:T(8,128)S(1)}, u32[]{:S(2)}, u32[]{:S(2)}) %collective-permute-start.5) | collective-permute-done | bytes 524320 | tf_op jit(solution)/shard_map/ppermute | solution.py:57
  124.5 4.0 %collective-permute-start.7 = (f32[128,1024]{1,0:T(8,128)S(1)}, f32[128,1024]{1,0:T(8,128)}, u32[]{:S(2)}, u32[]{:S(2)}) collective-permute-start(f32[128,1024]{1,0:T(8,128)S(1)} %collective-permute-done.5), channel_id=1, source_target_pairs={{0,1},{2,0},{4,2},{6,4},{7,6},{5,7},{3,5},{1,3},{8,9},{10,8},{12,1... | collective-permute-start | bytes 1572872 | tf_op jit(solution)/shard_map/ppermute | solution.py:57
  128.5 13.7 %collective-permute-done.6 = f32[128,1024]{1,0:T(8,128)S(1)} collective-permute-done((f32[128,1024]{1,0:T(8,128)S(1)}, f32[128,1024]{1,0:T(8,128)S(1)}, u32[]{:S(2)}, u32[]{:S(2)}) %collective-permute-start.6) | collective-permute-done | bytes 524320 | tf_op jit(solution)/shard_map/ppermute | solution.py:56
  142.2 9.7 %collective-permute-done.7 = f32[128,1024]{1,0:T(8,128)} collective-permute-done((f32[128,1024]{1,0:T(8,128)S(1)}, f32[128,1024]{1,0:T(8,128)}, u32[]{:S(2)}, u32[]{:S(2)}) %collective-permute-start.7) | collective-permute-done | bytes 524320 | tf_op jit(solution)/shard_map/ppermute | solution.py:57
  151.9 4.1 %collective-permute-start.9 = (f32[128,1024]{1,0:T(8,128)}, f32[128,1024]{1,0:T(8,128)}, u32[]{:S(2)}, u32[]{:S(2)}) collective-permute-start(f32[128,1024]{1,0:T(8,128)} %collective-permute-done.7), channel_id=1, source_target_pairs={{0,1},{2,0},{4,2},{6,4},{7,6},{5,7},{3,5},{1,3},{8,9},{10,8},{12,1... | collective-permute-start | bytes 1572872 | tf_op jit(solution)/shard_map/ppermute | solution.py:57
  156.5 10.1 %collective-permute-done.8 = f32[128,1024]{1,0:T(8,128)} collective-permute-done((f32[128,1024]{1,0:T(8,128)S(1)}, f32[128,1024]{1,0:T(8,128)}, u32[]{:S(2)}, u32[]{:S(2)}) %collective-permute-start.8) | collective-permute-done | bytes 524320 | tf_op jit(solution)/shard_map/ppermute | solution.py:56
  173.9 5.5 %collective-permute-done.9 = f32[128,1024]{1,0:T(8,128)} collective-permute-done((f32[128,1024]{1,0:T(8,128)}, f32[128,1024]{1,0:T(8,128)}, u32[]{:S(2)}, u32[]{:S(2)}) %collective-permute-start.9) | collective-permute-done | bytes 524320 | tf_op jit(solution)/shard_map/ppermute | solution.py:57
  179.4 4.0 %collective-permute-start.11 = (f32[128,1024]{1,0:T(8,128)}, f32[128,1024]{1,0:T(8,128)}, u32[]{:S(2)}, u32[]{:S(2)}) collective-permute-start(f32[128,1024]{1,0:T(8,128)} %collective-permute-done.9), channel_id=1, source_target_pairs={{0,1},{2,0},{4,2},{6,4},{7,6},{5,7},{3,5},{1,3},{8,9},{10,8},{12,1... | collective-permute-start | bytes 1572872 | tf_op jit(solution)/shard_map/ppermute | solution.py:57
  198.6 2.3 collective-permute-done.11
  200.9 4.0 %collective-permute-start.13 = (f32[128,1024]{1,0:T(8,128)}, f32[128,1024]{1,0:T(8,128)S(1)}, u32[]{:S(2)}, u32[]{:S(2)}) collective-permute-start(f32[128,1024]{1,0:T(8,128)} %collective-permute-done.11), channel_id=1, source_target_pairs={{0,1},{2,0},{4,2},{6,4},{7,6},{5,7},{3,5},{1,3},{8,9},{10,8},{12,1... | collective-permute-start | bytes 1572872 | tf_op jit(solution)/shard_map/ppermute | solution.py:57
  206.5 1.9 constant_dynamic-update-slice_fusion.8
  208.4 1.9 constant_dynamic-update-slice_fusion.7
  212.9 1.9 constant_dynamic-update-slice_fusion.6
  216.0 3.9 collective-permute-start.15
  219.9 1.9 constant_dynamic-update-slice_fusion.5
  221.7 1.9 constant_dynamic-update-slice_fusion.4
  226.2 3.6 collective-permute-done.15
  230.6 12.1 %fusion.7 = f32[2048,64]{0,1:T(8,128)} fusion(f32[2048,2048]{1,0:T(8,128)} %all-gather.2.cloned.1.call-done, f32[64,2048]{1,0:T(8,128)S(1)} %copy-done.1), kind=kOutput, calls=%fused_computation.47 | convolution fusion | flops 1610612736 | bytes 17825792 | tf_op jit(solution)/shard_map/dot_general | solution.py:73
  242.7 33.9 %select_add_fusion = f32[1024,2048]{1,0:T(8,128)} fusion(f32[2048]{0:T(1024)S(1)} %copy-done.3, s32[2048]{0:T(1024)S(1)} %iota_add_fusion, s32[1024]{0:T(1024)S(1)} %iota_add_fusion.1, f32[2048,1024]{1,0:T(8,128)} %constant_dynamic-update-slice_fusion, f32[2048,2048]{1,0:T(8,128)} %all-gather.2.cloned.1.call-done), kind=kOutput, calls=%fused_computation.1 | convolution fusion | flops 25776095232 | bytes 33574912 | tf_op jit(solution)/shard_map/dot_general | solution.py:66
  276.6 40.4 %reduce-scatter.2.cloned.1.call-done = f32[256,64]{0,1:T(8,128)} async-done(((f32[2048,64]{0,1:T(8,128)}), f32[256,64]{0,1:T(8,128)}) %reduce-scatter.2.cloned.1.call-update) | async-done | bytes 65552 | tf_op jit(solution)/shard_map/reduce_scatter | solution.py:77
  318.1 64.7 %psum.7 = f32[2,1024]{1,0:T(2,128)S(1)} all-reduce(f32[2,1024]{1,0:T(2,128)S(1)} %compare_select_fusion), channel_id=1, replica_groups=mesh['row'=16,'col'=8] {'row','col'}, use_global_device_ids=true, to_apply=%region_3.4 | all-reduce | flops 2048 | bytes 16384 | tf_op jit(solution)/shard_map/psum | solution.py:85
  382.8 3.4 gather_fusion
  (63 shorter events, 20.2 us)
Async XLA Ops:
  7.2 148.8 %copy-start = (f32[2048]{0:T(1024)S(1)}, f32[2048]{0:T(1024)}, u32[]{:S(2)}) copy-start(f32[2048]{0:T(1024)} %param.13) | copy-start | bytes 24580
  7.2 223.4 %all-gather.2.cloned.1.call-start = ((), (), s32[]{:S(2)}) async-start(), calls=%async_computation.1 | async-start | bytes 17825792 | tf_op jit(solution)/shard_map/all_gather | solution.py:23
  11.5 305.5 %reduce-scatter.2.cloned.1.call-start = ((), (), s32[]{:S(2)}) async-start(), calls=%async_computation.2 | async-start | bytes 589824 | tf_op jit(solution)/shard_map/reduce_scatter | solution.py:77
  13.7 128.5 %copy-start.4 = (s32[512]{0:T(512)S(1)}, s32[512]{0:T(512)}, u32[]{:S(2)}) copy-start(s32[512]{0:T(512)} %param.12) | copy-start | bytes 6148
  13.7 142.3 %copy-start.1 = (f32[64,2048]{1,0:T(8,128)S(1)}, f32[64,2048]{1,0:T(8,128)}, u32[]{:S(2)}) copy-start(f32[64,2048]{1,0:T(8,128)} %param.11) | copy-start | bytes 1572868
  13.7 152.9 %copy-start.5 = (s32[8]{0:T(128)S(1)}, s32[8]{0:T(128)}, u32[]{:S(2)}) copy-start(s32[8]{0:T(128)} %constant.211.clone) | copy-start | bytes 100
  14.6 171.5 %copy-start.2 = (s32[8]{0:T(128)S(1)}, s32[8]{0:T(128)}, u32[]{:S(2)}) copy-start(s32[8]{0:T(128)} %constant.210.clone) | copy-start | bytes 100
  14.6 181.3 %copy-start.3 = (f32[2048]{0:T(1024)S(1)}, f32[2048]{0:T(1024)}, u32[]{:S(2)}) copy-start(f32[2048]{0:T(1024)} %param.10) | copy-start | bytes 24580
  14.8 0.9 collective-permute-start
  15.6 2.0 collective-permute-start.1
  22.8 67.5 %collective-permute-start.2 = (f32[128,1024]{1,0:T(8,128)S(1)}, f32[128,1024]{1,0:T(8,128)S(1)}, u32[]{:S(2)}, u32[]{:S(2)}) collective-permute-start(f32[128,1024]{1,0:T(8,128)S(1)} %get-tuple-element.5), channel_id=1, source_target_pairs={{0,2},{2,4},{4,6},{6,7},{7,5},{5,3},{3,1},{1,0},{8,10},{10,12},{12... | collective-permute-start | bytes 1572872 | tf_op jit(solution)/shard_map/ppermute | solution.py:56
  69.8 27.4 %collective-permute-start.3 = (f32[128,1024]{1,0:T(8,128)S(1)}, f32[128,1024]{1,0:T(8,128)S(1)}, u32[]{:S(2)}, u32[]{:S(2)}) collective-permute-start(f32[128,1024]{1,0:T(8,128)S(1)} %get-tuple-element.3), channel_id=1, source_target_pairs={{0,1},{2,0},{4,2},{6,4},{7,6},{5,7},{3,5},{1,3},{8,9},{10,8},{12,1... | collective-permute-start | bytes 1572872 | tf_op jit(solution)/shard_map/ppermute | solution.py:57
  90.3 25.8 %collective-permute-start.4 = (f32[128,1024]{1,0:T(8,128)S(1)}, f32[128,1024]{1,0:T(8,128)S(1)}, u32[]{:S(2)}, u32[]{:S(2)}) collective-permute-start(f32[128,1024]{1,0:T(8,128)S(1)} %collective-permute-done.2), channel_id=1, source_target_pairs={{0,2},{2,4},{4,6},{6,7},{7,5},{5,3},{3,1},{1,0},{8,10},{10,12},{12... | collective-permute-start | bytes 1572872 | tf_op jit(solution)/shard_map/ppermute | solution.py:56
  97.3 27.2 %collective-permute-start.5 = (f32[128,1024]{1,0:T(8,128)S(1)}, f32[128,1024]{1,0:T(8,128)S(1)}, u32[]{:S(2)}, u32[]{:S(2)}) collective-permute-start(f32[128,1024]{1,0:T(8,128)S(1)} %collective-permute-done.3), channel_id=1, source_target_pairs={{0,1},{2,0},{4,2},{6,4},{7,6},{5,7},{3,5},{1,3},{8,9},{10,8},{12,1... | collective-permute-start | bytes 1572872 | tf_op jit(solution)/shard_map/ppermute | solution.py:57
  116.0 26.1 %collective-permute-start.6 = (f32[128,1024]{1,0:T(8,128)S(1)}, f32[128,1024]{1,0:T(8,128)S(1)}, u32[]{:S(2)}, u32[]{:S(2)}) collective-permute-start(f32[128,1024]{1,0:T(8,128)S(1)} %collective-permute-done.4), channel_id=1, source_target_pairs={{0,2},{2,4},{4,6},{6,7},{7,5},{5,3},{3,1},{1,0},{8,10},{10,12},{12... | collective-permute-start | bytes 1572872 | tf_op jit(solution)/shard_map/ppermute | solution.py:56
  124.5 27.4 %collective-permute-start.7 = (f32[128,1024]{1,0:T(8,128)S(1)}, f32[128,1024]{1,0:T(8,128)}, u32[]{:S(2)}, u32[]{:S(2)}) collective-permute-start(f32[128,1024]{1,0:T(8,128)S(1)} %collective-permute-done.5), channel_id=1, source_target_pairs={{0,1},{2,0},{4,2},{6,4},{7,6},{5,7},{3,5},{1,3},{8,9},{10,8},{12,1... | collective-permute-start | bytes 1572872 | tf_op jit(solution)/shard_map/ppermute | solution.py:57
  142.1 24.5 %collective-permute-start.8 = (f32[128,1024]{1,0:T(8,128)S(1)}, f32[128,1024]{1,0:T(8,128)}, u32[]{:S(2)}, u32[]{:S(2)}) collective-permute-start(f32[128,1024]{1,0:T(8,128)S(1)} %collective-permute-done.6), channel_id=1, source_target_pairs={{0,2},{2,4},{4,6},{6,7},{7,5},{5,3},{3,1},{1,0},{8,10},{10,12},{12... | collective-permute-start | bytes 1572872 | tf_op jit(solution)/shard_map/ppermute | solution.py:56
  151.9 27.5 %collective-permute-start.9 = (f32[128,1024]{1,0:T(8,128)}, f32[128,1024]{1,0:T(8,128)}, u32[]{:S(2)}, u32[]{:S(2)}) collective-permute-start(f32[128,1024]{1,0:T(8,128)} %collective-permute-done.7), channel_id=1, source_target_pairs={{0,1},{2,0},{4,2},{6,4},{7,6},{5,7},{3,5},{1,3},{8,9},{10,8},{12,1... | collective-permute-start | bytes 1572872 | tf_op jit(solution)/shard_map/ppermute | solution.py:57
  166.6 31.1 %collective-permute-start.10 = (f32[128,1024]{1,0:T(8,128)}, f32[128,1024]{1,0:T(8,128)}, u32[]{:S(2)}, u32[]{:S(2)}) collective-permute-start(f32[128,1024]{1,0:T(8,128)} %collective-permute-done.8), channel_id=1, source_target_pairs={{0,2},{2,4},{4,6},{6,7},{7,5},{5,3},{3,1},{1,0},{8,10},{10,12},{12... | collective-permute-start | bytes 1572872 | tf_op jit(solution)/shard_map/ppermute | solution.py:56
  179.4 21.4 %collective-permute-start.11 = (f32[128,1024]{1,0:T(8,128)}, f32[128,1024]{1,0:T(8,128)}, u32[]{:S(2)}, u32[]{:S(2)}) collective-permute-start(f32[128,1024]{1,0:T(8,128)} %collective-permute-done.9), channel_id=1, source_target_pairs={{0,1},{2,0},{4,2},{6,4},{7,6},{5,7},{3,5},{1,3},{8,9},{10,8},{12,1... | collective-permute-start | bytes 1572872 | tf_op jit(solution)/shard_map/ppermute | solution.py:57
  197.8 14.3 %collective-permute-start.12 = (f32[128,1024]{1,0:T(8,128)}, f32[128,1024]{1,0:T(8,128)S(1)}, u32[]{:S(2)}, u32[]{:S(2)}) collective-permute-start(f32[128,1024]{1,0:T(8,128)} %collective-permute-done.10), channel_id=1, source_target_pairs={{0,2},{2,4},{4,6},{6,7},{7,5},{5,3},{3,1},{1,0},{8,10},{10,12},{12... | collective-permute-start | bytes 1572872 | tf_op jit(solution)/shard_map/ppermute | solution.py:56
  200.9 15.1 %collective-permute-start.13 = (f32[128,1024]{1,0:T(8,128)}, f32[128,1024]{1,0:T(8,128)S(1)}, u32[]{:S(2)}, u32[]{:S(2)}) collective-permute-start(f32[128,1024]{1,0:T(8,128)} %collective-permute-done.11), channel_id=1, source_target_pairs={{0,1},{2,0},{4,2},{6,4},{7,6},{5,7},{3,5},{1,3},{8,9},{10,8},{12,1... | collective-permute-start | bytes 1572872 | tf_op jit(solution)/shard_map/ppermute | solution.py:57
  212.0 13.3 %collective-permute-start.14 = (f32[128,1024]{1,0:T(8,128)S(1)}, f32[128,1024]{1,0:T(8,128)S(1)}, u32[]{:S(2)}, u32[]{:S(2)}) collective-permute-start(f32[128,1024]{1,0:T(8,128)S(1)} %collective-permute-done.12), channel_id=1, source_target_pairs={{0,2},{2,4},{4,6},{6,7},{7,5},{5,3},{3,1},{1,0},{8,10},{10,12},{12... | collective-permute-start | bytes 1572872 | tf_op jit(solution)/shard_map/ppermute | solution.py:56
  216.0 13.8 %collective-permute-start.15 = (f32[128,1024]{1,0:T(8,128)S(1)}, f32[128,1024]{1,0:T(8,128)S(1)}, u32[]{:S(2)}, u32[]{:S(2)}) collective-permute-start(f32[128,1024]{1,0:T(8,128)S(1)} %collective-permute-done.13), channel_id=1, source_target_pairs={{0,1},{2,0},{4,2},{6,4},{7,6},{5,7},{3,5},{1,3},{8,9},{10,8},{12,1... | collective-permute-start | bytes 1572872 | tf_op jit(solution)/shard_map/ppermute | solution.py:57
Sparse Core Ops, SparseCore 0:
  11.6 184.1 all-gather.1
  242.8 74.0 reduce-scatter.1

commit v3 on v2

--- a/solution.py
+++ b/solution.py
@@ -74,17 +74,28 @@
         col_all, items, (((1,), (1,)), ((), ())), precision=high,
         preferred_element_type=jnp.float32,
     )
-    z = lax.psum_scatter(z_part, "col", scatter_dimension=0, tiled=True)
-    q_ev = jnp.sum(z * z, axis=0)
     q_ridge = jnp.sum(ridge[None, :] * items * items, axis=1)
     lin = jnp.dot(items, theta, precision=highest, preferred_element_type=jnp.float32)
+    packed = jnp.concatenate([z_part, q_ridge[None, :], lin[None, :]], axis=0)
+    step = n_col // 2
+    while step >= 1:
+        pairs = [(c, c ^ step) for c in range(n_col)]
+        packed = packed + lax.ppermute(packed, "col", pairs)
+        step //= 2
+    ev_all = z_part.shape[0]
+    z = packed[:ev_all]
+    quad = jnp.sum(z * z, axis=0) + packed[ev_all]
+    item_scores = packed[ev_all + 1] + jnp.sqrt(quad / F)
     items_dev = items.shape[0]
-    mine = jnp.stack([q_ev + q_ridge, lin])
-    slot_of = lax.broadcasted_iota(jnp.int32, (2, n_row * items_dev), 1) // items_dev
-    spread_out = jnp.where(slot_of == row_pos, jnp.tile(mine, (1, n_row)), jnp.float32(0.0))
-    tot = lax.psum(spread_out, ("row", "col"))
-    all_scores = tot[1] + jnp.sqrt(tot[0] / F)
-    scores = all_scores[cand_ids]
+    held = item_scores
+    step = 1
+    while step < n_row:
+        pairs = [(r, r ^ step) for r in range(n_row)]
+        other = lax.ppermute(held, "row", pairs)
+        low = (row_pos & step) == 0
+        held = jnp.where(low, jnp.concatenate([held, other]), jnp.concatenate([other, held]))
+        step *= 2
+    scores = held[cand_ids]
     return (tile, scores)
 
 

time: 394 us -> 324 us (0.82)
  blocking collectives: 64.7 us -> 0 us
  waiting for transfers between devices: 136 us -> 126 us
    psum x1 -> x0, blocking collectives: 64.7 us -> none  [body(): tot = lax.psum(spread_out, ('row', 'col'))]
    reduce_scatter x1 -> x0, waiting for transfers between devices: 40.4 us -> none  [body(): z = lax.psum_scatter(z_part, 'col', scatter_dimension=0, tiled=True)]
    all_gather x1, waiting for transfers between devices: 0.01 us -> 32.5 us  [body(): col_all = lax.all_gather(masked, 'row', axis=0, tiled=True)]
    ppermute x0 -> x7, waiting for transfers between devices: none -> 28.7 us  [the longest x3 24.2 us: body(): packed = packed + lax.ppermute(packed, 'col', pairs)]
    ppermute x7, waiting for transfers between devices: 37.7 us -> 12.9 us  [body(): behind = lax.ppermute(behind, 'col', backward)]
    ppermute x7, starting transfers between devices: 28.5 us -> 20.9 us  [body(): behind = lax.ppermute(behind, 'col', backward)]
    ppermute x7, waiting for transfers between devices: 56.2 us -> 50.7 us  [body(): ahead = lax.ppermute(ahead, 'col', forward)]
    ppermute x7, starting transfers between devices: 46.9 us -> 52.2 us  [body(): ahead = lax.ppermute(ahead, 'col', forward)]
  transfers between devices with their start and end apart: 18 -> 24, of which waited for: 14 -> 16; matrix products, arithmetic and copies ran while one was open for 16% -> 24% of each run, Pallas kernels for 0% -> 0%
where the time goes in v3:
time: 324 us
  waiting for transfers between devices  126 us (39%)
  starting transfers between devices  79.1 us (24%)
  matrix products  48.1 us (15%)
  local copies, waits for them, and re-layouts  32.5 us (10%)
  between operations  32.4 us (10%)
  other arithmetic  5.48 us (2%)
    ppermute x7, starting transfers between devices, body(): ahead = lax.ppermute(ahead, 'col', forward)  52.2 us
    ppermute x7, waiting for transfers between devices, body(): ahead = lax.ppermute(ahead, 'col', forward)  50.7 us
    dot_general x1, matrix products, body(): lax.dot_general(row_all, col_all, contract, precision=high, preferred_ele...  36.3 us
    all_gather x1, waiting for transfers between devices, body(): col_all = lax.all_gather(masked, 'row', axis=0, tiled=True)  32.5 us
    ppermute x3, waiting for transfers between devices, body(): packed = packed + lax.ppermute(packed, 'col', pairs)  24.2 us
    ppermute x7, starting transfers between devices, body(): behind = lax.ppermute(behind, 'col', backward)  20.9 us
    ppermute x7, waiting for transfers between devices, body(): behind = lax.ppermute(behind, 'col', backward)  12.9 us
    dot_general x1, matrix products, body(): lax.dot_general(col_all, items, (((1,), (1,)), ((), ())), precision=high,...  11.3 us
  transfers between devices with their start and end apart: 24, of which 16 were waited for; matrix products, arithmetic and copies ran while one was open for 24% of the time, Pallas kernels for 0%

profile of v3, /device:TPU:0, one launch (start us, length us, event | category | flops | bytes accessed | tf_op | source)
XLA Modules:
  0.0 323.5 jit_solution(15876703623407671301)
XLA Ops:
  7.2 1.2 dynamic_slice.54
  9.1 2.3 broadcast_select_fusion
  11.5 2.1 reshape.96
  16.7 4.4 %broadcast_in_dim.46 = f32[2048,1024]{1,0:T(8,128)} broadcast(f32[]{:T(128)} %constant.159.clone.1), dimensions={} | broadcast | bytes 8388612 | tf_op jit(solution)/shard_map/broadcast_in_dim | solution.py:51
  22.0 43.8 %collective-permute-start.2 = (f32[128,1024]{1,0:T(8,128)S(1)}, f32[128,1024]{1,0:T(8,128)S(1)}, u32[]{:S(2)}, u32[]{:S(2)}) collective-permute-start(f32[128,1024]{1,0:T(8,128)S(1)} %get-tuple-element.7), channel_id=1, source_target_pairs={{0,2},{2,4},{4,6},{6,7},{7,5},{5,3},{3,1},{1,0},{8,10},{10,12},{12... | collective-permute-start | bytes 1572872 | tf_op jit(solution)/shard_map/ppermute | solution.py:56
  66.7 8.6 %collective-permute-start.3 = (f32[128,1024]{1,0:T(8,128)S(1)}, f32[128,1024]{1,0:T(8,128)S(1)}, u32[]{:S(2)}, u32[]{:S(2)}) collective-permute-start(f32[128,1024]{1,0:T(8,128)S(1)} %get-tuple-element.5), channel_id=1, source_target_pairs={{0,1},{2,0},{4,2},{6,4},{7,6},{5,7},{3,5},{1,3},{8,9},{10,8},{12,1... | collective-permute-start | bytes 1572872 | tf_op jit(solution)/shard_map/ppermute | solution.py:57
  75.3 21.9 %collective-permute-done.2 = f32[128,1024]{1,0:T(8,128)S(1)} collective-permute-done((f32[128,1024]{1,0:T(8,128)S(1)}, f32[128,1024]{1,0:T(8,128)S(1)}, u32[]{:S(2)}, u32[]{:S(2)}) %collective-permute-start.2) | collective-permute-done | bytes 524320 | tf_op jit(solution)/shard_map/ppermute | solution.py:56
  97.3 1.2 collective-permute-done.3
  98.5 4.0 %collective-permute-start.5 = (f32[128,1024]{1,0:T(8,128)S(1)}, f32[128,1024]{1,0:T(8,128)S(1)}, u32[]{:S(2)}, u32[]{:S(2)}) collective-permute-start(f32[128,1024]{1,0:T(8,128)S(1)} %collective-permute-done.3), channel_id=1, source_target_pairs={{0,1},{2,0},{4,2},{6,4},{7,6},{5,7},{3,5},{1,3},{8,9},{10,8},{12,1... | collective-permute-start | bytes 1572872 | tf_op jit(solution)/shard_map/ppermute | solution.py:57
  102.5 21.2 %collective-permute-done.4 = f32[128,1024]{1,0:T(8,128)S(1)} collective-permute-done((f32[128,1024]{1,0:T(8,128)S(1)}, f32[128,1024]{1,0:T(8,128)S(1)}, u32[]{:S(2)}, u32[]{:S(2)}) %collective-permute-start.4) | collective-permute-done | bytes 524320 | tf_op jit(solution)/shard_map/ppermute | solution.py:56
  123.6 1.7 collective-permute-done.5
  125.3 4.0 %collective-permute-start.7 = (f32[128,1024]{1,0:T(8,128)S(1)}, f32[128,1024]{1,0:T(8,128)S(1)}, u32[]{:S(2)}, u32[]{:S(2)}) collective-permute-start(f32[128,1024]{1,0:T(8,128)S(1)} %collective-permute-done.5), channel_id=1, source_target_pairs={{0,1},{2,0},{4,2},{6,4},{7,6},{5,7},{3,5},{1,3},{8,9},{10,8},{12,1... | collective-permute-start | bytes 1572872 | tf_op jit(solution)/shard_map/ppermute | solution.py:57
  149.8 2.0 collective-permute-done.7
  151.8 4.0 %collective-permute-start.9 = (f32[128,1024]{1,0:T(8,128)S(1)}, f32[128,1024]{1,0:T(8,128)}, u32[]{:S(2)}, u32[]{:S(2)}) collective-permute-start(f32[128,1024]{1,0:T(8,128)S(1)} %collective-permute-done.7), channel_id=1, source_target_pairs={{0,1},{2,0},{4,2},{6,4},{7,6},{5,7},{3,5},{1,3},{8,9},{10,8},{12,1... | collective-permute-start | bytes 1572872 | tf_op jit(solution)/shard_map/ppermute | solution.py:57
  155.8 32.5 %all-gather.2.cloned.1.call-done = f32[2048,2048]{1,0:T(8,128)} async-done(((f32[128,2048]{1,0:T(8,128)}), f32[2048,2048]{1,0:T(8,128)}) %all-gather.2.cloned.1.call-update) | async-done | bytes 16777232 | tf_op jit(solution)/shard_map/all_gather | solution.py:23
  188.3 11.3 %fusion.3 = f32[2048,64]{0,1:T(8,128)S(1)} fusion(f32[2048,2048]{1,0:T(8,128)} %all-gather.2.cloned.1.call-done, f32[64,2048]{1,0:T(8,128)S(1)} %copy-done.2), kind=kOutput, calls=%fused_computation.42 | convolution fusion | flops 1610612736 | bytes 17825792 | tf_op jit(solution)/shard_map/dot_general | solution.py:73
  199.8 8.4 %collective-permute-start.10 = (f32[128,1024]{1,0:T(8,128)}, f32[128,1024]{1,0:T(8,128)S(1)}, u32[]{:S(2)}, u32[]{:S(2)}) collective-permute-start(f32[128,1024]{1,0:T(8,128)} %collective-permute-done.8), channel_id=1, source_target_pairs={{0,2},{2,4},{4,6},{6,7},{7,5},{5,3},{3,1},{1,0},{8,10},{10,12},{12... | collective-permute-start | bytes 1572872 | tf_op jit(solution)/shard_map/ppermute | solution.py:56
  209.0 7.7 %collective-permute-done.16 = f32[2050,64]{0,1:T(8,128)S(1)} collective-permute-done((f32[2050,64]{0,1:T(8,128)S(1)}, f32[2050,64]{0,1:T(8,128)S(1)}, u32[]{:S(2)}, u32[]{:S(2)}) %collective-permute-start.16) | collective-permute-done | bytes 524832 | tf_op jit(solution)/shard_map/ppermute | solution.py:83
  216.8 4.8 %collective-permute-start.17 = (f32[2050,64]{0,1:T(8,128)S(1)}, f32[2050,64]{0,1:T(8,128)S(1)}, u32[]{:S(2)}, u32[]{:S(2)}) collective-permute-start(f32[2050,64]{0,1:T(8,128)S(1)} %add.424), channel_id=1, source_target_pairs={{0,2},{1,3},{2,0},{3,1},{4,6},{5,7},{6,4},{7,5},{8,10},{9,11},{10,... | collective-permute-start | bytes 1574408 | tf_op jit(solution)/shard_map/ppermute | solution.py:83
  222.5 2.4 constant_dynamic-update-slice_fusion.11
  225.0 2.6 constant_dynamic-update-slice_fusion.10
  227.6 1.9 constant_dynamic-update-slice_fusion.9
  229.5 3.2 collective-permute-done.11
  233.9 10.8 %collective-permute-done.17 = f32[2050,64]{0,1:T(8,128)S(1)} collective-permute-done((f32[2050,64]{0,1:T(8,128)S(1)}, f32[2050,64]{0,1:T(8,128)S(1)}, u32[]{:S(2)}, u32[]{:S(2)}) %collective-permute-start.17) | collective-permute-done | bytes 524832 | tf_op jit(solution)/shard_map/ppermute | solution.py:83
  244.8 1.9 constant_dynamic-update-slice_fusion.7
  246.7 2.0 constant_dynamic-update-slice_fusion.6
  250.4 4.8 %collective-permute-done.13 = f32[128,1024]{1,0:T(8,128)S(1)} collective-permute-done((f32[128,1024]{1,0:T(8,128)S(1)}, f32[128,1024]{1,0:T(8,128)S(1)}, u32[]{:S(2)}, u32[]{:S(2)}) %collective-permute-start.13) | collective-permute-done | bytes 524320 | tf_op jit(solution)/shard_map/ppermute | solution.py:57
  256.1 5.8 %collective-permute-done.18 = f32[2050,64]{0,1:T(8,128)S(1)} collective-permute-done((f32[2050,64]{0,1:T(8,128)S(1)}, f32[2050,64]{0,1:T(8,128)S(1)}, u32[]{:S(2)}, u32[]{:S(2)}) %collective-permute-start.18) | collective-permute-done | bytes 524832 | tf_op jit(solution)/shard_map/ppermute | solution.py:83
  263.6 7.3 %collective-permute-done.14 = f32[128,1024]{1,0:T(8,128)S(1)} collective-permute-done((f32[128,1024]{1,0:T(8,128)S(1)}, f32[128,1024]{1,0:T(8,128)S(1)}, u32[]{:S(2)}, u32[]{:S(2)}) %collective-permute-start.14) | collective-permute-done | bytes 524320 | tf_op jit(solution)/shard_map/ppermute | solution.py:56
  272.7 4.2 %collective-permute-done.21 = f32[256]{0:T(256)S(1)} collective-permute-done((f32[256]{0:T(256)S(1)}, f32[256]{0:T(256)S(1)}, u32[]{:S(2)}, u32[]{:S(2)}) %collective-permute-start.21) | collective-permute-done | bytes 1056 | tf_op jit(solution)/shard_map/ppermute | solution.py:94
  276.9 36.3 %select_add_fusion = f32[1024,2048]{1,0:T(8,128)} fusion(f32[2048]{0:T(1024)S(1)} %copy-done.6, s32[2048]{0:T(1024)S(1)} %iota_add_fusion, s32[1024]{0:T(1024)S(1)} %iota_add_fusion.1, f32[2048,1024]{1,0:T(8,128)} %constant_dynamic-update-slice_fusion, f32[2048,2048]{1,0:T(8,128)S(1)} %copy-done.1), kind=kOutput, calls=%fused_computation.1 | convolution fusion | flops 25776095232 | bytes 33574912 | tf_op jit(solution)/shard_map/dot_general | solution.py:66
  313.2 3.4 %gather_fusion = f32[512]{0:T(512)} fusion(f32[1024]{0:T(1024)S(1)} %maximum_select_fusion, s32[1024]{0:T(1024)S(1)} %pad_clamp_fusion), kind=kCustom, calls=%fused_computation | custom fusion | bytes 6144 | tf_op jit(solution)/shard_map/gather | solution.py:98
  (82 shorter events, 17.4 us)
Async XLA Ops:
  7.2 141.7 %copy-start = (f32[2048]{0:T(1024)S(1)}, f32[2048]{0:T(1024)}, u32[]{:S(2)}) copy-start(f32[2048]{0:T(1024)} %param.13) | copy-start | bytes 24580
  7.2 181.2 %all-gather.2.cloned.1.call-start = ((), (), s32[]{:S(2)}) async-start(), calls=%async_computation | async-start | bytes 17825792 | tf_op jit(solution)/shard_map/all_gather | solution.py:23
  13.6 115.7 %copy-start.8 = (s32[8]{0:T(128)S(1)}, s32[8]{0:T(128)}, u32[]{:S(2)}) copy-start(s32[8]{0:T(128)} %constant.194.clone) | copy-start | bytes 100
  13.6 125.6 %copy-start.5 = (s32[8]{0:T(128)S(1)}, s32[8]{0:T(128)}, u32[]{:S(2)}) copy-start(s32[8]{0:T(128)} %constant.193.clone) | copy-start | bytes 100
  13.7 135.0 %copy-start.2 = (f32[64,2048]{1,0:T(8,128)S(1)}, f32[64,2048]{1,0:T(8,128)}, u32[]{:S(2)}) copy-start(f32[64,2048]{1,0:T(8,128)} %param.11) | copy-start | bytes 1572868
  13.7 134.9 %copy-start.6 = (f32[2048]{0:T(1024)S(1)}, f32[2048]{0:T(1024)}, u32[]{:S(2)}) copy-start(f32[2048]{0:T(1024)} %param.10) | copy-start | bytes 24580
  14.7 2.0 collective-permute-start.1
  14.9 1.8 collective-permute-start
  22.0 75.3 %collective-permute-start.2 = (f32[128,1024]{1,0:T(8,128)S(1)}, f32[128,1024]{1,0:T(8,128)S(1)}, u32[]{:S(2)}, u32[]{:S(2)}) collective-permute-start(f32[128,1024]{1,0:T(8,128)S(1)} %get-tuple-element.7), channel_id=1, source_target_pairs={{0,2},{2,4},{4,6},{6,7},{7,5},{5,3},{3,1},{1,0},{8,10},{10,12},{12... | collective-permute-start | bytes 1572872 | tf_op jit(solution)/shard_map/ppermute | solution.py:56
  66.7 31.8 %collective-permute-start.3 = (f32[128,1024]{1,0:T(8,128)S(1)}, f32[128,1024]{1,0:T(8,128)S(1)}, u32[]{:S(2)}, u32[]{:S(2)}) collective-permute-start(f32[128,1024]{1,0:T(8,128)S(1)} %get-tuple-element.5), channel_id=1, source_target_pairs={{0,1},{2,0},{4,2},{6,4},{7,6},{5,7},{3,5},{1,3},{8,9},{10,8},{12,1... | collective-permute-start | bytes 1572872 | tf_op jit(solution)/shard_map/ppermute | solution.py:57
  97.3 26.4 %collective-permute-start.4 = (f32[128,1024]{1,0:T(8,128)S(1)}, f32[128,1024]{1,0:T(8,128)S(1)}, u32[]{:S(2)}, u32[]{:S(2)}) collective-permute-start(f32[128,1024]{1,0:T(8,128)S(1)} %collective-permute-done.2), channel_id=1, source_target_pairs={{0,2},{2,4},{4,6},{6,7},{7,5},{5,3},{3,1},{1,0},{8,10},{10,12},{12... | collective-permute-start | bytes 1572872 | tf_op jit(solution)/shard_map/ppermute | solution.py:56
  98.5 26.8 %collective-permute-start.5 = (f32[128,1024]{1,0:T(8,128)S(1)}, f32[128,1024]{1,0:T(8,128)S(1)}, u32[]{:S(2)}, u32[]{:S(2)}) collective-permute-start(f32[128,1024]{1,0:T(8,128)S(1)} %collective-permute-done.3), channel_id=1, source_target_pairs={{0,1},{2,0},{4,2},{6,4},{7,6},{5,7},{3,5},{1,3},{8,9},{10,8},{12,1... | collective-permute-start | bytes 1572872 | tf_op jit(solution)/shard_map/ppermute | solution.py:57
  123.6 64.7 %copy-start.3 = (f32[128,1024]{1,0:T(8,128)}, f32[128,1024]{1,0:T(8,128)S(1)}, u32[]{:S(2)}) copy-start(f32[128,1024]{1,0:T(8,128)S(1)} %collective-permute-done.4) | copy-start | bytes 1572868
  123.6 26.2 %collective-permute-start.6 = (f32[128,1024]{1,0:T(8,128)S(1)}, f32[128,1024]{1,0:T(8,128)}, u32[]{:S(2)}, u32[]{:S(2)}) collective-permute-start(f32[128,1024]{1,0:T(8,128)S(1)} %collective-permute-done.4), channel_id=1, source_target_pairs={{0,2},{2,4},{4,6},{6,7},{7,5},{5,3},{3,1},{1,0},{8,10},{10,12},{12... | collective-permute-start | bytes 1572872 | tf_op jit(solution)/shard_map/ppermute | solution.py:56
  125.3 26.5 %collective-permute-start.7 = (f32[128,1024]{1,0:T(8,128)S(1)}, f32[128,1024]{1,0:T(8,128)S(1)}, u32[]{:S(2)}, u32[]{:S(2)}) collective-permute-start(f32[128,1024]{1,0:T(8,128)S(1)} %collective-permute-done.5), channel_id=1, source_target_pairs={{0,1},{2,0},{4,2},{6,4},{7,6},{5,7},{3,5},{1,3},{8,9},{10,8},{12,1... | collective-permute-start | bytes 1572872 | tf_op jit(solution)/shard_map/ppermute | solution.py:57
  149.5 50.3 %copy-start.7 = (s32[512]{0:T(512)S(1)}, s32[512]{0:T(512)}, u32[]{:S(2)}) copy-start(s32[512]{0:T(512)} %param.12) | copy-start | bytes 6148
  149.8 50.0 %collective-permute-start.8 = (f32[128,1024]{1,0:T(8,128)}, f32[128,1024]{1,0:T(8,128)}, u32[]{:S(2)}, u32[]{:S(2)}) collective-permute-start(f32[128,1024]{1,0:T(8,128)} %collective-permute-done.6), channel_id=1, source_target_pairs={{0,2},{2,4},{4,6},{6,7},{7,5},{5,3},{3,1},{1,0},{8,10},{10,12},{12... | collective-permute-start | bytes 1572872 | tf_op jit(solution)/shard_map/ppermute | solution.py:56
  151.8 56.3 %collective-permute-start.9 = (f32[128,1024]{1,0:T(8,128)S(1)}, f32[128,1024]{1,0:T(8,128)}, u32[]{:S(2)}, u32[]{:S(2)}) collective-permute-start(f32[128,1024]{1,0:T(8,128)S(1)} %collective-permute-done.7), channel_id=1, source_target_pairs={{0,1},{2,0},{4,2},{6,4},{7,6},{5,7},{3,5},{1,3},{8,9},{10,8},{12,1... | collective-permute-start | bytes 1572872 | tf_op jit(solution)/shard_map/ppermute | solution.py:57
  199.7 17.0 %collective-permute-start.16 = (f32[2050,64]{0,1:T(8,128)S(1)}, f32[2050,64]{0,1:T(8,128)S(1)}, u32[]{:S(2)}, u32[]{:S(2)}) collective-permute-start(f32[2050,64]{0,1:T(8,128)S(1)} %concatenate.27), channel_id=1, source_target_pairs={{0,4},{1,5},{2,6},{3,7},{4,0},{5,1},{6,2},{7,3},{8,12},{9,13},{10,... | collective-permute-start | bytes 1574408 | tf_op jit(solution)/shard_map/ppermute | solution.py:83
  199.8 29.7 %collective-permute-start.10 = (f32[128,1024]{1,0:T(8,128)}, f32[128,1024]{1,0:T(8,128)S(1)}, u32[]{:S(2)}, u32[]{:S(2)}) collective-permute-start(f32[128,1024]{1,0:T(8,128)} %collective-permute-done.8), channel_id=1, source_target_pairs={{0,2},{2,4},{4,6},{6,7},{7,5},{5,3},{3,1},{1,0},{8,10},{10,12},{12... | collective-permute-start | bytes 1572872 | tf_op jit(solution)/shard_map/ppermute | solution.py:56
  208.2 24.5 %collective-permute-start.11 = (f32[128,1024]{1,0:T(8,128)}, f32[128,1024]{1,0:T(8,128)S(1)}, u32[]{:S(2)}, u32[]{:S(2)}) collective-permute-start(f32[128,1024]{1,0:T(8,128)} %collective-permute-done.9), channel_id=1, source_target_pairs={{0,1},{2,0},{4,2},{6,4},{7,6},{5,7},{3,5},{1,3},{8,9},{10,8},{12,1... | collective-permute-start | bytes 1572872 | tf_op jit(solution)/shard_map/ppermute | solution.py:57
  216.8 27.9 %collective-permute-start.17 = (f32[2050,64]{0,1:T(8,128)S(1)}, f32[2050,64]{0,1:T(8,128)S(1)}, u32[]{:S(2)}, u32[]{:S(2)}) collective-permute-start(f32[2050,64]{0,1:T(8,128)S(1)} %add.424), channel_id=1, source_target_pairs={{0,2},{1,3},{2,0},{3,1},{4,6},{5,7},{6,4},{7,5},{8,10},{9,11},{10,... | collective-permute-start | bytes 1574408 | tf_op jit(solution)/shard_map/ppermute | solution.py:83
  221.6 55.3 %copy-start.1 = (f32[2048,2048]{1,0:T(8,128)S(1)}, f32[2048,2048]{1,0:T(8,128)}, u32[]{:S(2)}) copy-start(f32[2048,2048]{1,0:T(8,128)} %all-gather.2.cloned.1.call-done) | copy-start | bytes 50331652
  229.5 20.9 %collective-permute-start.12 = (f32[128,1024]{1,0:T(8,128)S(1)}, f32[128,1024]{1,0:T(8,128)S(1)}, u32[]{:S(2)}, u32[]{:S(2)}) collective-permute-start(f32[128,1024]{1,0:T(8,128)S(1)} %collective-permute-done.10), channel_id=1, source_target_pairs={{0,2},{2,4},{4,6},{6,7},{7,5},{5,3},{3,1},{1,0},{8,10},{10,12},{12... | collective-permute-start | bytes 1572872 | tf_op jit(solution)/shard_map/ppermute | solution.py:56
  232.7 22.5 %collective-permute-start.13 = (f32[128,1024]{1,0:T(8,128)S(1)}, f32[128,1024]{1,0:T(8,128)S(1)}, u32[]{:S(2)}, u32[]{:S(2)}) collective-permute-start(f32[128,1024]{1,0:T(8,128)S(1)} %collective-permute-done.11), channel_id=1, source_target_pairs={{0,1},{2,0},{4,2},{6,4},{7,6},{5,7},{3,5},{1,3},{8,9},{10,8},{12,1... | collective-permute-start | bytes 1572872 | tf_op jit(solution)/shard_map/ppermute | solution.py:57
  244.7 17.1 %collective-permute-start.18 = (f32[2050,64]{0,1:T(8,128)S(1)}, f32[2050,64]{0,1:T(8,128)S(1)}, u32[]{:S(2)}, u32[]{:S(2)}) collective-permute-start(f32[2050,64]{0,1:T(8,128)S(1)} %add.425), channel_id=1, source_target_pairs={{0,1},{1,0},{2,3},{3,2},{4,5},{5,4},{6,7},{7,6},{8,9},{9,8},{10,11... | collective-permute-start | bytes 1574408 | tf_op jit(solution)/shard_map/ppermute | solution.py:83
  250.4 20.5 %collective-permute-start.14 = (f32[128,1024]{1,0:T(8,128)S(1)}, f32[128,1024]{1,0:T(8,128)S(1)}, u32[]{:S(2)}, u32[]{:S(2)}) collective-permute-start(f32[128,1024]{1,0:T(8,128)S(1)} %collective-permute-done.12), channel_id=1, source_target_pairs={{0,2},{2,4},{4,6},{6,7},{7,5},{5,3},{3,1},{1,0},{8,10},{10,12},{12... | collective-permute-start | bytes 1572872 | tf_op jit(solution)/shard_map/ppermute | solution.py:56
  255.2 16.6 %collective-permute-start.15 = (f32[128,1024]{1,0:T(8,128)S(1)}, f32[128,1024]{1,0:T(8,128)S(1)}, u32[]{:S(2)}, u32[]{:S(2)}) collective-permute-start(f32[128,1024]{1,0:T(8,128)S(1)} %collective-permute-done.13), channel_id=1, source_target_pairs={{0,1},{2,0},{4,2},{6,4},{7,6},{5,7},{3,5},{1,3},{8,9},{10,8},{12,1... | collective-permute-start | bytes 1572872 | tf_op jit(solution)/shard_map/ppermute | solution.py:57
  262.3 1.2 collective-permute-start.19
  263.5 8.2 %collective-permute-start.20 = (f32[128]{0:T(128)S(1)}, f32[128]{0:T(128)S(1)}, u32[]{:S(2)}, u32[]{:S(2)}) collective-permute-start(f32[128]{0:T(128)S(1)} %broadcast_select_fusion.1), channel_id=1, source_target_pairs={{0,16},{8,24},{16,0},{24,8},{32,48},{40,56},{48,32},{56,40},{64,80... | collective-permute-start | bytes 1544 | tf_op jit(solution)/shard_map/ppermute | solution.py:94
  271.7 5.2 %collective-permute-start.21 = (f32[256]{0:T(256)S(1)}, f32[256]{0:T(256)S(1)}, u32[]{:S(2)}, u32[]{:S(2)}) collective-permute-start(f32[256]{0:T(256)S(1)} %maximum_select_fusion.2), channel_id=1, source_target_pairs={{0,32},{8,40},{16,48},{24,56},{32,0},{40,8},{48,16},{56,24},{64,96... | collective-permute-start | bytes 3080 | tf_op jit(solution)/shard_map/ppermute | solution.py:94
  276.9 36.3 %collective-permute-start.22 = (f32[512]{0:T(512)S(1)}, f32[512]{0:T(512)S(1)}, u32[]{:S(2)}, u32[]{:S(2)}) collective-permute-start(f32[512]{0:T(512)S(1)} %maximum_select_fusion.1), channel_id=1, source_target_pairs={{0,64},{8,72},{16,80},{24,88},{32,96},{40,104},{48,112},{56,120},{... | collective-permute-start | bytes 6152 | tf_op jit(solution)/shard_map/ppermute | solution.py:94
  (1 other events, 30.5 us)
Sparse Core Ops, SparseCore 0:
  11.6 176.6 all-gather.1

commit v4 on v3

--- a/solution.py
+++ b/solution.py
@@ -39,29 +39,15 @@
     ]
     row_block = jnp.concatenate(ordered, axis=0)
 
-    n_y = n_col // 2
-    ring = [y * 2 for y in range(n_y)] + [y * 2 + 1 for y in reversed(range(n_y))]
-    where_in_ring = [ring.index(c) for c in range(n_col)]
-    forward = [(ring[p], ring[(p + 1) % n_col]) for p in range(n_col)]
-    backward = [(ring[p], ring[(p - 1) % n_col]) for p in range(n_col)]
     block_rows = row_block.shape[0]
-    half_rows = block_rows // 2
-    ring_tab = jnp.array(ring, jnp.int32)
-    me = jnp.array(where_in_ring, jnp.int32)[col_pos]
     row_all = jnp.zeros((n_col * block_rows, width_row), jnp.float32)
-    ahead, behind = row_block[:half_rows], row_block[half_rows:]
-    row_all = lax.dynamic_update_slice_in_dim(row_all, ahead, col_pos * block_rows, 0)
-    row_all = lax.dynamic_update_slice_in_dim(row_all, behind, col_pos * block_rows + half_rows, 0)
+    row_all = lax.dynamic_update_slice_in_dim(row_all, row_block, col_pos * block_rows, 0)
     for k in range(1, n_col):
-        ahead = lax.ppermute(ahead, "col", forward)
-        behind = lax.ppermute(behind, "col", backward)
-        from_ahead = ring_tab[(me - k) % n_col]
-        from_behind = ring_tab[(me + k) % n_col]
-        row_all = lax.dynamic_update_slice_in_dim(row_all, ahead, from_ahead * block_rows, 0)
-        row_all = lax.dynamic_update_slice_in_dim(
-            row_all, behind, from_behind * block_rows + half_rows, 0
-        )
+        pairs = [(c, c ^ k) for c in range(n_col)]
+        got = lax.ppermute(row_block, "col", pairs)
+        row_all = lax.dynamic_update_slice_in_dim(row_all, got, (col_pos ^ k) * block_rows, 0)
 
+    col_all, row_all = lax.optimization_barrier((col_all, row_all))
     contract = (((0,), (0,)), ((), ()))
     tile = lax.dot_general(
         row_all, col_all, contract, precision=high, preferred_element_type=jnp.float32

time: 324 us -> 351 us (1.083)
  waiting for transfers between devices: 126 us -> 178 us
  between operations: 32.4 us -> 14.3 us
  local copies, waits for them, and re-layouts: 32.5 us -> 25.2 us
    ppermute x14 -> x7, waiting for transfers between devices: 63.7 us -> 110 us  [body(): got = lax.ppermute(row_block, 'col', pairs)]
    ppermute x3, waiting for transfers between devices: 24.2 us -> 40.8 us  [body(): packed = packed + lax.ppermute(packed, 'col', pairs)]
    all_gather x1, waiting for transfers between devices: 32.5 us -> 17.1 us  [body(): col_all = lax.all_gather(masked, 'row', axis=0, tiled=True)]
    dynamic_update_slice x14 -> x7, local copies, waits for them, and re-layouts: 18.5 us -> 12.6 us  [body(): lax.dynamic_update_slice_in_dim(row_all, got, (col_pos ^ k) * block_rows, 0)]
    ppermute x3, starting transfers between devices: 5 us -> 8.54 us  [body(): packed = packed + lax.ppermute(packed, 'col', pairs)]
    ppermute x14 -> x7, starting transfers between devices: 73.1 us -> 70.1 us  [body(): got = lax.ppermute(row_block, 'col', pairs)]
  transfers between devices with their start and end apart: 24 -> 17, of which waited for: 16 -> 12; matrix products, arithmetic and copies ran while one was open for 24% -> 16% of each run, Pallas kernels for 0% -> 0%
where the time goes in v4:
time: 351 us
  waiting for transfers between devices  178 us (51%)
  starting transfers between devices  82.5 us (24%)
  matrix products  45.7 us (13%)
  local copies, waits for them, and re-layouts  25.2 us (7%)
  between operations  14.3 us (4%)
  other arithmetic  5.34 us (2%)
    ppermute x7, waiting for transfers between devices, body(): got = lax.ppermute(row_block, 'col', pairs)  110 us
    ppermute x7, starting transfers between devices, body(): got = lax.ppermute(row_block, 'col', pairs)  70.1 us
    ppermute x3, waiting for transfers between devices, body(): packed = packed + lax.ppermute(packed, 'col', pairs)  40.8 us
    dot_general x1, matrix products, body(): lax.dot_general(row_all, col_all, contract, precision=high, preferred_ele...  33.9 us
    all_gather x1, waiting for transfers between devices, body(): col_all = lax.all_gather(masked, 'row', axis=0, tiled=True)  17.1 us
    dynamic_update_slice x7, local copies, waits for them, and re-layouts, body(): lax.dynamic_update_slice_in_dim(row_all, got, (col_pos ^ k) * block_rows, 0)  12.6 us
    dot_general x1, matrix products, body(): lax.dot_general(col_all, items, (((1,), (1,)), ((), ())), precision=high,...  11.3 us
    ppermute x3, starting transfers between devices, body(): packed = packed + lax.ppermute(packed, 'col', pairs)  8.54 us
  transfers between devices with their start and end apart: 17, of which 12 were waited for; matrix products, arithmetic and copies ran while one was open for 16% of the time, Pallas kernels for 0%

profile of v4, /device:TPU:0, one launch (start us, length us, event | category | flops | bytes accessed | tf_op | source)
XLA Modules:
  0.0 350.7 jit_solution(8679107006915693346)
XLA Ops:
  7.2 1.2 dynamic_slice.9
  9.1 2.3 broadcast_select_fusion
  11.5 2.1 reshape.12
  15.7 1.9 collective-permute-done.1
  17.8 4.3 %broadcast_in_dim.48 = f32[2048,1024]{1,0:T(8,128)} broadcast(f32[]{:T(128)} %constant.22.clone.1), dimensions={} | broadcast | bytes 8388612 | tf_op jit(solution)/shard_map/broadcast_in_dim | solution.py:43
  22.1 1.6 pad_maximum_fusion
  23.7 50.7 %collective-permute-start.2 = (f32[256,1024]{1,0:T(8,128)}, f32[256,1024]{1,0:T(8,128)}, u32[]{:S(2)}, u32[]{:S(2)}) collective-permute-start(f32[256,1024]{1,0:T(8,128)} %get-tuple-element.8), channel_id=1, source_target_pairs={{0,1},{1,0},{2,3},{3,2},{4,5},{5,4},{6,7},{7,6},{8,9},{9,8},{10,11... | collective-permute-start | bytes 3145736 | tf_op jit(solution)/shard_map/ppermute | solution.py:47
  74.4 4.3 %collective-permute-start.3 = (f32[256,1024]{1,0:T(8,128)}, f32[256,1024]{1,0:T(8,128)}, u32[]{:S(2)}, u32[]{:S(2)}) collective-permute-start(f32[256,1024]{1,0:T(8,128)} %get-tuple-element.8), channel_id=1, source_target_pairs={{0,2},{1,3},{2,0},{3,1},{4,6},{5,7},{6,4},{7,5},{8,10},{9,11},{10,... | collective-permute-start | bytes 3145736 | tf_op jit(solution)/shard_map/ppermute | solution.py:47
  78.7 2.5 collective-permute-start.5
  81.2 3.4 collective-permute-start.6
  84.6 57.9 %collective-permute-done.2 = f32[256,1024]{1,0:T(8,128)} collective-permute-done((f32[256,1024]{1,0:T(8,128)}, f32[256,1024]{1,0:T(8,128)}, u32[]{:S(2)}, u32[]{:S(2)}) %collective-permute-start.2) | collective-permute-done | bytes 1048608 | tf_op jit(solution)/shard_map/ppermute | solution.py:47
  142.5 5.9 %collective-permute-start.7 = (f32[256,1024]{1,0:T(8,128)}, f32[256,1024]{1,0:T(8,128)}, u32[]{:S(2)}, u32[]{:S(2)}) collective-permute-start(f32[256,1024]{1,0:T(8,128)} %get-tuple-element.8), channel_id=1, source_target_pairs={{0,6},{1,7},{2,4},{3,5},{4,2},{5,3},{6,0},{7,1},{8,14},{9,15},{10,... | collective-permute-start | bytes 3145736 | tf_op jit(solution)/shard_map/ppermute | solution.py:47
  148.7 3.3 collective-permute-start.8
  152.5 2.3 constant_dynamic-update-slice_fusion.6
  154.9 2.3 constant_dynamic-update-slice_fusion.5
  157.2 2.3 constant_dynamic-update-slice_fusion.4
  160.6 11.0 %collective-permute-done.6 = f32[256,1024]{1,0:T(8,128)S(1)} collective-permute-done((f32[256,1024]{1,0:T(8,128)}, f32[256,1024]{1,0:T(8,128)S(1)}, u32[]{:S(2)}, u32[]{:S(2)}) %collective-permute-start.6) | collective-permute-done | bytes 1048608 | tf_op jit(solution)/shard_map/ppermute | solution.py:47
  172.7 21.7 %collective-permute-done.7 = f32[256,1024]{1,0:T(8,128)} collective-permute-done((f32[256,1024]{1,0:T(8,128)}, f32[256,1024]{1,0:T(8,128)}, u32[]{:S(2)}, u32[]{:S(2)}) %collective-permute-start.7) | collective-permute-done | bytes 1048608 | tf_op jit(solution)/shard_map/ppermute | solution.py:47
  194.4 2.4 constant_dynamic-update-slice_fusion.1
  196.7 19.6 %collective-permute-done.8 = f32[256,1024]{1,0:T(8,128)S(1)} collective-permute-done((f32[256,1024]{1,0:T(8,128)}, f32[256,1024]{1,0:T(8,128)S(1)}, u32[]{:S(2)}, u32[]{:S(2)}) %collective-permute-start.8) | collective-permute-done | bytes 1048608 | tf_op jit(solution)/shard_map/ppermute | solution.py:47
  217.5 17.1 %all-gather.2.cloned.1.call-done = f32[2048,2048]{1,0:T(8,128)} async-done(((f32[128,2048]{1,0:T(8,128)}), f32[2048,2048]{1,0:T(8,128)}) %all-gather.2.cloned.1.call-update) | async-done | bytes 16777232 | tf_op jit(solution)/shard_map/all_gather | solution.py:23
  234.6 11.3 %fusion.2 = f32[2048,64]{0,1:T(8,128)S(1)} fusion(f32[2048,2048]{1,0:T(8,128)} %all-gather.2.cloned.1.call-done, f32[64,2048]{1,0:T(8,128)S(1)} %copy-done.1), kind=kOutput, calls=%fused_computation.34 | convolution fusion | flops 1610612736 | bytes 17825792 | tf_op jit(solution)/shard_map/dot_general | solution.py:59
  246.0 5.6 %collective-permute-start.9 = (f32[2050,64]{0,1:T(8,128)S(1)}, f32[2050,64]{0,1:T(8,128)S(1)}, u32[]{:S(2)}, u32[]{:S(2)}) collective-permute-start(f32[2050,64]{0,1:T(8,128)S(1)} %concatenate.31), channel_id=1, source_target_pairs={{0,4},{1,5},{2,6},{3,7},{4,0},{5,1},{6,2},{7,3},{8,12},{9,13},{10,... | collective-permute-start | bytes 1574408 | tf_op jit(solution)/shard_map/ppermute | solution.py:69
  251.6 13.0 %collective-permute-done.9 = f32[2050,64]{0,1:T(8,128)S(1)} collective-permute-done((f32[2050,64]{0,1:T(8,128)S(1)}, f32[2050,64]{0,1:T(8,128)S(1)}, u32[]{:S(2)}, u32[]{:S(2)}) %collective-permute-start.9) | collective-permute-done | bytes 524832 | tf_op jit(solution)/shard_map/ppermute | solution.py:69
  264.7 2.9 collective-permute-start.10
  267.6 12.6 %collective-permute-done.10 = f32[2050,64]{0,1:T(8,128)S(1)} collective-permute-done((f32[2050,64]{0,1:T(8,128)S(1)}, f32[2050,64]{0,1:T(8,128)S(1)}, u32[]{:S(2)}, u32[]{:S(2)}) %collective-permute-start.10) | collective-permute-done | bytes 524832 | tf_op jit(solution)/shard_map/ppermute | solution.py:69
  280.3 15.2 %collective-permute-done.11 = f32[2050,64]{0,1:T(8,128)S(1)} collective-permute-done((f32[2050,64]{0,1:T(8,128)S(1)}, f32[2050,64]{0,1:T(8,128)S(1)}, u32[]{:S(2)}, u32[]{:S(2)}) %collective-permute-start.11) | collective-permute-done | bytes 524832 | tf_op jit(solution)/shard_map/ppermute | solution.py:69
  297.2 3.5 %collective-permute-done.13 = f32[128]{0:T(128)S(1)} collective-permute-done((f32[128]{0:T(128)S(1)}, f32[128]{0:T(128)S(1)}, u32[]{:S(2)}, u32[]{:S(2)}) %collective-permute-start.13) | collective-permute-done | bytes 544 | tf_op jit(solution)/shard_map/ppermute | solution.py:80
  300.7 2.0 collective-permute-start.14
  302.7 3.1 collective-permute-done.14
  306.6 33.9 %select_add_fusion = f32[1024,2048]{1,0:T(8,128)} fusion(f32[2048]{0:T(1024)S(1)} %copy-done.2, s32[2048]{0:T(1024)S(1)} %iota_add_fusion, s32[1024]{0:T(1024)S(1)} %iota_add_fusion.1, f32[2048,1024]{1,0:T(8,128)} %constant_dynamic-update-slice_fusion, f32[2048,2048]{1,0:T(8,128)} %all-gather.2.cloned.1.call-done), kind=kOutput, calls=%fused_computation.1 | convolution fusion | flops 25776095232 | bytes 33574912 | tf_op jit(solution)/shard_map/dot_general | solution.py:52
  340.4 3.4 gather_fusion
  (49 shorter events, 9.7 us)
Async XLA Ops:
  7.2 144.8 %copy-start = (f32[2048]{0:T(1024)S(1)}, f32[2048]{0:T(1024)}, u32[]{:S(2)}) copy-start(f32[2048]{0:T(1024)} %param.11) | copy-start | bytes 24580
  7.2 227.5 %all-gather.2.cloned.1.call-start = ((), (), s32[]{:S(2)}) async-start(), calls=%async_computation | async-start | bytes 17825792 | tf_op jit(solution)/shard_map/all_gather | solution.py:23
  14.5 133.9 %copy-start.1 = (f32[64,2048]{1,0:T(8,128)S(1)}, f32[64,2048]{1,0:T(8,128)}, u32[]{:S(2)}) copy-start(f32[64,2048]{1,0:T(8,128)} %param.9) | copy-start | bytes 1572868
  14.6 133.9 %copy-start.2 = (f32[2048]{0:T(1024)S(1)}, f32[2048]{0:T(1024)}, u32[]{:S(2)}) copy-start(f32[2048]{0:T(1024)} %param.8) | copy-start | bytes 24580
  14.7 1.1 collective-permute-start
  15.6 2.0 collective-permute-start.1
  23.7 118.9 %collective-permute-start.2 = (f32[256,1024]{1,0:T(8,128)}, f32[256,1024]{1,0:T(8,128)}, u32[]{:S(2)}, u32[]{:S(2)}) collective-permute-start(f32[256,1024]{1,0:T(8,128)} %get-tuple-element.8), channel_id=1, source_target_pairs={{0,1},{1,0},{2,3},{3,2},{4,5},{5,4},{6,7},{7,6},{8,9},{9,8},{10,11... | collective-permute-start | bytes 3145736 | tf_op jit(solution)/shard_map/ppermute | solution.py:47
  74.4 74.3 %collective-permute-start.3 = (f32[256,1024]{1,0:T(8,128)}, f32[256,1024]{1,0:T(8,128)}, u32[]{:S(2)}, u32[]{:S(2)}) collective-permute-start(f32[256,1024]{1,0:T(8,128)} %get-tuple-element.8), channel_id=1, source_target_pairs={{0,2},{1,3},{2,0},{3,1},{4,6},{5,7},{6,4},{7,5},{8,10},{9,11},{10,... | collective-permute-start | bytes 3145736 | tf_op jit(solution)/shard_map/ppermute | solution.py:47
  78.7 78.5 %collective-permute-start.4 = (f32[256,1024]{1,0:T(8,128)}, f32[256,1024]{1,0:T(8,128)}, u32[]{:S(2)}, u32[]{:S(2)}) collective-permute-start(f32[256,1024]{1,0:T(8,128)} %get-tuple-element.8), channel_id=1, source_target_pairs={{0,3},{1,2},{2,1},{3,0},{4,7},{5,6},{6,5},{7,4},{8,11},{9,10},{10,... | collective-permute-start | bytes 3145736 | tf_op jit(solution)/shard_map/ppermute | solution.py:47
  78.7 80.9 %collective-permute-start.5 = (f32[256,1024]{1,0:T(8,128)}, f32[256,1024]{1,0:T(8,128)S(1)}, u32[]{:S(2)}, u32[]{:S(2)}) collective-permute-start(f32[256,1024]{1,0:T(8,128)} %get-tuple-element.8), channel_id=1, source_target_pairs={{0,4},{1,5},{2,6},{3,7},{4,0},{5,1},{6,2},{7,3},{8,12},{9,13},{10,... | collective-permute-start | bytes 3145736 | tf_op jit(solution)/shard_map/ppermute | solution.py:47
  81.2 90.4 %collective-permute-start.6 = (f32[256,1024]{1,0:T(8,128)}, f32[256,1024]{1,0:T(8,128)S(1)}, u32[]{:S(2)}, u32[]{:S(2)}) collective-permute-start(f32[256,1024]{1,0:T(8,128)} %get-tuple-element.8), channel_id=1, source_target_pairs={{0,5},{1,4},{2,7},{3,6},{4,1},{5,0},{6,3},{7,2},{8,13},{9,12},{10,... | collective-permute-start | bytes 3145736 | tf_op jit(solution)/shard_map/ppermute | solution.py:47
  142.5 51.9 %collective-permute-start.7 = (f32[256,1024]{1,0:T(8,128)}, f32[256,1024]{1,0:T(8,128)}, u32[]{:S(2)}, u32[]{:S(2)}) collective-permute-start(f32[256,1024]{1,0:T(8,128)} %get-tuple-element.8), channel_id=1, source_target_pairs={{0,6},{1,7},{2,4},{3,5},{4,2},{5,3},{6,0},{7,1},{8,14},{9,15},{10,... | collective-permute-start | bytes 3145736 | tf_op jit(solution)/shard_map/ppermute | solution.py:47
  148.7 67.7 %collective-permute-start.8 = (f32[256,1024]{1,0:T(8,128)}, f32[256,1024]{1,0:T(8,128)S(1)}, u32[]{:S(2)}, u32[]{:S(2)}) collective-permute-start(f32[256,1024]{1,0:T(8,128)} %get-tuple-element.8), channel_id=1, source_target_pairs={{0,7},{1,6},{2,5},{3,4},{4,3},{5,2},{6,1},{7,0},{8,15},{9,14},{10,... | collective-permute-start | bytes 3145736 | tf_op jit(solution)/shard_map/ppermute | solution.py:47
  217.5 62.8 %copy-start.3 = (s32[512]{0:T(512)S(1)}, s32[512]{0:T(512)}, u32[]{:S(2)}) copy-start(s32[512]{0:T(512)} %param.10) | copy-start | bytes 6148
  246.0 18.6 %collective-permute-start.9 = (f32[2050,64]{0,1:T(8,128)S(1)}, f32[2050,64]{0,1:T(8,128)S(1)}, u32[]{:S(2)}, u32[]{:S(2)}) collective-permute-start(f32[2050,64]{0,1:T(8,128)S(1)} %concatenate.31), channel_id=1, source_target_pairs={{0,4},{1,5},{2,6},{3,7},{4,0},{5,1},{6,2},{7,3},{8,12},{9,13},{10,... | collective-permute-start | bytes 1574408 | tf_op jit(solution)/shard_map/ppermute | solution.py:69
  264.7 15.4 %collective-permute-start.10 = (f32[2050,64]{0,1:T(8,128)S(1)}, f32[2050,64]{0,1:T(8,128)S(1)}, u32[]{:S(2)}, u32[]{:S(2)}) collective-permute-start(f32[2050,64]{0,1:T(8,128)S(1)} %add.102), channel_id=1, source_target_pairs={{0,2},{1,3},{2,0},{3,1},{4,6},{5,7},{6,4},{7,5},{8,10},{9,11},{10,... | collective-permute-start | bytes 1574408 | tf_op jit(solution)/shard_map/ppermute | solution.py:69
  280.2 15.3 %collective-permute-start.11 = (f32[2050,64]{0,1:T(8,128)S(1)}, f32[2050,64]{0,1:T(8,128)S(1)}, u32[]{:S(2)}, u32[]{:S(2)}) collective-permute-start(f32[2050,64]{0,1:T(8,128)S(1)} %add.103), channel_id=1, source_target_pairs={{0,1},{1,0},{2,3},{3,2},{4,5},{5,4},{6,7},{7,6},{8,9},{9,8},{10,11... | collective-permute-start | bytes 1574408 | tf_op jit(solution)/shard_map/ppermute | solution.py:69
  295.9 1.2 collective-permute-start.12
  297.2 3.6 %collective-permute-start.13 = (f32[128]{0:T(128)S(1)}, f32[128]{0:T(128)S(1)}, u32[]{:S(2)}, u32[]{:S(2)}) collective-permute-start(f32[128]{0:T(128)S(1)} %broadcast_select_fusion.1), channel_id=1, source_target_pairs={{0,16},{8,24},{16,0},{24,8},{32,48},{40,56},{48,32},{56,40},{64,80... | collective-permute-start | bytes 1544 | tf_op jit(solution)/shard_map/ppermute | solution.py:80
  300.7 5.1 %collective-permute-start.14 = (f32[256]{0:T(256)S(1)}, f32[256]{0:T(256)S(1)}, u32[]{:S(2)}, u32[]{:S(2)}) collective-permute-start(f32[256]{0:T(256)S(1)} %maximum_select_fusion.2), channel_id=1, source_target_pairs={{0,32},{8,40},{16,48},{24,56},{32,0},{40,8},{48,16},{56,24},{64,96... | collective-permute-start | bytes 3080 | tf_op jit(solution)/shard_map/ppermute | solution.py:80
  305.8 34.6 %collective-permute-start.15 = (f32[512]{0:T(512)S(1)}, f32[512]{0:T(512)S(1)}, u32[]{:S(2)}, u32[]{:S(2)}) collective-permute-start(f32[512]{0:T(512)S(1)} %maximum_select_fusion.1), channel_id=1, source_target_pairs={{0,64},{8,72},{16,80},{24,88},{32,96},{40,104},{48,112},{56,120},{... | collective-permute-start | bytes 6152 | tf_op jit(solution)/shard_map/ppermute | solution.py:80
Sparse Core Ops, SparseCore 0:
  11.6 222.9 all-gather.1

commit v5 on v4

v5 whole, which is shorter than its diff:
```python
import jax
import jax.numpy as jnp
from jax import lax
from jax.sharding import Mesh
from jax.sharding import PartitionSpec as P

F = 16384

highest = lax.Precision.HIGHEST
high = lax.Precision.HIGH
ROW = ("chip", "core")


def body(shared_rows, event_counts, ridge, items, cand_ids, theta):
    n_chip = lax.axis_size("chip")
    n_core = lax.axis_size("core")
    n_row = n_chip * n_core
    n_col = lax.axis_size("col")
    ratio = n_row // n_col
    core = lax.axis_index("core")
    row_pos = lax.axis_index("chip") * n_core + core
    col_pos = lax.axis_index("col")
    ev_slots, width_col = shared_rows.shape
    width_row = width_col // ratio
    slot = lax.iota(jnp.int32, ev_slots)
    masked = jnp.where((slot < event_counts[row_pos])[:, None], shared_rows, jnp.float32(0.0))

    col_mine = lax.all_gather(masked, "chip", axis=0, tiled=True)

    halves = masked.reshape(ev_slots, ratio, width_row)
    received = []
    for t in range(ratio):
        perm = []
        for s in range(n_row):
            for c in range(n_col):
                b = (s % ratio) ^ t
                perm.append((s * n_col + c, (ratio * c + b) * n_col + s // ratio))
        piece = halves[:, (row_pos % ratio) ^ t, :]
        received.append(lax.ppermute(piece, ("chip", "core", "col"), perm))
    row_block = jnp.concatenate(received, axis=0)

    half = ev_slots * n_col
    pieces = [(col_pos, row_block)]
    for k in range(1, n_col):
        pairs = [(c, c ^ k) for c in range(n_col)]
        pieces.append((col_pos ^ k, lax.ppermute(row_block, "col", pairs)))
    row_all = jnp.zeros((2 * half, width_row), jnp.float32)
    for src, got in pieces:
        row_all = lax.dynamic_update_slice_in_dim(row_all, got[:ev_slots], src * ev_slots, 0)
        row_all = lax.dynamic_update_slice_in_dim(
            row_all, got[ev_slots:], half + src * ev_slots, 0
        )

    col_mine, row_all = lax.optimization_barrier((col_mine, row_all))
    col_other = lax.ppermute(col_mine, "core", [(0, 1), (1, 0)])

    contract = (((0,), (0,)), ((), ()))
    tile = lax.dot_general(
        row_all[:half], col_mine, contract, precision=high, preferred_element_type=jnp.float32
    )
    tile = tile + lax.dot_general(
        row_all[half:], col_other, contract, precision=high, preferred_element_type=jnp.float32
    )
    rows_global = row_pos * width_row + lax.broadcasted_iota(jnp.int32, (width_row, width_col), 0)
    cols_global = col_pos * width_col + lax.broadcasted_iota(jnp.int32, (width_row, width_col), 1)
    tile = tile + jnp.where(rows_global == cols_global, ridge[None, :], jnp.float32(0.0))

    across = (((1,), (1,)), ((), ()))
    z_part = jnp.concatenate([
        lax.dot_general(col_mine, items, across, precision=high, preferred_element_type=jnp.float32),
        lax.dot_general(col_other, items, across, precision=high, preferred_element_type=jnp.float32),
    ], axis=0)
    q_ridge = jnp.sum(ridge[None, :] * items * items, axis=1)
    lin = jnp.dot(items, theta, precision=highest, preferred_element_type=jnp.float32)
    packed = jnp.concatenate([z_part, q_ridge[None, :], lin[None, :]], axis=0)
    step = n_col // 2
    while step >= 1:
        pairs = [(c, c ^ step) for c in range(n_col)]
        packed = packed + lax.ppermute(packed, "col", pairs)
        step //= 2
    ev_all = z_part.shape[0]
    z = packed[:ev_all]
    quad = jnp.sum(z * z, axis=0) + packed[ev_all]
    item_scores = packed[ev_all + 1] + jnp.sqrt(quad / F)
    held = item_scores
    step = 1
    while step < n_row:
        pairs = [(r, r ^ step) for r in range(n_row)]
        other = lax.ppermute(held, ROW, pairs)
        low = (row_pos & step) == 0
        held = jnp.where(low, jnp.concatenate([held, other]), jnp.concatenate([other, held]))
        step *= 2
    scores = held[cand_ids]
    return (tile, scores)


def solution(mesh):
    n_row = mesh.shape["row"]
    n_col = mesh.shape["col"]
    inner = Mesh(mesh.devices.reshape(n_row // 2, 2, n_col), ("chip", "core", "col"))
    return jax.shard_map(
        body,
        mesh=inner,
        in_specs=(P(ROW, "col"), P(), P("col"), P(ROW, "col"), P(), P("col")),
        out_specs=(P(ROW, "col"), P()),
        check_vma=False,
    )
```

time: 351 us -> 400 us (1.14)
  starting transfers between devices: 82.5 us -> 120 us
  matrix products: 45.7 us -> 51.3 us
  waiting for transfers between devices: 178 us -> 182 us
    ppermute x13 -> x14, starting transfers between devices: 73.9 us -> 104 us  [the longest x7 99 us: body(): pieces.append((col_pos ^ k, lax.ppermute(row_block, 'col', pairs)))]
    ppermute x13 -> x14, waiting for transfers between devices: 120 us -> 143 us  [the longest x7 133 us: body(): pieces.append((col_pos ^ k, lax.ppermute(row_block, 'col', pairs)))]
    all_gather x1, waiting for transfers between devices: 17.1 us -> 0.01 us  [body(): col_mine = lax.all_gather(masked, 'chip', axis=0, tiled=True)]
    ppermute x3, starting transfers between devices: 8.54 us -> 16 us  [body(): packed = packed + lax.ppermute(packed, 'col', pairs)]
    dot_general x2 -> x4, matrix products: 45.1 us -> 50.8 us  [the longest x1 19.4 us: body(): lax.dot_general(row_all[half:], col_other, contract, precision=high, pref...]
    dynamic_update_slice x7 -> x14, local copies, waits for them, and re-layouts: 12.6 us -> 13.9 us  [the longest x7 6.97 us: body(): lax.dynamic_update_slice_in_dim(row_all, got[ev_slots:], half + src * ev_...]
  transfers between devices with their start and end apart: 17 -> 18, of which waited for: 12 -> 9; matrix products, arithmetic and copies ran while one was open for 16% -> 17% of each run, Pallas kernels for 0% -> 0%
where the time goes in v5:
time: 400 us
  waiting for transfers between devices  182 us (46%)
  starting transfers between devices  120 us (30%)
  matrix products  51.3 us (13%)
  local copies, waits for them, and re-layouts  28.7 us (7%)
  between operations  14.3 us (4%)
    ppermute x7, waiting for transfers between devices, body(): pieces.append((col_pos ^ k, lax.ppermute(row_block, 'col', pairs)))  133 us
    ppermute x7, starting transfers between devices, body(): pieces.append((col_pos ^ k, lax.ppermute(row_block, 'col', pairs)))  99 us
    ppermute x3, waiting for transfers between devices, body(): packed = packed + lax.ppermute(packed, 'col', pairs)  38.5 us
    dot_general x1, matrix products, body(): lax.dot_general(row_all[half:], col_other, contract, precision=high, pref...  19.4 us
    dot_general x1, matrix products, body(): lax.dot_general(row_all[:half], col_mine, contract, precision=high, prefe...  16.8 us
    ppermute x3, starting transfers between devices, body(): packed = packed + lax.ppermute(packed, 'col', pairs)  16 us
  transfers between devices with their start and end apart: 18, of which 9 were waited for; matrix products, arithmetic and copies ran while one was open for 17% of the time, Pallas kernels for 0%

profile of v5, /device:TPU:0, one launch (start us, length us, event | category | flops | bytes accessed | tf_op | source)
XLA Modules:
  0.0 399.8 jit_solution(11527646517919340690)
XLA Ops:
  7.2 1.2 dynamic_slice.9
  9.1 2.3 broadcast_select_fusion
  11.5 2.1 reshape.12
  13.6 0.9 constant_dynamic-slice_fusion
  15.6 4.3 %broadcast_in_dim.41 = f32[2048,1024]{1,0:T(8,128)} broadcast(f32[]{:T(128)} %constant.54.clone.1), dimensions={} | broadcast | bytes 8388612 | tf_op jit(solution)/shard_map/broadcast_in_dim | solution.py:47
  19.9 1.1 constant_dynamic-update-slice_fusion.3
  21.0 1.1 constant_dynamic-update-slice_fusion.2
  22.1 64.0 %collective-permute-start.2 = (f32[256,1024]{1,0:T(8,128)}, f32[256,1024]{1,0:T(8,128)}, u32[]{:S(2)}, u32[]{:S(2)}) collective-permute-start(f32[256,1024]{1,0:T(8,128)} %get-tuple-element.10), channel_id=1, source_target_pairs={{0,1},{1,0},{2,3},{3,2},{4,5},{5,4},{6,7},{7,6},{8,9},{9,8},{10,11... | collective-permute-start | bytes 3145736 | tf_op jit(solution)/shard_map/ppermute | solution.py:46
  86.1 17.4 %collective-permute-start.3 = (f32[256,1024]{1,0:T(8,128)}, f32[256,1024]{1,0:T(8,128)S(1)}, u32[]{:S(2)}, u32[]{:S(2)}) collective-permute-start(f32[256,1024]{1,0:T(8,128)} %get-tuple-element.10), channel_id=1, source_target_pairs={{0,2},{1,3},{2,0},{3,1},{4,6},{5,7},{6,4},{7,5},{8,10},{9,11},{10,... | collective-permute-start | bytes 3145736 | tf_op jit(solution)/shard_map/ppermute | solution.py:46
  103.5 8.5 %collective-permute-start.5 = (f32[256,1024]{1,0:T(8,128)}, f32[256,1024]{1,0:T(8,128)S(1)}, u32[]{:S(2)}, u32[]{:S(2)}) collective-permute-start(f32[256,1024]{1,0:T(8,128)} %get-tuple-element.10), channel_id=1, source_target_pairs={{0,4},{1,5},{2,6},{3,7},{4,0},{5,1},{6,2},{7,3},{8,12},{9,13},{10,... | collective-permute-start | bytes 3145736 | tf_op jit(solution)/shard_map/ppermute | solution.py:46
  112.1 2.4 collective-permute-start.6
  114.5 98.8 %collective-permute-done.2 = f32[256,1024]{1,0:T(8,128)} collective-permute-done((f32[256,1024]{1,0:T(8,128)}, f32[256,1024]{1,0:T(8,128)}, u32[]{:S(2)}, u32[]{:S(2)}) %collective-permute-start.2) | collective-permute-done | bytes 1048608 | tf_op jit(solution)/shard_map/ppermute | solution.py:46
  213.2 4.5 %collective-permute-start.7 = (f32[256,1024]{1,0:T(8,128)}, f32[256,1024]{1,0:T(8,128)S(1)}, u32[]{:S(2)}, u32[]{:S(2)}) collective-permute-start(f32[256,1024]{1,0:T(8,128)} %get-tuple-element.10), channel_id=1, source_target_pairs={{0,6},{1,7},{2,4},{3,5},{4,2},{5,3},{6,0},{7,1},{8,14},{9,15},{10,... | collective-permute-start | bytes 3145736 | tf_op jit(solution)/shard_map/ppermute | solution.py:46
  217.7 1.9 slice_dynamic-update-slice_fusion.13
  219.6 1.9 slice_dynamic-update-slice_fusion.12
  221.5 2.2 collective-permute-start.8
  230.4 11.4 %collective-permute-done.7 = f32[256,1024]{1,0:T(8,128)S(1)} collective-permute-done((f32[256,1024]{1,0:T(8,128)}, f32[256,1024]{1,0:T(8,128)S(1)}, u32[]{:S(2)}, u32[]{:S(2)}) %collective-permute-start.7) | collective-permute-done | bytes 1048608 | tf_op jit(solution)/shard_map/ppermute | solution.py:46
  243.6 23.0 %collective-permute-done.8 = f32[256,1024]{1,0:T(8,128)S(1)} collective-permute-done((f32[256,1024]{1,0:T(8,128)}, f32[256,1024]{1,0:T(8,128)S(1)}, u32[]{:S(2)}, u32[]{:S(2)}) %collective-permute-start.8) | collective-permute-done | bytes 1048608 | tf_op jit(solution)/shard_map/ppermute | solution.py:46
  269.2 7.3 %fusion.8 = f32[1024,64]{0,1:T(8,128)S(1)} fusion(f32[1024,2048]{1,0:T(8,128)} %all-gather.2.cloned.1.call-done, f32[64,2048]{1,0:T(8,128)S(1)} %copy-done.1), kind=kOutput, calls=%fused_computation.45 | convolution fusion | flops 805306368 | bytes 9175040 | tf_op jit(solution)/shard_map/dot_general | solution.py:70
  276.6 5.2 %collective-permute-done.9 = f32[1024,2048]{1,0:T(8,128)} collective-permute-done((f32[1024,2048]{1,0:T(8,128)}, f32[1024,2048]{1,0:T(8,128)}, u32[]{:S(2)}, u32[]{:S(2)}) %collective-permute-start.9) | collective-permute-done | bytes 8388640 | tf_op jit(solution)/shard_map/ppermute | solution.py:55
  281.8 7.3 %fusion.9 = f32[1024,64]{0,1:T(8,128)S(1)} fusion(f32[1024,2048]{1,0:T(8,128)} %collective-permute-done.9, f32[64,2048]{1,0:T(8,128)S(1)} %copy-done.1), kind=kOutput, calls=%fused_computation.46 | convolution fusion | flops 805306368 | bytes 9175040 | tf_op jit(solution)/shard_map/dot_general | solution.py:71
  289.2 11.4 %collective-permute-start.10 = (f32[2050,64]{0,1:T(8,128)S(1)}, f32[2050,64]{0,1:T(8,128)S(1)}, u32[]{:S(2)}, u32[]{:S(2)}) collective-permute-start(f32[2050,64]{0,1:T(8,128)S(1)} %concatenate.31), channel_id=1, source_target_pairs={{0,4},{1,5},{2,6},{3,7},{4,0},{5,1},{6,2},{7,3},{8,12},{9,13},{10,... | collective-permute-start | bytes 1574408 | tf_op jit(solution)/shard_map/ppermute | solution.py:79
  300.6 12.9 %collective-permute-done.10 = f32[2050,64]{0,1:T(8,128)S(1)} collective-permute-done((f32[2050,64]{0,1:T(8,128)S(1)}, f32[2050,64]{0,1:T(8,128)S(1)}, u32[]{:S(2)}, u32[]{:S(2)}) %collective-permute-start.10) | collective-permute-done | bytes 524832 | tf_op jit(solution)/shard_map/ppermute | solution.py:79
  313.7 14.1 %collective-permute-done.11 = f32[2050,64]{0,1:T(8,128)S(1)} collective-permute-done((f32[2050,64]{0,1:T(8,128)S(1)}, f32[2050,64]{0,1:T(8,128)S(1)}, u32[]{:S(2)}, u32[]{:S(2)}) %collective-permute-start.11) | collective-permute-done | bytes 524832 | tf_op jit(solution)/shard_map/ppermute | solution.py:79
  327.9 4.5 %collective-permute-start.12 = (f32[2050,64]{0,1:T(8,128)S(1)}, f32[2050,64]{0,1:T(8,128)S(1)}, u32[]{:S(2)}, u32[]{:S(2)}) collective-permute-start(f32[2050,64]{0,1:T(8,128)S(1)} %add.182), channel_id=1, source_target_pairs={{0,1},{1,0},{2,3},{3,2},{4,5},{5,4},{6,7},{7,6},{8,9},{9,8},{10,11... | collective-permute-start | bytes 1574408 | tf_op jit(solution)/shard_map/ppermute | solution.py:79
  332.4 11.5 %collective-permute-done.12 = f32[2050,64]{0,1:T(8,128)S(1)} collective-permute-done((f32[2050,64]{0,1:T(8,128)S(1)}, f32[2050,64]{0,1:T(8,128)S(1)}, u32[]{:S(2)}, u32[]{:S(2)}) %collective-permute-start.12) | collective-permute-done | bytes 524832 | tf_op jit(solution)/shard_map/ppermute | solution.py:79
  344.4 1.1 collective-permute-done.13
  345.6 3.5 collective-permute-done.14
  349.1 4.1 %collective-permute-start.15 = (f32[256]{0:T(256)S(1)}, f32[256]{0:T(256)S(1)}, u32[]{:S(2)}, u32[]{:S(2)}) collective-permute-start(f32[256]{0:T(256)S(1)} %maximum_select_fusion.2), channel_id=1, source_target_pairs={{0,32},{8,40},{16,48},{24,56},{32,0},{40,8},{48,16},{56,24},{64,96... | collective-permute-start | bytes 3080 | tf_op jit(solution)/shard_map/ppermute | solution.py:89
  353.2 16.8 %fusion.2 = f32[1024,2048]{1,0:T(8,128)S(1)} fusion(f32[1024,2048]{1,0:T(8,128)} %all-gather.2.cloned.1.call-done, f32[2048,1024]{1,0:T(8,128)} %slice_dynamic-update-slice_fusion), kind=kOutput, calls=%fused_computation.4 | convolution fusion | flops 12884901888 | bytes 20971520 | tf_op jit(solution)/shard_map/dot_general | solution.py:58
  370.1 19.4 %select_add_fusion = f32[1024,2048]{1,0:T(8,128)} fusion(f32[1024,2048]{1,0:T(8,128)S(1)} %fusion.2, f32[2048]{0:T(1024)S(1)} %copy-done.2, s32[2048]{0:T(1024)S(1)} %iota_add_fusion, s32[1024]{0:T(1024)S(1)} %iota_add_fusion.1, f32[1024,2048]{1,0:T(8,128)} %collective-permute-done.9, f32[2048,1024]{1,0:T(8,128)} %slice_dynamic-update-slice_fusion), kind=kOutput, calls=%fused_computation.1 | convolution fusion | flops 12893290496 | bytes 29380608 | tf_op jit(solution)/shard_map/dot_general | solution.py:61
  389.5 3.4 gather_fusion
  (60 shorter events, 13.8 us)
Async XLA Ops:
  7.2 261.5 %copy-start = (f32[2048]{0:T(1024)S(1)}, f32[2048]{0:T(1024)}, u32[]{:S(2)}) copy-start(f32[2048]{0:T(1024)} %param.11) | copy-start | bytes 24580
  7.2 261.1 %all-gather.2.cloned.1.call-start = ((), (), s32[]{:S(2)}) async-start(), calls=%async_computation | async-start | bytes 9437184 | tf_op jit(solution)/shard_map/all_gather | solution.py:28
  14.6 0.9 collective-permute-start
  15.5 5.5 %collective-permute-start.1 = (f32[128,1024]{1,0:T(8,128)S(1)}, f32[128,1024]{1,0:T(8,128)S(1)}, u32[]{:S(2)}, u32[]{:S(2)}) collective-permute-start(f32[128,1024]{1,0:T(8,128)S(1)} %bitcast.19), channel_id=1, source_target_pairs={{0,8},{1,24},{2,40},{3,56},{4,72},{5,88},{6,104},{7,120},{8,0},{9,... | collective-permute-start | bytes 1572872 | tf_op jit(solution)/shard_map/ppermute | solution.py:39
  21.0 247.4 %copy-start.1 = (f32[64,2048]{1,0:T(8,128)S(1)}, f32[64,2048]{1,0:T(8,128)}, u32[]{:S(2)}) copy-start(f32[64,2048]{1,0:T(8,128)} %param.9) | copy-start | bytes 1572868
  21.0 247.4 %copy-start.2 = (f32[2048]{0:T(1024)S(1)}, f32[2048]{0:T(1024)}, u32[]{:S(2)}) copy-start(f32[2048]{0:T(1024)} %param.8) | copy-start | bytes 24580
  22.1 191.1 %collective-permute-start.2 = (f32[256,1024]{1,0:T(8,128)}, f32[256,1024]{1,0:T(8,128)}, u32[]{:S(2)}, u32[]{:S(2)}) collective-permute-start(f32[256,1024]{1,0:T(8,128)} %get-tuple-element.10), channel_id=1, source_target_pairs={{0,1},{1,0},{2,3},{3,2},{4,5},{5,4},{6,7},{7,6},{8,9},{9,8},{10,11... | collective-permute-start | bytes 3145736 | tf_op jit(solution)/shard_map/ppermute | solution.py:46
  86.1 135.4 %collective-permute-start.3 = (f32[256,1024]{1,0:T(8,128)}, f32[256,1024]{1,0:T(8,128)S(1)}, u32[]{:S(2)}, u32[]{:S(2)}) collective-permute-start(f32[256,1024]{1,0:T(8,128)} %get-tuple-element.10), channel_id=1, source_target_pairs={{0,2},{1,3},{2,0},{3,1},{4,6},{5,7},{6,4},{7,5},{8,10},{9,11},{10,... | collective-permute-start | bytes 3145736 | tf_op jit(solution)/shard_map/ppermute | solution.py:46
  103.5 121.9 %collective-permute-start.4 = (f32[256,1024]{1,0:T(8,128)}, f32[256,1024]{1,0:T(8,128)S(1)}, u32[]{:S(2)}, u32[]{:S(2)}) collective-permute-start(f32[256,1024]{1,0:T(8,128)} %get-tuple-element.10), channel_id=1, source_target_pairs={{0,3},{1,2},{2,1},{3,0},{4,7},{5,6},{6,5},{7,4},{8,11},{9,10},{10,... | collective-permute-start | bytes 3145736 | tf_op jit(solution)/shard_map/ppermute | solution.py:46
  103.5 123.6 %collective-permute-start.5 = (f32[256,1024]{1,0:T(8,128)}, f32[256,1024]{1,0:T(8,128)S(1)}, u32[]{:S(2)}, u32[]{:S(2)}) collective-permute-start(f32[256,1024]{1,0:T(8,128)} %get-tuple-element.10), channel_id=1, source_target_pairs={{0,4},{1,5},{2,6},{3,7},{4,0},{5,1},{6,2},{7,3},{8,12},{9,13},{10,... | collective-permute-start | bytes 3145736 | tf_op jit(solution)/shard_map/ppermute | solution.py:46
  112.1 116.7 %collective-permute-start.6 = (f32[256,1024]{1,0:T(8,128)}, f32[256,1024]{1,0:T(8,128)S(1)}, u32[]{:S(2)}, u32[]{:S(2)}) collective-permute-start(f32[256,1024]{1,0:T(8,128)} %get-tuple-element.10), channel_id=1, source_target_pairs={{0,5},{1,4},{2,7},{3,6},{4,1},{5,0},{6,3},{7,2},{8,13},{9,12},{10,... | collective-permute-start | bytes 3145736 | tf_op jit(solution)/shard_map/ppermute | solution.py:46
  213.2 28.6 %collective-permute-start.7 = (f32[256,1024]{1,0:T(8,128)}, f32[256,1024]{1,0:T(8,128)S(1)}, u32[]{:S(2)}, u32[]{:S(2)}) collective-permute-start(f32[256,1024]{1,0:T(8,128)} %get-tuple-element.10), channel_id=1, source_target_pairs={{0,6},{1,7},{2,4},{3,5},{4,2},{5,3},{6,0},{7,1},{8,14},{9,15},{10,... | collective-permute-start | bytes 3145736 | tf_op jit(solution)/shard_map/ppermute | solution.py:46
  221.5 45.1 %collective-permute-start.8 = (f32[256,1024]{1,0:T(8,128)}, f32[256,1024]{1,0:T(8,128)S(1)}, u32[]{:S(2)}, u32[]{:S(2)}) collective-permute-start(f32[256,1024]{1,0:T(8,128)} %get-tuple-element.10), channel_id=1, source_target_pairs={{0,7},{1,6},{2,5},{3,4},{4,3},{5,2},{6,1},{7,0},{8,15},{9,14},{10,... | collective-permute-start | bytes 3145736 | tf_op jit(solution)/shard_map/ppermute | solution.py:46
  268.3 13.5 %collective-permute-start.9 = (f32[1024,2048]{1,0:T(8,128)}, f32[1024,2048]{1,0:T(8,128)}, u32[]{:S(2)}, u32[]{:S(2)}) collective-permute-start(f32[1024,2048]{1,0:T(8,128)} %all-gather.2.cloned.1.call-done), channel_id=1, source_target_pairs={{0,8},{8,0},{1,9},{9,1},{2,10},{10,2},{3,11},{11,3},{4,12},{12,4},... | collective-permute-start | bytes 25165832 | tf_op jit(solution)/shard_map/ppermute | solution.py:55
  276.5 55.8 %copy-start.3 = (s32[512]{0:T(512)S(1)}, s32[512]{0:T(512)}, u32[]{:S(2)}) copy-start(s32[512]{0:T(512)} %param.10) | copy-start | bytes 6148
  289.2 24.3 %collective-permute-start.10 = (f32[2050,64]{0,1:T(8,128)S(1)}, f32[2050,64]{0,1:T(8,128)S(1)}, u32[]{:S(2)}, u32[]{:S(2)}) collective-permute-start(f32[2050,64]{0,1:T(8,128)S(1)} %concatenate.31), channel_id=1, source_target_pairs={{0,4},{1,5},{2,6},{3,7},{4,0},{5,1},{6,2},{7,3},{8,12},{9,13},{10,... | collective-permute-start | bytes 1574408 | tf_op jit(solution)/shard_map/ppermute | solution.py:79
  313.6 14.2 %collective-permute-start.11 = (f32[2050,64]{0,1:T(8,128)S(1)}, f32[2050,64]{0,1:T(8,128)S(1)}, u32[]{:S(2)}, u32[]{:S(2)}) collective-permute-start(f32[2050,64]{0,1:T(8,128)S(1)} %add.181), channel_id=1, source_target_pairs={{0,2},{1,3},{2,0},{3,1},{4,6},{5,7},{6,4},{7,5},{8,10},{9,11},{10,... | collective-permute-start | bytes 1574408 | tf_op jit(solution)/shard_map/ppermute | solution.py:79
  327.9 16.0 %collective-permute-start.12 = (f32[2050,64]{0,1:T(8,128)S(1)}, f32[2050,64]{0,1:T(8,128)S(1)}, u32[]{:S(2)}, u32[]{:S(2)}) collective-permute-start(f32[2050,64]{0,1:T(8,128)S(1)} %add.182), channel_id=1, source_target_pairs={{0,1},{1,0},{2,3},{3,2},{4,5},{5,4},{6,7},{7,6},{8,9},{9,8},{10,11... | collective-permute-start | bytes 1574408 | tf_op jit(solution)/shard_map/ppermute | solution.py:79
  344.3 1.2 collective-permute-start.13
  345.5 3.6 collective-permute-start.14
  349.1 20.9 %collective-permute-start.15 = (f32[256]{0:T(256)S(1)}, f32[256]{0:T(256)S(1)}, u32[]{:S(2)}, u32[]{:S(2)}) collective-permute-start(f32[256]{0:T(256)S(1)} %maximum_select_fusion.2), channel_id=1, source_target_pairs={{0,32},{8,40},{16,48},{24,56},{32,0},{40,8},{48,16},{56,24},{64,96... | collective-permute-start | bytes 3080 | tf_op jit(solution)/shard_map/ppermute | solution.py:89
  370.0 19.5 %collective-permute-start.16 = (f32[512]{0:T(512)S(1)}, f32[512]{0:T(512)S(1)}, u32[]{:S(2)}, u32[]{:S(2)}) collective-permute-start(f32[512]{0:T(512)S(1)} %maximum_select_fusion.1), channel_id=1, source_target_pairs={{0,64},{8,72},{16,80},{24,88},{32,96},{40,104},{48,112},{56,120},{... | collective-permute-start | bytes 6152 | tf_op jit(solution)/shard_map/ppermute | solution.py:89
Sparse Core Ops, SparseCore 0:
  11.6 162.2 all-gather.1

commit v6 on v3

--- a/solution.py
+++ b/solution.py
@@ -37,34 +37,38 @@
         sum(jnp.where(parity ^ t == a, received[t], 0.0) for t in range(ratio))
         for a in range(ratio)
     ]
-    row_block = jnp.concatenate(ordered, axis=0)
-
     n_y = n_col // 2
     ring = [y * 2 for y in range(n_y)] + [y * 2 + 1 for y in reversed(range(n_y))]
     where_in_ring = [ring.index(c) for c in range(n_col)]
     forward = [(ring[p], ring[(p + 1) % n_col]) for p in range(n_col)]
     backward = [(ring[p], ring[(p - 1) % n_col]) for p in range(n_col)]
-    block_rows = row_block.shape[0]
-    half_rows = block_rows // 2
+    half_rows = ev_slots // 2
     ring_tab = jnp.array(ring, jnp.int32)
     me = jnp.array(where_in_ring, jnp.int32)[col_pos]
-    row_all = jnp.zeros((n_col * block_rows, width_row), jnp.float32)
-    ahead, behind = row_block[:half_rows], row_block[half_rows:]
-    row_all = lax.dynamic_update_slice_in_dim(row_all, ahead, col_pos * block_rows, 0)
-    row_all = lax.dynamic_update_slice_in_dim(row_all, behind, col_pos * block_rows + half_rows, 0)
+    row_even = jnp.zeros((n_col * ev_slots, width_row), jnp.float32)
+    ahead, behind = ordered[0][:half_rows], ordered[0][half_rows:]
+    row_even = lax.dynamic_update_slice_in_dim(row_even, ahead, col_pos * ev_slots, 0)
+    row_even = lax.dynamic_update_slice_in_dim(row_even, behind, col_pos * ev_slots + half_rows, 0)
     for k in range(1, n_col):
         ahead = lax.ppermute(ahead, "col", forward)
         behind = lax.ppermute(behind, "col", backward)
         from_ahead = ring_tab[(me - k) % n_col]
         from_behind = ring_tab[(me + k) % n_col]
-        row_all = lax.dynamic_update_slice_in_dim(row_all, ahead, from_ahead * block_rows, 0)
-        row_all = lax.dynamic_update_slice_in_dim(
-            row_all, behind, from_behind * block_rows + half_rows, 0
+        row_even = lax.dynamic_update_slice_in_dim(row_even, ahead, from_ahead * ev_slots, 0)
+        row_even = lax.dynamic_update_slice_in_dim(
+            row_even, behind, from_behind * ev_slots + half_rows, 0
         )
+    row_odd = lax.all_gather(ordered[1], "col", axis=0, tiled=True)
 
+    by_shard = col_all.reshape(n_col, ratio, ev_slots, width_col)
     contract = (((0,), (0,)), ((), ()))
     tile = lax.dot_general(
-        row_all, col_all, contract, precision=high, preferred_element_type=jnp.float32
+        row_even, by_shard[:, 0].reshape(n_col * ev_slots, width_col), contract,
+        precision=high, preferred_element_type=jnp.float32,
+    )
+    tile = tile + lax.dot_general(
+        row_odd, by_shard[:, 1].reshape(n_col * ev_slots, width_col), contract,
+        precision=high, preferred_element_type=jnp.float32,
     )
     rows_global = row_pos * width_row + lax.broadcasted_iota(jnp.int32, (width_row, width_col), 0)
     cols_global = col_pos * width_col + lax.broadcasted_iota(jnp.int32, (width_row, width_col), 1)

time: 324 us -> 331 us (1.022)
  starting transfers between devices: 79.1 us -> 89.5 us
  waiting for transfers between devices: 126 us -> 117 us
    ppermute x3, waiting for transfers between devices: 24.2 us -> 0.01 us  [body(): packed = packed + lax.ppermute(packed, 'col', pairs)]
    ppermute x7, waiting for transfers between devices: 12.9 us -> 32.6 us  [body(): behind = lax.ppermute(behind, 'col', backward)]
    ppermute x7, waiting for transfers between devices: 50.7 us -> 32.5 us  [body(): ahead = lax.ppermute(ahead, 'col', forward)]
    all_gather x1, waiting for transfers between devices: 32.5 us -> 50 us  [body(): col_all = lax.all_gather(masked, 'row', axis=0, tiled=True)]
    slice x0 -> x2, local copies, waits for them, and re-layouts: none -> 11.7 us  [the longest x1 10.9 us: body(): by_shard[:, 0].reshape(n_col * ev_slots, width_col)]
    ppermute x7, starting transfers between devices: 52.2 us -> 61.8 us  [body(): ahead = lax.ppermute(ahead, 'col', forward)]
    ppermute x4, starting transfers between devices: 0.2 us -> 9.82 us  [body(): other = lax.ppermute(held, 'row', pairs)]
    dynamic_update_slice x14 -> x15, local copies, waits for them, and re-layouts: 18.5 us -> 11.8 us  [the longest x7 5.99 us: body(): lax.dynamic_update_slice_in_dim(row_even, behind, from_behind * ev_slots...]
  transfers between devices with their start and end apart: 24 -> 25, of which waited for: 16 -> 12; matrix products, arithmetic and copies ran while one was open for 24% -> 25% of each run, Pallas kernels for 0% -> 0%
where the time goes in v6:
time: 331 us; the launch traced here: 330 us
  waiting for transfers between devices  117 us (35%)
  starting transfers between devices  89.5 us (27%)
  matrix products  50.9 us (15%)
  local copies, waits for them, and re-layouts  35.6 us (11%)
  between operations  32.3 us (10%)
  other arithmetic  4.53 us (1%)
    ppermute x7, starting transfers between devices, body(): ahead = lax.ppermute(ahead, 'col', forward)  61.8 us
    all_gather x1, waiting for transfers between devices, body(): col_all = lax.all_gather(masked, 'row', axis=0, tiled=True)  50 us
    ppermute x7, waiting for transfers between devices, body(): behind = lax.ppermute(behind, 'col', backward)  32.6 us
    ppermute x7, waiting for transfers between devices, body(): ahead = lax.ppermute(ahead, 'col', forward)  32.5 us
    dot_general x1, matrix products, body(): lax.dot_general(row_even, by_shard[:, 0].reshape(n_col * ev_slots, width_...  20.8 us
    dot_general x1, matrix products, body(): lax.dot_general(row_odd, by_shard[:, 1].reshape(n_col * ev_slots, width_c...  18.3 us
    ppermute x7, starting transfers between devices, body(): behind = lax.ppermute(behind, 'col', backward)  16 us
    dot_general x1, matrix products, body(): lax.dot_general(col_all, items, (((1,), (1,)), ((), ())), precision=high,...  11.2 us
  transfers between devices with their start and end apart: 25, of which 12 were waited for; matrix products, arithmetic and copies ran while one was open for 25% of the time, Pallas kernels for 0%

profile of v6, /device:TPU:0, one launch (start us, length us, event | category | flops | bytes accessed | tf_op | source)
XLA Modules:
  0.0 329.7 jit_solution(3485583003679443657)
XLA Ops:
  7.2 1.2 dynamic_slice.54
  9.1 2.3 broadcast_select_fusion
  11.6 2.1 reshape.99
  15.7 1.8 collective-permute-done.1
  17.5 0.9 select_add_fusion.2
  18.5 2.5 broadcast_in_dim.46
  21.8 46.0 %collective-permute-start.2 = (f32[64,1024]{1,0:T(8,128)S(1)}, f32[64,1024]{1,0:T(8,128)S(1)}, u32[]{:S(2)}, u32[]{:S(2)}) collective-permute-start(f32[64,1024]{1,0:T(8,128)S(1)} %get-tuple-element.12), channel_id=1, source_target_pairs={{0,2},{2,4},{4,6},{6,7},{7,5},{5,3},{3,1},{1,0},{8,10},{10,12},{12... | collective-permute-start | bytes 786440 | tf_op jit(solution)/shard_map/ppermute | solution.py:53
  67.8 4.5 %collective-permute-start.3 = (f32[64,1024]{1,0:T(8,128)S(1)}, f32[64,1024]{1,0:T(8,128)S(1)}, u32[]{:S(2)}, u32[]{:S(2)}) collective-permute-start(f32[64,1024]{1,0:T(8,128)S(1)} %get-tuple-element.10), channel_id=1, source_target_pairs={{0,1},{2,0},{4,2},{6,4},{7,6},{5,7},{3,5},{1,3},{8,9},{10,8},{12,1... | collective-permute-start | bytes 786440 | tf_op jit(solution)/shard_map/ppermute | solution.py:54
  72.5 4.6 %collective-permute-done.2 = f32[64,1024]{1,0:T(8,128)S(1)} collective-permute-done((f32[64,1024]{1,0:T(8,128)S(1)}, f32[64,1024]{1,0:T(8,128)S(1)}, u32[]{:S(2)}, u32[]{:S(2)}) %collective-permute-start.2) | collective-permute-done | bytes 262176 | tf_op jit(solution)/shard_map/ppermute | solution.py:53
  77.2 6.8 %collective-permute-done.3 = f32[64,1024]{1,0:T(8,128)S(1)} collective-permute-done((f32[64,1024]{1,0:T(8,128)S(1)}, f32[64,1024]{1,0:T(8,128)S(1)}, u32[]{:S(2)}, u32[]{:S(2)}) %collective-permute-start.3) | collective-permute-done | bytes 262176 | tf_op jit(solution)/shard_map/ppermute | solution.py:54
  84.0 4.0 %collective-permute-start.5 = (f32[64,1024]{1,0:T(8,128)S(1)}, f32[64,1024]{1,0:T(8,128)S(1)}, u32[]{:S(2)}, u32[]{:S(2)}) collective-permute-start(f32[64,1024]{1,0:T(8,128)S(1)} %collective-permute-done.3), channel_id=1, source_target_pairs={{0,1},{2,0},{4,2},{6,4},{7,6},{5,7},{3,5},{1,3},{8,9},{10,8},{12,1... | collective-permute-start | bytes 786440 | tf_op jit(solution)/shard_map/ppermute | solution.py:54
  108.0 3.5 %collective-permute-start.7 = (f32[64,1024]{1,0:T(8,128)S(1)}, f32[64,1024]{1,0:T(8,128)}, u32[]{:S(2)}, u32[]{:S(2)}) collective-permute-start(f32[64,1024]{1,0:T(8,128)S(1)} %collective-permute-done.5), channel_id=1, source_target_pairs={{0,1},{2,0},{4,2},{6,4},{7,6},{5,7},{3,5},{1,3},{8,9},{10,8},{12,1... | collective-permute-start | bytes 786440 | tf_op jit(solution)/shard_map/ppermute | solution.py:54
  111.5 50.0 %all-gather.3.cloned.1.call-done = f32[2048,2048]{1,0:T(8,128)} async-done(((f32[128,2048]{1,0:T(8,128)}), f32[2048,2048]{1,0:T(8,128)}) %all-gather.3.cloned.1.call-update) | async-done | bytes 16777232 | tf_op jit(solution)/shard_map/all_gather | solution.py:23
  161.5 11.2 %fusion.6 = f32[2048,64]{0,1:T(8,128)S(1)} fusion(f32[2048,2048]{1,0:T(8,128)} %all-gather.3.cloned.1.call-done, f32[64,2048]{1,0:T(8,128)S(1)} %copy-done.3), kind=kOutput, calls=%fused_computation.45 | convolution fusion | flops 1610612736 | bytes 17825792 | tf_op jit(solution)/shard_map/dot_general | solution.py:77
  173.7 8.3 %collective-permute-start.8 = (f32[64,1024]{1,0:T(8,128)S(1)}, f32[64,1024]{1,0:T(8,128)S(1)}, u32[]{:S(2)}, u32[]{:S(2)}) collective-permute-start(f32[64,1024]{1,0:T(8,128)S(1)} %collective-permute-done.6), channel_id=1, source_target_pairs={{0,2},{2,4},{4,6},{6,7},{7,5},{5,3},{3,1},{1,0},{8,10},{10,12},{12... | collective-permute-start | bytes 786440 | tf_op jit(solution)/shard_map/ppermute | solution.py:53
  184.2 15.2 %collective-permute-done.8 = f32[64,1024]{1,0:T(8,128)S(1)} collective-permute-done((f32[64,1024]{1,0:T(8,128)S(1)}, f32[64,1024]{1,0:T(8,128)S(1)}, u32[]{:S(2)}, u32[]{:S(2)}) %collective-permute-start.8) | collective-permute-done | bytes 262176 | tf_op jit(solution)/shard_map/ppermute | solution.py:53
  199.4 2.5 collective-permute-start.10
  203.4 2.2 collective-permute-done.9
  206.3 1.7 constant_dynamic-update-slice_fusion.8
  208.6 2.4 collective-permute-start.12
  211.8 18.1 %collective-permute-done.11 = f32[64,1024]{1,0:T(8,128)S(1)} collective-permute-done((f32[64,1024]{1,0:T(8,128)S(1)}, f32[64,1024]{1,0:T(8,128)S(1)}, u32[]{:S(2)}, u32[]{:S(2)}) %collective-permute-start.11) | collective-permute-done | bytes 262176 | tf_op jit(solution)/shard_map/ppermute | solution.py:54
  231.5 1.7 collective-permute-done.12
  233.2 2.5 collective-permute-start.14
  236.4 5.1 %collective-permute-done.13 = f32[64,1024]{1,0:T(8,128)S(1)} collective-permute-done((f32[64,1024]{1,0:T(8,128)S(1)}, f32[64,1024]{1,0:T(8,128)S(1)}, u32[]{:S(2)}, u32[]{:S(2)}) %collective-permute-start.13) | collective-permute-done | bytes 262176 | tf_op jit(solution)/shard_map/ppermute | solution.py:54
  241.6 4.0 %collective-permute-start.15 = (f32[64,1024]{1,0:T(8,128)S(1)}, f32[64,1024]{1,0:T(8,128)S(1)}, u32[]{:S(2)}, u32[]{:S(2)}) collective-permute-start(f32[64,1024]{1,0:T(8,128)S(1)} %collective-permute-done.13), channel_id=1, source_target_pairs={{0,1},{2,0},{4,2},{6,4},{7,6},{5,7},{3,5},{1,3},{8,9},{10,8},{12,1... | collective-permute-start | bytes 786440 | tf_op jit(solution)/shard_map/ppermute | solution.py:54
  247.0 10.3 %collective-permute-done.14 = f32[64,1024]{1,0:T(8,128)S(1)} collective-permute-done((f32[64,1024]{1,0:T(8,128)S(1)}, f32[64,1024]{1,0:T(8,128)S(1)}, u32[]{:S(2)}, u32[]{:S(2)}) %collective-permute-start.14) | collective-permute-done | bytes 262176 | tf_op jit(solution)/shard_map/ppermute | solution.py:53
  259.7 1.7 collective-permute-start.20
  261.4 10.9 %fusion.2 = (f32[8,1,128,2048]{3,2,1,0:T(8,128)}, f32[8,1,128,2048]{3,2,1,0:T(8,128)}) fusion(f32[8,2,128,2048]{3,2,1,0:T(8,128)} %bitcast.57), kind=kLoop, calls=%fused_computation.41 | loop fusion | bytes 33554432 | tf_op jit(solution)/shard_map/slice | solution.py:66
  272.3 8.0 %collective-permute-start.21 = (f32[256]{0:T(256)S(1)}, f32[256]{0:T(256)S(1)}, u32[]{:S(2)}, u32[]{:S(2)}) collective-permute-start(f32[256]{0:T(256)S(1)} %maximum_select_fusion.2), channel_id=1, source_target_pairs={{0,32},{8,40},{16,48},{24,56},{32,0},{40,8},{48,16},{56,24},{64,96... | collective-permute-start | bytes 3080 | tf_op jit(solution)/shard_map/ppermute | solution.py:98
  280.3 18.3 %fusion.5 = f32[1024,2048]{1,0:T(8,128)} fusion(f32[1024,1024]{1,0:T(8,128)} %all-gather.5.cloned.1.call-done, f32[1024,2048]{1,0:T(8,128)} %bitcast.59), kind=kOutput, calls=%fused_computation.44 | convolution fusion | flops 12884901888 | bytes 20971520 | tf_op jit(solution)/shard_map/dot_general | solution.py:69
  298.7 20.8 %select_add_fusion = f32[1024,2048]{1,0:T(8,128)} fusion(f32[1024,2048]{1,0:T(8,128)} %fusion.5, f32[2048]{0:T(1024)S(1)} %copy-done.5, s32[2048]{0:T(1024)S(1)} %iota_add_fusion, s32[1024]{0:T(1024)S(1)} %iota_add_fusion.1, f32[1024,1024]{1,0:T(8,128)} %constant_dynamic-update-slice_fusion, f32[1024,2048]{1,0:T(8,128)S(1)} %bitcast.58), kind=kOutput, calls=%fused_computation.1 | convolution fusion | flops 12893290496 | bytes 29380608 | tf_op jit(solution)/shard_map/dot_general | solution.py:65
  319.5 3.4 %gather_fusion = f32[512]{0:T(512)} fusion(f32[1024]{0:T(1024)S(1)} %maximum_select_fusion, s32[1024]{0:T(1024)S(1)} %pad_clamp_fusion), kind=kCustom, calls=%fused_computation | custom fusion | bytes 6144 | tf_op jit(solution)/shard_map/gather | solution.py:102
  (86 shorter events, 18.7 us)
Async XLA Ops:
  7.2 100.2 %copy-start = (f32[2048]{0:T(1024)S(1)}, f32[2048]{0:T(1024)}, u32[]{:S(2)}) copy-start(f32[2048]{0:T(1024)} %param.13) | copy-start | bytes 24580
  7.2 154.3 %all-gather.3.cloned.1.call-start = ((), (), s32[]{:S(2)}) async-start(), calls=%async_computation | async-start | bytes 17825792 | tf_op jit(solution)/shard_map/all_gather | solution.py:23
  11.5 268.8 %all-gather.5.cloned.1.call-start = ((), (), s32[]{:S(2)}) async-start(), calls=%async_computation.1 | async-start | bytes 4718592 | tf_op jit(solution)/shard_map/all_gather | solution.py:61
  14.7 1.0 collective-permute-start
  15.5 56.8 %copy-start.3 = (f32[64,2048]{1,0:T(8,128)S(1)}, f32[64,2048]{1,0:T(8,128)}, u32[]{:S(2)}) copy-start(f32[64,2048]{1,0:T(8,128)} %param.11) | copy-start | bytes 1572868
  15.5 56.8 %copy-start.5 = (f32[2048]{0:T(1024)S(1)}, f32[2048]{0:T(1024)}, u32[]{:S(2)}) copy-start(f32[2048]{0:T(1024)} %param.10) | copy-start | bytes 24580
  15.5 2.0 collective-permute-start.1
  15.7 72.3 %copy-start.7 = (s32[8]{0:T(128)S(1)}, s32[8]{0:T(128)}, u32[]{:S(2)}) copy-start(s32[8]{0:T(128)} %constant.194.clone) | copy-start | bytes 100
  15.7 82.2 %copy-start.4 = (s32[8]{0:T(128)S(1)}, s32[8]{0:T(128)}, u32[]{:S(2)}) copy-start(s32[8]{0:T(128)} %constant.193.clone) | copy-start | bytes 100
  21.8 55.4 %collective-permute-start.2 = (f32[64,1024]{1,0:T(8,128)S(1)}, f32[64,1024]{1,0:T(8,128)S(1)}, u32[]{:S(2)}, u32[]{:S(2)}) collective-permute-start(f32[64,1024]{1,0:T(8,128)S(1)} %get-tuple-element.12), channel_id=1, source_target_pairs={{0,2},{2,4},{4,6},{6,7},{7,5},{5,3},{3,1},{1,0},{8,10},{10,12},{12... | collective-permute-start | bytes 786440 | tf_op jit(solution)/shard_map/ppermute | solution.py:53
  67.8 16.2 %collective-permute-start.3 = (f32[64,1024]{1,0:T(8,128)S(1)}, f32[64,1024]{1,0:T(8,128)S(1)}, u32[]{:S(2)}, u32[]{:S(2)}) collective-permute-start(f32[64,1024]{1,0:T(8,128)S(1)} %get-tuple-element.10), channel_id=1, source_target_pairs={{0,1},{2,0},{4,2},{6,4},{7,6},{5,7},{3,5},{1,3},{8,9},{10,8},{12,1... | collective-permute-start | bytes 786440 | tf_op jit(solution)/shard_map/ppermute | solution.py:54
  77.2 30.7 %collective-permute-start.4 = (f32[64,1024]{1,0:T(8,128)S(1)}, f32[64,1024]{1,0:T(8,128)S(1)}, u32[]{:S(2)}, u32[]{:S(2)}) collective-permute-start(f32[64,1024]{1,0:T(8,128)S(1)} %collective-permute-done.2), channel_id=1, source_target_pairs={{0,2},{2,4},{4,6},{6,7},{7,5},{5,3},{3,1},{1,0},{8,10},{10,12},{12... | collective-permute-start | bytes 786440 | tf_op jit(solution)/shard_map/ppermute | solution.py:53
  84.0 24.0 %collective-permute-start.5 = (f32[64,1024]{1,0:T(8,128)S(1)}, f32[64,1024]{1,0:T(8,128)S(1)}, u32[]{:S(2)}, u32[]{:S(2)}) collective-permute-start(f32[64,1024]{1,0:T(8,128)S(1)} %collective-permute-done.3), channel_id=1, source_target_pairs={{0,1},{2,0},{4,2},{6,4},{7,6},{5,7},{3,5},{1,3},{8,9},{10,8},{12,1... | collective-permute-start | bytes 786440 | tf_op jit(solution)/shard_map/ppermute | solution.py:54
  107.9 65.7 %collective-permute-start.6 = (f32[64,1024]{1,0:T(8,128)S(1)}, f32[64,1024]{1,0:T(8,128)S(1)}, u32[]{:S(2)}, u32[]{:S(2)}) collective-permute-start(f32[64,1024]{1,0:T(8,128)S(1)} %collective-permute-done.4), channel_id=1, source_target_pairs={{0,2},{2,4},{4,6},{6,7},{7,5},{5,3},{3,1},{1,0},{8,10},{10,12},{12... | collective-permute-start | bytes 786440 | tf_op jit(solution)/shard_map/ppermute | solution.py:53
  108.0 74.7 %collective-permute-start.7 = (f32[64,1024]{1,0:T(8,128)S(1)}, f32[64,1024]{1,0:T(8,128)}, u32[]{:S(2)}, u32[]{:S(2)}) collective-permute-start(f32[64,1024]{1,0:T(8,128)S(1)} %collective-permute-done.5), channel_id=1, source_target_pairs={{0,1},{2,0},{4,2},{6,4},{7,6},{5,7},{3,5},{1,3},{8,9},{10,8},{12,1... | collective-permute-start | bytes 786440 | tf_op jit(solution)/shard_map/ppermute | solution.py:54
  172.9 29.0 %collective-permute-start.16 = (f32[2050,64]{0,1:T(8,128)S(1)}, f32[2050,64]{0,1:T(8,128)S(1)}, u32[]{:S(2)}, u32[]{:S(2)}) collective-permute-start(f32[2050,64]{0,1:T(8,128)S(1)} %concatenate.27), channel_id=1, source_target_pairs={{0,4},{1,5},{2,6},{3,7},{4,0},{5,1},{6,2},{7,3},{8,12},{9,13},{10,... | collective-permute-start | bytes 1574408 | tf_op jit(solution)/shard_map/ppermute | solution.py:87
  173.7 25.7 %collective-permute-start.8 = (f32[64,1024]{1,0:T(8,128)S(1)}, f32[64,1024]{1,0:T(8,128)S(1)}, u32[]{:S(2)}, u32[]{:S(2)}) collective-permute-start(f32[64,1024]{1,0:T(8,128)S(1)} %collective-permute-done.6), channel_id=1, source_target_pairs={{0,2},{2,4},{4,6},{6,7},{7,5},{5,3},{3,1},{1,0},{8,10},{10,12},{12... | collective-permute-start | bytes 786440 | tf_op jit(solution)/shard_map/ppermute | solution.py:53
  182.7 22.9 %collective-permute-start.9 = (f32[64,1024]{1,0:T(8,128)}, f32[64,1024]{1,0:T(8,128)S(1)}, u32[]{:S(2)}, u32[]{:S(2)}) collective-permute-start(f32[64,1024]{1,0:T(8,128)} %collective-permute-done.7), channel_id=1, source_target_pairs={{0,1},{2,0},{4,2},{6,4},{7,6},{5,7},{3,5},{1,3},{8,9},{10,8},{12,1... | collective-permute-start | bytes 786440 | tf_op jit(solution)/shard_map/ppermute | solution.py:54
  199.4 9.3 %collective-permute-start.10 = (f32[64,1024]{1,0:T(8,128)S(1)}, f32[64,1024]{1,0:T(8,128)S(1)}, u32[]{:S(2)}, u32[]{:S(2)}) collective-permute-start(f32[64,1024]{1,0:T(8,128)S(1)} %collective-permute-done.8), channel_id=1, source_target_pairs={{0,2},{2,4},{4,6},{6,7},{7,5},{5,3},{3,1},{1,0},{8,10},{10,12},{12... | collective-permute-start | bytes 786440 | tf_op jit(solution)/shard_map/ppermute | solution.py:53
  201.9 28.7 %collective-permute-start.17 = (f32[2050,64]{0,1:T(8,128)S(1)}, f32[2050,64]{0,1:T(8,128)S(1)}, u32[]{:S(2)}, u32[]{:S(2)}) collective-permute-start(f32[2050,64]{0,1:T(8,128)S(1)} %add.428), channel_id=1, source_target_pairs={{0,2},{1,3},{2,0},{3,1},{4,6},{5,7},{6,4},{7,5},{8,10},{9,11},{10,... | collective-permute-start | bytes 1574408 | tf_op jit(solution)/shard_map/ppermute | solution.py:87
  205.6 24.3 %collective-permute-start.11 = (f32[64,1024]{1,0:T(8,128)S(1)}, f32[64,1024]{1,0:T(8,128)S(1)}, u32[]{:S(2)}, u32[]{:S(2)}) collective-permute-start(f32[64,1024]{1,0:T(8,128)S(1)} %collective-permute-done.9), channel_id=1, source_target_pairs={{0,1},{2,0},{4,2},{6,4},{7,6},{5,7},{3,5},{1,3},{8,9},{10,8},{12,1... | collective-permute-start | bytes 786440 | tf_op jit(solution)/shard_map/ppermute | solution.py:54
  208.6 24.6 %collective-permute-start.12 = (f32[64,1024]{1,0:T(8,128)S(1)}, f32[64,1024]{1,0:T(8,128)S(1)}, u32[]{:S(2)}, u32[]{:S(2)}) collective-permute-start(f32[64,1024]{1,0:T(8,128)S(1)} %collective-permute-done.10), channel_id=1, source_target_pairs={{0,2},{2,4},{4,6},{6,7},{7,5},{5,3},{3,1},{1,0},{8,10},{10,12},{12... | collective-permute-start | bytes 786440 | tf_op jit(solution)/shard_map/ppermute | solution.py:53
  229.9 11.6 %collective-permute-start.13 = (f32[64,1024]{1,0:T(8,128)S(1)}, f32[64,1024]{1,0:T(8,128)S(1)}, u32[]{:S(2)}, u32[]{:S(2)}) collective-permute-start(f32[64,1024]{1,0:T(8,128)S(1)} %collective-permute-done.11), channel_id=1, source_target_pairs={{0,1},{2,0},{4,2},{6,4},{7,6},{5,7},{3,5},{1,3},{8,9},{10,8},{12,1... | collective-permute-start | bytes 786440 | tf_op jit(solution)/shard_map/ppermute | solution.py:54
  230.7 27.3 %collective-permute-start.18 = (f32[2050,64]{0,1:T(8,128)S(1)}, f32[2050,64]{0,1:T(8,128)S(1)}, u32[]{:S(2)}, u32[]{:S(2)}) collective-permute-start(f32[2050,64]{0,1:T(8,128)S(1)} %add.429), channel_id=1, source_target_pairs={{0,1},{1,0},{2,3},{3,2},{4,5},{5,4},{6,7},{7,6},{8,9},{9,8},{10,11... | collective-permute-start | bytes 1574408 | tf_op jit(solution)/shard_map/ppermute | solution.py:87
  233.2 24.1 %collective-permute-start.14 = (f32[64,1024]{1,0:T(8,128)S(1)}, f32[64,1024]{1,0:T(8,128)S(1)}, u32[]{:S(2)}, u32[]{:S(2)}) collective-permute-start(f32[64,1024]{1,0:T(8,128)S(1)} %collective-permute-done.12), channel_id=1, source_target_pairs={{0,2},{2,4},{4,6},{6,7},{7,5},{5,3},{3,1},{1,0},{8,10},{10,12},{12... | collective-permute-start | bytes 786440 | tf_op jit(solution)/shard_map/ppermute | solution.py:53
  241.6 17.3 %collective-permute-start.15 = (f32[64,1024]{1,0:T(8,128)S(1)}, f32[64,1024]{1,0:T(8,128)S(1)}, u32[]{:S(2)}, u32[]{:S(2)}) collective-permute-start(f32[64,1024]{1,0:T(8,128)S(1)} %collective-permute-done.13), channel_id=1, source_target_pairs={{0,1},{2,0},{4,2},{6,4},{7,6},{5,7},{3,5},{1,3},{8,9},{10,8},{12,1... | collective-permute-start | bytes 786440 | tf_op jit(solution)/shard_map/ppermute | solution.py:54
  258.4 1.2 collective-permute-start.19
  259.7 12.6 %collective-permute-start.20 = (f32[128]{0:T(128)S(1)}, f32[128]{0:T(128)S(1)}, u32[]{:S(2)}, u32[]{:S(2)}) collective-permute-start(f32[128]{0:T(128)S(1)} %broadcast_select_fusion.1), channel_id=1, source_target_pairs={{0,16},{8,24},{16,0},{24,8},{32,48},{40,56},{48,32},{56,40},{64,80... | collective-permute-start | bytes 1544 | tf_op jit(solution)/shard_map/ppermute | solution.py:98
  272.3 26.3 %collective-permute-start.21 = (f32[256]{0:T(256)S(1)}, f32[256]{0:T(256)S(1)}, u32[]{:S(2)}, u32[]{:S(2)}) collective-permute-start(f32[256]{0:T(256)S(1)} %maximum_select_fusion.2), channel_id=1, source_target_pairs={{0,32},{8,40},{16,48},{24,56},{32,0},{40,8},{48,16},{56,24},{64,96... | collective-permute-start | bytes 3080 | tf_op jit(solution)/shard_map/ppermute | solution.py:98
  280.3 18.4 %copy-start.2 = (f32[8,1,128,2048]{3,2,1,0:T(8,128)S(1)}, f32[8,1,128,2048]{3,2,1,0:T(8,128)}, u32[]{:S(2)}) copy-start(f32[8,1,128,2048]{3,2,1,0:T(8,128)} %get-tuple-element.4) | copy-start | bytes 25165828
  298.6 20.9 %collective-permute-start.22 = (f32[512]{0:T(512)S(1)}, f32[512]{0:T(512)S(1)}, u32[]{:S(2)}, u32[]{:S(2)}) collective-permute-start(f32[512]{0:T(512)S(1)} %maximum_select_fusion.1), channel_id=1, source_target_pairs={{0,64},{8,72},{16,80},{24,88},{32,96},{40,104},{48,112},{56,120},{... | collective-permute-start | bytes 6152 | tf_op jit(solution)/shard_map/ppermute | solution.py:98
  298.7 24.2 %copy-start.1 = (f32[2048]{0:T(1024)S(1)}, f32[2048]{0:T(1024)}, u32[]{:S(2)}) copy-start(f32[2048]{0:T(1024)} %param.13) | copy-start | bytes 24580
  (1 other events, 6.9 us)
Sparse Core Ops, SparseCore 0:
  11.6 149.8 all-gather.2
  163.9 94.8 all-gather.4

commit v7 on v3

--- a/solution.py
+++ b/solution.py
@@ -48,24 +48,32 @@
     half_rows = block_rows // 2
     ring_tab = jnp.array(ring, jnp.int32)
     me = jnp.array(where_in_ring, jnp.int32)[col_pos]
-    row_all = jnp.zeros((n_col * block_rows, width_row), jnp.float32)
     ahead, behind = row_block[:half_rows], row_block[half_rows:]
-    row_all = lax.dynamic_update_slice_in_dim(row_all, ahead, col_pos * block_rows, 0)
-    row_all = lax.dynamic_update_slice_in_dim(row_all, behind, col_pos * block_rows + half_rows, 0)
+    pieces = [(ahead, col_pos * block_rows), (behind, col_pos * block_rows + half_rows)]
+    contract = (((0,), (0,)), ((), ()))
+    early = 2 * (n_col // 2 + 1)
+
+    def part_product(part):
+        rows = jnp.concatenate([p for p, _ in part], axis=0)
+        cols = jnp.concatenate(
+            [lax.dynamic_slice_in_dim(col_all, off, half_rows, 0) for _, off in part], axis=0
+        )
+        return lax.dot_general(
+            rows, cols, contract, precision=high, preferred_element_type=jnp.float32
+        )
+
+    tile = None
     for k in range(1, n_col):
         ahead = lax.ppermute(ahead, "col", forward)
         behind = lax.ppermute(behind, "col", backward)
-        from_ahead = ring_tab[(me - k) % n_col]
-        from_behind = ring_tab[(me + k) % n_col]
-        row_all = lax.dynamic_update_slice_in_dim(row_all, ahead, from_ahead * block_rows, 0)
-        row_all = lax.dynamic_update_slice_in_dim(
-            row_all, behind, from_behind * block_rows + half_rows, 0
-        )
-
-    contract = (((0,), (0,)), ((), ()))
-    tile = lax.dot_general(
-        row_all, col_all, contract, precision=high, preferred_element_type=jnp.float32
-    )
+        pieces.append((ahead, ring_tab[(me - k) % n_col] * block_rows))
+        pieces.append((behind, ring_tab[(me + k) % n_col] * block_rows + half_rows))
+        if k == n_col // 2:
+            col_all, ahead, behind = lax.optimization_barrier((col_all, ahead, behind))
+        if k == n_col // 2 + 1:
+            tile = part_product(pieces[:early])
+            tile, col_all, ahead, behind = lax.optimization_barrier((tile, col_all, ahead, behind))
+    tile = tile + part_product(pieces[early:])
     rows_global = row_pos * width_row + lax.broadcasted_iota(jnp.int32, (width_row, width_col), 0)
     cols_global = col_pos * width_col + lax.broadcasted_iota(jnp.int32, (width_row, width_col), 1)
     tile = tile + jnp.where(rows_global == cols_global, ridge[None, :], jnp.float32(0.0))

time: 324 us -> 333 us (1.028)
  local copies, waits for them, and re-layouts: 32.5 us -> 38.9 us
  starting transfers between devices: 79.1 us -> 85.2 us
    unnamed x20 -> x48, local copies, waits for them, and re-layouts: 0.25 us -> 27 us
    all_gather x1, waiting for transfers between devices: 32.5 us -> 13.3 us  [body(): col_all = lax.all_gather(masked, 'row', axis=0, tiled=True)]
    dynamic_update_slice x14 -> x0, local copies, waits for them, and re-layouts: 18.5 us -> none  [the longest x7 9.69 us: body(): lax.dynamic_update_slice_in_dim(row_all, ahead, from_ahead * block_rows, 0)]
    ppermute x7, starting transfers between devices: 20.9 us -> 29.9 us  [body(): behind = lax.ppermute(behind, 'col', backward)]
    ppermute x7, waiting for transfers between devices: 50.7 us -> 59.5 us  [body(): ahead = lax.ppermute(ahead, 'col', forward)]
    ppermute x7, starting transfers between devices: 52.2 us -> 45.3 us  [body(): ahead = lax.ppermute(ahead, 'col', forward)]
    ppermute x3, waiting for transfers between devices: 24.2 us -> 31 us  [body(): packed = packed + lax.ppermute(packed, 'col', pairs)]
    broadcast_in_dim x1 -> x0, local copies, waits for them, and re-layouts: 4.35 us -> none  [body(): row_all = jnp.zeros((n_col * block_rows, width_row), jnp.float32)]
  transfers between devices with their start and end apart: 24 -> 24, of which waited for: 16 -> 16; matrix products, arithmetic and copies ran while one was open for 24% -> 22% of each run, Pallas kernels for 0% -> 0%
where the time goes in v7:
time: 333 us
  waiting for transfers between devices  125 us (38%)
  starting transfers between devices  85.2 us (26%)
  matrix products  45.1 us (14%)
  local copies, waits for them, and re-layouts  38.9 us (12%)
  between operations  32.8 us (10%)
  other arithmetic  5.45 us (2%)
    ppermute x7, waiting for transfers between devices, body(): ahead = lax.ppermute(ahead, 'col', forward)  59.5 us
    ppermute x7, starting transfers between devices, body(): ahead = lax.ppermute(ahead, 'col', forward)  45.3 us
    dot_general x2, matrix products, part_product(): lax.dot_general(rows, cols, contract, precision=high, preferred_element_t...  36.8 us
    ppermute x3, waiting for transfers between devices, body(): packed = packed + lax.ppermute(packed, 'col', pairs)  31 us
    ppermute x7, starting transfers between devices, body(): behind = lax.ppermute(behind, 'col', backward)  29.9 us
    unnamed x48, local copies, waits for them, and re-layouts  27 us
    ppermute x7, waiting for transfers between devices, body(): behind = lax.ppermute(behind, 'col', backward)  14.3 us
    all_gather x1, waiting for transfers between devices, body(): col_all = lax.all_gather(masked, 'row', axis=0, tiled=True)  13.3 us
  transfers between devices with their start and end apart: 24, of which 16 were waited for; matrix products, arithmetic and copies ran while one was open for 22% of the time, Pallas kernels for 0%

profile of v7, /device:TPU:0, one launch (start us, length us, event | category | flops | bytes accessed | tf_op | source)
XLA Modules:
  0.0 332.6 jit_solution(18004657962433016641)
XLA Ops:
  9.1 2.3 broadcast_select_fusion
  11.5 2.2 reshape.96
  17.6 43.8 %collective-permute-start.2 = (f32[128,1024]{1,0:T(8,128)S(1)}, f32[128,1024]{1,0:T(8,128)S(1)}, u32[]{:S(2)}, u32[]{:S(2)}) collective-permute-start(f32[128,1024]{1,0:T(8,128)S(1)} %get-tuple-element.21), channel_id=1, source_target_pairs={{0,2},{2,4},{4,6},{6,7},{7,5},{5,3},{3,1},{1,0},{8,10},{10,12},{12... | collective-permute-start | bytes 1572872 | tf_op jit(solution)/shard_map/ppermute | solution.py:67
  62.3 8.7 %collective-permute-start.3 = (f32[128,1024]{1,0:T(8,128)S(1)}, f32[128,1024]{1,0:T(8,128)S(1)}, u32[]{:S(2)}, u32[]{:S(2)}) collective-permute-start(f32[128,1024]{1,0:T(8,128)S(1)} %get-tuple-element.19), channel_id=1, source_target_pairs={{0,1},{2,0},{4,2},{6,4},{7,6},{5,7},{3,5},{1,3},{8,9},{10,8},{12,1... | collective-permute-start | bytes 1572872 | tf_op jit(solution)/shard_map/ppermute | solution.py:68
  71.0 20.4 %collective-permute-done.2 = f32[128,1024]{1,0:T(8,128)S(1)} collective-permute-done((f32[128,1024]{1,0:T(8,128)S(1)}, f32[128,1024]{1,0:T(8,128)S(1)}, u32[]{:S(2)}, u32[]{:S(2)}) %collective-permute-start.2) | collective-permute-done | bytes 524320 | tf_op jit(solution)/shard_map/ppermute | solution.py:67
  91.5 2.7 collective-permute-done.3
  94.1 4.0 %collective-permute-start.5 = (f32[128,1024]{1,0:T(8,128)S(1)}, f32[128,1024]{1,0:T(8,128)S(1)}, u32[]{:S(2)}, u32[]{:S(2)}) collective-permute-start(f32[128,1024]{1,0:T(8,128)S(1)} %collective-permute-done.3), channel_id=1, source_target_pairs={{0,1},{2,0},{4,2},{6,4},{7,6},{5,7},{3,5},{1,3},{8,9},{10,8},{12,1... | collective-permute-start | bytes 1572872 | tf_op jit(solution)/shard_map/ppermute | solution.py:68
  98.3 19.6 %collective-permute-done.4 = f32[128,1024]{1,0:T(8,128)S(1)} collective-permute-done((f32[128,1024]{1,0:T(8,128)S(1)}, f32[128,1024]{1,0:T(8,128)S(1)}, u32[]{:S(2)}, u32[]{:S(2)}) %collective-permute-start.4) | collective-permute-done | bytes 524320 | tf_op jit(solution)/shard_map/ppermute | solution.py:67
  117.9 3.0 collective-permute-done.5
  121.0 4.0 %collective-permute-start.7 = (f32[128,1024]{1,0:T(8,128)S(1)}, f32[128,1024]{1,0:T(8,128)}, u32[]{:S(2)}, u32[]{:S(2)}) collective-permute-start(f32[128,1024]{1,0:T(8,128)S(1)} %collective-permute-done.5), channel_id=1, source_target_pairs={{0,1},{2,0},{4,2},{6,4},{7,6},{5,7},{3,5},{1,3},{8,9},{10,8},{12,1... | collective-permute-start | bytes 1572872 | tf_op jit(solution)/shard_map/ppermute | solution.py:68
  142.3 2.2 collective-permute-done.6
  145.3 2.2 collective-permute-done.7
  147.5 4.1 %collective-permute-start.9 = (f32[128,1024]{1,0:T(8,128)}, f32[128,1024]{1,0:T(8,128)S(1)}, u32[]{:S(2)}, u32[]{:S(2)}) collective-permute-start(f32[128,1024]{1,0:T(8,128)} %collective-permute-done.7), channel_id=1, source_target_pairs={{0,1},{2,0},{4,2},{6,4},{7,6},{5,7},{3,5},{1,3},{8,9},{10,8},{12,1... | collective-permute-start | bytes 1572872 | tf_op jit(solution)/shard_map/ppermute | solution.py:68
  154.2 1.9 constant_dynamic-update-slice_fusion.2
  156.1 9.9 %collective-permute-done.8 = f32[128,1024]{1,0:T(8,128)} collective-permute-done((f32[128,1024]{1,0:T(8,128)S(1)}, f32[128,1024]{1,0:T(8,128)}, u32[]{:S(2)}, u32[]{:S(2)}) %collective-permute-start.8) | collective-permute-done | bytes 524320 | tf_op jit(solution)/shard_map/ppermute | solution.py:67
  166.0 1.9 constant_dynamic-update-slice_fusion.1
  167.9 6.3 %collective-permute-done.9 = f32[128,1024]{1,0:T(8,128)S(1)} collective-permute-done((f32[128,1024]{1,0:T(8,128)}, f32[128,1024]{1,0:T(8,128)S(1)}, u32[]{:S(2)}, u32[]{:S(2)}) %collective-permute-start.9) | collective-permute-done | bytes 524320 | tf_op jit(solution)/shard_map/ppermute | solution.py:68
  175.1 13.3 %all-gather.2.cloned.1.call-done = f32[2048,2048]{1,0:T(8,128)} async-done(((f32[128,2048]{1,0:T(8,128)}), f32[2048,2048]{1,0:T(8,128)}) %all-gather.2.cloned.1.call-update) | async-done | bytes 16777232 | tf_op jit(solution)/shard_map/all_gather | solution.py:23
  188.4 3.5 %collective-permute-start.11 = (f32[128,1024]{1,0:T(8,128)S(1)}, f32[128,1024]{1,0:T(8,128)S(1)}, u32[]{:S(2)}, u32[]{:S(2)}) collective-permute-start(f32[128,1024]{1,0:T(8,128)S(1)} %collective-permute-done.9), channel_id=1, source_target_pairs={{0,1},{2,0},{4,2},{6,4},{7,6},{5,7},{3,5},{1,3},{8,9},{10,8},{12,1... | collective-permute-start | bytes 1572872 | tf_op jit(solution)/shard_map/ppermute | solution.py:68
  203.8 22.8 %fusion.3 = f32[1024,2048]{1,0:T(8,128)} fusion(f32[1280,1024]{1,0:T(8,128)} %constant_dynamic-update-slice_fusion, f32[1280,2048]{1,0:T(8,128)S(1)} %dynamic-slice_dynamic-update-slice_fusion.6), kind=kOutput, calls=%fused_computation.58 | convolution fusion | flops 16106127360 | bytes 24117248 | tf_op jit(solution)/shard_map/dot_general | solution.py:61
  226.6 7.7 %fusion.4 = f32[2048,64]{0,1:T(8,128)S(1)} fusion(f32[2048,2048]{1,0:T(8,128)S(1)} %copy-done.2, f32[64,2048]{1,0:T(8,128)S(1)} %copy-done.3), kind=kOutput, calls=%fused_computation.59 | convolution fusion | flops 1610612736 | bytes 17825792 | tf_op jit(solution)/shard_map/dot_general | solution.py:81
  234.4 5.5 %collective-permute-start.16 = (f32[2050,64]{0,1:T(8,128)S(1)}, f32[2050,64]{0,1:T(8,128)S(1)}, u32[]{:S(2)}, u32[]{:S(2)}) collective-permute-start(f32[2050,64]{0,1:T(8,128)S(1)} %concatenate.43), channel_id=1, source_target_pairs={{0,4},{1,5},{2,6},{3,7},{4,0},{5,1},{6,2},{7,3},{8,12},{9,13},{10,... | collective-permute-start | bytes 1574408 | tf_op jit(solution)/shard_map/ppermute | solution.py:91
  245.2 2.1 collective-permute-start.13
  249.9 3.4 %collective-permute-done.16 = f32[2050,64]{0,1:T(8,128)S(1)} collective-permute-done((f32[2050,64]{0,1:T(8,128)S(1)}, f32[2050,64]{0,1:T(8,128)S(1)}, u32[]{:S(2)}, u32[]{:S(2)}) %collective-permute-start.16) | collective-permute-done | bytes 524832 | tf_op jit(solution)/shard_map/ppermute | solution.py:91
  259.2 17.5 %collective-permute-done.17 = f32[2050,64]{0,1:T(8,128)S(1)} collective-permute-done((f32[2050,64]{0,1:T(8,128)S(1)}, f32[2050,64]{0,1:T(8,128)S(1)}, u32[]{:S(2)}, u32[]{:S(2)}) %collective-permute-start.17) | collective-permute-done | bytes 524832 | tf_op jit(solution)/shard_map/ppermute | solution.py:91
  276.8 1.9 collective-permute-start.18
  280.3 3.5 %collective-permute-start.15 = (f32[128,1024]{1,0:T(8,128)S(1)}, f32[128,1024]{1,0:T(8,128)S(1)}, u32[]{:S(2)}, u32[]{:S(2)}) collective-permute-start(f32[128,1024]{1,0:T(8,128)S(1)} %collective-permute-done.13), channel_id=1, source_target_pairs={{0,1},{2,0},{4,2},{6,4},{7,6},{5,7},{3,5},{1,3},{8,9},{10,8},{12,1... | collective-permute-start | bytes 1572872 | tf_op jit(solution)/shard_map/ppermute | solution.py:68
  283.9 10.0 %collective-permute-done.18 = f32[2050,64]{0,1:T(8,128)S(1)} collective-permute-done((f32[2050,64]{0,1:T(8,128)S(1)}, f32[2050,64]{0,1:T(8,128)S(1)}, u32[]{:S(2)}, u32[]{:S(2)}) %collective-permute-start.18) | collective-permute-done | bytes 524832 | tf_op jit(solution)/shard_map/ppermute | solution.py:91
  295.6 7.3 %collective-permute-done.14 = f32[128,1024]{1,0:T(8,128)S(1)} collective-permute-done((f32[128,1024]{1,0:T(8,128)S(1)}, f32[128,1024]{1,0:T(8,128)S(1)}, u32[]{:S(2)}, u32[]{:S(2)}) %collective-permute-start.14) | collective-permute-done | bytes 524320 | tf_op jit(solution)/shard_map/ppermute | solution.py:67
  303.2 5.0 %collective-permute-done.21 = f32[256]{0:T(256)S(1)} collective-permute-done((f32[256]{0:T(256)S(1)}, f32[256]{0:T(256)S(1)}, u32[]{:S(2)}, u32[]{:S(2)}) %collective-permute-start.21) | collective-permute-done | bytes 1056 | tf_op jit(solution)/shard_map/ppermute | solution.py:102
  308.2 14.1 %select_add_fusion = f32[1024,2048]{1,0:T(8,128)} fusion(f32[1024,2048]{1,0:T(8,128)S(1)} %bitcast.58, f32[2048]{0:T(1024)S(1)} %copy-done.5, s32[2048]{0:T(1024)S(1)} %iota_add_fusion, s32[1024]{0:T(1024)S(1)} %iota_add_fusion.1, f32[768,1024]{1,0:T(8,128)S(1)} %constant_dynamic-update-slice_fusion.10, ...), kind=kOutput, calls=%fused_computation.1 | convolution fusion | flops 9672065024 | bytes 26234880 | tf_op jit(solution)/shard_map/dot_general | solution.py:61
  322.3 3.4 %gather_fusion = f32[512]{0:T(512)} fusion(f32[1024]{0:T(1024)S(1)} %maximum_select_fusion, s32[1024]{0:T(1024)S(1)} %pad_clamp_fusion), kind=kCustom, calls=%fused_computation | custom fusion | bytes 6144 | tf_op jit(solution)/shard_map/gather | solution.py:106
  (101 shorter events, 39.5 us)
Async XLA Ops:
  7.2 133.7 %copy-start = (f32[2048]{0:T(1024)S(1)}, f32[2048]{0:T(1024)}, u32[]{:S(2)}) copy-start(f32[2048]{0:T(1024)} %param.13) | copy-start | bytes 24580
  7.2 181.2 %all-gather.2.cloned.1.call-start = ((), (), s32[]{:S(2)}) async-start(), calls=%async_computation | async-start | bytes 17825792 | tf_op jit(solution)/shard_map/all_gather | solution.py:23
  11.5 86.7 %copy-start.3 = (f32[64,2048]{1,0:T(8,128)S(1)}, f32[64,2048]{1,0:T(8,128)}, u32[]{:S(2)}) copy-start(f32[64,2048]{1,0:T(8,128)} %param.11) | copy-start | bytes 1572868
  11.5 86.7 %copy-start.5 = (f32[2048]{0:T(1024)S(1)}, f32[2048]{0:T(1024)}, u32[]{:S(2)}) copy-start(f32[2048]{0:T(1024)} %param.10) | copy-start | bytes 24580
  11.5 86.8 %copy-start.6 = (s32[512]{0:T(512)S(1)}, s32[512]{0:T(512)}, u32[]{:S(2)}) copy-start(s32[512]{0:T(512)} %param.12) | copy-start | bytes 6148
  11.5 113.5 %copy-start.7 = (s32[8]{0:T(128)S(1)}, s32[8]{0:T(128)}, u32[]{:S(2)}) copy-start(s32[8]{0:T(128)} %constant.193.clone) | copy-start | bytes 100
  11.5 123.4 %copy-start.4 = (s32[8]{0:T(128)S(1)}, s32[8]{0:T(128)}, u32[]{:S(2)}) copy-start(s32[8]{0:T(128)} %constant.192.clone) | copy-start | bytes 100
  14.7 2.0 collective-permute-start.1
  14.9 1.8 collective-permute-start
  17.6 73.8 %collective-permute-start.2 = (f32[128,1024]{1,0:T(8,128)S(1)}, f32[128,1024]{1,0:T(8,128)S(1)}, u32[]{:S(2)}, u32[]{:S(2)}) collective-permute-start(f32[128,1024]{1,0:T(8,128)S(1)} %get-tuple-element.21), channel_id=1, source_target_pairs={{0,2},{2,4},{4,6},{6,7},{7,5},{5,3},{3,1},{1,0},{8,10},{10,12},{12... | collective-permute-start | bytes 1572872 | tf_op jit(solution)/shard_map/ppermute | solution.py:67
  62.3 31.8 %collective-permute-start.3 = (f32[128,1024]{1,0:T(8,128)S(1)}, f32[128,1024]{1,0:T(8,128)S(1)}, u32[]{:S(2)}, u32[]{:S(2)}) collective-permute-start(f32[128,1024]{1,0:T(8,128)S(1)} %get-tuple-element.19), channel_id=1, source_target_pairs={{0,1},{2,0},{4,2},{6,4},{7,6},{5,7},{3,5},{1,3},{8,9},{10,8},{12,1... | collective-permute-start | bytes 1572872 | tf_op jit(solution)/shard_map/ppermute | solution.py:68
  91.5 26.5 %collective-permute-start.4 = (f32[128,1024]{1,0:T(8,128)S(1)}, f32[128,1024]{1,0:T(8,128)S(1)}, u32[]{:S(2)}, u32[]{:S(2)}) collective-permute-start(f32[128,1024]{1,0:T(8,128)S(1)} %collective-permute-done.2), channel_id=1, source_target_pairs={{0,2},{2,4},{4,6},{6,7},{7,5},{5,3},{3,1},{1,0},{8,10},{10,12},{12... | collective-permute-start | bytes 1572872 | tf_op jit(solution)/shard_map/ppermute | solution.py:67
  94.1 26.8 %collective-permute-start.5 = (f32[128,1024]{1,0:T(8,128)S(1)}, f32[128,1024]{1,0:T(8,128)S(1)}, u32[]{:S(2)}, u32[]{:S(2)}) collective-permute-start(f32[128,1024]{1,0:T(8,128)S(1)} %collective-permute-done.3), channel_id=1, source_target_pairs={{0,1},{2,0},{4,2},{6,4},{7,6},{5,7},{3,5},{1,3},{8,9},{10,8},{12,1... | collective-permute-start | bytes 1572872 | tf_op jit(solution)/shard_map/ppermute | solution.py:68
  117.9 26.6 %collective-permute-start.6 = (f32[128,1024]{1,0:T(8,128)S(1)}, f32[128,1024]{1,0:T(8,128)S(1)}, u32[]{:S(2)}, u32[]{:S(2)}) collective-permute-start(f32[128,1024]{1,0:T(8,128)S(1)} %collective-permute-done.4), channel_id=1, source_target_pairs={{0,2},{2,4},{4,6},{6,7},{7,5},{5,3},{3,1},{1,0},{8,10},{10,12},{12... | collective-permute-start | bytes 1572872 | tf_op jit(solution)/shard_map/ppermute | solution.py:67
  121.0 26.6 %collective-permute-start.7 = (f32[128,1024]{1,0:T(8,128)S(1)}, f32[128,1024]{1,0:T(8,128)}, u32[]{:S(2)}, u32[]{:S(2)}) collective-permute-start(f32[128,1024]{1,0:T(8,128)S(1)} %collective-permute-done.5), channel_id=1, source_target_pairs={{0,1},{2,0},{4,2},{6,4},{7,6},{5,7},{3,5},{1,3},{8,9},{10,8},{12,1... | collective-permute-start | bytes 1572872 | tf_op jit(solution)/shard_map/ppermute | solution.py:68
  144.5 21.5 %collective-permute-start.8 = (f32[128,1024]{1,0:T(8,128)S(1)}, f32[128,1024]{1,0:T(8,128)}, u32[]{:S(2)}, u32[]{:S(2)}) collective-permute-start(f32[128,1024]{1,0:T(8,128)S(1)} %collective-permute-done.6), channel_id=1, source_target_pairs={{0,2},{2,4},{4,6},{6,7},{7,5},{5,3},{3,1},{1,0},{8,10},{10,12},{12... | collective-permute-start | bytes 1572872 | tf_op jit(solution)/shard_map/ppermute | solution.py:67
  147.5 26.7 %collective-permute-start.9 = (f32[128,1024]{1,0:T(8,128)}, f32[128,1024]{1,0:T(8,128)S(1)}, u32[]{:S(2)}, u32[]{:S(2)}) collective-permute-start(f32[128,1024]{1,0:T(8,128)} %collective-permute-done.7), channel_id=1, source_target_pairs={{0,1},{2,0},{4,2},{6,4},{7,6},{5,7},{3,5},{1,3},{8,9},{10,8},{12,1... | collective-permute-start | bytes 1572872 | tf_op jit(solution)/shard_map/ppermute | solution.py:68
  188.4 38.2 %collective-permute-start.10 = (f32[128,1024]{1,0:T(8,128)}, f32[128,1024]{1,0:T(8,128)S(1)}, u32[]{:S(2)}, u32[]{:S(2)}) collective-permute-start(f32[128,1024]{1,0:T(8,128)} %collective-permute-done.8), channel_id=1, source_target_pairs={{0,2},{2,4},{4,6},{6,7},{7,5},{5,3},{3,1},{1,0},{8,10},{10,12},{12... | collective-permute-start | bytes 1572872 | tf_op jit(solution)/shard_map/ppermute | solution.py:67
  188.4 38.2 %collective-permute-start.11 = (f32[128,1024]{1,0:T(8,128)S(1)}, f32[128,1024]{1,0:T(8,128)S(1)}, u32[]{:S(2)}, u32[]{:S(2)}) collective-permute-start(f32[128,1024]{1,0:T(8,128)S(1)} %collective-permute-done.9), channel_id=1, source_target_pairs={{0,1},{2,0},{4,2},{6,4},{7,6},{5,7},{3,5},{1,3},{8,9},{10,8},{12,1... | collective-permute-start | bytes 1572872 | tf_op jit(solution)/shard_map/ppermute | solution.py:68
  234.4 18.9 %collective-permute-start.16 = (f32[2050,64]{0,1:T(8,128)S(1)}, f32[2050,64]{0,1:T(8,128)S(1)}, u32[]{:S(2)}, u32[]{:S(2)}) collective-permute-start(f32[2050,64]{0,1:T(8,128)S(1)} %concatenate.43), channel_id=1, source_target_pairs={{0,4},{1,5},{2,6},{3,7},{4,0},{5,1},{6,2},{7,3},{8,12},{9,13},{10,... | collective-permute-start | bytes 1574408 | tf_op jit(solution)/shard_map/ppermute | solution.py:91
  243.7 36.5 %collective-permute-start.12 = (f32[128,1024]{1,0:T(8,128)S(1)}, f32[128,1024]{1,0:T(8,128)S(1)}, u32[]{:S(2)}, u32[]{:S(2)}) collective-permute-start(f32[128,1024]{1,0:T(8,128)S(1)} %collective-permute-done.10), channel_id=1, source_target_pairs={{0,2},{2,4},{4,6},{6,7},{7,5},{5,3},{3,1},{1,0},{8,10},{10,12},{12... | collective-permute-start | bytes 1572872 | tf_op jit(solution)/shard_map/ppermute | solution.py:67
  245.2 35.1 %collective-permute-start.13 = (f32[128,1024]{1,0:T(8,128)S(1)}, f32[128,1024]{1,0:T(8,128)S(1)}, u32[]{:S(2)}, u32[]{:S(2)}) collective-permute-start(f32[128,1024]{1,0:T(8,128)S(1)} %collective-permute-done.11), channel_id=1, source_target_pairs={{0,1},{2,0},{4,2},{6,4},{7,6},{5,7},{3,5},{1,3},{8,9},{10,8},{12,1... | collective-permute-start | bytes 1572872 | tf_op jit(solution)/shard_map/ppermute | solution.py:68
  253.4 23.3 %collective-permute-start.17 = (f32[2050,64]{0,1:T(8,128)S(1)}, f32[2050,64]{0,1:T(8,128)S(1)}, u32[]{:S(2)}, u32[]{:S(2)}) collective-permute-start(f32[2050,64]{0,1:T(8,128)S(1)} %add.428), channel_id=1, source_target_pairs={{0,2},{1,3},{2,0},{3,1},{4,6},{5,7},{6,4},{7,5},{8,10},{9,11},{10,... | collective-permute-start | bytes 1574408 | tf_op jit(solution)/shard_map/ppermute | solution.py:91
  256.3 51.9 %slice-start = ((s8[8388608]{0:T(1024)(128)(4,1)}), s8[4194304]{0:T(1024)(128)(4,1)S(1)}, s32[]{:S(2)}) async-start(s8[8388608]{0:T(1024)(128)(4,1)} %bitcast.57), calls=%async_computation.1 | async-start | bytes 8388608
  276.8 17.1 %collective-permute-start.18 = (f32[2050,64]{0,1:T(8,128)S(1)}, f32[2050,64]{0,1:T(8,128)S(1)}, u32[]{:S(2)}, u32[]{:S(2)}) collective-permute-start(f32[2050,64]{0,1:T(8,128)S(1)} %add.429), channel_id=1, source_target_pairs={{0,1},{1,0},{2,3},{3,2},{4,5},{5,4},{6,7},{7,6},{8,9},{9,8},{10,11... | collective-permute-start | bytes 1574408 | tf_op jit(solution)/shard_map/ppermute | solution.py:91
  278.7 29.5 %slice-start.1 = ((s8[8388608]{0:T(1024)(128)(4,1)}), s8[4194304]{0:T(1024)(128)(4,1)S(1)}, s32[]{:S(2)}) async-start(s8[8388608]{0:T(1024)(128)(4,1)} %bitcast.57), calls=%async_computation.2 | async-start | bytes 8388608
  280.2 22.7 %collective-permute-start.14 = (f32[128,1024]{1,0:T(8,128)S(1)}, f32[128,1024]{1,0:T(8,128)S(1)}, u32[]{:S(2)}, u32[]{:S(2)}) collective-permute-start(f32[128,1024]{1,0:T(8,128)S(1)} %collective-permute-done.12), channel_id=1, source_target_pairs={{0,2},{2,4},{4,6},{6,7},{7,5},{5,3},{3,1},{1,0},{8,10},{10,12},{12... | collective-permute-start | bytes 1572872 | tf_op jit(solution)/shard_map/ppermute | solution.py:67
  280.3 22.8 %collective-permute-start.15 = (f32[128,1024]{1,0:T(8,128)S(1)}, f32[128,1024]{1,0:T(8,128)S(1)}, u32[]{:S(2)}, u32[]{:S(2)}) collective-permute-start(f32[128,1024]{1,0:T(8,128)S(1)} %collective-permute-done.13), channel_id=1, source_target_pairs={{0,1},{2,0},{4,2},{6,4},{7,6},{5,7},{3,5},{1,3},{8,9},{10,8},{12,1... | collective-permute-start | bytes 1572872 | tf_op jit(solution)/shard_map/ppermute | solution.py:68
  294.3 1.2 collective-permute-start.19
  295.6 7.4 %collective-permute-start.20 = (f32[128]{0:T(128)S(1)}, f32[128]{0:T(128)S(1)}, u32[]{:S(2)}, u32[]{:S(2)}) collective-permute-start(f32[128]{0:T(128)S(1)} %broadcast_select_fusion.1), channel_id=1, source_target_pairs={{0,16},{8,24},{16,0},{24,8},{32,48},{40,56},{48,32},{56,40},{64,80... | collective-permute-start | bytes 1544 | tf_op jit(solution)/shard_map/ppermute | solution.py:102
  303.0 5.2 %collective-permute-start.21 = (f32[256]{0:T(256)S(1)}, f32[256]{0:T(256)S(1)}, u32[]{:S(2)}, u32[]{:S(2)}) collective-permute-start(f32[256]{0:T(256)S(1)} %maximum_select_fusion.2), channel_id=1, source_target_pairs={{0,32},{8,40},{16,48},{24,56},{32,0},{40,8},{48,16},{56,24},{64,96... | collective-permute-start | bytes 3080 | tf_op jit(solution)/shard_map/ppermute | solution.py:102
  308.2 14.1 %collective-permute-start.22 = (f32[512]{0:T(512)S(1)}, f32[512]{0:T(512)S(1)}, u32[]{:S(2)}, u32[]{:S(2)}) collective-permute-start(f32[512]{0:T(512)S(1)} %maximum_select_fusion.1), channel_id=1, source_target_pairs={{0,64},{8,72},{16,80},{24,88},{32,96},{40,104},{48,112},{56,120},{... | collective-permute-start | bytes 6152 | tf_op jit(solution)/shard_map/ppermute | solution.py:102
  (2 other events, 29.3 us)
Sparse Core Ops, SparseCore 0:
  11.6 176.6 all-gather.1

commit v8 on v4

v8 whole, which is shorter than its diff:
```python
import jax
import jax.numpy as jnp
from jax import lax
from jax.sharding import Mesh
from jax.sharding import PartitionSpec as P

F = 16384

highest = lax.Precision.HIGHEST
high = lax.Precision.HIGH
ROW = ("zl", "x", "core")
COL = ("y", "zh")


def body(shared_rows, event_counts, ridge, items, cand_ids, theta):
    n_row = lax.axis_size("zl") * lax.axis_size("x") * lax.axis_size("core")
    n_col = lax.axis_size("y") * lax.axis_size("zh")
    ratio = n_row // n_col
    row_pos = (lax.axis_index("zl") * lax.axis_size("x") + lax.axis_index("x")) * lax.axis_size(
        "core"
    ) + lax.axis_index("core")
    col_pos = lax.axis_index("y") * lax.axis_size("zh") + lax.axis_index("zh")
    ev_slots, width_col = shared_rows.shape
    width_row = width_col // ratio
    slot = lax.iota(jnp.int32, ev_slots)
    masked = jnp.where((slot < event_counts[row_pos])[:, None], shared_rows, jnp.float32(0.0))

    col_all = masked
    for name in reversed(ROW):
        col_all = lax.all_gather(col_all, name, axis=0, tiled=True)

    halves = masked.reshape(ev_slots, ratio, width_row)
    received = []
    for t in range(ratio):
        perm = []
        for s in range(n_row):
            for c in range(n_col):
                b = (s % ratio) ^ t
                perm.append((s * n_col + c, (ratio * c + b) * n_col + s // ratio))
        piece = halves[:, (row_pos % ratio) ^ t, :]
        received.append(lax.ppermute(piece, ROW + COL, perm))
    parity = row_pos % ratio
    ordered = [
        sum(jnp.where(parity ^ t == a, received[t], 0.0) for t in range(ratio))
        for a in range(ratio)
    ]
    row_block = jnp.concatenate(ordered, axis=0)

    row_all = row_block
    for name in reversed(COL):
        row_all = lax.all_gather(row_all, name, axis=0, tiled=True)

    contract = (((0,), (0,)), ((), ()))
    tile = lax.dot_general(
        row_all, col_all, contract, precision=high, preferred_element_type=jnp.float32
    )
    rows_global = row_pos * width_row + lax.broadcasted_iota(jnp.int32, (width_row, width_col), 0)
    cols_global = col_pos * width_col + lax.broadcasted_iota(jnp.int32, (width_row, width_col), 1)
    tile = tile + jnp.where(rows_global == cols_global, ridge[None, :], jnp.float32(0.0))

    z_part = lax.dot_general(
        col_all, items, (((1,), (1,)), ((), ())), precision=high,
        preferred_element_type=jnp.float32,
    )
    q_ridge = jnp.sum(ridge[None, :] * items * items, axis=1)
    lin = jnp.dot(items, theta, precision=highest, preferred_element_type=jnp.float32)
    packed = jnp.concatenate([z_part, q_ridge[None, :], lin[None, :]], axis=0)
    step = n_col // 2
    while step >= 1:
        pairs = [(c, c ^ step) for c in range(n_col)]
        packed = packed + lax.ppermute(packed, COL, pairs)
        step //= 2
    ev_all = z_part.shape[0]
    z = packed[:ev_all]
    quad = jnp.sum(z * z, axis=0) + packed[ev_all]
    item_scores = packed[ev_all + 1] + jnp.sqrt(quad / F)
    items_dev = items.shape[0]
    held = item_scores
    step = 1
    while step < n_row:
        pairs = [(r, r ^ step) for r in range(n_row)]
        other = lax.ppermute(held, ROW, pairs)
        low = (row_pos & step) == 0
        held = jnp.where(low, jnp.concatenate([held, other]), jnp.concatenate([other, held]))
        step *= 2
    scores = held[cand_ids]
    return (tile, scores)


def solution(mesh):
    n_row = mesh.shape["row"]
    n_col = mesh.shape["col"]
    inner = Mesh(mesh.devices.reshape(2, n_row // 4, 2, n_col // 2, 2), ROW + COL)
    return jax.shard_map(
        body,
        mesh=inner,
        in_specs=(P(ROW, COL), P(), P(COL), P(ROW, COL), P(), P(COL)),
        out_specs=(P(ROW, COL), P()),
        check_vma=False,
    )
```

time: 351 us -> 543 us (1.55)
  waiting for transfers between devices: 178 us -> 458 us
  starting transfers between devices: 82.5 us -> 10.3 us
  local copies, waits for them, and re-layouts: 25.2 us -> 8.25 us
    all_gather x1 -> x5, waiting for transfers between devices: 17.1 us -> 388 us  [the longest x3 332 us: body(): col_all = lax.all_gather(col_all, name, axis=0, tiled=True)]
    ppermute x16 -> x9, waiting for transfers between devices: 161 us -> 70.2 us  [the longest x3 63 us: body(): packed = packed + lax.ppermute(packed, COL, pairs)]
    ppermute x16 -> x9, starting transfers between devices: 82.4 us -> 10.1 us  [the longest x3 5.71 us: body(): packed = packed + lax.ppermute(packed, COL, pairs)]
    dynamic_update_slice x7 -> x0, local copies, waits for them, and re-layouts: 12.6 us -> none  [body(): lax.dynamic_update_slice_in_dim(row_all, got, (col_pos ^ k) * block_rows, 0)]
  transfers between devices with their start and end apart: 17 -> 14, of which waited for: 12 -> 12; matrix products, arithmetic and copies ran while one was open for 16% -> 9% of each run, Pallas kernels for 0% -> 0%
where the time goes in v8:
time: 543 us; the launch traced here: 541 us
  waiting for transfers between devices  458 us (84%)
  matrix products  45.6 us (8%)
  between operations  14 us (3%)
  starting transfers between devices  10.3 us (2%)
  local copies, waits for them, and re-layouts  8.25 us (2%)
    all_gather x3, waiting for transfers between devices, body(): col_all = lax.all_gather(col_all, name, axis=0, tiled=True)  332 us
    ppermute x3, waiting for transfers between devices, body(): packed = packed + lax.ppermute(packed, COL, pairs)  63 us
    all_gather x2, waiting for transfers between devices, body(): row_all = lax.all_gather(row_all, name, axis=0, tiled=True)  55.9 us
    dot_general x1, matrix products, body(): lax.dot_general(row_all, col_all, contract, precision=high, preferred_ele...  33.8 us
    dot_general x1, matrix products, body(): lax.dot_general(col_all, items, (((1,), (1,)), ((), ())), precision=high,...  11.2 us
  transfers between devices with their start and end apart: 14, of which 12 were waited for; matrix products, arithmetic and copies ran while one was open for 9% of the time, Pallas kernels for 0%

profile of v8, /device:TPU:0, one launch (start us, length us, event | category | flops | bytes accessed | tf_op | source)
XLA Modules:
  0.0 541.4 jit_solution(11801109031130123210)
XLA Ops:
  7.2 1.2 dynamic_slice.9
  8.5 0.6 iota_compare_fusion
  9.1 2.3 broadcast_select_fusion
  11.5 15.8 %all-gather.10.cloned.1.call-done = f32[256,2048]{1,0:T(8,128)} async-done(((f32[128,2048]{1,0:T(8,128)}), f32[256,2048]{1,0:T(8,128)}) %all-gather.10.cloned.1.call-update) | async-done | bytes 2097168 | tf_op jit(solution)/shard_map/all_gather | solution.py:30
  27.4 2.1 reshape.12
  29.6 0.9 constant_dynamic-slice_fusion.1
  30.6 0.4 collective-permute-start.1
  31.1 0.8 collective-permute-start
  31.9 0.7 collective-permute-done.1
  32.6 0.2 select_add_fusion.2
  32.8 1.0 pad_maximum_fusion
  33.9 115.0 %all-gather.12.cloned.1.call-done = f32[1024,2048]{1,0:T(8,128)} async-done(((f32[256,2048]{1,0:T(8,128)}), f32[1024,2048]{1,0:T(8,128)}) %all-gather.12.cloned.1.call-update) | async-done | bytes 8388624 | tf_op jit(solution)/shard_map/all_gather | solution.py:30
  149.0 39.3 %all-gather.6.cloned.1.call-done = f32[512,1024]{1,0:T(8,128)} async-done(((f32[256,1024]{1,0:T(8,128)}), f32[512,1024]{1,0:T(8,128)}) %all-gather.6.cloned.1.call-update) | async-done | bytes 2097168 | tf_op jit(solution)/shard_map/all_gather | solution.py:51
  188.4 0.2 fusion
  188.6 0.6 fusion.3
  189.2 201.3 %all-gather.14.cloned.1.call-done = f32[2048,2048]{1,0:T(8,128)} async-done(((f32[1024,2048]{1,0:T(8,128)}), f32[2048,2048]{1,0:T(8,128)}) %all-gather.14.cloned.1.call-update) | async-done | bytes 16777232 | tf_op jit(solution)/shard_map/all_gather | solution.py:30
  390.5 11.2 %fusion.2 = f32[2048,64]{0,1:T(8,128)S(1)} fusion(f32[2048,2048]{1,0:T(8,128)} %all-gather.14.cloned.1.call-done, f32[64,2048]{1,0:T(8,128)S(1)} %copy-done.1), kind=kOutput, calls=%fused_computation.26 | convolution fusion | flops 1610612736 | bytes 17825792 | tf_op jit(solution)/shard_map/dot_general | solution.py:61
  401.9 3.1 collective-permute-start.2
  404.9 24.2 %collective-permute-done.2 = f32[2050,64]{0,1:T(8,128)S(1)} collective-permute-done((f32[2050,64]{0,1:T(8,128)S(1)}, f32[2050,64]{0,1:T(8,128)S(1)}, u32[]{:S(2)}, u32[]{:S(2)}) %collective-permute-start.2) | collective-permute-done | bytes 524832 | tf_op jit(solution)/shard_map/ppermute | solution.py:71
  429.3 26.8 %collective-permute-done.3 = f32[2050,64]{0,1:T(8,128)S(1)} collective-permute-done((f32[2050,64]{0,1:T(8,128)S(1)}, f32[2050,64]{0,1:T(8,128)S(1)}, u32[]{:S(2)}, u32[]{:S(2)}) %collective-permute-start.3) | collective-permute-done | bytes 524832 | tf_op jit(solution)/shard_map/ppermute | solution.py:71
  456.2 2.6 collective-permute-start.4
  458.7 12.0 %collective-permute-done.4 = f32[2050,64]{0,1:T(8,128)S(1)} collective-permute-done((f32[2050,64]{0,1:T(8,128)S(1)}, f32[2050,64]{0,1:T(8,128)S(1)}, u32[]{:S(2)}, u32[]{:S(2)}) %collective-permute-start.4) | collective-permute-done | bytes 524832 | tf_op jit(solution)/shard_map/ppermute | solution.py:71
  470.8 0.2 slice_reduce_fusion
  471.0 0.1 fusion.1
  471.2 1.1 collective-permute-done.5
  472.4 0.8 collective-permute-start.6
  473.2 2.7 collective-permute-done.6
  476.0 2.3 collective-permute-start.7
  478.3 2.8 collective-permute-done.7
  481.0 16.6 %all-gather.8.cloned.1.call-done = f32[2048,1024]{1,0:T(8,128)} async-done(((f32[512,1024]{1,0:T(8,128)}), f32[2048,1024]{1,0:T(8,128)}) %all-gather.8.cloned.1.call-update) | async-done | bytes 8388624 | tf_op jit(solution)/shard_map/all_gather | solution.py:51
  497.6 33.8 %select_add_fusion = f32[1024,2048]{1,0:T(8,128)} fusion(f32[2048]{0:T(1024)S(1)} %copy-done.2, s32[2048]{0:T(1024)S(1)} %iota_add_fusion, s32[1024]{0:T(1024)S(1)} %iota_add_fusion.1, f32[2048,1024]{1,0:T(8,128)} %all-gather.8.cloned.1.call-done, f32[2048,2048]{1,0:T(8,128)} %all-gather.14.cloned.1.call-done), kind=kOutput, calls=%fused_computation.1 | convolution fusion | flops 25776095232 | bytes 33574912 | tf_op jit(solution)/shard_map/dot_general | solution.py:54
  531.4 3.4 gather_fusion
  (39 shorter events, 1.2 us)
Async XLA Ops:
  7.2 181.5 %copy-start = (f32[2048]{0:T(1024)S(1)}, f32[2048]{0:T(1024)}, u32[]{:S(2)}) copy-start(f32[2048]{0:T(1024)} %param.11) | copy-start | bytes 24580
  7.2 20.2 %all-gather.10.cloned.1.call-start = ((), (), s32[]{:S(2)}) async-start(), calls=%async_computation.2 | async-start | bytes 3145728 | tf_op jit(solution)/shard_map/all_gather | solution.py:30
  11.5 137.4 %all-gather.12.cloned.1.call-start = ((), (), s32[]{:S(2)}) async-start(), calls=%async_computation.3 | async-start | bytes 10485760 | tf_op jit(solution)/shard_map/all_gather | solution.py:30
  27.4 161.0 %all-gather.6.cloned.1.call-start = ((), (), s32[]{:S(2)}) async-start(), calls=%async_computation | async-start | bytes 3145728 | tf_op jit(solution)/shard_map/all_gather | solution.py:51
  30.6 2.0 collective-permute-start.1
  31.0 157.4 %copy-start.1 = (f32[64,2048]{1,0:T(8,128)S(1)}, f32[64,2048]{1,0:T(8,128)}, u32[]{:S(2)}) copy-start(f32[64,2048]{1,0:T(8,128)} %param.9) | copy-start | bytes 1572868
  31.0 157.4 %copy-start.2 = (f32[2048]{0:T(1024)S(1)}, f32[2048]{0:T(1024)}, u32[]{:S(2)}) copy-start(f32[2048]{0:T(1024)} %param.8) | copy-start | bytes 24580
  31.1 1.5 collective-permute-start
  33.8 356.7 %all-gather.14.cloned.1.call-start = ((), (), s32[]{:S(2)}) async-start(), calls=%async_computation.4 | async-start | bytes 25165824 | tf_op jit(solution)/shard_map/all_gather | solution.py:30
  149.0 348.6 %all-gather.8.cloned.1.call-start = ((), (), s32[]{:S(2)}) async-start(), calls=%async_computation.1 | async-start | bytes 10485760 | tf_op jit(solution)/shard_map/all_gather | solution.py:51
  189.2 269.5 %copy-start.3 = (s32[512]{0:T(512)S(1)}, s32[512]{0:T(512)}, u32[]{:S(2)}) copy-start(s32[512]{0:T(512)} %param.10) | copy-start | bytes 6148
  401.9 27.3 %collective-permute-start.2 = (f32[2050,64]{0,1:T(8,128)S(1)}, f32[2050,64]{0,1:T(8,128)S(1)}, u32[]{:S(2)}, u32[]{:S(2)}) collective-permute-start(f32[2050,64]{0,1:T(8,128)S(1)} %concatenate.31), channel_id=1, source_target_pairs={{0,4},{1,5},{2,6},{3,7},{4,0},{5,1},{6,2},{7,3},{8,12},{9,13},{10,... | collective-permute-start | bytes 1574408 | tf_op jit(solution)/shard_map/ppermute | solution.py:71
  429.2 26.9 %collective-permute-start.3 = (f32[2050,64]{0,1:T(8,128)S(1)}, f32[2050,64]{0,1:T(8,128)S(1)}, u32[]{:S(2)}, u32[]{:S(2)}) collective-permute-start(f32[2050,64]{0,1:T(8,128)S(1)} %add.82), channel_id=1, source_target_pairs={{0,2},{1,3},{2,0},{3,1},{4,6},{5,7},{6,4},{7,5},{8,10},{9,11},{10,... | collective-permute-start | bytes 1574408 | tf_op jit(solution)/shard_map/ppermute | solution.py:71
  456.2 14.5 %collective-permute-start.4 = (f32[2050,64]{0,1:T(8,128)S(1)}, f32[2050,64]{0,1:T(8,128)S(1)}, u32[]{:S(2)}, u32[]{:S(2)}) collective-permute-start(f32[2050,64]{0,1:T(8,128)S(1)} %add.83), channel_id=1, source_target_pairs={{0,1},{1,0},{2,3},{3,2},{4,5},{5,4},{6,7},{7,6},{8,9},{9,8},{10,11... | collective-permute-start | bytes 1574408 | tf_op jit(solution)/shard_map/ppermute | solution.py:71
  471.1 1.2 collective-permute-start.5
  472.4 3.6 collective-permute-start.6
  476.0 5.1 collective-permute-start.7
  481.0 50.4 %collective-permute-start.8 = (f32[512]{0:T(512)S(1)}, f32[512]{0:T(512)S(1)}, u32[]{:S(2)}, u32[]{:S(2)}) collective-permute-start(f32[512]{0:T(512)S(1)} %maximum_select_fusion.1), channel_id=1, source_target_pairs={{0,64},{8,72},{16,80},{24,88},{32,96},{40,104},{48,112},{56,120},{... | collective-permute-start | bytes 6152 | tf_op jit(solution)/shard_map/ppermute | solution.py:82
Sparse Core Ops, SparseCore 0:
  11.6 15.7 all-gather.9
  29.0 119.8 all-gather.11
  151.2 37.1 all-gather.5
  189.8 200.6 all-gather.13
  392.0 105.5 all-gather.7

commit v9 on v4

--- a/solution.py
+++ b/solution.py
@@ -39,23 +39,39 @@
     ]
     row_block = jnp.concatenate(ordered, axis=0)
 
+    n_y = n_col // 2
+    ring = [y * 2 for y in range(n_y)] + [y * 2 + 1 for y in reversed(range(n_y))]
+    where_in_ring = [ring.index(c) for c in range(n_col)]
+    forward = [(ring[p], ring[(p + 1) % n_col]) for p in range(n_col)]
+    backward = [(ring[p], ring[(p - 1) % n_col]) for p in range(n_col)]
     block_rows = row_block.shape[0]
+    ring_tab = jnp.array(ring, jnp.int32)
+    me = jnp.array(where_in_ring, jnp.int32)[col_pos]
     row_all = jnp.zeros((n_col * block_rows, width_row), jnp.float32)
     row_all = lax.dynamic_update_slice_in_dim(row_all, row_block, col_pos * block_rows, 0)
-    for k in range(1, n_col):
-        pairs = [(c, c ^ k) for c in range(n_col)]
-        got = lax.ppermute(row_block, "col", pairs)
-        row_all = lax.dynamic_update_slice_in_dim(row_all, got, (col_pos ^ k) * block_rows, 0)
+    ahead = behind = row_block
+    for k in range(1, n_col // 2 + 1):
+        ahead = lax.ppermute(ahead, "col", forward)
+        row_all = lax.dynamic_update_slice_in_dim(
+            row_all, ahead, ring_tab[(me - k) % n_col] * block_rows, 0
+        )
+        if k < n_col // 2:
+            behind = lax.ppermute(behind, "col", backward)
+            row_all = lax.dynamic_update_slice_in_dim(
+                row_all, behind, ring_tab[(me + k) % n_col] * block_rows, 0
+            )
 
     col_all, row_all = lax.optimization_barrier((col_all, row_all))
     contract = (((0,), (0,)), ((), ()))
-    tile = lax.dot_general(
-        row_all, col_all, contract, precision=high, preferred_element_type=jnp.float32
-    )
-    rows_global = row_pos * width_row + lax.broadcasted_iota(jnp.int32, (width_row, width_col), 0)
-    cols_global = col_pos * width_col + lax.broadcasted_iota(jnp.int32, (width_row, width_col), 1)
-    tile = tile + jnp.where(rows_global == cols_global, ridge[None, :], jnp.float32(0.0))
+    def rows_of_tile(lo, hi):
+        return lax.dot_general(
+            row_all[:, lo:hi], col_all, contract, precision=high,
+            preferred_element_type=jnp.float32,
+        )
 
+    n_parts = 2
+    part_rows = width_row // n_parts
+    parts = []
     z_part = lax.dot_general(
         col_all, items, (((1,), (1,)), ((), ())), precision=high,
         preferred_element_type=jnp.float32,
@@ -67,7 +83,17 @@
     while step >= 1:
         pairs = [(c, c ^ step) for c in range(n_col)]
         packed = packed + lax.ppermute(packed, "col", pairs)
+        if len(parts) < n_parts:
+            lo = len(parts) * part_rows
+            part = rows_of_tile(lo, lo + part_rows)
+            part, packed = lax.optimization_barrier((part, packed))
+            parts.append(part)
         step //= 2
+    tile = jnp.concatenate(parts, axis=0)
+    rows_global = row_pos * width_row + lax.broadcasted_iota(jnp.int32, (width_row, width_col), 0)
+    cols_global = col_pos * width_col + lax.broadcasted_iota(jnp.int32, (width_row, width_col), 1)
+    tile = tile + jnp.where(rows_global == cols_global, ridge[None, :], jnp.float32(0.0))
+
     ev_all = z_part.shape[0]
     z = packed[:ev_all]
     quad = jnp.sum(z * z, axis=0) + packed[ev_all]

time: 351 us -> 336 us (0.957)
  waiting for transfers between devices: 178 us -> 128 us
  starting transfers between devices: 82.5 us -> 98.1 us
  between operations: 14.3 us -> 23.4 us
  other arithmetic: 5.34 us -> 11 us
    ppermute x3, waiting for transfers between devices: 40.8 us -> 10.5 us  [body(): packed = packed + lax.ppermute(packed, 'col', pairs)]
    ppermute x3, starting transfers between devices: 8.54 us -> 28.2 us  [body(): packed = packed + lax.ppermute(packed, 'col', pairs)]
    all_gather x1, waiting for transfers between devices: 17.1 us -> 0.01 us  [body(): col_all = lax.all_gather(masked, 'row', axis=0, tiled=True)]
    ppermute x7, starting transfers between devices: 70.1 us -> 58.3 us  [the longest x4 46.2 us: body(): ahead = lax.ppermute(ahead, 'col', forward)]
    ppermute x4, starting transfers between devices: 2.87 us -> 10.7 us  [body(): other = lax.ppermute(held, 'row', pairs)]
    add x0 -> x1, other arithmetic: none -> 6.1 us  [body(): tile + jnp.where(rows_global == cols_global, ridge[None, :], jnp.float32(...]
    dot_general x1 -> x2, matrix products: 33.9 us -> 36.8 us  [rows_of_tile(): lax.dot_general(row_all[:, lo:hi], col_all, contract, precision=high, pre...]
  transfers between devices with their start and end apart: 17 -> 17, of which waited for: 12 -> 10; matrix products, arithmetic and copies ran while one was open for 16% -> 20% of each run, Pallas kernels for 0% -> 0%
where the time goes in v9:
time: 336 us; the launch traced here: 335 us
  waiting for transfers between devices  128 us (38%)
  starting transfers between devices  98.1 us (29%)
  matrix products  48.6 us (14%)
  local copies, waits for them, and re-layouts  26.4 us (8%)
  between operations  23.4 us (7%)
  other arithmetic  11 us (3%)
    ppermute x4, waiting for transfers between devices, body(): ahead = lax.ppermute(ahead, 'col', forward)  90.7 us
    ppermute x4, starting transfers between devices, body(): ahead = lax.ppermute(ahead, 'col', forward)  46.2 us
    dot_general x2, matrix products, rows_of_tile(): lax.dot_general(row_all[:, lo:hi], col_all, contract, precision=high, pre...  36.8 us
    ppermute x3, starting transfers between devices, body(): packed = packed + lax.ppermute(packed, 'col', pairs)  28.2 us
    ppermute x3, waiting for transfers between devices, body(): behind = lax.ppermute(behind, 'col', backward)  18.4 us
    ppermute x3, starting transfers between devices, body(): behind = lax.ppermute(behind, 'col', backward)  12.1 us
    dot_general x1, matrix products, body(): lax.dot_general(col_all, items, (((1,), (1,)), ((), ())), precision=high,...  11.3 us
    ppermute x4, starting transfers between devices, body(): other = lax.ppermute(held, 'row', pairs)  10.7 us
  transfers between devices with their start and end apart: 17, of which 10 were waited for; matrix products, arithmetic and copies ran while one was open for 20% of the time, Pallas kernels for 0%

profile of v9, /device:TPU:0, one launch (start us, length us, event | category | flops | bytes accessed | tf_op | source)
XLA Modules:
  0.0 335.3 jit_solution(16911260170760622007)
XLA Ops:
  7.2 1.2 dynamic_slice.33
  9.1 2.3 broadcast_select_fusion
  11.5 2.1 reshape.40
  15.8 1.9 collective-permute-done.1
  17.8 4.5 %broadcast_in_dim.48 = f32[2048,1024]{1,0:T(8,128)} broadcast(f32[]{:T(128)} %constant.92.clone.1), dimensions={} | broadcast | bytes 8388612 | tf_op jit(solution)/shard_map/broadcast_in_dim | solution.py:50
  22.3 1.1 pad_maximum_fusion
  23.4 46.2 %collective-permute-start.2 = (f32[256,1024]{1,0:T(8,128)S(1)}, f32[256,1024]{1,0:T(8,128)S(1)}, u32[]{:S(2)}, u32[]{:S(2)}) collective-permute-start(f32[256,1024]{1,0:T(8,128)S(1)} %get-tuple-element.16), channel_id=1, source_target_pairs={{0,2},{2,4},{4,6},{6,7},{7,5},{5,3},{3,1},{1,0},{8,10},{10,12},{12... | collective-permute-start | bytes 3145736 | tf_op jit(solution)/shard_map/ppermute | solution.py:54
  69.5 4.5 %collective-permute-start.3 = (f32[256,1024]{1,0:T(8,128)S(1)}, f32[256,1024]{1,0:T(8,128)S(1)}, u32[]{:S(2)}, u32[]{:S(2)}) collective-permute-start(f32[256,1024]{1,0:T(8,128)S(1)} %get-tuple-element.16), channel_id=1, source_target_pairs={{0,1},{2,0},{4,2},{6,4},{7,6},{5,7},{3,5},{1,3},{8,9},{10,8},{12,1... | collective-permute-start | bytes 3145736 | tf_op jit(solution)/shard_map/ppermute | solution.py:59
  74.1 40.8 %collective-permute-done.2 = f32[256,1024]{1,0:T(8,128)S(1)} collective-permute-done((f32[256,1024]{1,0:T(8,128)S(1)}, f32[256,1024]{1,0:T(8,128)S(1)}, u32[]{:S(2)}, u32[]{:S(2)}) %collective-permute-start.2) | collective-permute-done | bytes 1048608 | tf_op jit(solution)/shard_map/ppermute | solution.py:54
  114.9 4.6 %collective-permute-done.3 = f32[256,1024]{1,0:T(8,128)S(1)} collective-permute-done((f32[256,1024]{1,0:T(8,128)S(1)}, f32[256,1024]{1,0:T(8,128)S(1)}, u32[]{:S(2)}, u32[]{:S(2)}) %collective-permute-start.3) | collective-permute-done | bytes 1048608 | tf_op jit(solution)/shard_map/ppermute | solution.py:59
  119.4 4.0 %collective-permute-start.5 = (f32[256,1024]{1,0:T(8,128)S(1)}, f32[256,1024]{1,0:T(8,128)}, u32[]{:S(2)}, u32[]{:S(2)}) collective-permute-start(f32[256,1024]{1,0:T(8,128)S(1)} %collective-permute-done.3), channel_id=1, source_target_pairs={{0,1},{2,0},{4,2},{6,4},{7,6},{5,7},{3,5},{1,3},{8,9},{10,8},{12,1... | collective-permute-start | bytes 3145736 | tf_op jit(solution)/shard_map/ppermute | solution.py:59
  123.4 40.1 %collective-permute-done.4 = f32[256,1024]{1,0:T(8,128)} collective-permute-done((f32[256,1024]{1,0:T(8,128)S(1)}, f32[256,1024]{1,0:T(8,128)}, u32[]{:S(2)}, u32[]{:S(2)}) %collective-permute-start.4) | collective-permute-done | bytes 1048608 | tf_op jit(solution)/shard_map/ppermute | solution.py:54
  173.9 3.6 %collective-permute-start.7 = (f32[256,1024]{1,0:T(8,128)}, f32[256,1024]{1,0:T(8,128)}, u32[]{:S(2)}, u32[]{:S(2)}) collective-permute-start(f32[256,1024]{1,0:T(8,128)} %collective-permute-done.5), channel_id=1, source_target_pairs={{0,1},{2,0},{4,2},{6,4},{7,6},{5,7},{3,5},{1,3},{8,9},{10,8},{12,1... | collective-permute-start | bytes 3145736 | tf_op jit(solution)/shard_map/ppermute | solution.py:59
  177.8 9.9 %collective-permute-done.6 = f32[256,1024]{1,0:T(8,128)} collective-permute-done((f32[256,1024]{1,0:T(8,128)}, f32[256,1024]{1,0:T(8,128)}, u32[]{:S(2)}, u32[]{:S(2)}) %collective-permute-start.6) | collective-permute-done | bytes 1048608 | tf_op jit(solution)/shard_map/ppermute | solution.py:54
  190.3 2.3 constant_dynamic-update-slice_fusion.4
  192.6 2.3 constant_dynamic-update-slice_fusion.3
  194.9 2.3 constant_dynamic-update-slice_fusion.2
  197.2 13.9 %collective-permute-done.7 = f32[256,1024]{1,0:T(8,128)} collective-permute-done((f32[256,1024]{1,0:T(8,128)}, f32[256,1024]{1,0:T(8,128)}, u32[]{:S(2)}, u32[]{:S(2)}) %collective-permute-start.7) | collective-permute-done | bytes 1048608 | tf_op jit(solution)/shard_map/ppermute | solution.py:59
  211.1 2.3 constant_dynamic-update-slice_fusion.1
  214.5 11.3 %fusion.7 = f32[2048,64]{0,1:T(8,128)S(1)} fusion(f32[2048,2048]{1,0:T(8,128)} %all-gather.2.cloned.1.call-done, f32[64,2048]{1,0:T(8,128)S(1)} %copy-done.1), kind=kOutput, calls=%fused_computation.39 | convolution fusion | flops 1610612736 | bytes 17825792 | tf_op jit(solution)/shard_map/dot_general | solution.py:75
  225.8 20.8 %collective-permute-start.9 = (f32[2050,64]{0,1:T(8,128)S(1)}, f32[2050,64]{0,1:T(8,128)S(1)}, u32[]{:S(2)}, u32[]{:S(2)}) collective-permute-start(f32[2050,64]{0,1:T(8,128)S(1)} %concatenate.34), channel_id=1, source_target_pairs={{0,4},{1,5},{2,6},{3,7},{4,0},{5,1},{6,2},{7,3},{8,12},{9,13},{10,... | collective-permute-start | bytes 1574408 | tf_op jit(solution)/shard_map/ppermute | solution.py:85
  246.6 18.4 %fusion.2 = f32[512,2048]{1,0:T(8,128)} fusion(f32[2048,2048]{1,0:T(8,128)} %all-gather.2.cloned.1.call-done, f32[2048,1024]{1,0:T(8,128)} %constant_dynamic-update-slice_fusion), kind=kOutput, calls=%fused_computation.4 | convolution fusion | flops 12884901888 | bytes 25165824 | tf_op jit(solution)/shard_map/dot_general | solution.py:67
  265.2 3.5 %collective-permute-start.10 = (f32[2050,64]{0,1:T(8,128)S(1)}, f32[2050,64]{0,1:T(8,128)S(1)}, u32[]{:S(2)}, u32[]{:S(2)}) collective-permute-start(f32[2050,64]{0,1:T(8,128)S(1)} %add.189), channel_id=1, source_target_pairs={{0,2},{1,3},{2,0},{3,1},{4,6},{5,7},{6,4},{7,5},{8,10},{9,11},{10,... | collective-permute-start | bytes 1574408 | tf_op jit(solution)/shard_map/ppermute | solution.py:85
  268.6 18.4 %fusion = f32[512,2048]{1,0:T(8,128)} fusion(f32[2048,2048]{1,0:T(8,128)} %all-gather.2.cloned.1.call-done, f32[2048,1024]{1,0:T(8,128)} %constant_dynamic-update-slice_fusion), kind=kOutput, calls=%fused_computation.2 | convolution fusion | flops 12884901888 | bytes 25165824 | tf_op jit(solution)/shard_map/dot_general | solution.py:67
  287.1 4.0 %collective-permute-start.11 = (f32[2050,64]{0,1:T(8,128)S(1)}, f32[2050,64]{0,1:T(8,128)S(1)}, u32[]{:S(2)}, u32[]{:S(2)}) collective-permute-start(f32[2050,64]{0,1:T(8,128)S(1)} %add.190), channel_id=1, source_target_pairs={{0,1},{1,0},{2,3},{3,2},{4,5},{5,4},{6,7},{7,6},{8,9},{9,8},{10,11... | collective-permute-start | bytes 1574408 | tf_op jit(solution)/shard_map/ppermute | solution.py:85
  291.0 10.5 %collective-permute-done.11 = f32[2050,64]{0,1:T(8,128)S(1)} collective-permute-done((f32[2050,64]{0,1:T(8,128)S(1)}, f32[2050,64]{0,1:T(8,128)S(1)}, u32[]{:S(2)}, u32[]{:S(2)}) %collective-permute-start.11) | collective-permute-done | bytes 524832 | tf_op jit(solution)/shard_map/ppermute | solution.py:85
  303.3 3.5 %collective-permute-done.13 = f32[128]{0:T(128)S(1)} collective-permute-done((f32[128]{0:T(128)S(1)}, f32[128]{0:T(128)S(1)}, u32[]{:S(2)}, u32[]{:S(2)}) %collective-permute-start.13) | collective-permute-done | bytes 544 | tf_op jit(solution)/shard_map/ppermute | solution.py:106
  306.8 8.3 %collective-permute-start.14 = (f32[256]{0:T(256)S(1)}, f32[256]{0:T(256)S(1)}, u32[]{:S(2)}, u32[]{:S(2)}) collective-permute-start(f32[256]{0:T(256)S(1)} %maximum_select_fusion.2), channel_id=1, source_target_pairs={{0,32},{8,40},{16,48},{24,56},{32,0},{40,8},{48,16},{56,24},{64,96... | collective-permute-start | bytes 3080 | tf_op jit(solution)/shard_map/ppermute | solution.py:106
  315.0 1.5 collective-permute-done.14
  316.6 2.3 collective-permute-start.15
  318.9 6.1 %maximum_add_fusion = f32[1024,2048]{1,0:T(8,128)} fusion(f32[512,2048]{1,0:T(8,128)} %fusion, f32[512,2048]{1,0:T(8,128)} %fusion.2, f32[2048]{0:T(1024)S(1)} %copy-done.2, s32[2048]{0:T(1024)S(1)} %iota_add_fusion, s32[1024]{0:T(1024)S(1)} %iota_add_fusion.1), kind=kLoop, calls=%fused_computation.1 | loop fusion | flops 8388608 | bytes 16797696 | tf_op jit(solution)/shard_map/add | solution.py:95
  325.0 3.4 %gather_fusion = f32[512]{0:T(512)} fusion(f32[1024]{0:T(1024)S(1)} %maximum_select_fusion, s32[1024]{0:T(1024)S(1)} %pad_clamp_fusion), kind=kCustom, calls=%fused_computation | custom fusion | bytes 6144 | tf_op jit(solution)/shard_map/gather | solution.py:110
  (57 shorter events, 10.1 us)
Async XLA Ops:
  7.2 180.5 %copy-start = (f32[2048]{0:T(1024)S(1)}, f32[2048]{0:T(1024)}, u32[]{:S(2)}) copy-start(f32[2048]{0:T(1024)} %param.13) | copy-start | bytes 24580
  7.2 207.3 %all-gather.2.cloned.1.call-start = ((), (), s32[]{:S(2)}) async-start(), calls=%async_computation | async-start | bytes 17825792 | tf_op jit(solution)/shard_map/all_gather | solution.py:23
  14.6 148.9 %copy-start.5 = (s32[8]{0:T(128)S(1)}, s32[8]{0:T(128)}, u32[]{:S(2)}) copy-start(s32[8]{0:T(128)} %constant.112.clone) | copy-start | bytes 100
  14.6 154.2 %copy-start.3 = (s32[8]{0:T(128)S(1)}, s32[8]{0:T(128)}, u32[]{:S(2)}) copy-start(s32[8]{0:T(128)} %constant.111.clone) | copy-start | bytes 100
  14.6 162.9 %copy-start.1 = (f32[64,2048]{1,0:T(8,128)S(1)}, f32[64,2048]{1,0:T(8,128)}, u32[]{:S(2)}) copy-start(f32[64,2048]{1,0:T(8,128)} %param.11) | copy-start | bytes 1572868
  14.6 162.9 %copy-start.2 = (f32[2048]{0:T(1024)S(1)}, f32[2048]{0:T(1024)}, u32[]{:S(2)}) copy-start(f32[2048]{0:T(1024)} %param.10) | copy-start | bytes 24580
  14.7 1.1 collective-permute-start
  15.6 2.0 collective-permute-start.1
  23.4 91.5 %collective-permute-start.2 = (f32[256,1024]{1,0:T(8,128)S(1)}, f32[256,1024]{1,0:T(8,128)S(1)}, u32[]{:S(2)}, u32[]{:S(2)}) collective-permute-start(f32[256,1024]{1,0:T(8,128)S(1)} %get-tuple-element.16), channel_id=1, source_target_pairs={{0,2},{2,4},{4,6},{6,7},{7,5},{5,3},{3,1},{1,0},{8,10},{10,12},{12... | collective-permute-start | bytes 3145736 | tf_op jit(solution)/shard_map/ppermute | solution.py:54
  69.5 49.9 %collective-permute-start.3 = (f32[256,1024]{1,0:T(8,128)S(1)}, f32[256,1024]{1,0:T(8,128)S(1)}, u32[]{:S(2)}, u32[]{:S(2)}) collective-permute-start(f32[256,1024]{1,0:T(8,128)S(1)} %get-tuple-element.16), channel_id=1, source_target_pairs={{0,1},{2,0},{4,2},{6,4},{7,6},{5,7},{3,5},{1,3},{8,9},{10,8},{12,1... | collective-permute-start | bytes 3145736 | tf_op jit(solution)/shard_map/ppermute | solution.py:59
  114.9 48.6 %collective-permute-start.4 = (f32[256,1024]{1,0:T(8,128)S(1)}, f32[256,1024]{1,0:T(8,128)}, u32[]{:S(2)}, u32[]{:S(2)}) collective-permute-start(f32[256,1024]{1,0:T(8,128)S(1)} %collective-permute-done.2), channel_id=1, source_target_pairs={{0,2},{2,4},{4,6},{6,7},{7,5},{5,3},{3,1},{1,0},{8,10},{10,12},{12... | collective-permute-start | bytes 3145736 | tf_op jit(solution)/shard_map/ppermute | solution.py:54
  119.4 54.5 %collective-permute-start.5 = (f32[256,1024]{1,0:T(8,128)S(1)}, f32[256,1024]{1,0:T(8,128)}, u32[]{:S(2)}, u32[]{:S(2)}) collective-permute-start(f32[256,1024]{1,0:T(8,128)S(1)} %collective-permute-done.3), channel_id=1, source_target_pairs={{0,1},{2,0},{4,2},{6,4},{7,6},{5,7},{3,5},{1,3},{8,9},{10,8},{12,1... | collective-permute-start | bytes 3145736 | tf_op jit(solution)/shard_map/ppermute | solution.py:59
  163.5 24.2 %collective-permute-start.6 = (f32[256,1024]{1,0:T(8,128)}, f32[256,1024]{1,0:T(8,128)}, u32[]{:S(2)}, u32[]{:S(2)}) collective-permute-start(f32[256,1024]{1,0:T(8,128)} %collective-permute-done.4), channel_id=1, source_target_pairs={{0,2},{2,4},{4,6},{6,7},{7,5},{5,3},{3,1},{1,0},{8,10},{10,12},{12... | collective-permute-start | bytes 3145736 | tf_op jit(solution)/shard_map/ppermute | solution.py:54
  173.9 37.2 %collective-permute-start.7 = (f32[256,1024]{1,0:T(8,128)}, f32[256,1024]{1,0:T(8,128)}, u32[]{:S(2)}, u32[]{:S(2)}) collective-permute-start(f32[256,1024]{1,0:T(8,128)} %collective-permute-done.5), channel_id=1, source_target_pairs={{0,1},{2,0},{4,2},{6,4},{7,6},{5,7},{3,5},{1,3},{8,9},{10,8},{12,1... | collective-permute-start | bytes 3145736 | tf_op jit(solution)/shard_map/ppermute | solution.py:59
  187.6 25.7 %collective-permute-start.8 = (f32[256,1024]{1,0:T(8,128)}, f32[256,1024]{1,0:T(8,128)S(1)}, u32[]{:S(2)}, u32[]{:S(2)}) collective-permute-start(f32[256,1024]{1,0:T(8,128)} %collective-permute-done.6), channel_id=1, source_target_pairs={{0,2},{2,4},{4,6},{6,7},{7,5},{5,3},{3,1},{1,0},{8,10},{10,12},{12... | collective-permute-start | bytes 3145736 | tf_op jit(solution)/shard_map/ppermute | solution.py:54
  225.8 39.2 %collective-permute-start.9 = (f32[2050,64]{0,1:T(8,128)S(1)}, f32[2050,64]{0,1:T(8,128)S(1)}, u32[]{:S(2)}, u32[]{:S(2)}) collective-permute-start(f32[2050,64]{0,1:T(8,128)S(1)} %concatenate.34), channel_id=1, source_target_pairs={{0,4},{1,5},{2,6},{3,7},{4,0},{5,1},{6,2},{7,3},{8,12},{9,13},{10,... | collective-permute-start | bytes 1574408 | tf_op jit(solution)/shard_map/ppermute | solution.py:85
  265.1 25.9 %copy-start.4 = (s32[512]{0:T(512)S(1)}, s32[512]{0:T(512)}, u32[]{:S(2)}) copy-start(s32[512]{0:T(512)} %param.12) | copy-start | bytes 6148
  265.2 21.8 %collective-permute-start.10 = (f32[2050,64]{0,1:T(8,128)S(1)}, f32[2050,64]{0,1:T(8,128)S(1)}, u32[]{:S(2)}, u32[]{:S(2)}) collective-permute-start(f32[2050,64]{0,1:T(8,128)S(1)} %add.189), channel_id=1, source_target_pairs={{0,2},{1,3},{2,0},{3,1},{4,6},{5,7},{6,4},{7,5},{8,10},{9,11},{10,... | collective-permute-start | bytes 1574408 | tf_op jit(solution)/shard_map/ppermute | solution.py:85
  287.1 14.5 %collective-permute-start.11 = (f32[2050,64]{0,1:T(8,128)S(1)}, f32[2050,64]{0,1:T(8,128)S(1)}, u32[]{:S(2)}, u32[]{:S(2)}) collective-permute-start(f32[2050,64]{0,1:T(8,128)S(1)} %add.190), channel_id=1, source_target_pairs={{0,1},{1,0},{2,3},{3,2},{4,5},{5,4},{6,7},{7,6},{8,9},{9,8},{10,11... | collective-permute-start | bytes 1574408 | tf_op jit(solution)/shard_map/ppermute | solution.py:85
  301.9 1.2 collective-permute-start.12
  303.2 3.6 %collective-permute-start.13 = (f32[128]{0:T(128)S(1)}, f32[128]{0:T(128)S(1)}, u32[]{:S(2)}, u32[]{:S(2)}) collective-permute-start(f32[128]{0:T(128)S(1)} %broadcast_select_fusion.1), channel_id=1, source_target_pairs={{0,16},{8,24},{16,0},{24,8},{32,48},{40,56},{48,32},{56,40},{64,80... | collective-permute-start | bytes 1544 | tf_op jit(solution)/shard_map/ppermute | solution.py:106
  306.8 9.8 %collective-permute-start.14 = (f32[256]{0:T(256)S(1)}, f32[256]{0:T(256)S(1)}, u32[]{:S(2)}, u32[]{:S(2)}) collective-permute-start(f32[256]{0:T(256)S(1)} %maximum_select_fusion.2), channel_id=1, source_target_pairs={{0,32},{8,40},{16,48},{24,56},{32,0},{40,8},{48,16},{56,24},{64,96... | collective-permute-start | bytes 3080 | tf_op jit(solution)/shard_map/ppermute | solution.py:106
  316.6 8.4 %collective-permute-start.15 = (f32[512]{0:T(512)S(1)}, f32[512]{0:T(512)S(1)}, u32[]{:S(2)}, u32[]{:S(2)}) collective-permute-start(f32[512]{0:T(512)S(1)} %maximum_select_fusion.1), channel_id=1, source_target_pairs={{0,64},{8,72},{16,80},{24,88},{32,96},{40,104},{48,112},{56,120},{... | collective-permute-start | bytes 6152 | tf_op jit(solution)/shard_map/ppermute | solution.py:106
Sparse Core Ops, SparseCore 0:
  11.6 187.7 all-gather.1

commit v10 on v9

--- a/solution.py
+++ b/solution.py
@@ -63,15 +63,10 @@
 
     col_all, row_all = lax.optimization_barrier((col_all, row_all))
     contract = (((0,), (0,)), ((), ()))
-    def rows_of_tile(lo, hi):
-        return lax.dot_general(
-            row_all[:, lo:hi], col_all, contract, precision=high,
-            preferred_element_type=jnp.float32,
-        )
-
-    n_parts = 2
-    part_rows = width_row // n_parts
-    parts = []
+    tile = lax.dot_general(
+        row_all, col_all, contract, precision=high, preferred_element_type=jnp.float32
+    )
+    tile, col_all = lax.optimization_barrier((tile, col_all))
     z_part = lax.dot_general(
         col_all, items, (((1,), (1,)), ((), ())), precision=high,
         preferred_element_type=jnp.float32,
@@ -83,13 +78,7 @@
     while step >= 1:
         pairs = [(c, c ^ step) for c in range(n_col)]
         packed = packed + lax.ppermute(packed, "col", pairs)
-        if len(parts) < n_parts:
-            lo = len(parts) * part_rows
-            part = rows_of_tile(lo, lo + part_rows)
-            part, packed = lax.optimization_barrier((part, packed))
-            parts.append(part)
         step //= 2
-    tile = jnp.concatenate(parts, axis=0)
     rows_global = row_pos * width_row + lax.broadcasted_iota(jnp.int32, (width_row, width_col), 0)
     cols_global = col_pos * width_col + lax.broadcasted_iota(jnp.int32, (width_row, width_col), 1)
     tile = tile + jnp.where(rows_global == cols_global, ridge[None, :], jnp.float32(0.0))

time: 336 us -> 352 us (1.048)
  waiting for transfers between devices: 128 us -> 150 us
  matrix products: 48.6 us -> 41.4 us
    ppermute x3, waiting for transfers between devices: 10.5 us -> 32.9 us  [body(): packed = packed + lax.ppermute(packed, 'col', pairs)]
    dot_general x2 -> x1, matrix products: 36.8 us -> 33.1 us  [body(): lax.dot_general(row_all, col_all, contract, precision=high, preferred_ele...]
    dot_general x1, matrix products: 11.3 us -> 7.74 us  [body(): lax.dot_general(col_all, items, (((1,), (1,)), ((), ())), precision=high,...]
  transfers between devices with their start and end apart: 17 -> 17, of which waited for: 10 -> 12; matrix products, arithmetic and copies ran while one was open for 20% -> 8% of each run, Pallas kernels for 0% -> 0%
where the time goes in v10:
time: 352 us; the launch traced here: 351 us
  waiting for transfers between devices  150 us (43%)
  starting transfers between devices  98.2 us (28%)
  matrix products  41.4 us (12%)
  local copies, waits for them, and re-layouts  26.4 us (8%)
  between operations  23.3 us (7%)
  other arithmetic  11.1 us (3%)
    ppermute x4, waiting for transfers between devices, body(): ahead = lax.ppermute(ahead, 'col', forward)  90.8 us
    ppermute x4, starting transfers between devices, body(): ahead = lax.ppermute(ahead, 'col', forward)  46.2 us
    dot_general x1, matrix products, body(): lax.dot_general(row_all, col_all, contract, precision=high, preferred_ele...  33.1 us
    ppermute x3, waiting for transfers between devices, body(): packed = packed + lax.ppermute(packed, 'col', pairs)  32.9 us
    ppermute x3, starting transfers between devices, body(): packed = packed + lax.ppermute(packed, 'col', pairs)  28.3 us
    ppermute x3, waiting for transfers between devices, body(): behind = lax.ppermute(behind, 'col', backward)  18.4 us
    ppermute x3, starting transfers between devices, body(): behind = lax.ppermute(behind, 'col', backward)  12.1 us
    ppermute x4, starting transfers between devices, body(): other = lax.ppermute(held, 'row', pairs)  10.6 us
  transfers between devices with their start and end apart: 17, of which 12 were waited for; matrix products, arithmetic and copies ran while one was open for 8% of the time, Pallas kernels for 0%

profile of v10, /device:TPU:0, one launch (start us, length us, event | category | flops | bytes accessed | tf_op | source)
XLA Modules:
  0.0 350.5 jit_solution(15645866874840598803)
XLA Ops:
  7.2 1.2 dynamic_slice.33
  9.1 2.3 broadcast_select_fusion
  11.5 2.1 reshape.40
  15.8 1.9 collective-permute-done.1
  17.8 4.5 %broadcast_in_dim.48 = f32[2048,1024]{1,0:T(8,128)} broadcast(f32[]{:T(128)} %constant.92.clone.1), dimensions={} | broadcast | bytes 8388612 | tf_op jit(solution)/shard_map/broadcast_in_dim | solution.py:50
  22.3 1.1 pad_maximum_fusion
  23.4 46.2 %collective-permute-start.2 = (f32[256,1024]{1,0:T(8,128)S(1)}, f32[256,1024]{1,0:T(8,128)S(1)}, u32[]{:S(2)}, u32[]{:S(2)}) collective-permute-start(f32[256,1024]{1,0:T(8,128)S(1)} %get-tuple-element.12), channel_id=1, source_target_pairs={{0,2},{2,4},{4,6},{6,7},{7,5},{5,3},{3,1},{1,0},{8,10},{10,12},{12... | collective-permute-start | bytes 3145736 | tf_op jit(solution)/shard_map/ppermute | solution.py:54
  69.5 4.5 %collective-permute-start.3 = (f32[256,1024]{1,0:T(8,128)S(1)}, f32[256,1024]{1,0:T(8,128)S(1)}, u32[]{:S(2)}, u32[]{:S(2)}) collective-permute-start(f32[256,1024]{1,0:T(8,128)S(1)} %get-tuple-element.12), channel_id=1, source_target_pairs={{0,1},{2,0},{4,2},{6,4},{7,6},{5,7},{3,5},{1,3},{8,9},{10,8},{12,1... | collective-permute-start | bytes 3145736 | tf_op jit(solution)/shard_map/ppermute | solution.py:59
  74.1 40.8 %collective-permute-done.2 = f32[256,1024]{1,0:T(8,128)S(1)} collective-permute-done((f32[256,1024]{1,0:T(8,128)S(1)}, f32[256,1024]{1,0:T(8,128)S(1)}, u32[]{:S(2)}, u32[]{:S(2)}) %collective-permute-start.2) | collective-permute-done | bytes 1048608 | tf_op jit(solution)/shard_map/ppermute | solution.py:54
  114.8 4.6 %collective-permute-done.3 = f32[256,1024]{1,0:T(8,128)S(1)} collective-permute-done((f32[256,1024]{1,0:T(8,128)S(1)}, f32[256,1024]{1,0:T(8,128)S(1)}, u32[]{:S(2)}, u32[]{:S(2)}) %collective-permute-start.3) | collective-permute-done | bytes 1048608 | tf_op jit(solution)/shard_map/ppermute | solution.py:59
  119.4 4.0 %collective-permute-start.5 = (f32[256,1024]{1,0:T(8,128)S(1)}, f32[256,1024]{1,0:T(8,128)}, u32[]{:S(2)}, u32[]{:S(2)}) collective-permute-start(f32[256,1024]{1,0:T(8,128)S(1)} %collective-permute-done.3), channel_id=1, source_target_pairs={{0,1},{2,0},{4,2},{6,4},{7,6},{5,7},{3,5},{1,3},{8,9},{10,8},{12,1... | collective-permute-start | bytes 3145736 | tf_op jit(solution)/shard_map/ppermute | solution.py:59
  123.4 40.1 %collective-permute-done.4 = f32[256,1024]{1,0:T(8,128)} collective-permute-done((f32[256,1024]{1,0:T(8,128)S(1)}, f32[256,1024]{1,0:T(8,128)}, u32[]{:S(2)}, u32[]{:S(2)}) %collective-permute-start.4) | collective-permute-done | bytes 1048608 | tf_op jit(solution)/shard_map/ppermute | solution.py:54
  173.8 3.6 %collective-permute-start.7 = (f32[256,1024]{1,0:T(8,128)}, f32[256,1024]{1,0:T(8,128)}, u32[]{:S(2)}, u32[]{:S(2)}) collective-permute-start(f32[256,1024]{1,0:T(8,128)} %collective-permute-done.5), channel_id=1, source_target_pairs={{0,1},{2,0},{4,2},{6,4},{7,6},{5,7},{3,5},{1,3},{8,9},{10,8},{12,1... | collective-permute-start | bytes 3145736 | tf_op jit(solution)/shard_map/ppermute | solution.py:59
  177.7 10.0 %collective-permute-done.6 = f32[256,1024]{1,0:T(8,128)} collective-permute-done((f32[256,1024]{1,0:T(8,128)}, f32[256,1024]{1,0:T(8,128)}, u32[]{:S(2)}, u32[]{:S(2)}) %collective-permute-start.6) | collective-permute-done | bytes 1048608 | tf_op jit(solution)/shard_map/ppermute | solution.py:54
  190.3 2.3 constant_dynamic-update-slice_fusion.4
  192.6 2.3 constant_dynamic-update-slice_fusion.3
  194.9 2.3 constant_dynamic-update-slice_fusion.2
  197.2 13.9 %collective-permute-done.7 = f32[256,1024]{1,0:T(8,128)} collective-permute-done((f32[256,1024]{1,0:T(8,128)}, f32[256,1024]{1,0:T(8,128)}, u32[]{:S(2)}, u32[]{:S(2)}) %collective-permute-start.7) | collective-permute-done | bytes 1048608 | tf_op jit(solution)/shard_map/ppermute | solution.py:59
  211.1 2.3 constant_dynamic-update-slice_fusion.1
  214.5 33.1 %fusion.3 = f32[1024,2048]{1,0:T(8,128)} fusion(f32[2048,1024]{1,0:T(8,128)} %constant_dynamic-update-slice_fusion, f32[2048,2048]{1,0:T(8,128)} %all-gather.2.cloned.1.call-done), kind=kOutput, calls=%fused_computation.35 | convolution fusion | flops 25769803776 | bytes 33554432 | tf_op jit(solution)/shard_map/dot_general | solution.py:66
  247.5 7.7 %fusion.4 = f32[2048,64]{0,1:T(8,128)S(1)} fusion(f32[2048,2048]{1,0:T(8,128)S(1)} %copy-done.1, f32[64,2048]{1,0:T(8,128)S(1)} %copy-done.2), kind=kOutput, calls=%fused_computation.36 | convolution fusion | flops 1610612736 | bytes 17825792 | tf_op jit(solution)/shard_map/dot_general | solution.py:70
  255.4 20.6 %collective-permute-start.9 = (f32[2050,64]{0,1:T(8,128)S(1)}, f32[2050,64]{0,1:T(8,128)S(1)}, u32[]{:S(2)}, u32[]{:S(2)}) collective-permute-start(f32[2050,64]{0,1:T(8,128)S(1)} %concatenate.31), channel_id=1, source_target_pairs={{0,4},{1,5},{2,6},{3,7},{4,0},{5,1},{6,2},{7,3},{8,12},{9,13},{10,... | collective-permute-start | bytes 1574408 | tf_op jit(solution)/shard_map/ppermute | solution.py:80
  276.0 11.1 %collective-permute-done.9 = f32[2050,64]{0,1:T(8,128)S(1)} collective-permute-done((f32[2050,64]{0,1:T(8,128)S(1)}, f32[2050,64]{0,1:T(8,128)S(1)}, u32[]{:S(2)}, u32[]{:S(2)}) %collective-permute-start.9) | collective-permute-done | bytes 524832 | tf_op jit(solution)/shard_map/ppermute | solution.py:80
  287.1 3.7 %collective-permute-start.10 = (f32[2050,64]{0,1:T(8,128)S(1)}, f32[2050,64]{0,1:T(8,128)S(1)}, u32[]{:S(2)}, u32[]{:S(2)}) collective-permute-start(f32[2050,64]{0,1:T(8,128)S(1)} %add.194), channel_id=1, source_target_pairs={{0,2},{1,3},{2,0},{3,1},{4,6},{5,7},{6,4},{7,5},{8,10},{9,11},{10,... | collective-permute-start | bytes 1574408 | tf_op jit(solution)/shard_map/ppermute | solution.py:80
  290.9 11.2 %collective-permute-done.10 = f32[2050,64]{0,1:T(8,128)S(1)} collective-permute-done((f32[2050,64]{0,1:T(8,128)S(1)}, f32[2050,64]{0,1:T(8,128)S(1)}, u32[]{:S(2)}, u32[]{:S(2)}) %collective-permute-start.10) | collective-permute-done | bytes 524832 | tf_op jit(solution)/shard_map/ppermute | solution.py:80
  302.2 4.0 %collective-permute-start.11 = (f32[2050,64]{0,1:T(8,128)S(1)}, f32[2050,64]{0,1:T(8,128)S(1)}, u32[]{:S(2)}, u32[]{:S(2)}) collective-permute-start(f32[2050,64]{0,1:T(8,128)S(1)} %add.195), channel_id=1, source_target_pairs={{0,1},{1,0},{2,3},{3,2},{4,5},{5,4},{6,7},{7,6},{8,9},{9,8},{10,11... | collective-permute-start | bytes 1574408 | tf_op jit(solution)/shard_map/ppermute | solution.py:80
  306.1 10.6 %collective-permute-done.11 = f32[2050,64]{0,1:T(8,128)S(1)} collective-permute-done((f32[2050,64]{0,1:T(8,128)S(1)}, f32[2050,64]{0,1:T(8,128)S(1)}, u32[]{:S(2)}, u32[]{:S(2)}) %collective-permute-start.11) | collective-permute-done | bytes 524832 | tf_op jit(solution)/shard_map/ppermute | solution.py:80
  318.4 3.5 %collective-permute-done.13 = f32[128]{0:T(128)S(1)} collective-permute-done((f32[128]{0:T(128)S(1)}, f32[128]{0:T(128)S(1)}, u32[]{:S(2)}, u32[]{:S(2)}) %collective-permute-start.13) | collective-permute-done | bytes 544 | tf_op jit(solution)/shard_map/ppermute | solution.py:95
  322.0 10.2 %collective-permute-start.14 = (f32[256]{0:T(256)S(1)}, f32[256]{0:T(256)S(1)}, u32[]{:S(2)}, u32[]{:S(2)}) collective-permute-start(f32[256]{0:T(256)S(1)} %maximum_select_fusion.2), channel_id=1, source_target_pairs={{0,32},{8,40},{16,48},{24,56},{32,0},{40,8},{48,16},{56,24},{64,96... | collective-permute-start | bytes 3080 | tf_op jit(solution)/shard_map/ppermute | solution.py:95
  332.2 1.5 collective-permute-done.14
  334.1 6.2 %select_add_fusion = f32[1024,2048]{1,0:T(8,128)} fusion(f32[1024,2048]{1,0:T(8,128)} %fusion.3, f32[2048]{0:T(1024)S(1)} %copy-done.3, s32[2048]{0:T(1024)S(1)} %iota_add_fusion, s32[1024]{0:T(1024)S(1)} %iota_add_fusion.1), kind=kLoop, calls=%fused_computation.1 | loop fusion | flops 6291456 | bytes 16797696 | tf_op jit(solution)/shard_map/add | solution.py:84
  340.2 3.4 gather_fusion
  (58 shorter events, 10.4 us)
Async XLA Ops:
  7.2 180.5 %copy-start = (f32[2048]{0:T(1024)S(1)}, f32[2048]{0:T(1024)}, u32[]{:S(2)}) copy-start(f32[2048]{0:T(1024)} %param.13) | copy-start | bytes 24580
  7.2 207.3 %all-gather.2.cloned.1.call-start = ((), (), s32[]{:S(2)}) async-start(), calls=%async_computation | async-start | bytes 17825792 | tf_op jit(solution)/shard_map/all_gather | solution.py:23
  14.5 148.9 %copy-start.6 = (s32[8]{0:T(128)S(1)}, s32[8]{0:T(128)}, u32[]{:S(2)}) copy-start(s32[8]{0:T(128)} %constant.112.clone) | copy-start | bytes 100
  14.6 154.2 %copy-start.4 = (s32[8]{0:T(128)S(1)}, s32[8]{0:T(128)}, u32[]{:S(2)}) copy-start(s32[8]{0:T(128)} %constant.111.clone) | copy-start | bytes 100
  14.6 162.9 %copy-start.2 = (f32[64,2048]{1,0:T(8,128)S(1)}, f32[64,2048]{1,0:T(8,128)}, u32[]{:S(2)}) copy-start(f32[64,2048]{1,0:T(8,128)} %param.11) | copy-start | bytes 1572868
  14.6 162.8 %copy-start.3 = (f32[2048]{0:T(1024)S(1)}, f32[2048]{0:T(1024)}, u32[]{:S(2)}) copy-start(f32[2048]{0:T(1024)} %param.10) | copy-start | bytes 24580
  14.7 1.1 collective-permute-start
  15.6 2.0 collective-permute-start.1
  23.4 91.5 %collective-permute-start.2 = (f32[256,1024]{1,0:T(8,128)S(1)}, f32[256,1024]{1,0:T(8,128)S(1)}, u32[]{:S(2)}, u32[]{:S(2)}) collective-permute-start(f32[256,1024]{1,0:T(8,128)S(1)} %get-tuple-element.12), channel_id=1, source_target_pairs={{0,2},{2,4},{4,6},{6,7},{7,5},{5,3},{3,1},{1,0},{8,10},{10,12},{12... | collective-permute-start | bytes 3145736 | tf_op jit(solution)/shard_map/ppermute | solution.py:54
  69.5 49.9 %collective-permute-start.3 = (f32[256,1024]{1,0:T(8,128)S(1)}, f32[256,1024]{1,0:T(8,128)S(1)}, u32[]{:S(2)}, u32[]{:S(2)}) collective-permute-start(f32[256,1024]{1,0:T(8,128)S(1)} %get-tuple-element.12), channel_id=1, source_target_pairs={{0,1},{2,0},{4,2},{6,4},{7,6},{5,7},{3,5},{1,3},{8,9},{10,8},{12,1... | collective-permute-start | bytes 3145736 | tf_op jit(solution)/shard_map/ppermute | solution.py:59
  114.8 48.6 %collective-permute-start.4 = (f32[256,1024]{1,0:T(8,128)S(1)}, f32[256,1024]{1,0:T(8,128)}, u32[]{:S(2)}, u32[]{:S(2)}) collective-permute-start(f32[256,1024]{1,0:T(8,128)S(1)} %collective-permute-done.2), channel_id=1, source_target_pairs={{0,2},{2,4},{4,6},{6,7},{7,5},{5,3},{3,1},{1,0},{8,10},{10,12},{12... | collective-permute-start | bytes 3145736 | tf_op jit(solution)/shard_map/ppermute | solution.py:54
  119.4 54.4 %collective-permute-start.5 = (f32[256,1024]{1,0:T(8,128)S(1)}, f32[256,1024]{1,0:T(8,128)}, u32[]{:S(2)}, u32[]{:S(2)}) collective-permute-start(f32[256,1024]{1,0:T(8,128)S(1)} %collective-permute-done.3), channel_id=1, source_target_pairs={{0,1},{2,0},{4,2},{6,4},{7,6},{5,7},{3,5},{1,3},{8,9},{10,8},{12,1... | collective-permute-start | bytes 3145736 | tf_op jit(solution)/shard_map/ppermute | solution.py:59
  163.5 24.2 %collective-permute-start.6 = (f32[256,1024]{1,0:T(8,128)}, f32[256,1024]{1,0:T(8,128)}, u32[]{:S(2)}, u32[]{:S(2)}) collective-permute-start(f32[256,1024]{1,0:T(8,128)} %collective-permute-done.4), channel_id=1, source_target_pairs={{0,2},{2,4},{4,6},{6,7},{7,5},{5,3},{3,1},{1,0},{8,10},{10,12},{12... | collective-permute-start | bytes 3145736 | tf_op jit(solution)/shard_map/ppermute | solution.py:54
  173.8 37.2 %collective-permute-start.7 = (f32[256,1024]{1,0:T(8,128)}, f32[256,1024]{1,0:T(8,128)}, u32[]{:S(2)}, u32[]{:S(2)}) collective-permute-start(f32[256,1024]{1,0:T(8,128)} %collective-permute-done.5), channel_id=1, source_target_pairs={{0,1},{2,0},{4,2},{6,4},{7,6},{5,7},{3,5},{1,3},{8,9},{10,8},{12,1... | collective-permute-start | bytes 3145736 | tf_op jit(solution)/shard_map/ppermute | solution.py:59
  187.6 25.7 %collective-permute-start.8 = (f32[256,1024]{1,0:T(8,128)}, f32[256,1024]{1,0:T(8,128)S(1)}, u32[]{:S(2)}, u32[]{:S(2)}) collective-permute-start(f32[256,1024]{1,0:T(8,128)} %collective-permute-done.6), channel_id=1, source_target_pairs={{0,2},{2,4},{4,6},{6,7},{7,5},{5,3},{3,1},{1,0},{8,10},{10,12},{12... | collective-permute-start | bytes 3145736 | tf_op jit(solution)/shard_map/ppermute | solution.py:54
  214.5 33.1 %copy-start.1 = (f32[2048,2048]{1,0:T(8,128)S(1)}, f32[2048,2048]{1,0:T(8,128)}, u32[]{:S(2)}) copy-start(f32[2048,2048]{1,0:T(8,128)} %all-gather.2.cloned.1.call-done) | copy-start | bytes 50331652
  247.5 58.6 %copy-start.5 = (s32[512]{0:T(512)S(1)}, s32[512]{0:T(512)}, u32[]{:S(2)}) copy-start(s32[512]{0:T(512)} %param.12) | copy-start | bytes 6148
  255.4 31.7 %collective-permute-start.9 = (f32[2050,64]{0,1:T(8,128)S(1)}, f32[2050,64]{0,1:T(8,128)S(1)}, u32[]{:S(2)}, u32[]{:S(2)}) collective-permute-start(f32[2050,64]{0,1:T(8,128)S(1)} %concatenate.31), channel_id=1, source_target_pairs={{0,4},{1,5},{2,6},{3,7},{4,0},{5,1},{6,2},{7,3},{8,12},{9,13},{10,... | collective-permute-start | bytes 1574408 | tf_op jit(solution)/shard_map/ppermute | solution.py:80
  287.1 15.0 %collective-permute-start.10 = (f32[2050,64]{0,1:T(8,128)S(1)}, f32[2050,64]{0,1:T(8,128)S(1)}, u32[]{:S(2)}, u32[]{:S(2)}) collective-permute-start(f32[2050,64]{0,1:T(8,128)S(1)} %add.194), channel_id=1, source_target_pairs={{0,2},{1,3},{2,0},{3,1},{4,6},{5,7},{6,4},{7,5},{8,10},{9,11},{10,... | collective-permute-start | bytes 1574408 | tf_op jit(solution)/shard_map/ppermute | solution.py:80
  302.2 14.6 %collective-permute-start.11 = (f32[2050,64]{0,1:T(8,128)S(1)}, f32[2050,64]{0,1:T(8,128)S(1)}, u32[]{:S(2)}, u32[]{:S(2)}) collective-permute-start(f32[2050,64]{0,1:T(8,128)S(1)} %add.195), channel_id=1, source_target_pairs={{0,1},{1,0},{2,3},{3,2},{4,5},{5,4},{6,7},{7,6},{8,9},{9,8},{10,11... | collective-permute-start | bytes 1574408 | tf_op jit(solution)/shard_map/ppermute | solution.py:80
  317.1 1.2 collective-permute-start.12
  318.4 3.6 %collective-permute-start.13 = (f32[128]{0:T(128)S(1)}, f32[128]{0:T(128)S(1)}, u32[]{:S(2)}, u32[]{:S(2)}) collective-permute-start(f32[128]{0:T(128)S(1)} %broadcast_select_fusion.1), channel_id=1, source_target_pairs={{0,16},{8,24},{16,0},{24,8},{32,48},{40,56},{48,32},{56,40},{64,80... | collective-permute-start | bytes 1544 | tf_op jit(solution)/shard_map/ppermute | solution.py:95
  322.0 11.8 %collective-permute-start.14 = (f32[256]{0:T(256)S(1)}, f32[256]{0:T(256)S(1)}, u32[]{:S(2)}, u32[]{:S(2)}) collective-permute-start(f32[256]{0:T(256)S(1)} %maximum_select_fusion.2), channel_id=1, source_target_pairs={{0,32},{8,40},{16,48},{24,56},{32,0},{40,8},{48,16},{56,24},{64,96... | collective-permute-start | bytes 3080 | tf_op jit(solution)/shard_map/ppermute | solution.py:95
  333.7 6.5 %collective-permute-start.15 = (f32[512]{0:T(512)S(1)}, f32[512]{0:T(512)S(1)}, u32[]{:S(2)}, u32[]{:S(2)}) collective-permute-start(f32[512]{0:T(512)S(1)} %maximum_select_fusion.1), channel_id=1, source_target_pairs={{0,64},{8,72},{16,80},{24,88},{32,96},{40,104},{48,112},{56,120},{... | collective-permute-start | bytes 6152 | tf_op jit(solution)/shard_map/ppermute | solution.py:95
Sparse Core Ops, SparseCore 0:
  11.6 187.8 all-gather.1

commit v11 on v10

--- a/solution.py
+++ b/solution.py
@@ -66,23 +66,18 @@
     tile = lax.dot_general(
         row_all, col_all, contract, precision=high, preferred_element_type=jnp.float32
     )
-    tile, col_all = lax.optimization_barrier((tile, col_all))
     z_part = lax.dot_general(
         col_all, items, (((1,), (1,)), ((), ())), precision=high,
         preferred_element_type=jnp.float32,
     )
     q_ridge = jnp.sum(ridge[None, :] * items * items, axis=1)
     lin = jnp.dot(items, theta, precision=highest, preferred_element_type=jnp.float32)
-    packed = jnp.concatenate([z_part, q_ridge[None, :], lin[None, :]], axis=0)
-    step = n_col // 2
-    while step >= 1:
-        pairs = [(c, c ^ step) for c in range(n_col)]
-        packed = packed + lax.ppermute(packed, "col", pairs)
-        step //= 2
+    packed = lax.psum(jnp.concatenate([z_part, q_ridge[None, :], lin[None, :]], axis=0), "col")
     rows_global = row_pos * width_row + lax.broadcasted_iota(jnp.int32, (width_row, width_col), 0)
     cols_global = col_pos * width_col + lax.broadcasted_iota(jnp.int32, (width_row, width_col), 1)
     tile = tile + jnp.where(rows_global == cols_global, ridge[None, :], jnp.float32(0.0))
 
+    packed, tile = lax.optimization_barrier((packed, tile))
     ev_all = z_part.shape[0]
     z = packed[:ev_all]
     quad = jnp.sum(z * z, axis=0) + packed[ev_all]

time: 352 us -> 365 us (1.037)
  waiting for transfers between devices: 150 us -> 197 us
  starting transfers between devices: 98.2 us -> 65 us
  other arithmetic: 11.1 us -> 5.75 us
  matrix products: 41.4 us -> 45.7 us
    psum x0 -> x1, waiting for transfers between devices: none -> 77.3 us  [body(): lax.psum(jnp.concatenate([z_part, q_ridge[None, :], lin[None, :]], axis=0...]
    ppermute x3 -> x0, waiting for transfers between devices: 32.9 us -> none  [body(): packed = packed + lax.ppermute(packed, 'col', pairs)]
    ppermute x3 -> x0, starting transfers between devices: 28.3 us -> none  [body(): packed = packed + lax.ppermute(packed, 'col', pairs)]
    add x4 -> x0, other arithmetic: 6.36 us -> none  [the longest x1 6.19 us: body(): tile + jnp.where(rows_global == cols_global, ridge[None, :], jnp.float32(...]
    ppermute x4, starting transfers between devices: 10.6 us -> 5.2 us  [body(): other = lax.ppermute(held, 'row', pairs)]
  transfers between devices with their start and end apart: 17 -> 15, of which waited for: 12 -> 12; matrix products, arithmetic and copies ran while one was open for 8% -> 16% of each run, Pallas kernels for 0% -> 0%
where the time goes in v11:
time: 365 us
  waiting for transfers between devices  197 us (54%)
  starting transfers between devices  65 us (18%)
  matrix products  45.7 us (13%)
  local copies, waits for them, and re-layouts  28.2 us (8%)
  between operations  23.5 us (6%)
  other arithmetic  5.75 us (2%)
    ppermute x4, waiting for transfers between devices, body(): ahead = lax.ppermute(ahead, 'col', forward)  87.3 us
    psum x1, waiting for transfers between devices, body(): lax.psum(jnp.concatenate([z_part, q_ridge[None, :], lin[None, :]], axis=0...  77.3 us
    ppermute x4, starting transfers between devices, body(): ahead = lax.ppermute(ahead, 'col', forward)  46.2 us
    dot_general x1, matrix products, body(): lax.dot_general(row_all, col_all, contract, precision=high, preferred_ele...  33.9 us
    ppermute x3, waiting for transfers between devices, body(): behind = lax.ppermute(behind, 'col', backward)  21.9 us
    ppermute x3, starting transfers between devices, body(): behind = lax.ppermute(behind, 'col', backward)  12.6 us
    dot_general x1, matrix products, body(): lax.dot_general(col_all, items, (((1,), (1,)), ((), ())), precision=high,...  11.3 us
    ppermute x4, waiting for transfers between devices, body(): other = lax.ppermute(held, 'row', pairs)  8.19 us
  transfers between devices with their start and end apart: 15, of which 12 were waited for; matrix products, arithmetic and copies ran while one was open for 16% of the time, Pallas kernels for 0%

profile of v11, /device:TPU:0, one launch (start us, length us, event | category | flops | bytes accessed | tf_op | source)
XLA Modules:
  0.0 364.6 jit_solution(2525174256028792048)
XLA Ops:
  7.2 1.2 dynamic_slice.33
  9.1 2.3 broadcast_select_fusion
  11.6 2.1 reshape.40
  15.8 1.9 collective-permute-done.1
  17.9 4.3 %broadcast_in_dim.48 = f32[2048,1024]{1,0:T(8,128)} broadcast(f32[]{:T(128)} %constant.92.clone.1), dimensions={} | broadcast | bytes 8388612 | tf_op jit(solution)/shard_map/broadcast_in_dim | solution.py:50
  22.1 1.1 pad_maximum_fusion
  23.3 46.2 %collective-permute-start.2 = (f32[256,1024]{1,0:T(8,128)S(1)}, f32[256,1024]{1,0:T(8,128)S(1)}, u32[]{:S(2)}, u32[]{:S(2)}) collective-permute-start(f32[256,1024]{1,0:T(8,128)S(1)} %get-tuple-element.12), channel_id=1, source_target_pairs={{0,2},{2,4},{4,6},{6,7},{7,5},{5,3},{3,1},{1,0},{8,10},{10,12},{12... | collective-permute-start | bytes 3145736 | tf_op jit(solution)/shard_map/ppermute | solution.py:54
  69.5 4.6 %collective-permute-start.3 = (f32[256,1024]{1,0:T(8,128)S(1)}, f32[256,1024]{1,0:T(8,128)S(1)}, u32[]{:S(2)}, u32[]{:S(2)}) collective-permute-start(f32[256,1024]{1,0:T(8,128)S(1)} %get-tuple-element.12), channel_id=1, source_target_pairs={{0,1},{2,0},{4,2},{6,4},{7,6},{5,7},{3,5},{1,3},{8,9},{10,8},{12,1... | collective-permute-start | bytes 3145736 | tf_op jit(solution)/shard_map/ppermute | solution.py:59
  74.0 40.5 %collective-permute-done.2 = f32[256,1024]{1,0:T(8,128)S(1)} collective-permute-done((f32[256,1024]{1,0:T(8,128)S(1)}, f32[256,1024]{1,0:T(8,128)S(1)}, u32[]{:S(2)}, u32[]{:S(2)}) %collective-permute-start.2) | collective-permute-done | bytes 1048608 | tf_op jit(solution)/shard_map/ppermute | solution.py:54
  114.5 4.9 %collective-permute-done.3 = f32[256,1024]{1,0:T(8,128)S(1)} collective-permute-done((f32[256,1024]{1,0:T(8,128)S(1)}, f32[256,1024]{1,0:T(8,128)S(1)}, u32[]{:S(2)}, u32[]{:S(2)}) %collective-permute-start.3) | collective-permute-done | bytes 1048608 | tf_op jit(solution)/shard_map/ppermute | solution.py:59
  119.4 4.0 %collective-permute-start.5 = (f32[256,1024]{1,0:T(8,128)S(1)}, f32[256,1024]{1,0:T(8,128)}, u32[]{:S(2)}, u32[]{:S(2)}) collective-permute-start(f32[256,1024]{1,0:T(8,128)S(1)} %collective-permute-done.3), channel_id=1, source_target_pairs={{0,1},{2,0},{4,2},{6,4},{7,6},{5,7},{3,5},{1,3},{8,9},{10,8},{12,1... | collective-permute-start | bytes 3145736 | tf_op jit(solution)/shard_map/ppermute | solution.py:59
  123.4 39.7 %collective-permute-done.4 = f32[256,1024]{1,0:T(8,128)} collective-permute-done((f32[256,1024]{1,0:T(8,128)S(1)}, f32[256,1024]{1,0:T(8,128)}, u32[]{:S(2)}, u32[]{:S(2)}) %collective-permute-start.4) | collective-permute-done | bytes 1048608 | tf_op jit(solution)/shard_map/ppermute | solution.py:54
  167.2 1.9 collective-permute-done.5
  169.1 4.1 %collective-permute-start.7 = (f32[256,1024]{1,0:T(8,128)}, f32[256,1024]{1,0:T(8,128)}, u32[]{:S(2)}, u32[]{:S(2)}) collective-permute-start(f32[256,1024]{1,0:T(8,128)} %collective-permute-done.5), channel_id=1, source_target_pairs={{0,1},{2,0},{4,2},{6,4},{7,6},{5,7},{3,5},{1,3},{8,9},{10,8},{12,1... | collective-permute-start | bytes 3145736 | tf_op jit(solution)/shard_map/ppermute | solution.py:59
  179.9 7.1 %collective-permute-done.6 = f32[256,1024]{1,0:T(8,128)} collective-permute-done((f32[256,1024]{1,0:T(8,128)}, f32[256,1024]{1,0:T(8,128)}, u32[]{:S(2)}, u32[]{:S(2)}) %collective-permute-start.6) | collective-permute-done | bytes 1048608 | tf_op jit(solution)/shard_map/ppermute | solution.py:54
  187.5 1.1 constant_dynamic-update-slice_fusion.6
  189.7 2.3 constant_dynamic-update-slice_fusion.4
  192.1 2.3 constant_dynamic-update-slice_fusion.3
  194.4 2.3 constant_dynamic-update-slice_fusion.2
  196.7 15.1 %collective-permute-done.7 = f32[256,1024]{1,0:T(8,128)} collective-permute-done((f32[256,1024]{1,0:T(8,128)}, f32[256,1024]{1,0:T(8,128)}, u32[]{:S(2)}, u32[]{:S(2)}) %collective-permute-start.7) | collective-permute-done | bytes 1048608 | tf_op jit(solution)/shard_map/ppermute | solution.py:59
  211.8 2.3 constant_dynamic-update-slice_fusion.1
  214.1 1.1 constant_dynamic-update-slice_fusion
  215.3 11.3 %fusion.2 = f32[2048,64]{0,1:T(8,128)S(1)} fusion(f32[2048,2048]{1,0:T(8,128)} %all-gather.2.cloned.1.call-done, f32[64,2048]{1,0:T(8,128)S(1)} %copy-done.1), kind=kOutput, calls=%fused_computation.34 | convolution fusion | flops 1610612736 | bytes 17825792 | tf_op jit(solution)/shard_map/dot_general | solution.py:69
  227.5 33.9 %select_add_fusion = f32[1024,2048]{1,0:T(8,128)} fusion(f32[2048]{0:T(1024)S(1)} %copy-done.3, s32[2048]{0:T(1024)S(1)} %iota_add_fusion, s32[1024]{0:T(1024)S(1)} %iota_add_fusion.1, f32[2048,1024]{1,0:T(8,128)} %constant_dynamic-update-slice_fusion, f32[2048,2048]{1,0:T(8,128)} %all-gather.2.cloned.1.call-done), kind=kOutput, calls=%fused_computation.1 | convolution fusion | flops 25776095232 | bytes 33574912 | tf_op jit(solution)/shard_map/dot_general | solution.py:66
  261.3 77.3 %all-reduce.2.cloned.1.call-done = f32[2050,64]{0,1:T(8,128)} async-done(((f32[2050,64]{0,1:T(8,128)}), f32[2050,64]{0,1:T(8,128)}) %all-reduce.2.cloned.1.call-update) | async-done | bytes 524816 | tf_op jit(solution)/shard_map/psum | solution.py:75
  339.6 1.2 multiply_reduce_fusion
  342.1 1.5 collective-permute-start.10
  343.6 2.1 collective-permute-done.10
  345.7 3.0 collective-permute-start.11
  348.7 2.1 collective-permute-done.11
  351.4 2.9 collective-permute-done.12
  354.4 3.4 gather_fusion
  (49 shorter events, 10.0 us)
Async XLA Ops:
  7.2 179.8 %copy-start = (f32[2048]{0:T(1024)S(1)}, f32[2048]{0:T(1024)}, u32[]{:S(2)}) copy-start(f32[2048]{0:T(1024)} %param.13) | copy-start | bytes 24580
  7.2 208.1 %all-gather.2.cloned.1.call-start = ((), (), s32[]{:S(2)}) async-start(), calls=%async_computation | async-start | bytes 17825792 | tf_op jit(solution)/shard_map/all_gather | solution.py:23
  11.5 327.1 %all-reduce.2.cloned.1.call-start = ((), (), s32[]{:S(2)}) async-start(), calls=%async_computation.1 | async-start | bytes 1114112 | tf_op jit(solution)/shard_map/psum | solution.py:75
  14.6 148.5 %copy-start.5 = (s32[8]{0:T(128)S(1)}, s32[8]{0:T(128)}, u32[]{:S(2)}) copy-start(s32[8]{0:T(128)} %constant.112.clone) | copy-start | bytes 100
  14.6 152.4 %copy-start.1 = (f32[64,2048]{1,0:T(8,128)S(1)}, f32[64,2048]{1,0:T(8,128)}, u32[]{:S(2)}) copy-start(f32[64,2048]{1,0:T(8,128)} %param.11) | copy-start | bytes 1572868
  14.6 152.4 %copy-start.3 = (f32[2048]{0:T(1024)S(1)}, f32[2048]{0:T(1024)}, u32[]{:S(2)}) copy-start(f32[2048]{0:T(1024)} %param.10) | copy-start | bytes 24580
  14.6 159.9 %copy-start.2 = (s32[8]{0:T(128)S(1)}, s32[8]{0:T(128)}, u32[]{:S(2)}) copy-start(s32[8]{0:T(128)} %constant.111.clone) | copy-start | bytes 100
  14.7 1.1 collective-permute-start
  15.7 2.0 collective-permute-start.1
  23.3 91.2 %collective-permute-start.2 = (f32[256,1024]{1,0:T(8,128)S(1)}, f32[256,1024]{1,0:T(8,128)S(1)}, u32[]{:S(2)}, u32[]{:S(2)}) collective-permute-start(f32[256,1024]{1,0:T(8,128)S(1)} %get-tuple-element.12), channel_id=1, source_target_pairs={{0,2},{2,4},{4,6},{6,7},{7,5},{5,3},{3,1},{1,0},{8,10},{10,12},{12... | collective-permute-start | bytes 3145736 | tf_op jit(solution)/shard_map/ppermute | solution.py:54
  69.5 49.9 %collective-permute-start.3 = (f32[256,1024]{1,0:T(8,128)S(1)}, f32[256,1024]{1,0:T(8,128)S(1)}, u32[]{:S(2)}, u32[]{:S(2)}) collective-permute-start(f32[256,1024]{1,0:T(8,128)S(1)} %get-tuple-element.12), channel_id=1, source_target_pairs={{0,1},{2,0},{4,2},{6,4},{7,6},{5,7},{3,5},{1,3},{8,9},{10,8},{12,1... | collective-permute-start | bytes 3145736 | tf_op jit(solution)/shard_map/ppermute | solution.py:59
  114.5 48.6 %collective-permute-start.4 = (f32[256,1024]{1,0:T(8,128)S(1)}, f32[256,1024]{1,0:T(8,128)}, u32[]{:S(2)}, u32[]{:S(2)}) collective-permute-start(f32[256,1024]{1,0:T(8,128)S(1)} %collective-permute-done.2), channel_id=1, source_target_pairs={{0,2},{2,4},{4,6},{6,7},{7,5},{5,3},{3,1},{1,0},{8,10},{10,12},{12... | collective-permute-start | bytes 3145736 | tf_op jit(solution)/shard_map/ppermute | solution.py:54
  119.4 49.7 %collective-permute-start.5 = (f32[256,1024]{1,0:T(8,128)S(1)}, f32[256,1024]{1,0:T(8,128)}, u32[]{:S(2)}, u32[]{:S(2)}) collective-permute-start(f32[256,1024]{1,0:T(8,128)S(1)} %collective-permute-done.3), channel_id=1, source_target_pairs={{0,1},{2,0},{4,2},{6,4},{7,6},{5,7},{3,5},{1,3},{8,9},{10,8},{12,1... | collective-permute-start | bytes 3145736 | tf_op jit(solution)/shard_map/ppermute | solution.py:59
  163.1 23.8 %collective-permute-start.6 = (f32[256,1024]{1,0:T(8,128)}, f32[256,1024]{1,0:T(8,128)}, u32[]{:S(2)}, u32[]{:S(2)}) collective-permute-start(f32[256,1024]{1,0:T(8,128)} %collective-permute-done.4), channel_id=1, source_target_pairs={{0,2},{2,4},{4,6},{6,7},{7,5},{5,3},{3,1},{1,0},{8,10},{10,12},{12... | collective-permute-start | bytes 3145736 | tf_op jit(solution)/shard_map/ppermute | solution.py:54
  169.1 42.7 %collective-permute-start.7 = (f32[256,1024]{1,0:T(8,128)}, f32[256,1024]{1,0:T(8,128)}, u32[]{:S(2)}, u32[]{:S(2)}) collective-permute-start(f32[256,1024]{1,0:T(8,128)} %collective-permute-done.5), channel_id=1, source_target_pairs={{0,1},{2,0},{4,2},{6,4},{7,6},{5,7},{3,5},{1,3},{8,9},{10,8},{12,1... | collective-permute-start | bytes 3145736 | tf_op jit(solution)/shard_map/ppermute | solution.py:59
  187.0 27.2 %collective-permute-start.8 = (f32[256,1024]{1,0:T(8,128)}, f32[256,1024]{1,0:T(8,128)S(1)}, u32[]{:S(2)}, u32[]{:S(2)}) collective-permute-start(f32[256,1024]{1,0:T(8,128)} %collective-permute-done.6), channel_id=1, source_target_pairs={{0,2},{2,4},{4,6},{6,7},{7,5},{5,3},{3,1},{1,0},{8,10},{10,12},{12... | collective-permute-start | bytes 3145736 | tf_op jit(solution)/shard_map/ppermute | solution.py:54
  227.5 121.2 %copy-start.4 = (s32[512]{0:T(512)S(1)}, s32[512]{0:T(512)}, u32[]{:S(2)}) copy-start(s32[512]{0:T(512)} %param.12) | copy-start | bytes 6148
  340.9 1.2 collective-permute-start.9
  342.1 3.6 collective-permute-start.10
  345.7 5.1 %collective-permute-start.11 = (f32[256]{0:T(256)S(1)}, f32[256]{0:T(256)S(1)}, u32[]{:S(2)}, u32[]{:S(2)}) collective-permute-start(f32[256]{0:T(256)S(1)} %maximum_select_fusion.2), channel_id=1, source_target_pairs={{0,32},{8,40},{16,48},{24,56},{32,0},{40,8},{48,16},{56,24},{64,96... | collective-permute-start | bytes 3080 | tf_op jit(solution)/shard_map/ppermute | solution.py:90
  350.8 3.6 collective-permute-start.12
Sparse Core Ops, SparseCore 0:
  11.6 192.8 all-gather.1
  227.6 110.9 all-reduce.1

commit v12 on v9

--- a/solution.py
+++ b/solution.py
@@ -78,26 +78,35 @@
     )
     q_ridge = jnp.sum(ridge[None, :] * items * items, axis=1)
     lin = jnp.dot(items, theta, precision=highest, preferred_element_type=jnp.float32)
-    packed = jnp.concatenate([z_part, q_ridge[None, :], lin[None, :]], axis=0)
+    cur = z_part
     step = n_col // 2
     while step >= 1:
         pairs = [(c, c ^ step) for c in range(n_col)]
-        packed = packed + lax.ppermute(packed, "col", pairs)
+        rows_half = cur.shape[0] // 2
+        lo_half, hi_half = cur[:rows_half], cur[rows_half:]
+        upper = (col_pos & step) != 0
+        keep = jnp.where(upper, hi_half, lo_half)
+        send = jnp.where(upper, lo_half, hi_half)
+        cur = keep + lax.ppermute(send, "col", pairs)
         if len(parts) < n_parts:
             lo = len(parts) * part_rows
             part = rows_of_tile(lo, lo + part_rows)
-            part, packed = lax.optimization_barrier((part, packed))
+            part, cur = lax.optimization_barrier((part, cur))
             parts.append(part)
+        step //= 2
+    small = jnp.stack([jnp.sum(cur * cur, axis=0), q_ridge, lin])
+    step = n_col // 2
+    while step >= 1:
+        pairs = [(c, c ^ step) for c in range(n_col)]
+        small = small + lax.ppermute(small, "col", pairs)
         step //= 2
     tile = jnp.concatenate(parts, axis=0)
     rows_global = row_pos * width_row + lax.broadcasted_iota(jnp.int32, (width_row, width_col), 0)
     cols_global = col_pos * width_col + lax.broadcasted_iota(jnp.int32, (width_row, width_col), 1)
     tile = tile + jnp.where(rows_global == cols_global, ridge[None, :], jnp.float32(0.0))
 
-    ev_all = z_part.shape[0]
-    z = packed[:ev_all]
-    quad = jnp.sum(z * z, axis=0) + packed[ev_all]
-    item_scores = packed[ev_all + 1] + jnp.sqrt(quad / F)
+    quad = small[0] + small[1]
+    item_scores = small[2] + jnp.sqrt(quad / F)
     items_dev = items.shape[0]
     held = item_scores
     step = 1

time: 336 us -> 341 us (1.015)
  starting transfers between devices: 98.1 us -> 102 us
    ppermute x3, waiting for transfers between devices: 18.4 us -> 25.3 us  [body(): behind = lax.ppermute(behind, 'col', backward)]
    ppermute x4, waiting for transfers between devices: 90.7 us -> 84.8 us  [body(): ahead = lax.ppermute(ahead, 'col', forward)]
    ppermute x3 -> x6, starting transfers between devices: 28.2 us -> 31.6 us  [the longest x3 27.1 us: body(): cur = keep + lax.ppermute(send, 'col', pairs)]
    ppermute x3 -> x6, waiting for transfers between devices: 10.5 us -> 11.6 us  [the longest x3 9.55 us: body(): small = small + lax.ppermute(small, 'col', pairs)]
  transfers between devices with their start and end apart: 17 -> 20, of which waited for: 10 -> 14; matrix products, arithmetic and copies ran while one was open for 20% -> 19% of each run, Pallas kernels for 0% -> 0%
where the time goes in v12:
time: 341 us; the launch traced here: 340 us
  waiting for transfers between devices  130 us (38%)
  starting transfers between devices  102 us (30%)
  matrix products  47.9 us (14%)
  local copies, waits for them, and re-layouts  26.1 us (8%)
  between operations  23.4 us (7%)
  other arithmetic  11 us (3%)
    ppermute x4, waiting for transfers between devices, body(): ahead = lax.ppermute(ahead, 'col', forward)  84.8 us
    ppermute x4, starting transfers between devices, body(): ahead = lax.ppermute(ahead, 'col', forward)  46.1 us
    dot_general x2, matrix products, rows_of_tile(): lax.dot_general(row_all[:, lo:hi], col_all, contract, precision=high, pre...  34.2 us
    ppermute x3, starting transfers between devices, body(): cur = keep + lax.ppermute(send, 'col', pairs)  27.1 us
    ppermute x3, waiting for transfers between devices, body(): behind = lax.ppermute(behind, 'col', backward)  25.3 us
    dot_general x1, matrix products, body(): lax.dot_general(col_all, items, (((1,), (1,)), ((), ())), precision=high,...  13.2 us
    ppermute x3, starting transfers between devices, body(): behind = lax.ppermute(behind, 'col', backward)  12.6 us
    ppermute x4, starting transfers between devices, body(): other = lax.ppermute(held, 'row', pairs)  10.7 us
  transfers between devices with their start and end apart: 20, of which 14 were waited for; matrix products, arithmetic and copies ran while one was open for 19% of the time, Pallas kernels for 0%

profile of v12, /device:TPU:0, one launch (start us, length us, event | category | flops | bytes accessed | tf_op | source)
XLA Modules:
  0.0 340.1 jit_solution(5183282388055698297)
XLA Ops:
  9.1 2.4 broadcast_select_fusion
  11.5 2.1 reshape.45
  17.8 4.5 %broadcast_in_dim.42 = f32[2048,1024]{1,0:T(8,128)} broadcast(f32[]{:T(128)} %constant.92.clone.1), dimensions={} | broadcast | bytes 8388612 | tf_op jit(solution)/shard_map/broadcast_in_dim | solution.py:50
  23.4 46.1 %collective-permute-start.2 = (f32[256,1024]{1,0:T(8,128)S(1)}, f32[256,1024]{1,0:T(8,128)S(1)}, u32[]{:S(2)}, u32[]{:S(2)}) collective-permute-start(f32[256,1024]{1,0:T(8,128)S(1)} %get-tuple-element.14), channel_id=1, source_target_pairs={{0,2},{2,4},{4,6},{6,7},{7,5},{5,3},{3,1},{1,0},{8,10},{10,12},{12... | collective-permute-start | bytes 3145736 | tf_op jit(solution)/shard_map/ppermute | solution.py:54
  69.5 4.5 %collective-permute-start.3 = (f32[256,1024]{1,0:T(8,128)S(1)}, f32[256,1024]{1,0:T(8,128)S(1)}, u32[]{:S(2)}, u32[]{:S(2)}) collective-permute-start(f32[256,1024]{1,0:T(8,128)S(1)} %get-tuple-element.14), channel_id=1, source_target_pairs={{0,1},{2,0},{4,2},{6,4},{7,6},{5,7},{3,5},{1,3},{8,9},{10,8},{12,1... | collective-permute-start | bytes 3145736 | tf_op jit(solution)/shard_map/ppermute | solution.py:59
  74.1 40.8 %collective-permute-done.2 = f32[256,1024]{1,0:T(8,128)S(1)} collective-permute-done((f32[256,1024]{1,0:T(8,128)S(1)}, f32[256,1024]{1,0:T(8,128)S(1)}, u32[]{:S(2)}, u32[]{:S(2)}) %collective-permute-start.2) | collective-permute-done | bytes 1048608 | tf_op jit(solution)/shard_map/ppermute | solution.py:54
  114.8 4.6 %collective-permute-done.3 = f32[256,1024]{1,0:T(8,128)S(1)} collective-permute-done((f32[256,1024]{1,0:T(8,128)S(1)}, f32[256,1024]{1,0:T(8,128)S(1)}, u32[]{:S(2)}, u32[]{:S(2)}) %collective-permute-start.3) | collective-permute-done | bytes 1048608 | tf_op jit(solution)/shard_map/ppermute | solution.py:59
  119.4 4.0 %collective-permute-start.5 = (f32[256,1024]{1,0:T(8,128)S(1)}, f32[256,1024]{1,0:T(8,128)}, u32[]{:S(2)}, u32[]{:S(2)}) collective-permute-start(f32[256,1024]{1,0:T(8,128)S(1)} %collective-permute-done.3), channel_id=1, source_target_pairs={{0,1},{2,0},{4,2},{6,4},{7,6},{5,7},{3,5},{1,3},{8,9},{10,8},{12,1... | collective-permute-start | bytes 3145736 | tf_op jit(solution)/shard_map/ppermute | solution.py:59
  123.4 40.1 %collective-permute-done.4 = f32[256,1024]{1,0:T(8,128)} collective-permute-done((f32[256,1024]{1,0:T(8,128)S(1)}, f32[256,1024]{1,0:T(8,128)}, u32[]{:S(2)}, u32[]{:S(2)}) %collective-permute-start.4) | collective-permute-done | bytes 1048608 | tf_op jit(solution)/shard_map/ppermute | solution.py:54
  163.5 5.6 %collective-permute-done.5 = f32[256,1024]{1,0:T(8,128)} collective-permute-done((f32[256,1024]{1,0:T(8,128)S(1)}, f32[256,1024]{1,0:T(8,128)}, u32[]{:S(2)}, u32[]{:S(2)}) %collective-permute-start.5) | collective-permute-done | bytes 1048608 | tf_op jit(solution)/shard_map/ppermute | solution.py:59
  169.1 4.1 %collective-permute-start.7 = (f32[256,1024]{1,0:T(8,128)}, f32[256,1024]{1,0:T(8,128)}, u32[]{:S(2)}, u32[]{:S(2)}) collective-permute-start(f32[256,1024]{1,0:T(8,128)} %collective-permute-done.5), channel_id=1, source_target_pairs={{0,1},{2,0},{4,2},{6,4},{7,6},{5,7},{3,5},{1,3},{8,9},{10,8},{12,1... | collective-permute-start | bytes 3145736 | tf_op jit(solution)/shard_map/ppermute | solution.py:59
  183.6 4.0 %collective-permute-done.6 = f32[256,1024]{1,0:T(8,128)} collective-permute-done((f32[256,1024]{1,0:T(8,128)}, f32[256,1024]{1,0:T(8,128)}, u32[]{:S(2)}, u32[]{:S(2)}) %collective-permute-start.6) | collective-permute-done | bytes 1048608 | tf_op jit(solution)/shard_map/ppermute | solution.py:54
  190.2 2.3 constant_dynamic-update-slice_fusion.4
  192.5 2.3 constant_dynamic-update-slice_fusion.3
  194.9 2.3 constant_dynamic-update-slice_fusion.2
  197.2 15.0 %collective-permute-done.7 = f32[256,1024]{1,0:T(8,128)} collective-permute-done((f32[256,1024]{1,0:T(8,128)}, f32[256,1024]{1,0:T(8,128)}, u32[]{:S(2)}, u32[]{:S(2)}) %collective-permute-start.7) | collective-permute-done | bytes 1048608 | tf_op jit(solution)/shard_map/ppermute | solution.py:59
  212.2 2.3 constant_dynamic-update-slice_fusion.1
  215.6 13.2 %fusion.7 = f32[2048,64]{0,1:T(8,128)S(1)} fusion(f32[2048,2048]{1,0:T(8,128)} %all-gather.2.cloned.1.call-done, f32[64,2048]{1,0:T(8,128)S(1)} %copy-done.2), kind=kOutput, calls=%fused_computation.43 | convolution fusion | flops 1610612736 | bytes 17825792 | tf_op jit(solution)/shard_map/dot_general | solution.py:75
  228.9 19.7 %collective-permute-start.9 = (f32[1024,64]{0,1:T(8,128)S(1)}, f32[1024,64]{0,1:T(8,128)S(1)}, u32[]{:S(2)}, u32[]{:S(2)}) collective-permute-start(f32[1024,64]{0,1:T(8,128)S(1)} %slice_select_fusion), channel_id=1, source_target_pairs={{0,4},{1,5},{2,6},{3,7},{4,0},{5,1},{6,2},{7,3},{8,12},{9,13},{10,... | collective-permute-start | bytes 786440 | tf_op jit(solution)/shard_map/ppermute | solution.py:90
  248.6 17.2 %fusion.2 = f32[512,2048]{1,0:T(8,128)} fusion(f32[2048,2048]{1,0:T(8,128)S(1)} %copy-done.1, f32[2048,1024]{1,0:T(8,128)} %constant_dynamic-update-slice_fusion), kind=kOutput, calls=%fused_computation.4 | convolution fusion | flops 12884901888 | bytes 25165824 | tf_op jit(solution)/shard_map/dot_general | solution.py:67
  265.8 3.5 %collective-permute-start.10 = (f32[512,64]{0,1:T(8,128)S(1)}, f32[512,64]{0,1:T(8,128)S(1)}, u32[]{:S(2)}, u32[]{:S(2)}) collective-permute-start(f32[512,64]{0,1:T(8,128)S(1)} %slice_select_fusion.1), channel_id=1, source_target_pairs={{0,2},{1,3},{2,0},{3,1},{4,6},{5,7},{6,4},{7,5},{8,10},{9,11},{10,... | collective-permute-start | bytes 393224 | tf_op jit(solution)/shard_map/ppermute | solution.py:90
  269.3 17.1 %fusion = f32[512,2048]{1,0:T(8,128)} fusion(f32[2048,2048]{1,0:T(8,128)S(1)} %copy-done.1, f32[2048,1024]{1,0:T(8,128)} %constant_dynamic-update-slice_fusion), kind=kOutput, calls=%fused_computation.2 | convolution fusion | flops 12884901888 | bytes 25165824 | tf_op jit(solution)/shard_map/dot_general | solution.py:67
  286.4 4.0 %collective-permute-start.11 = (f32[256,64]{0,1:T(8,128)S(1)}, f32[256,64]{0,1:T(8,128)S(1)}, u32[]{:S(2)}, u32[]{:S(2)}) collective-permute-start(f32[256,64]{0,1:T(8,128)S(1)} %slice_select_fusion.2), channel_id=1, source_target_pairs={{0,1},{1,0},{2,3},{3,2},{4,5},{5,4},{6,7},{7,6},{8,9},{9,8},{10,11... | collective-permute-start | bytes 196616 | tf_op jit(solution)/shard_map/ppermute | solution.py:90
  290.5 2.1 collective-permute-done.11
  293.5 4.4 %collective-permute-done.12 = f32[3,64]{1,0:T(4,128)S(1)} collective-permute-done((f32[3,64]{1,0:T(4,128)S(1)}, f32[3,64]{1,0:T(4,128)S(1)}, u32[]{:S(2)}, u32[]{:S(2)}) %collective-permute-start.12) | collective-permute-done | bytes 800 | tf_op jit(solution)/shard_map/ppermute | solution.py:101
  298.0 3.5 %collective-permute-done.13 = f32[3,64]{1,0:T(4,128)S(1)} collective-permute-done((f32[3,64]{1,0:T(4,128)S(1)}, f32[3,64]{1,0:T(4,128)S(1)}, u32[]{:S(2)}, u32[]{:S(2)}) %collective-permute-start.13) | collective-permute-done | bytes 800 | tf_op jit(solution)/shard_map/ppermute | solution.py:101
  301.6 3.6 %collective-permute-start.14 = (f32[3,64]{1,0:T(4,128)S(1)}, f32[3,64]{1,0:T(4,128)S(1)}, u32[]{:S(2)}, u32[]{:S(2)}) collective-permute-start(f32[3,64]{1,0:T(4,128)S(1)} %fusion.15), channel_id=1, source_target_pairs={{0,1},{1,0},{2,3},{3,2},{4,5},{5,4},{6,7},{7,6},{8,9},{9,8},{10,11... | collective-permute-start | bytes 2312 | tf_op jit(solution)/shard_map/ppermute | solution.py:101
  308.1 3.5 %collective-permute-done.16 = f32[128]{0:T(128)S(1)} collective-permute-done((f32[128]{0:T(128)S(1)}, f32[128]{0:T(128)S(1)}, u32[]{:S(2)}, u32[]{:S(2)}) %collective-permute-start.16) | collective-permute-done | bytes 544 | tf_op jit(solution)/shard_map/ppermute | solution.py:115
  311.6 7.6 %collective-permute-start.17 = (f32[256]{0:T(256)S(1)}, f32[256]{0:T(256)S(1)}, u32[]{:S(2)}, u32[]{:S(2)}) collective-permute-start(f32[256]{0:T(256)S(1)} %maximum_select_fusion.2), channel_id=1, source_target_pairs={{0,32},{8,40},{16,48},{24,56},{32,0},{40,8},{48,16},{56,24},{64,96... | collective-permute-start | bytes 3080 | tf_op jit(solution)/shard_map/ppermute | solution.py:115
  320.7 3.0 collective-permute-start.18
  323.7 6.1 %maximum_add_fusion = f32[1024,2048]{1,0:T(8,128)} fusion(f32[512,2048]{1,0:T(8,128)} %fusion, f32[512,2048]{1,0:T(8,128)} %fusion.2, f32[2048]{0:T(1024)S(1)} %copy-done.3, s32[2048]{0:T(1024)S(1)} %iota_add_fusion, s32[1024]{0:T(1024)S(1)} %iota_add_fusion.1), kind=kLoop, calls=%fused_computation.1 | loop fusion | flops 8388608 | bytes 16797696 | tf_op jit(solution)/shard_map/add | solution.py:106
  329.8 3.4 %gather_fusion = f32[512]{0:T(512)} fusion(f32[1024]{0:T(1024)S(1)} %maximum_select_fusion, s32[1024]{0:T(1024)S(1)} %pad_clamp_fusion), kind=kCustom, calls=%fused_computation | custom fusion | bytes 6144 | tf_op jit(solution)/shard_map/gather | solution.py:119
  (68 shorter events, 17.9 us)
Async XLA Ops:
  7.2 180.5 %copy-start = (f32[2048]{0:T(1024)S(1)}, f32[2048]{0:T(1024)}, u32[]{:S(2)}) copy-start(f32[2048]{0:T(1024)} %param.13) | copy-start | bytes 24580
  7.2 208.4 %all-gather.2.cloned.1.call-start = ((), (), s32[]{:S(2)}) async-start(), calls=%async_computation | async-start | bytes 17825792 | tf_op jit(solution)/shard_map/all_gather | solution.py:23
  14.6 158.6 %copy-start.6 = (s32[8]{0:T(128)S(1)}, s32[8]{0:T(128)}, u32[]{:S(2)}) copy-start(s32[8]{0:T(128)} %constant.112.clone) | copy-start | bytes 100
  14.6 163.9 %copy-start.4 = (s32[8]{0:T(128)S(1)}, s32[8]{0:T(128)}, u32[]{:S(2)}) copy-start(s32[8]{0:T(128)} %constant.111.clone) | copy-start | bytes 100
  14.6 173.0 %copy-start.2 = (f32[64,2048]{1,0:T(8,128)S(1)}, f32[64,2048]{1,0:T(8,128)}, u32[]{:S(2)}) copy-start(f32[64,2048]{1,0:T(8,128)} %param.11) | copy-start | bytes 1572868
  14.7 1.1 collective-permute-start
  15.7 2.0 collective-permute-start.1
  23.4 91.4 %collective-permute-start.2 = (f32[256,1024]{1,0:T(8,128)S(1)}, f32[256,1024]{1,0:T(8,128)S(1)}, u32[]{:S(2)}, u32[]{:S(2)}) collective-permute-start(f32[256,1024]{1,0:T(8,128)S(1)} %get-tuple-element.14), channel_id=1, source_target_pairs={{0,2},{2,4},{4,6},{6,7},{7,5},{5,3},{3,1},{1,0},{8,10},{10,12},{12... | collective-permute-start | bytes 3145736 | tf_op jit(solution)/shard_map/ppermute | solution.py:54
  69.5 49.9 %collective-permute-start.3 = (f32[256,1024]{1,0:T(8,128)S(1)}, f32[256,1024]{1,0:T(8,128)S(1)}, u32[]{:S(2)}, u32[]{:S(2)}) collective-permute-start(f32[256,1024]{1,0:T(8,128)S(1)} %get-tuple-element.14), channel_id=1, source_target_pairs={{0,1},{2,0},{4,2},{6,4},{7,6},{5,7},{3,5},{1,3},{8,9},{10,8},{12,1... | collective-permute-start | bytes 3145736 | tf_op jit(solution)/shard_map/ppermute | solution.py:59
  114.8 48.6 %collective-permute-start.4 = (f32[256,1024]{1,0:T(8,128)S(1)}, f32[256,1024]{1,0:T(8,128)}, u32[]{:S(2)}, u32[]{:S(2)}) collective-permute-start(f32[256,1024]{1,0:T(8,128)S(1)} %collective-permute-done.2), channel_id=1, source_target_pairs={{0,2},{2,4},{4,6},{6,7},{7,5},{5,3},{3,1},{1,0},{8,10},{10,12},{12... | collective-permute-start | bytes 3145736 | tf_op jit(solution)/shard_map/ppermute | solution.py:54
  119.4 49.7 %collective-permute-start.5 = (f32[256,1024]{1,0:T(8,128)S(1)}, f32[256,1024]{1,0:T(8,128)}, u32[]{:S(2)}, u32[]{:S(2)}) collective-permute-start(f32[256,1024]{1,0:T(8,128)S(1)} %collective-permute-done.3), channel_id=1, source_target_pairs={{0,1},{2,0},{4,2},{6,4},{7,6},{5,7},{3,5},{1,3},{8,9},{10,8},{12,1... | collective-permute-start | bytes 3145736 | tf_op jit(solution)/shard_map/ppermute | solution.py:59
  163.5 24.1 %collective-permute-start.6 = (f32[256,1024]{1,0:T(8,128)}, f32[256,1024]{1,0:T(8,128)}, u32[]{:S(2)}, u32[]{:S(2)}) collective-permute-start(f32[256,1024]{1,0:T(8,128)} %collective-permute-done.4), channel_id=1, source_target_pairs={{0,2},{2,4},{4,6},{6,7},{7,5},{5,3},{3,1},{1,0},{8,10},{10,12},{12... | collective-permute-start | bytes 3145736 | tf_op jit(solution)/shard_map/ppermute | solution.py:54
  169.1 43.1 %collective-permute-start.7 = (f32[256,1024]{1,0:T(8,128)}, f32[256,1024]{1,0:T(8,128)}, u32[]{:S(2)}, u32[]{:S(2)}) collective-permute-start(f32[256,1024]{1,0:T(8,128)} %collective-permute-done.5), channel_id=1, source_target_pairs={{0,1},{2,0},{4,2},{6,4},{7,6},{5,7},{3,5},{1,3},{8,9},{10,8},{12,1... | collective-permute-start | bytes 3145736 | tf_op jit(solution)/shard_map/ppermute | solution.py:59
  187.6 26.9 %collective-permute-start.8 = (f32[256,1024]{1,0:T(8,128)}, f32[256,1024]{1,0:T(8,128)S(1)}, u32[]{:S(2)}, u32[]{:S(2)}) collective-permute-start(f32[256,1024]{1,0:T(8,128)} %collective-permute-done.6), channel_id=1, source_target_pairs={{0,2},{2,4},{4,6},{6,7},{7,5},{5,3},{3,1},{1,0},{8,10},{10,12},{12... | collective-permute-start | bytes 3145736 | tf_op jit(solution)/shard_map/ppermute | solution.py:54
  215.6 33.0 %copy-start.1 = (f32[2048,2048]{1,0:T(8,128)S(1)}, f32[2048,2048]{1,0:T(8,128)}, u32[]{:S(2)}) copy-start(f32[2048,2048]{1,0:T(8,128)} %all-gather.2.cloned.1.call-done) | copy-start | bytes 50331652
  228.9 36.9 %collective-permute-start.9 = (f32[1024,64]{0,1:T(8,128)S(1)}, f32[1024,64]{0,1:T(8,128)S(1)}, u32[]{:S(2)}, u32[]{:S(2)}) collective-permute-start(f32[1024,64]{0,1:T(8,128)S(1)} %slice_select_fusion), channel_id=1, source_target_pairs={{0,4},{1,5},{2,6},{3,7},{4,0},{5,1},{6,2},{7,3},{8,12},{9,13},{10,... | collective-permute-start | bytes 786440 | tf_op jit(solution)/shard_map/ppermute | solution.py:90
  265.8 24.6 %copy-start.3 = (f32[2048]{0:T(1024)S(1)}, f32[2048]{0:T(1024)}, u32[]{:S(2)}) copy-start(f32[2048]{0:T(1024)} %param.10) | copy-start | bytes 24580
  265.8 39.4 %copy-start.5 = (s32[512]{0:T(512)S(1)}, s32[512]{0:T(512)}, u32[]{:S(2)}) copy-start(s32[512]{0:T(512)} %param.12) | copy-start | bytes 6148
  265.8 20.5 %collective-permute-start.10 = (f32[512,64]{0,1:T(8,128)S(1)}, f32[512,64]{0,1:T(8,128)S(1)}, u32[]{:S(2)}, u32[]{:S(2)}) collective-permute-start(f32[512,64]{0,1:T(8,128)S(1)} %slice_select_fusion.1), channel_id=1, source_target_pairs={{0,2},{1,3},{2,0},{3,1},{4,6},{5,7},{6,4},{7,5},{8,10},{9,11},{10,... | collective-permute-start | bytes 393224 | tf_op jit(solution)/shard_map/ppermute | solution.py:90
  286.4 6.2 %collective-permute-start.11 = (f32[256,64]{0,1:T(8,128)S(1)}, f32[256,64]{0,1:T(8,128)S(1)}, u32[]{:S(2)}, u32[]{:S(2)}) collective-permute-start(f32[256,64]{0,1:T(8,128)S(1)} %slice_select_fusion.2), channel_id=1, source_target_pairs={{0,1},{1,0},{2,3},{3,2},{4,5},{5,4},{6,7},{7,6},{8,9},{9,8},{10,11... | collective-permute-start | bytes 196616 | tf_op jit(solution)/shard_map/ppermute | solution.py:90
  292.7 5.2 %collective-permute-start.12 = (f32[3,64]{1,0:T(4,128)S(1)}, f32[3,64]{1,0:T(4,128)S(1)}, u32[]{:S(2)}, u32[]{:S(2)}) collective-permute-start(f32[3,64]{1,0:T(4,128)S(1)} %pad_maximum_fusion.1), channel_id=1, source_target_pairs={{0,4},{1,5},{2,6},{3,7},{4,0},{5,1},{6,2},{7,3},{8,12},{9,13},{10,... | collective-permute-start | bytes 2312 | tf_op jit(solution)/shard_map/ppermute | solution.py:101
  297.9 3.7 %collective-permute-start.13 = (f32[3,64]{1,0:T(4,128)S(1)}, f32[3,64]{1,0:T(4,128)S(1)}, u32[]{:S(2)}, u32[]{:S(2)}) collective-permute-start(f32[3,64]{1,0:T(4,128)S(1)} %fusion.5), channel_id=1, source_target_pairs={{0,2},{1,3},{2,0},{3,1},{4,6},{5,7},{6,4},{7,5},{8,10},{9,11},{10,... | collective-permute-start | bytes 2312 | tf_op jit(solution)/shard_map/ppermute | solution.py:101
  301.6 5.2 %collective-permute-start.14 = (f32[3,64]{1,0:T(4,128)S(1)}, f32[3,64]{1,0:T(4,128)S(1)}, u32[]{:S(2)}, u32[]{:S(2)}) collective-permute-start(f32[3,64]{1,0:T(4,128)S(1)} %fusion.15), channel_id=1, source_target_pairs={{0,1},{1,0},{2,3},{3,2},{4,5},{5,4},{6,7},{7,6},{8,9},{9,8},{10,11... | collective-permute-start | bytes 2312 | tf_op jit(solution)/shard_map/ppermute | solution.py:101
  306.8 1.2 collective-permute-start.15
  308.0 3.6 %collective-permute-start.16 = (f32[128]{0:T(128)S(1)}, f32[128]{0:T(128)S(1)}, u32[]{:S(2)}, u32[]{:S(2)}) collective-permute-start(f32[128]{0:T(128)S(1)} %broadcast_select_fusion.1), channel_id=1, source_target_pairs={{0,16},{8,24},{16,0},{24,8},{32,48},{40,56},{48,32},{56,40},{64,80... | collective-permute-start | bytes 1544 | tf_op jit(solution)/shard_map/ppermute | solution.py:115
  311.6 9.1 %collective-permute-start.17 = (f32[256]{0:T(256)S(1)}, f32[256]{0:T(256)S(1)}, u32[]{:S(2)}, u32[]{:S(2)}) collective-permute-start(f32[256]{0:T(256)S(1)} %maximum_select_fusion.2), channel_id=1, source_target_pairs={{0,32},{8,40},{16,48},{24,56},{32,0},{40,8},{48,16},{56,24},{64,96... | collective-permute-start | bytes 3080 | tf_op jit(solution)/shard_map/ppermute | solution.py:115
  320.7 9.1 %collective-permute-start.18 = (f32[512]{0:T(512)S(1)}, f32[512]{0:T(512)S(1)}, u32[]{:S(2)}, u32[]{:S(2)}) collective-permute-start(f32[512]{0:T(512)S(1)} %maximum_select_fusion.1), channel_id=1, source_target_pairs={{0,64},{8,72},{16,80},{24,88},{32,96},{40,104},{48,112},{56,120},{... | collective-permute-start | bytes 6152 | tf_op jit(solution)/shard_map/ppermute | solution.py:115
Sparse Core Ops, SparseCore 0:
  11.6 193.4 all-gather.1

commit v13 on v3

--- a/solution.py
+++ b/solution.py
@@ -62,14 +62,6 @@
             row_all, behind, from_behind * block_rows + half_rows, 0
         )
 
-    contract = (((0,), (0,)), ((), ()))
-    tile = lax.dot_general(
-        row_all, col_all, contract, precision=high, preferred_element_type=jnp.float32
-    )
-    rows_global = row_pos * width_row + lax.broadcasted_iota(jnp.int32, (width_row, width_col), 0)
-    cols_global = col_pos * width_col + lax.broadcasted_iota(jnp.int32, (width_row, width_col), 1)
-    tile = tile + jnp.where(rows_global == cols_global, ridge[None, :], jnp.float32(0.0))
-
     z_part = lax.dot_general(
         col_all, items, (((1,), (1,)), ((), ())), precision=high,
         preferred_element_type=jnp.float32,
@@ -96,6 +88,15 @@
         held = jnp.where(low, jnp.concatenate([held, other]), jnp.concatenate([other, held]))
         step *= 2
     scores = held[cand_ids]
+    row_all, scores = lax.optimization_barrier((row_all, scores))
+    contract = (((0,), (0,)), ((), ()))
+    tile = lax.dot_general(
+        row_all, col_all, contract, precision=high, preferred_element_type=jnp.float32
+    )
+    rows_global = row_pos * width_row + lax.broadcasted_iota(jnp.int32, (width_row, width_col), 0)
+    cols_global = col_pos * width_col + lax.broadcasted_iota(jnp.int32, (width_row, width_col), 1)
+    tile = tile + jnp.where(rows_global == cols_global, ridge[None, :], jnp.float32(0.0))
+
     return (tile, scores)
 
 

time: 324 us -> 321 us (level)
    ppermute x7, waiting for transfers between devices: 50.7 us -> 47.1 us  [body(): ahead = lax.ppermute(ahead, 'col', forward)]
  transfers between devices with their start and end apart: 24 -> 24, of which waited for: 16 -> 18; matrix products, arithmetic and copies ran while one was open for 24% -> 13% of each run, Pallas kernels for 0% -> 0%
where the time goes in v13:
time: 321 us; the launch traced here: 320 us
  waiting for transfers between devices  127 us (40%)
  starting transfers between devices  78.7 us (25%)
  matrix products  45.7 us (14%)
  between operations  32.5 us (10%)
  local copies, waits for them, and re-layouts  31.1 us (10%)
  other arithmetic  5.48 us (2%)
    ppermute x7, starting transfers between devices, body(): ahead = lax.ppermute(ahead, 'col', forward)  52.1 us
    ppermute x7, waiting for transfers between devices, body(): ahead = lax.ppermute(ahead, 'col', forward)  47.1 us
    dot_general x1, matrix products, body(): lax.dot_general(row_all, col_all, contract, precision=high, preferred_ele...  33.9 us
    all_gather x1, waiting for transfers between devices, body(): col_all = lax.all_gather(masked, 'row', axis=0, tiled=True)  32.5 us
    ppermute x3, waiting for transfers between devices, body(): packed = packed + lax.ppermute(packed, 'col', pairs)  27.1 us
    ppermute x7, starting transfers between devices, body(): behind = lax.ppermute(behind, 'col', backward)  20.6 us
    ppermute x7, waiting for transfers between devices, body(): behind = lax.ppermute(behind, 'col', backward)  12.6 us
    dot_general x1, matrix products, body(): lax.dot_general(col_all, items, (((1,), (1,)), ((), ())), precision=high,...  11.3 us
  transfers between devices with their start and end apart: 24, of which 18 were waited for; matrix products, arithmetic and copies ran while one was open for 13% of the time, Pallas kernels for 0%

profile of v13, /device:TPU:0, one launch (start us, length us, event | category | flops | bytes accessed | tf_op | source)
XLA Modules:
  0.0 319.9 jit_solution(4999436728826578776)
XLA Ops:
  7.2 1.2 dynamic_slice.54
  9.1 2.3 broadcast_select_fusion
  11.5 2.1 reshape.96
  16.7 4.3 %broadcast_in_dim.46 = f32[2048,1024]{1,0:T(8,128)} broadcast(f32[]{:T(128)} %constant.159.clone.1), dimensions={} | broadcast | bytes 8388612 | tf_op jit(solution)/shard_map/broadcast_in_dim | solution.py:51
  22.0 43.8 %collective-permute-start.2 = (f32[128,1024]{1,0:T(8,128)S(1)}, f32[128,1024]{1,0:T(8,128)S(1)}, u32[]{:S(2)}, u32[]{:S(2)}) collective-permute-start(f32[128,1024]{1,0:T(8,128)S(1)} %get-tuple-element.11), channel_id=1, source_target_pairs={{0,2},{2,4},{4,6},{6,7},{7,5},{5,3},{3,1},{1,0},{8,10},{10,12},{12... | collective-permute-start | bytes 1572872 | tf_op jit(solution)/shard_map/ppermute | solution.py:56
  66.7 8.7 %collective-permute-start.3 = (f32[128,1024]{1,0:T(8,128)S(1)}, f32[128,1024]{1,0:T(8,128)S(1)}, u32[]{:S(2)}, u32[]{:S(2)}) collective-permute-start(f32[128,1024]{1,0:T(8,128)S(1)} %get-tuple-element.9), channel_id=1, source_target_pairs={{0,1},{2,0},{4,2},{6,4},{7,6},{5,7},{3,5},{1,3},{8,9},{10,8},{12,1... | collective-permute-start | bytes 1572872 | tf_op jit(solution)/shard_map/ppermute | solution.py:57
  75.3 21.9 %collective-permute-done.2 = f32[128,1024]{1,0:T(8,128)S(1)} collective-permute-done((f32[128,1024]{1,0:T(8,128)S(1)}, f32[128,1024]{1,0:T(8,128)S(1)}, u32[]{:S(2)}, u32[]{:S(2)}) %collective-permute-start.2) | collective-permute-done | bytes 524320 | tf_op jit(solution)/shard_map/ppermute | solution.py:56
  98.5 4.0 %collective-permute-start.5 = (f32[128,1024]{1,0:T(8,128)S(1)}, f32[128,1024]{1,0:T(8,128)S(1)}, u32[]{:S(2)}, u32[]{:S(2)}) collective-permute-start(f32[128,1024]{1,0:T(8,128)S(1)} %collective-permute-done.3), channel_id=1, source_target_pairs={{0,1},{2,0},{4,2},{6,4},{7,6},{5,7},{3,5},{1,3},{8,9},{10,8},{12,1... | collective-permute-start | bytes 1572872 | tf_op jit(solution)/shard_map/ppermute | solution.py:57
  102.4 21.2 %collective-permute-done.4 = f32[128,1024]{1,0:T(8,128)S(1)} collective-permute-done((f32[128,1024]{1,0:T(8,128)S(1)}, f32[128,1024]{1,0:T(8,128)S(1)}, u32[]{:S(2)}, u32[]{:S(2)}) %collective-permute-start.4) | collective-permute-done | bytes 524320 | tf_op jit(solution)/shard_map/ppermute | solution.py:56
  123.6 1.7 collective-permute-done.5
  125.3 4.0 %collective-permute-start.7 = (f32[128,1024]{1,0:T(8,128)S(1)}, f32[128,1024]{1,0:T(8,128)S(1)}, u32[]{:S(2)}, u32[]{:S(2)}) collective-permute-start(f32[128,1024]{1,0:T(8,128)S(1)} %collective-permute-done.5), channel_id=1, source_target_pairs={{0,1},{2,0},{4,2},{6,4},{7,6},{5,7},{3,5},{1,3},{8,9},{10,8},{12,1... | collective-permute-start | bytes 1572872 | tf_op jit(solution)/shard_map/ppermute | solution.py:57
  149.8 2.0 collective-permute-done.7
  151.8 4.0 %collective-permute-start.9 = (f32[128,1024]{1,0:T(8,128)S(1)}, f32[128,1024]{1,0:T(8,128)}, u32[]{:S(2)}, u32[]{:S(2)}) collective-permute-start(f32[128,1024]{1,0:T(8,128)S(1)} %collective-permute-done.7), channel_id=1, source_target_pairs={{0,1},{2,0},{4,2},{6,4},{7,6},{5,7},{3,5},{1,3},{8,9},{10,8},{12,1... | collective-permute-start | bytes 1572872 | tf_op jit(solution)/shard_map/ppermute | solution.py:57
  155.8 32.5 %all-gather.2.cloned.1.call-done = f32[2048,2048]{1,0:T(8,128)} async-done(((f32[128,2048]{1,0:T(8,128)}), f32[2048,2048]{1,0:T(8,128)}) %all-gather.2.cloned.1.call-update) | async-done | bytes 16777232 | tf_op jit(solution)/shard_map/all_gather | solution.py:23
  188.3 11.3 %fusion.3 = f32[2048,64]{0,1:T(8,128)S(1)} fusion(f32[2048,2048]{1,0:T(8,128)} %all-gather.2.cloned.1.call-done, f32[64,2048]{1,0:T(8,128)S(1)} %copy-done.1), kind=kOutput, calls=%fused_computation.42 | convolution fusion | flops 1610612736 | bytes 17825792 | tf_op jit(solution)/shard_map/dot_general | solution.py:65
  199.8 8.4 %collective-permute-start.10 = (f32[128,1024]{1,0:T(8,128)}, f32[128,1024]{1,0:T(8,128)S(1)}, u32[]{:S(2)}, u32[]{:S(2)}) collective-permute-start(f32[128,1024]{1,0:T(8,128)} %collective-permute-done.8), channel_id=1, source_target_pairs={{0,2},{2,4},{4,6},{6,7},{7,5},{5,3},{3,1},{1,0},{8,10},{10,12},{12... | collective-permute-start | bytes 1572872 | tf_op jit(solution)/shard_map/ppermute | solution.py:56
  208.2 8.5 %collective-permute-done.16 = f32[2050,64]{0,1:T(8,128)S(1)} collective-permute-done((f32[2050,64]{0,1:T(8,128)S(1)}, f32[2050,64]{0,1:T(8,128)S(1)}, u32[]{:S(2)}, u32[]{:S(2)}) %collective-permute-start.16) | collective-permute-done | bytes 524832 | tf_op jit(solution)/shard_map/ppermute | solution.py:75
  216.8 4.8 %collective-permute-start.17 = (f32[2050,64]{0,1:T(8,128)S(1)}, f32[2050,64]{0,1:T(8,128)S(1)}, u32[]{:S(2)}, u32[]{:S(2)}) collective-permute-start(f32[2050,64]{0,1:T(8,128)S(1)} %add.419), channel_id=1, source_target_pairs={{0,2},{1,3},{2,0},{3,1},{4,6},{5,7},{6,4},{7,5},{8,10},{9,11},{10,... | collective-permute-start | bytes 1574408 | tf_op jit(solution)/shard_map/ppermute | solution.py:75
  223.3 1.9 constant_dynamic-update-slice_fusion.11
  225.2 1.9 constant_dynamic-update-slice_fusion.10
  227.1 1.9 constant_dynamic-update-slice_fusion.9
  229.0 3.7 %collective-permute-done.11 = f32[128,1024]{1,0:T(8,128)S(1)} collective-permute-done((f32[128,1024]{1,0:T(8,128)}, f32[128,1024]{1,0:T(8,128)S(1)}, u32[]{:S(2)}, u32[]{:S(2)}) %collective-permute-start.11) | collective-permute-done | bytes 524320 | tf_op jit(solution)/shard_map/ppermute | solution.py:57
  232.7 11.9 %collective-permute-done.17 = f32[2050,64]{0,1:T(8,128)S(1)} collective-permute-done((f32[2050,64]{0,1:T(8,128)S(1)}, f32[2050,64]{0,1:T(8,128)S(1)}, u32[]{:S(2)}, u32[]{:S(2)}) %collective-permute-start.17) | collective-permute-done | bytes 524832 | tf_op jit(solution)/shard_map/ppermute | solution.py:75
  245.7 1.9 constant_dynamic-update-slice_fusion.7
  247.6 1.9 constant_dynamic-update-slice_fusion.6
  251.2 4.0 %collective-permute-done.13 = f32[128,1024]{1,0:T(8,128)S(1)} collective-permute-done((f32[128,1024]{1,0:T(8,128)S(1)}, f32[128,1024]{1,0:T(8,128)S(1)}, u32[]{:S(2)}, u32[]{:S(2)}) %collective-permute-start.13) | collective-permute-done | bytes 524320 | tf_op jit(solution)/shard_map/ppermute | solution.py:57
  255.2 6.6 %collective-permute-done.18 = f32[2050,64]{0,1:T(8,128)S(1)} collective-permute-done((f32[2050,64]{0,1:T(8,128)S(1)}, f32[2050,64]{0,1:T(8,128)S(1)}, u32[]{:S(2)}, u32[]{:S(2)}) %collective-permute-start.18) | collective-permute-done | bytes 524832 | tf_op jit(solution)/shard_map/ppermute | solution.py:75
  264.4 2.7 collective-permute-done.20
  267.1 3.7 %collective-permute-done.14 = f32[128,1024]{1,0:T(8,128)S(1)} collective-permute-done((f32[128,1024]{1,0:T(8,128)S(1)}, f32[128,1024]{1,0:T(8,128)S(1)}, u32[]{:S(2)}, u32[]{:S(2)}) %collective-permute-start.14) | collective-permute-done | bytes 524320 | tf_op jit(solution)/shard_map/ppermute | solution.py:56
  273.1 2.7 collective-permute-done.22
  275.8 3.4 %gather_fusion = f32[512]{0:T(512)} fusion(f32[1024]{0:T(1024)S(1)} %maximum_select_fusion, s32[1024]{0:T(1024)S(1)} %pad_clamp_fusion), kind=kCustom, calls=%fused_computation | custom fusion | bytes 6144 | tf_op jit(solution)/shard_map/gather | solution.py:90
  279.2 33.9 %select_add_fusion = f32[1024,2048]{1,0:T(8,128)} fusion(f32[2048]{0:T(1024)S(1)} %copy-done.5, s32[2048]{0:T(1024)S(1)} %iota_add_fusion, s32[1024]{0:T(1024)S(1)} %iota_add_fusion.1, f32[2048,1024]{1,0:T(8,128)} %constant_dynamic-update-slice_fusion, f32[2048,2048]{1,0:T(8,128)} %all-gather.2.cloned.1.call-done), kind=kOutput, calls=%fused_computation.1 | convolution fusion | flops 25776095232 | bytes 33574912 | tf_op jit(solution)/shard_map/dot_general | solution.py:93
  (80 shorter events, 18.5 us)
Async XLA Ops:
  7.2 141.8 %copy-start = (f32[2048]{0:T(1024)S(1)}, f32[2048]{0:T(1024)}, u32[]{:S(2)}) copy-start(f32[2048]{0:T(1024)} %param.13) | copy-start | bytes 24580
  7.2 181.2 %all-gather.2.cloned.1.call-start = ((), (), s32[]{:S(2)}) async-start(), calls=%async_computation | async-start | bytes 17825792 | tf_op jit(solution)/shard_map/all_gather | solution.py:23
  13.6 115.7 %copy-start.7 = (s32[8]{0:T(128)S(1)}, s32[8]{0:T(128)}, u32[]{:S(2)}) copy-start(s32[8]{0:T(128)} %constant.194.clone) | copy-start | bytes 100
  13.6 125.6 %copy-start.4 = (s32[8]{0:T(128)S(1)}, s32[8]{0:T(128)}, u32[]{:S(2)}) copy-start(s32[8]{0:T(128)} %constant.193.clone) | copy-start | bytes 100
  13.7 135.0 %copy-start.1 = (f32[64,2048]{1,0:T(8,128)S(1)}, f32[64,2048]{1,0:T(8,128)}, u32[]{:S(2)}) copy-start(f32[64,2048]{1,0:T(8,128)} %param.11) | copy-start | bytes 1572868
  13.7 135.0 %copy-start.5 = (f32[2048]{0:T(1024)S(1)}, f32[2048]{0:T(1024)}, u32[]{:S(2)}) copy-start(f32[2048]{0:T(1024)} %param.10) | copy-start | bytes 24580
  14.7 2.0 collective-permute-start.1
  14.9 1.8 collective-permute-start
  22.0 75.3 %collective-permute-start.2 = (f32[128,1024]{1,0:T(8,128)S(1)}, f32[128,1024]{1,0:T(8,128)S(1)}, u32[]{:S(2)}, u32[]{:S(2)}) collective-permute-start(f32[128,1024]{1,0:T(8,128)S(1)} %get-tuple-element.11), channel_id=1, source_target_pairs={{0,2},{2,4},{4,6},{6,7},{7,5},{5,3},{3,1},{1,0},{8,10},{10,12},{12... | collective-permute-start | bytes 1572872 | tf_op jit(solution)/shard_map/ppermute | solution.py:56
  66.7 31.8 %collective-permute-start.3 = (f32[128,1024]{1,0:T(8,128)S(1)}, f32[128,1024]{1,0:T(8,128)S(1)}, u32[]{:S(2)}, u32[]{:S(2)}) collective-permute-start(f32[128,1024]{1,0:T(8,128)S(1)} %get-tuple-element.9), channel_id=1, source_target_pairs={{0,1},{2,0},{4,2},{6,4},{7,6},{5,7},{3,5},{1,3},{8,9},{10,8},{12,1... | collective-permute-start | bytes 1572872 | tf_op jit(solution)/shard_map/ppermute | solution.py:57
  97.3 26.4 %collective-permute-start.4 = (f32[128,1024]{1,0:T(8,128)S(1)}, f32[128,1024]{1,0:T(8,128)S(1)}, u32[]{:S(2)}, u32[]{:S(2)}) collective-permute-start(f32[128,1024]{1,0:T(8,128)S(1)} %collective-permute-done.2), channel_id=1, source_target_pairs={{0,2},{2,4},{4,6},{6,7},{7,5},{5,3},{3,1},{1,0},{8,10},{10,12},{12... | collective-permute-start | bytes 1572872 | tf_op jit(solution)/shard_map/ppermute | solution.py:56
  98.5 26.8 %collective-permute-start.5 = (f32[128,1024]{1,0:T(8,128)S(1)}, f32[128,1024]{1,0:T(8,128)S(1)}, u32[]{:S(2)}, u32[]{:S(2)}) collective-permute-start(f32[128,1024]{1,0:T(8,128)S(1)} %collective-permute-done.3), channel_id=1, source_target_pairs={{0,1},{2,0},{4,2},{6,4},{7,6},{5,7},{3,5},{1,3},{8,9},{10,8},{12,1... | collective-permute-start | bytes 1572872 | tf_op jit(solution)/shard_map/ppermute | solution.py:57
  123.6 64.7 %copy-start.2 = (f32[128,1024]{1,0:T(8,128)}, f32[128,1024]{1,0:T(8,128)S(1)}, u32[]{:S(2)}) copy-start(f32[128,1024]{1,0:T(8,128)S(1)} %collective-permute-done.4) | copy-start | bytes 1572868
  123.6 26.2 %collective-permute-start.6 = (f32[128,1024]{1,0:T(8,128)S(1)}, f32[128,1024]{1,0:T(8,128)}, u32[]{:S(2)}, u32[]{:S(2)}) collective-permute-start(f32[128,1024]{1,0:T(8,128)S(1)} %collective-permute-done.4), channel_id=1, source_target_pairs={{0,2},{2,4},{4,6},{6,7},{7,5},{5,3},{3,1},{1,0},{8,10},{10,12},{12... | collective-permute-start | bytes 1572872 | tf_op jit(solution)/shard_map/ppermute | solution.py:56
  125.3 30.5 %copy-start.3 = (f32[128,1024]{1,0:T(8,128)}, f32[128,1024]{1,0:T(8,128)S(1)}, u32[]{:S(2)}) copy-start(f32[128,1024]{1,0:T(8,128)S(1)} %collective-permute-done.5) | copy-start | bytes 1572868
  125.3 26.5 %collective-permute-start.7 = (f32[128,1024]{1,0:T(8,128)S(1)}, f32[128,1024]{1,0:T(8,128)S(1)}, u32[]{:S(2)}, u32[]{:S(2)}) collective-permute-start(f32[128,1024]{1,0:T(8,128)S(1)} %collective-permute-done.5), channel_id=1, source_target_pairs={{0,1},{2,0},{4,2},{6,4},{7,6},{5,7},{3,5},{1,3},{8,9},{10,8},{12,1... | collective-permute-start | bytes 1572872 | tf_op jit(solution)/shard_map/ppermute | solution.py:57
  149.5 50.2 %copy-start.6 = (s32[512]{0:T(512)S(1)}, s32[512]{0:T(512)}, u32[]{:S(2)}) copy-start(s32[512]{0:T(512)} %param.12) | copy-start | bytes 6148
  149.8 50.0 %collective-permute-start.8 = (f32[128,1024]{1,0:T(8,128)}, f32[128,1024]{1,0:T(8,128)}, u32[]{:S(2)}, u32[]{:S(2)}) collective-permute-start(f32[128,1024]{1,0:T(8,128)} %collective-permute-done.6), channel_id=1, source_target_pairs={{0,2},{2,4},{4,6},{6,7},{7,5},{5,3},{3,1},{1,0},{8,10},{10,12},{12... | collective-permute-start | bytes 1572872 | tf_op jit(solution)/shard_map/ppermute | solution.py:56
  151.8 56.4 %collective-permute-start.9 = (f32[128,1024]{1,0:T(8,128)S(1)}, f32[128,1024]{1,0:T(8,128)}, u32[]{:S(2)}, u32[]{:S(2)}) collective-permute-start(f32[128,1024]{1,0:T(8,128)S(1)} %collective-permute-done.7), channel_id=1, source_target_pairs={{0,1},{2,0},{4,2},{6,4},{7,6},{5,7},{3,5},{1,3},{8,9},{10,8},{12,1... | collective-permute-start | bytes 1572872 | tf_op jit(solution)/shard_map/ppermute | solution.py:57
  199.7 17.0 %collective-permute-start.16 = (f32[2050,64]{0,1:T(8,128)S(1)}, f32[2050,64]{0,1:T(8,128)S(1)}, u32[]{:S(2)}, u32[]{:S(2)}) collective-permute-start(f32[2050,64]{0,1:T(8,128)S(1)} %concatenate.27), channel_id=1, source_target_pairs={{0,4},{1,5},{2,6},{3,7},{4,0},{5,1},{6,2},{7,3},{8,12},{9,13},{10,... | collective-permute-start | bytes 1574408 | tf_op jit(solution)/shard_map/ppermute | solution.py:75
  199.8 29.2 %collective-permute-start.10 = (f32[128,1024]{1,0:T(8,128)}, f32[128,1024]{1,0:T(8,128)S(1)}, u32[]{:S(2)}, u32[]{:S(2)}) collective-permute-start(f32[128,1024]{1,0:T(8,128)} %collective-permute-done.8), channel_id=1, source_target_pairs={{0,2},{2,4},{4,6},{6,7},{7,5},{5,3},{3,1},{1,0},{8,10},{10,12},{12... | collective-permute-start | bytes 1572872 | tf_op jit(solution)/shard_map/ppermute | solution.py:56
  208.2 24.5 %collective-permute-start.11 = (f32[128,1024]{1,0:T(8,128)}, f32[128,1024]{1,0:T(8,128)S(1)}, u32[]{:S(2)}, u32[]{:S(2)}) collective-permute-start(f32[128,1024]{1,0:T(8,128)} %collective-permute-done.9), channel_id=1, source_target_pairs={{0,1},{2,0},{4,2},{6,4},{7,6},{5,7},{3,5},{1,3},{8,9},{10,8},{12,1... | collective-permute-start | bytes 1572872 | tf_op jit(solution)/shard_map/ppermute | solution.py:57
  216.8 27.9 %collective-permute-start.17 = (f32[2050,64]{0,1:T(8,128)S(1)}, f32[2050,64]{0,1:T(8,128)S(1)}, u32[]{:S(2)}, u32[]{:S(2)}) collective-permute-start(f32[2050,64]{0,1:T(8,128)S(1)} %add.419), channel_id=1, source_target_pairs={{0,2},{1,3},{2,0},{3,1},{4,6},{5,7},{6,4},{7,5},{8,10},{9,11},{10,... | collective-permute-start | bytes 1574408 | tf_op jit(solution)/shard_map/ppermute | solution.py:75
  229.0 22.2 %collective-permute-start.12 = (f32[128,1024]{1,0:T(8,128)S(1)}, f32[128,1024]{1,0:T(8,128)S(1)}, u32[]{:S(2)}, u32[]{:S(2)}) collective-permute-start(f32[128,1024]{1,0:T(8,128)S(1)} %collective-permute-done.10), channel_id=1, source_target_pairs={{0,2},{2,4},{4,6},{6,7},{7,5},{5,3},{3,1},{1,0},{8,10},{10,12},{12... | collective-permute-start | bytes 1572872 | tf_op jit(solution)/shard_map/ppermute | solution.py:56
  232.7 22.5 %collective-permute-start.13 = (f32[128,1024]{1,0:T(8,128)S(1)}, f32[128,1024]{1,0:T(8,128)S(1)}, u32[]{:S(2)}, u32[]{:S(2)}) collective-permute-start(f32[128,1024]{1,0:T(8,128)S(1)} %collective-permute-done.11), channel_id=1, source_target_pairs={{0,1},{2,0},{4,2},{6,4},{7,6},{5,7},{3,5},{1,3},{8,9},{10,8},{12,1... | collective-permute-start | bytes 1572872 | tf_op jit(solution)/shard_map/ppermute | solution.py:57
  244.7 17.1 %collective-permute-start.18 = (f32[2050,64]{0,1:T(8,128)S(1)}, f32[2050,64]{0,1:T(8,128)S(1)}, u32[]{:S(2)}, u32[]{:S(2)}) collective-permute-start(f32[2050,64]{0,1:T(8,128)S(1)} %add.420), channel_id=1, source_target_pairs={{0,1},{1,0},{2,3},{3,2},{4,5},{5,4},{6,7},{7,6},{8,9},{9,8},{10,11... | collective-permute-start | bytes 1574408 | tf_op jit(solution)/shard_map/ppermute | solution.py:75
  251.2 19.7 %collective-permute-start.14 = (f32[128,1024]{1,0:T(8,128)S(1)}, f32[128,1024]{1,0:T(8,128)S(1)}, u32[]{:S(2)}, u32[]{:S(2)}) collective-permute-start(f32[128,1024]{1,0:T(8,128)S(1)} %collective-permute-done.12), channel_id=1, source_target_pairs={{0,2},{2,4},{4,6},{6,7},{7,5},{5,3},{3,1},{1,0},{8,10},{10,12},{12... | collective-permute-start | bytes 1572872 | tf_op jit(solution)/shard_map/ppermute | solution.py:56
  255.2 17.0 %collective-permute-start.15 = (f32[128,1024]{1,0:T(8,128)S(1)}, f32[128,1024]{1,0:T(8,128)S(1)}, u32[]{:S(2)}, u32[]{:S(2)}) collective-permute-start(f32[128,1024]{1,0:T(8,128)S(1)} %collective-permute-done.13), channel_id=1, source_target_pairs={{0,1},{2,0},{4,2},{6,4},{7,6},{5,7},{3,5},{1,3},{8,9},{10,8},{12,1... | collective-permute-start | bytes 1572872 | tf_op jit(solution)/shard_map/ppermute | solution.py:57
  262.3 1.2 collective-permute-start.19
  263.5 3.6 %collective-permute-start.20 = (f32[128]{0:T(128)S(1)}, f32[128]{0:T(128)S(1)}, u32[]{:S(2)}, u32[]{:S(2)}) collective-permute-start(f32[128]{0:T(128)S(1)} %broadcast_select_fusion.1), channel_id=1, source_target_pairs={{0,16},{8,24},{16,0},{24,8},{32,48},{40,56},{48,32},{56,40},{64,80... | collective-permute-start | bytes 1544 | tf_op jit(solution)/shard_map/ppermute | solution.py:86
  267.1 5.1 %collective-permute-start.21 = (f32[256]{0:T(256)S(1)}, f32[256]{0:T(256)S(1)}, u32[]{:S(2)}, u32[]{:S(2)}) collective-permute-start(f32[256]{0:T(256)S(1)} %maximum_select_fusion.2), channel_id=1, source_target_pairs={{0,32},{8,40},{16,48},{24,56},{32,0},{40,8},{48,16},{56,24},{64,96... | collective-permute-start | bytes 3080 | tf_op jit(solution)/shard_map/ppermute | solution.py:86
  272.2 3.6 %collective-permute-start.22 = (f32[512]{0:T(512)S(1)}, f32[512]{0:T(512)S(1)}, u32[]{:S(2)}, u32[]{:S(2)}) collective-permute-start(f32[512]{0:T(512)S(1)} %maximum_select_fusion.1), channel_id=1, source_target_pairs={{0,64},{8,72},{16,80},{24,88},{32,96},{40,104},{48,112},{56,120},{... | collective-permute-start | bytes 6152 | tf_op jit(solution)/shard_map/ppermute | solution.py:86
Sparse Core Ops, SparseCore 0:
  11.6 176.6 all-gather.1

commit v14 on v13

--- a/solution.py
+++ b/solution.py
@@ -20,7 +20,6 @@
     slot = lax.iota(jnp.int32, ev_slots)
     masked = jnp.where((slot < event_counts[row_pos])[:, None], shared_rows, jnp.float32(0.0))
 
-    col_all = lax.all_gather(masked, "row", axis=0, tiled=True)
 
     halves = masked.reshape(ev_slots, ratio, width_row)
     received = []
@@ -55,6 +54,9 @@
     for k in range(1, n_col):
         ahead = lax.ppermute(ahead, "col", forward)
         behind = lax.ppermute(behind, "col", backward)
+        if k == 1:
+            gather_from, ahead, behind = lax.optimization_barrier((masked, ahead, behind))
+            col_all = lax.all_gather(gather_from, "row", axis=0, tiled=True)
         from_ahead = ring_tab[(me - k) % n_col]
         from_behind = ring_tab[(me + k) % n_col]
         row_all = lax.dynamic_update_slice_in_dim(row_all, ahead, from_ahead * block_rows, 0)

time: 321 us -> 332 us (1.034)
  waiting for transfers between devices: 127 us -> 152 us
  starting transfers between devices: 78.7 us -> 64.7 us
    all_gather x1, waiting for transfers between devices: 32.5 us -> 71.6 us  [body(): col_all = lax.all_gather(gather_from, 'row', axis=0, tiled=True)]
    ppermute x7, starting transfers between devices: 52.1 us -> 35.6 us  [body(): ahead = lax.ppermute(ahead, 'col', forward)]
    ppermute x7, waiting for transfers between devices: 47.1 us -> 37.6 us  [body(): ahead = lax.ppermute(ahead, 'col', forward)]
    ppermute x3, waiting for transfers between devices: 27.1 us -> 22.8 us  [body(): packed = packed + lax.ppermute(packed, 'col', pairs)]
  transfers between devices with their start and end apart: 24 -> 24, of which waited for: 18 -> 15; matrix products, arithmetic and copies ran while one was open for 13% -> 10% of each run, Pallas kernels for 0% -> 0%
where the time goes in v14:
time: 332 us; the launch traced here: 331 us
  waiting for transfers between devices  152 us (46%)
  starting transfers between devices  64.7 us (19%)
  matrix products  45.7 us (14%)
  between operations  32.5 us (10%)
  local copies, waits for them, and re-layouts  31.8 us (10%)
  other arithmetic  4.48 us (1%)
    all_gather x1, waiting for transfers between devices, body(): col_all = lax.all_gather(gather_from, 'row', axis=0, tiled=True)  71.6 us
    ppermute x7, waiting for transfers between devices, body(): ahead = lax.ppermute(ahead, 'col', forward)  37.6 us
    ppermute x7, starting transfers between devices, body(): ahead = lax.ppermute(ahead, 'col', forward)  35.6 us
    dot_general x1, matrix products, body(): lax.dot_general(row_all, col_all, contract, precision=high, preferred_ele...  33.9 us
    ppermute x3, waiting for transfers between devices, body(): packed = packed + lax.ppermute(packed, 'col', pairs)  22.8 us
    ppermute x7, starting transfers between devices, body(): behind = lax.ppermute(behind, 'col', backward)  22.5 us
    ppermute x7, waiting for transfers between devices, body(): behind = lax.ppermute(behind, 'col', backward)  14.8 us
    dot_general x1, matrix products, body(): lax.dot_general(col_all, items, (((1,), (1,)), ((), ())), precision=high,...  11.3 us
  transfers between devices with their start and end apart: 24, of which 15 were waited for; matrix products, arithmetic and copies ran while one was open for 10% of the time, Pallas kernels for 0%

profile of v14, /device:TPU:0, one launch (start us, length us, event | category | flops | bytes accessed | tf_op | source)
XLA Modules:
  0.0 331.5 jit_solution(18405840652189624005)
XLA Ops:
  13.5 1.7 collective-permute-start
  15.2 4.3 %broadcast_in_dim.46 = f32[2048,1024]{1,0:T(8,128)} broadcast(f32[]{:T(128)} %constant.159.clone.1), dimensions={} | broadcast | bytes 8388612 | tf_op jit(solution)/shard_map/broadcast_in_dim | solution.py:50
  20.5 27.0 %collective-permute-start.2 = (f32[128,1024]{1,0:T(8,128)S(1)}, f32[128,1024]{1,0:T(8,128)S(1)}, u32[]{:S(2)}, u32[]{:S(2)}) collective-permute-start(f32[128,1024]{1,0:T(8,128)S(1)} %get-tuple-element.17), channel_id=1, source_target_pairs={{0,2},{2,4},{4,6},{6,7},{7,5},{5,3},{3,1},{1,0},{8,10},{10,12},{12... | collective-permute-start | bytes 1572872 | tf_op jit(solution)/shard_map/ppermute | solution.py:55
  48.4 4.8 %collective-permute-start.3 = (f32[128,1024]{1,0:T(8,128)S(1)}, f32[128,1024]{1,0:T(8,128)S(1)}, u32[]{:S(2)}, u32[]{:S(2)}) collective-permute-start(f32[128,1024]{1,0:T(8,128)S(1)} %get-tuple-element.15), channel_id=1, source_target_pairs={{0,1},{2,0},{4,2},{6,4},{7,6},{5,7},{3,5},{1,3},{8,9},{10,8},{12,1... | collective-permute-start | bytes 1572872 | tf_op jit(solution)/shard_map/ppermute | solution.py:56
  53.2 21.4 %collective-permute-done.2 = f32[128,1024]{1,0:T(8,128)S(1)} collective-permute-done((f32[128,1024]{1,0:T(8,128)S(1)}, f32[128,1024]{1,0:T(8,128)S(1)}, u32[]{:S(2)}, u32[]{:S(2)}) %collective-permute-start.2) | collective-permute-done | bytes 524320 | tf_op jit(solution)/shard_map/ppermute | solution.py:55
  74.6 10.1 %collective-permute-done.3 = f32[128,1024]{1,0:T(8,128)S(1)} collective-permute-done((f32[128,1024]{1,0:T(8,128)S(1)}, f32[128,1024]{1,0:T(8,128)S(1)}, u32[]{:S(2)}, u32[]{:S(2)}) %collective-permute-start.3) | collective-permute-done | bytes 524320 | tf_op jit(solution)/shard_map/ppermute | solution.py:56
  84.7 1.8 collective-permute-start.4
  86.5 1.8 collective-permute-start.5
  88.3 11.0 %collective-permute-done.4 = f32[128,1024]{1,0:T(8,128)S(1)} collective-permute-done((f32[128,1024]{1,0:T(8,128)S(1)}, f32[128,1024]{1,0:T(8,128)S(1)}, u32[]{:S(2)}, u32[]{:S(2)}) %collective-permute-start.4) | collective-permute-done | bytes 524320 | tf_op jit(solution)/shard_map/ppermute | solution.py:55
  100.4 2.1 collective-permute-done.5
  102.5 4.0 %collective-permute-start.7 = (f32[128,1024]{1,0:T(8,128)S(1)}, f32[128,1024]{1,0:T(8,128)S(1)}, u32[]{:S(2)}, u32[]{:S(2)}) collective-permute-start(f32[128,1024]{1,0:T(8,128)S(1)} %collective-permute-done.5), channel_id=1, source_target_pairs={{0,1},{2,0},{4,2},{6,4},{7,6},{5,7},{3,5},{1,3},{8,9},{10,8},{12,1... | collective-permute-start | bytes 1572872 | tf_op jit(solution)/shard_map/ppermute | solution.py:56
  128.4 4.0 %collective-permute-start.9 = (f32[128,1024]{1,0:T(8,128)S(1)}, f32[128,1024]{1,0:T(8,128)}, u32[]{:S(2)}, u32[]{:S(2)}) collective-permute-start(f32[128,1024]{1,0:T(8,128)S(1)} %collective-permute-done.7), channel_id=1, source_target_pairs={{0,1},{2,0},{4,2},{6,4},{7,6},{5,7},{3,5},{1,3},{8,9},{10,8},{12,1... | collective-permute-start | bytes 1572872 | tf_op jit(solution)/shard_map/ppermute | solution.py:56
  132.4 71.6 %all-gather.2.cloned.1.call-done = f32[2048,2048]{1,0:T(8,128)} async-done(((f32[128,2048]{1,0:T(8,128)}), f32[2048,2048]{1,0:T(8,128)}) %all-gather.2.cloned.1.call-update) | async-done | bytes 16777232 | tf_op jit(solution)/shard_map/all_gather | solution.py:59
  204.0 11.3 %fusion.3 = f32[2048,64]{0,1:T(8,128)S(1)} fusion(f32[2048,2048]{1,0:T(8,128)} %all-gather.2.cloned.1.call-done, f32[64,2048]{1,0:T(8,128)S(1)} %copy-done.2), kind=kOutput, calls=%fused_computation.42 | convolution fusion | flops 1610612736 | bytes 17825792 | tf_op jit(solution)/shard_map/dot_general | solution.py:67
  215.5 4.0 %collective-permute-start.10 = (f32[128,1024]{1,0:T(8,128)}, f32[128,1024]{1,0:T(8,128)S(1)}, u32[]{:S(2)}, u32[]{:S(2)}) collective-permute-start(f32[128,1024]{1,0:T(8,128)} %collective-permute-done.8), channel_id=1, source_target_pairs={{0,2},{2,4},{4,6},{6,7},{7,5},{5,3},{3,1},{1,0},{8,10},{10,12},{12... | collective-permute-start | bytes 1572872 | tf_op jit(solution)/shard_map/ppermute | solution.py:55
  219.5 12.9 %collective-permute-done.16 = f32[2050,64]{0,1:T(8,128)S(1)} collective-permute-done((f32[2050,64]{0,1:T(8,128)S(1)}, f32[2050,64]{0,1:T(8,128)S(1)}, u32[]{:S(2)}, u32[]{:S(2)}) %collective-permute-start.16) | collective-permute-done | bytes 524832 | tf_op jit(solution)/shard_map/ppermute | solution.py:77
  233.8 1.9 constant_dynamic-update-slice_fusion.12
  235.7 1.9 constant_dynamic-update-slice_fusion.11
  237.6 1.9 constant_dynamic-update-slice_fusion.10
  239.5 1.9 constant_dynamic-update-slice_fusion.9
  244.0 3.9 %collective-permute-start.13 = (f32[128,1024]{1,0:T(8,128)S(1)}, f32[128,1024]{1,0:T(8,128)S(1)}, u32[]{:S(2)}, u32[]{:S(2)}) collective-permute-start(f32[128,1024]{1,0:T(8,128)S(1)} %collective-permute-done.11), channel_id=1, source_target_pairs={{0,1},{2,0},{4,2},{6,4},{7,6},{5,7},{3,5},{1,3},{8,9},{10,8},{12,1... | collective-permute-start | bytes 1572872 | tf_op jit(solution)/shard_map/ppermute | solution.py:56
  247.9 8.0 %collective-permute-done.17 = f32[2050,64]{0,1:T(8,128)S(1)} collective-permute-done((f32[2050,64]{0,1:T(8,128)S(1)}, f32[2050,64]{0,1:T(8,128)S(1)}, u32[]{:S(2)}, u32[]{:S(2)}) %collective-permute-start.17) | collective-permute-done | bytes 524832 | tf_op jit(solution)/shard_map/ppermute | solution.py:77
  256.0 4.0 %collective-permute-start.18 = (f32[2050,64]{0,1:T(8,128)S(1)}, f32[2050,64]{0,1:T(8,128)S(1)}, u32[]{:S(2)}, u32[]{:S(2)}) collective-permute-start(f32[2050,64]{0,1:T(8,128)S(1)} %add.420), channel_id=1, source_target_pairs={{0,1},{1,0},{2,3},{3,2},{4,5},{5,4},{6,7},{7,6},{8,9},{9,8},{10,11... | collective-permute-start | bytes 1574408 | tf_op jit(solution)/shard_map/ppermute | solution.py:77
  260.9 1.9 constant_dynamic-update-slice_fusion.7
  262.8 1.9 constant_dynamic-update-slice_fusion.6
  266.5 3.9 %collective-permute-start.15 = (f32[128,1024]{1,0:T(8,128)S(1)}, f32[128,1024]{1,0:T(8,128)S(1)}, u32[]{:S(2)}, u32[]{:S(2)}) collective-permute-start(f32[128,1024]{1,0:T(8,128)S(1)} %collective-permute-done.13), channel_id=1, source_target_pairs={{0,1},{2,0},{4,2},{6,4},{7,6},{5,7},{3,5},{1,3},{8,9},{10,8},{12,1... | collective-permute-start | bytes 1572872 | tf_op jit(solution)/shard_map/ppermute | solution.py:56
  270.5 1.9 collective-permute-done.18
  274.9 2.7 collective-permute-done.20
  277.6 5.2 %collective-permute-done.14 = f32[128,1024]{1,0:T(8,128)S(1)} collective-permute-done((f32[128,1024]{1,0:T(8,128)S(1)}, f32[128,1024]{1,0:T(8,128)S(1)}, u32[]{:S(2)}, u32[]{:S(2)}) %collective-permute-start.14) | collective-permute-done | bytes 524320 | tf_op jit(solution)/shard_map/ppermute | solution.py:55
  284.6 2.7 collective-permute-done.22
  287.4 3.4 %gather_fusion = f32[512]{0:T(512)} fusion(f32[1024]{0:T(1024)S(1)} %maximum_select_fusion, s32[1024]{0:T(1024)S(1)} %pad_clamp_fusion), kind=kCustom, calls=%fused_computation | custom fusion | bytes 6144 | tf_op jit(solution)/shard_map/gather | solution.py:92
  290.8 33.9 %select_add_fusion = f32[1024,2048]{1,0:T(8,128)} fusion(f32[2048]{0:T(1024)S(1)} %copy-done.7, s32[2048]{0:T(1024)S(1)} %iota_add_fusion, s32[1024]{0:T(1024)S(1)} %iota_add_fusion.1, f32[2048,1024]{1,0:T(8,128)} %constant_dynamic-update-slice_fusion, f32[2048,2048]{1,0:T(8,128)} %all-gather.2.cloned.1.call-done), kind=kOutput, calls=%fused_computation.1 | convolution fusion | flops 25776095232 | bytes 33574912 | tf_op jit(solution)/shard_map/dot_general | solution.py:95
  (84 shorter events, 24.2 us)
Async XLA Ops:
  7.2 119.1 %copy-start = (f32[2048]{0:T(1024)S(1)}, f32[2048]{0:T(1024)}, u32[]{:S(2)}) copy-start(f32[2048]{0:T(1024)} %param.13) | copy-start | bytes 24580
  7.2 196.8 %all-gather.2.cloned.1.call-start = ((), (), s32[]{:S(2)}) async-start(), calls=%async_computation | async-start | bytes 17825792 | tf_op jit(solution)/shard_map/all_gather | solution.py:59
  12.3 94.2 %copy-start.9 = (s32[8]{0:T(128)S(1)}, s32[8]{0:T(128)}, u32[]{:S(2)}) copy-start(s32[8]{0:T(128)} %constant.194.clone) | copy-start | bytes 100
  12.4 104.1 %copy-start.6 = (s32[8]{0:T(128)S(1)}, s32[8]{0:T(128)}, u32[]{:S(2)}) copy-start(s32[8]{0:T(128)} %constant.193.clone) | copy-start | bytes 100
  12.4 113.6 %copy-start.2 = (f32[64,2048]{1,0:T(8,128)S(1)}, f32[64,2048]{1,0:T(8,128)}, u32[]{:S(2)}) copy-start(f32[64,2048]{1,0:T(8,128)} %param.11) | copy-start | bytes 1572868
  12.4 113.6 %copy-start.7 = (f32[2048]{0:T(1024)S(1)}, f32[2048]{0:T(1024)}, u32[]{:S(2)}) copy-start(f32[2048]{0:T(1024)} %param.10) | copy-start | bytes 24580
  12.5 2.7 collective-permute-start.1
  13.5 1.7 collective-permute-start
  20.5 54.2 %collective-permute-start.2 = (f32[128,1024]{1,0:T(8,128)S(1)}, f32[128,1024]{1,0:T(8,128)S(1)}, u32[]{:S(2)}, u32[]{:S(2)}) collective-permute-start(f32[128,1024]{1,0:T(8,128)S(1)} %get-tuple-element.17), channel_id=1, source_target_pairs={{0,2},{2,4},{4,6},{6,7},{7,5},{5,3},{3,1},{1,0},{8,10},{10,12},{12... | collective-permute-start | bytes 1572872 | tf_op jit(solution)/shard_map/ppermute | solution.py:55
  48.4 36.3 %collective-permute-start.3 = (f32[128,1024]{1,0:T(8,128)S(1)}, f32[128,1024]{1,0:T(8,128)S(1)}, u32[]{:S(2)}, u32[]{:S(2)}) collective-permute-start(f32[128,1024]{1,0:T(8,128)S(1)} %get-tuple-element.15), channel_id=1, source_target_pairs={{0,1},{2,0},{4,2},{6,4},{7,6},{5,7},{3,5},{1,3},{8,9},{10,8},{12,1... | collective-permute-start | bytes 1572872 | tf_op jit(solution)/shard_map/ppermute | solution.py:56
  84.7 119.3 %copy-start.3 = (f32[128,1024]{1,0:T(8,128)}, f32[128,1024]{1,0:T(8,128)S(1)}, u32[]{:S(2)}) copy-start(f32[128,1024]{1,0:T(8,128)S(1)} %collective-permute-done.3) | copy-start | bytes 1572868
  84.7 14.6 %collective-permute-start.4 = (f32[128,1024]{1,0:T(8,128)S(1)}, f32[128,1024]{1,0:T(8,128)S(1)}, u32[]{:S(2)}, u32[]{:S(2)}) collective-permute-start(f32[128,1024]{1,0:T(8,128)S(1)} %collective-permute-done.2), channel_id=1, source_target_pairs={{0,2},{2,4},{4,6},{6,7},{7,5},{5,3},{3,1},{1,0},{8,10},{10,12},{12... | collective-permute-start | bytes 1572872 | tf_op jit(solution)/shard_map/ppermute | solution.py:55
  86.5 16.0 %collective-permute-start.5 = (f32[128,1024]{1,0:T(8,128)S(1)}, f32[128,1024]{1,0:T(8,128)S(1)}, u32[]{:S(2)}, u32[]{:S(2)}) collective-permute-start(f32[128,1024]{1,0:T(8,128)S(1)} %collective-permute-done.3), channel_id=1, source_target_pairs={{0,1},{2,0},{4,2},{6,4},{7,6},{5,7},{3,5},{1,3},{8,9},{10,8},{12,1... | collective-permute-start | bytes 1572872 | tf_op jit(solution)/shard_map/ppermute | solution.py:56
  99.3 104.7 %copy-start.4 = (f32[128,1024]{1,0:T(8,128)}, f32[128,1024]{1,0:T(8,128)S(1)}, u32[]{:S(2)}) copy-start(f32[128,1024]{1,0:T(8,128)S(1)} %collective-permute-done.4) | copy-start | bytes 1572868
  99.3 27.5 %collective-permute-start.6 = (f32[128,1024]{1,0:T(8,128)S(1)}, f32[128,1024]{1,0:T(8,128)}, u32[]{:S(2)}, u32[]{:S(2)}) collective-permute-start(f32[128,1024]{1,0:T(8,128)S(1)} %collective-permute-done.4), channel_id=1, source_target_pairs={{0,2},{2,4},{4,6},{6,7},{7,5},{5,3},{3,1},{1,0},{8,10},{10,12},{12... | collective-permute-start | bytes 1572872 | tf_op jit(solution)/shard_map/ppermute | solution.py:55
  102.5 25.9 %collective-permute-start.7 = (f32[128,1024]{1,0:T(8,128)S(1)}, f32[128,1024]{1,0:T(8,128)S(1)}, u32[]{:S(2)}, u32[]{:S(2)}) collective-permute-start(f32[128,1024]{1,0:T(8,128)S(1)} %collective-permute-done.5), channel_id=1, source_target_pairs={{0,1},{2,0},{4,2},{6,4},{7,6},{5,7},{3,5},{1,3},{8,9},{10,8},{12,1... | collective-permute-start | bytes 1572872 | tf_op jit(solution)/shard_map/ppermute | solution.py:56
  126.8 88.6 %copy-start.8 = (s32[512]{0:T(512)S(1)}, s32[512]{0:T(512)}, u32[]{:S(2)}) copy-start(s32[512]{0:T(512)} %param.12) | copy-start | bytes 6148
  126.8 88.7 %collective-permute-start.8 = (f32[128,1024]{1,0:T(8,128)}, f32[128,1024]{1,0:T(8,128)}, u32[]{:S(2)}, u32[]{:S(2)}) collective-permute-start(f32[128,1024]{1,0:T(8,128)} %collective-permute-done.6), channel_id=1, source_target_pairs={{0,2},{2,4},{4,6},{6,7},{7,5},{5,3},{3,1},{1,0},{8,10},{10,12},{12... | collective-permute-start | bytes 1572872 | tf_op jit(solution)/shard_map/ppermute | solution.py:55
  128.4 91.0 %collective-permute-start.9 = (f32[128,1024]{1,0:T(8,128)S(1)}, f32[128,1024]{1,0:T(8,128)}, u32[]{:S(2)}, u32[]{:S(2)}) collective-permute-start(f32[128,1024]{1,0:T(8,128)S(1)} %collective-permute-done.7), channel_id=1, source_target_pairs={{0,1},{2,0},{4,2},{6,4},{7,6},{5,7},{3,5},{1,3},{8,9},{10,8},{12,1... | collective-permute-start | bytes 1572872 | tf_op jit(solution)/shard_map/ppermute | solution.py:56
  215.4 17.0 %collective-permute-start.16 = (f32[2050,64]{0,1:T(8,128)S(1)}, f32[2050,64]{0,1:T(8,128)S(1)}, u32[]{:S(2)}, u32[]{:S(2)}) collective-permute-start(f32[2050,64]{0,1:T(8,128)S(1)} %concatenate.27), channel_id=1, source_target_pairs={{0,4},{1,5},{2,6},{3,7},{4,0},{5,1},{6,2},{7,3},{8,12},{9,13},{10,... | collective-permute-start | bytes 1574408 | tf_op jit(solution)/shard_map/ppermute | solution.py:77
  215.5 25.9 %collective-permute-start.10 = (f32[128,1024]{1,0:T(8,128)}, f32[128,1024]{1,0:T(8,128)S(1)}, u32[]{:S(2)}, u32[]{:S(2)}) collective-permute-start(f32[128,1024]{1,0:T(8,128)} %collective-permute-done.8), channel_id=1, source_target_pairs={{0,2},{2,4},{4,6},{6,7},{7,5},{5,3},{3,1},{1,0},{8,10},{10,12},{12... | collective-permute-start | bytes 1572872 | tf_op jit(solution)/shard_map/ppermute | solution.py:55
  219.5 24.5 %collective-permute-start.11 = (f32[128,1024]{1,0:T(8,128)}, f32[128,1024]{1,0:T(8,128)S(1)}, u32[]{:S(2)}, u32[]{:S(2)}) collective-permute-start(f32[128,1024]{1,0:T(8,128)} %collective-permute-done.9), channel_id=1, source_target_pairs={{0,1},{2,0},{4,2},{6,4},{7,6},{5,7},{3,5},{1,3},{8,9},{10,8},{12,1... | collective-permute-start | bytes 1572872 | tf_op jit(solution)/shard_map/ppermute | solution.py:56
  232.4 23.5 %collective-permute-start.17 = (f32[2050,64]{0,1:T(8,128)S(1)}, f32[2050,64]{0,1:T(8,128)S(1)}, u32[]{:S(2)}, u32[]{:S(2)}) collective-permute-start(f32[2050,64]{0,1:T(8,128)S(1)} %add.419), channel_id=1, source_target_pairs={{0,2},{1,3},{2,0},{3,1},{4,6},{5,7},{6,4},{7,5},{8,10},{9,11},{10,... | collective-permute-start | bytes 1574408 | tf_op jit(solution)/shard_map/ppermute | solution.py:77
  241.4 25.1 %collective-permute-start.12 = (f32[128,1024]{1,0:T(8,128)S(1)}, f32[128,1024]{1,0:T(8,128)S(1)}, u32[]{:S(2)}, u32[]{:S(2)}) collective-permute-start(f32[128,1024]{1,0:T(8,128)S(1)} %collective-permute-done.10), channel_id=1, source_target_pairs={{0,2},{2,4},{4,6},{6,7},{7,5},{5,3},{3,1},{1,0},{8,10},{10,12},{12... | collective-permute-start | bytes 1572872 | tf_op jit(solution)/shard_map/ppermute | solution.py:55
  244.0 22.5 %collective-permute-start.13 = (f32[128,1024]{1,0:T(8,128)S(1)}, f32[128,1024]{1,0:T(8,128)S(1)}, u32[]{:S(2)}, u32[]{:S(2)}) collective-permute-start(f32[128,1024]{1,0:T(8,128)S(1)} %collective-permute-done.11), channel_id=1, source_target_pairs={{0,1},{2,0},{4,2},{6,4},{7,6},{5,7},{3,5},{1,3},{8,9},{10,8},{12,1... | collective-permute-start | bytes 1572872 | tf_op jit(solution)/shard_map/ppermute | solution.py:56
  256.0 16.4 %collective-permute-start.18 = (f32[2050,64]{0,1:T(8,128)S(1)}, f32[2050,64]{0,1:T(8,128)S(1)}, u32[]{:S(2)}, u32[]{:S(2)}) collective-permute-start(f32[2050,64]{0,1:T(8,128)S(1)} %add.420), channel_id=1, source_target_pairs={{0,1},{1,0},{2,3},{3,2},{4,5},{5,4},{6,7},{7,6},{8,9},{9,8},{10,11... | collective-permute-start | bytes 1574408 | tf_op jit(solution)/shard_map/ppermute | solution.py:77
  266.4 16.4 %collective-permute-start.14 = (f32[128,1024]{1,0:T(8,128)S(1)}, f32[128,1024]{1,0:T(8,128)S(1)}, u32[]{:S(2)}, u32[]{:S(2)}) collective-permute-start(f32[128,1024]{1,0:T(8,128)S(1)} %collective-permute-done.12), channel_id=1, source_target_pairs={{0,2},{2,4},{4,6},{6,7},{7,5},{5,3},{3,1},{1,0},{8,10},{10,12},{12... | collective-permute-start | bytes 1572872 | tf_op jit(solution)/shard_map/ppermute | solution.py:55
  266.5 17.3 %collective-permute-start.15 = (f32[128,1024]{1,0:T(8,128)S(1)}, f32[128,1024]{1,0:T(8,128)S(1)}, u32[]{:S(2)}, u32[]{:S(2)}) collective-permute-start(f32[128,1024]{1,0:T(8,128)S(1)} %collective-permute-done.13), channel_id=1, source_target_pairs={{0,1},{2,0},{4,2},{6,4},{7,6},{5,7},{3,5},{1,3},{8,9},{10,8},{12,1... | collective-permute-start | bytes 1572872 | tf_op jit(solution)/shard_map/ppermute | solution.py:56
  272.8 1.2 collective-permute-start.19
  274.0 3.6 %collective-permute-start.20 = (f32[128]{0:T(128)S(1)}, f32[128]{0:T(128)S(1)}, u32[]{:S(2)}, u32[]{:S(2)}) collective-permute-start(f32[128]{0:T(128)S(1)} %broadcast_select_fusion.1), channel_id=1, source_target_pairs={{0,16},{8,24},{16,0},{24,8},{32,48},{40,56},{48,32},{56,40},{64,80... | collective-permute-start | bytes 1544 | tf_op jit(solution)/shard_map/ppermute | solution.py:88
  277.6 6.1 %collective-permute-start.21 = (f32[256]{0:T(256)S(1)}, f32[256]{0:T(256)S(1)}, u32[]{:S(2)}, u32[]{:S(2)}) collective-permute-start(f32[256]{0:T(256)S(1)} %maximum_select_fusion.2), channel_id=1, source_target_pairs={{0,32},{8,40},{16,48},{24,56},{32,0},{40,8},{48,16},{56,24},{64,96... | collective-permute-start | bytes 3080 | tf_op jit(solution)/shard_map/ppermute | solution.py:88
  283.7 3.7 %collective-permute-start.22 = (f32[512]{0:T(512)S(1)}, f32[512]{0:T(512)S(1)}, u32[]{:S(2)}, u32[]{:S(2)}) collective-permute-start(f32[512]{0:T(512)S(1)} %maximum_select_fusion.1), channel_id=1, source_target_pairs={{0,64},{8,72},{16,80},{24,88},{32,96},{40,104},{48,112},{56,120},{... | collective-permute-start | bytes 6152 | tf_op jit(solution)/shard_map/ppermute | solution.py:88
  (2 other events, 39.9 us)
Sparse Core Ops, SparseCore 0:
  84.8 119.1 all-gather.1

commit v15 on v13

--- a/solution.py
+++ b/solution.py
@@ -57,6 +57,8 @@
         behind = lax.ppermute(behind, "col", backward)
         from_ahead = ring_tab[(me - k) % n_col]
         from_behind = ring_tab[(me + k) % n_col]
+        if k == n_col - 1:
+            break
         row_all = lax.dynamic_update_slice_in_dim(row_all, ahead, from_ahead * block_rows, 0)
         row_all = lax.dynamic_update_slice_in_dim(
             row_all, behind, from_behind * block_rows + half_rows, 0
@@ -93,6 +95,14 @@
     tile = lax.dot_general(
         row_all, col_all, contract, precision=high, preferred_element_type=jnp.float32
     )
+    last_rows = jnp.concatenate([ahead, behind], axis=0)
+    last_cols = jnp.concatenate([
+        lax.dynamic_slice_in_dim(col_all, from_ahead * block_rows, half_rows, 0),
+        lax.dynamic_slice_in_dim(col_all, from_behind * block_rows + half_rows, half_rows, 0),
+    ], axis=0)
+    tile = tile + lax.dot_general(
+        last_rows, last_cols, contract, precision=high, preferred_element_type=jnp.float32
+    )
     rows_global = row_pos * width_row + lax.broadcasted_iota(jnp.int32, (width_row, width_col), 0)
     cols_global = col_pos * width_col + lax.broadcasted_iota(jnp.int32, (width_row, width_col), 1)
     tile = tile + jnp.where(rows_global == cols_global, ridge[None, :], jnp.float32(0.0))

time: 321 us -> 340 us (1.059)
  matrix products: 45.7 us -> 53.1 us
  starting transfers between devices: 78.7 us -> 85.9 us
    all_gather x1, waiting for transfers between devices: 32.5 us -> 47.8 us  [body(): col_all = lax.all_gather(masked, 'row', axis=0, tiled=True)]
    ppermute x3, waiting for transfers between devices: 27.1 us -> 16.1 us  [body(): packed = packed + lax.ppermute(packed, 'col', pairs)]
    dot_general x0 -> x1, matrix products: none -> 7.46 us  [body(): lax.dot_general(last_rows, last_cols, contract, precision=high, preferred...]
    ppermute x7, starting transfers between devices: 20.6 us -> 27.8 us  [body(): behind = lax.ppermute(behind, 'col', backward)]
    dynamic_update_slice x7 -> x6, local copies, waits for them, and re-layouts: 8.06 us -> 9.21 us  [body(): lax.dynamic_update_slice_in_dim(row_all, behind, from_behind * block_rows...]
    dynamic_update_slice x7 -> x6, local copies, waits for them, and re-layouts: 9.08 us -> 8.16 us  [body(): lax.dynamic_update_slice_in_dim(row_all, ahead, from_ahead * block_rows, 0)]
  transfers between devices with their start and end apart: 24 -> 24, of which waited for: 18 -> 13; matrix products, arithmetic and copies ran while one was open for 13% -> 24% of each run, Pallas kernels for 0% -> 0%
where the time goes in v15:
time: 340 us
  waiting for transfers between devices  130 us (38%)
  starting transfers between devices  85.9 us (25%)
  matrix products  53.1 us (16%)
  local copies, waits for them, and re-layouts  33.1 us (10%)
  between operations  32.4 us (10%)
  other arithmetic  5.41 us (2%)
    ppermute x7, starting transfers between devices, body(): ahead = lax.ppermute(ahead, 'col', forward)  52.1 us
    ppermute x7, waiting for transfers between devices, body(): ahead = lax.ppermute(ahead, 'col', forward)  48.1 us
    all_gather x1, waiting for transfers between devices, body(): col_all = lax.all_gather(masked, 'row', axis=0, tiled=True)  47.8 us
    dot_general x1, matrix products, body(): lax.dot_general(row_all, col_all, contract, precision=high, preferred_ele...  33.9 us
    ppermute x7, starting transfers between devices, body(): behind = lax.ppermute(behind, 'col', backward)  27.8 us
    ppermute x3, waiting for transfers between devices, body(): packed = packed + lax.ppermute(packed, 'col', pairs)  16.1 us
    dot_general x1, matrix products, body(): lax.dot_general(col_all, items, (((1,), (1,)), ((), ())), precision=high,...  11.3 us
    ppermute x7, waiting for transfers between devices, body(): behind = lax.ppermute(behind, 'col', backward)  9.9 us
  transfers between devices with their start and end apart: 24, of which 13 were waited for; matrix products, arithmetic and copies ran while one was open for 24% of the time, Pallas kernels for 0%

profile of v15, /device:TPU:0, one launch (start us, length us, event | category | flops | bytes accessed | tf_op | source)
XLA Modules:
  0.0 339.6 jit_solution(11899726749590554401)
XLA Ops:
  9.1 2.4 broadcast_select_fusion
  11.5 2.1 reshape.96
  16.7 4.5 %broadcast_in_dim.46 = f32[2048,1024]{1,0:T(8,128)} broadcast(f32[]{:T(128)} %constant.159.clone.1), dimensions={} | broadcast | bytes 8388612 | tf_op jit(solution)/shard_map/broadcast_in_dim | solution.py:51
  22.1 43.7 %collective-permute-start.2 = (f32[128,1024]{1,0:T(8,128)S(1)}, f32[128,1024]{1,0:T(8,128)S(1)}, u32[]{:S(2)}, u32[]{:S(2)}) collective-permute-start(f32[128,1024]{1,0:T(8,128)S(1)} %get-tuple-element.11), channel_id=1, source_target_pairs={{0,2},{2,4},{4,6},{6,7},{7,5},{5,3},{3,1},{1,0},{8,10},{10,12},{12... | collective-permute-start | bytes 1572872 | tf_op jit(solution)/shard_map/ppermute | solution.py:56
  66.7 8.7 %collective-permute-start.3 = (f32[128,1024]{1,0:T(8,128)S(1)}, f32[128,1024]{1,0:T(8,128)S(1)}, u32[]{:S(2)}, u32[]{:S(2)}) collective-permute-start(f32[128,1024]{1,0:T(8,128)S(1)} %get-tuple-element.9), channel_id=1, source_target_pairs={{0,1},{2,0},{4,2},{6,4},{7,6},{5,7},{3,5},{1,3},{8,9},{10,8},{12,1... | collective-permute-start | bytes 1572872 | tf_op jit(solution)/shard_map/ppermute | solution.py:57
  75.4 22.0 %collective-permute-done.2 = f32[128,1024]{1,0:T(8,128)S(1)} collective-permute-done((f32[128,1024]{1,0:T(8,128)S(1)}, f32[128,1024]{1,0:T(8,128)S(1)}, u32[]{:S(2)}, u32[]{:S(2)}) %collective-permute-start.2) | collective-permute-done | bytes 524320 | tf_op jit(solution)/shard_map/ppermute | solution.py:56
  98.5 4.0 %collective-permute-start.5 = (f32[128,1024]{1,0:T(8,128)S(1)}, f32[128,1024]{1,0:T(8,128)S(1)}, u32[]{:S(2)}, u32[]{:S(2)}) collective-permute-start(f32[128,1024]{1,0:T(8,128)S(1)} %collective-permute-done.3), channel_id=1, source_target_pairs={{0,1},{2,0},{4,2},{6,4},{7,6},{5,7},{3,5},{1,3},{8,9},{10,8},{12,1... | collective-permute-start | bytes 1572872 | tf_op jit(solution)/shard_map/ppermute | solution.py:57
  103.4 20.5 %collective-permute-done.4 = f32[128,1024]{1,0:T(8,128)} collective-permute-done((f32[128,1024]{1,0:T(8,128)S(1)}, f32[128,1024]{1,0:T(8,128)}, u32[]{:S(2)}, u32[]{:S(2)}) %collective-permute-start.4) | collective-permute-done | bytes 524320 | tf_op jit(solution)/shard_map/ppermute | solution.py:56
  125.4 4.0 %collective-permute-start.7 = (f32[128,1024]{1,0:T(8,128)S(1)}, f32[128,1024]{1,0:T(8,128)}, u32[]{:S(2)}, u32[]{:S(2)}) collective-permute-start(f32[128,1024]{1,0:T(8,128)S(1)} %collective-permute-done.5), channel_id=1, source_target_pairs={{0,1},{2,0},{4,2},{6,4},{7,6},{5,7},{3,5},{1,3},{8,9},{10,8},{12,1... | collective-permute-start | bytes 1572872 | tf_op jit(solution)/shard_map/ppermute | solution.py:57
  129.3 47.8 %all-gather.2.cloned.1.call-done = f32[2048,2048]{1,0:T(8,128)} async-done(((f32[128,2048]{1,0:T(8,128)}), f32[2048,2048]{1,0:T(8,128)}) %all-gather.2.cloned.1.call-update) | async-done | bytes 16777232 | tf_op jit(solution)/shard_map/all_gather | solution.py:23
  177.1 11.3 %fusion.10 = f32[2048,64]{0,1:T(8,128)S(1)} fusion(f32[2048,2048]{1,0:T(8,128)} %all-gather.2.cloned.1.call-done, f32[64,2048]{1,0:T(8,128)S(1)} %copy-done.1), kind=kOutput, calls=%fused_computation.49 | convolution fusion | flops 1610612736 | bytes 17825792 | tf_op jit(solution)/shard_map/dot_general | solution.py:67
  188.6 8.3 %collective-permute-start.8 = (f32[128,1024]{1,0:T(8,128)S(1)}, f32[128,1024]{1,0:T(8,128)}, u32[]{:S(2)}, u32[]{:S(2)}) collective-permute-start(f32[128,1024]{1,0:T(8,128)S(1)} %collective-permute-done.6), channel_id=1, source_target_pairs={{0,2},{2,4},{4,6},{6,7},{7,5},{5,3},{3,1},{1,0},{8,10},{10,12},{12... | collective-permute-start | bytes 1572872 | tf_op jit(solution)/shard_map/ppermute | solution.py:56
  197.0 8.6 %collective-permute-done.14 = f32[2050,64]{0,1:T(8,128)S(1)} collective-permute-done((f32[2050,64]{0,1:T(8,128)S(1)}, f32[2050,64]{0,1:T(8,128)S(1)}, u32[]{:S(2)}, u32[]{:S(2)}) %collective-permute-start.14) | collective-permute-done | bytes 524832 | tf_op jit(solution)/shard_map/ppermute | solution.py:77
  205.6 4.8 %collective-permute-start.15 = (f32[2050,64]{0,1:T(8,128)S(1)}, f32[2050,64]{0,1:T(8,128)S(1)}, u32[]{:S(2)}, u32[]{:S(2)}) collective-permute-start(f32[2050,64]{0,1:T(8,128)S(1)} %add.411), channel_id=1, source_target_pairs={{0,2},{1,3},{2,0},{3,1},{4,6},{5,7},{6,4},{7,5},{8,10},{9,11},{10,... | collective-permute-start | bytes 1574408 | tf_op jit(solution)/shard_map/ppermute | solution.py:77
  230.6 1.9 constant_dynamic-update-slice_fusion.10
  232.5 1.9 constant_dynamic-update-slice_fusion.9
  234.4 3.5 %collective-permute-start.11 = (f32[128,1024]{1,0:T(8,128)}, f32[128,1024]{1,0:T(8,128)S(1)}, u32[]{:S(2)}, u32[]{:S(2)}) collective-permute-start(f32[128,1024]{1,0:T(8,128)} %collective-permute-done.9), channel_id=1, source_target_pairs={{0,1},{2,0},{4,2},{6,4},{7,6},{5,7},{3,5},{1,3},{8,9},{10,8},{12,1... | collective-permute-start | bytes 1572872 | tf_op jit(solution)/shard_map/ppermute | solution.py:57
  239.8 1.9 constant_dynamic-update-slice_fusion.6
  241.6 1.9 constant_dynamic-update-slice_fusion.5
  243.5 1.9 constant_dynamic-update-slice_fusion.4
  245.4 5.6 %collective-permute-done.10 = f32[128,1024]{1,0:T(8,128)S(1)} collective-permute-done((f32[128,1024]{1,0:T(8,128)}, f32[128,1024]{1,0:T(8,128)S(1)}, u32[]{:S(2)}, u32[]{:S(2)}) %collective-permute-start.10) | collective-permute-done | bytes 524320 | tf_op jit(solution)/shard_map/ppermute | solution.py:56
  251.0 3.5 %collective-permute-start.13 = (f32[128,1024]{1,0:T(8,128)S(1)}, f32[128,1024]{1,0:T(8,128)}, u32[]{:S(2)}, u32[]{:S(2)}) collective-permute-start(f32[128,1024]{1,0:T(8,128)S(1)} %collective-permute-done.11), channel_id=1, source_target_pairs={{0,1},{2,0},{4,2},{6,4},{7,6},{5,7},{3,5},{1,3},{8,9},{10,8},{12,1... | collective-permute-start | bytes 1572872 | tf_op jit(solution)/shard_map/ppermute | solution.py:57
  255.3 7.6 %collective-permute-done.16 = f32[2050,64]{0,1:T(8,128)S(1)} collective-permute-done((f32[2050,64]{0,1:T(8,128)S(1)}, f32[2050,64]{0,1:T(8,128)S(1)}, u32[]{:S(2)}, u32[]{:S(2)}) %collective-permute-start.16) | collective-permute-done | bytes 524832 | tf_op jit(solution)/shard_map/ppermute | solution.py:77
  264.2 7.3 %collective-permute-done.13 = f32[128,1024]{1,0:T(8,128)} collective-permute-done((f32[128,1024]{1,0:T(8,128)S(1)}, f32[128,1024]{1,0:T(8,128)}, u32[]{:S(2)}, u32[]{:S(2)}) %collective-permute-start.13) | collective-permute-done | bytes 524320 | tf_op jit(solution)/shard_map/ppermute | solution.py:57
  271.5 4.1 %collective-permute-start.22 = (f32[128,1024]{1,0:T(8,128)}, f32[128,1024]{1,0:T(8,128)S(1)}, u32[]{:S(2)}, u32[]{:S(2)}) collective-permute-start(f32[128,1024]{1,0:T(8,128)} %collective-permute-done.13), channel_id=1, source_target_pairs={{0,1},{2,0},{4,2},{6,4},{7,6},{5,7},{3,5},{1,3},{8,9},{10,8},{12,1... | collective-permute-start | bytes 1572872 | tf_op jit(solution)/shard_map/ppermute | solution.py:57
  275.7 1.9 constant_dynamic-update-slice_fusion.1
  279.3 1.9 constant_dynamic-update-slice_fusion
  281.2 3.2 collective-permute-done.19
  286.1 1.9 collective-permute-done.20
  288.0 3.4 %gather_fusion = f32[512]{0:T(512)} fusion(f32[1024]{0:T(1024)S(1)} %maximum_select_fusion, s32[1024]{0:T(1024)S(1)} %pad_clamp_fusion), kind=kCustom, calls=%fused_computation | custom fusion | bytes 6144 | tf_op jit(solution)/shard_map/gather | solution.py:92
  291.4 33.9 %fusion.12 = f32[1024,2048]{1,0:T(8,128)S(1)} fusion(f32[2048,1024]{1,0:T(8,128)} %constant_dynamic-update-slice_fusion, f32[2048,2048]{1,0:T(8,128)} %all-gather.2.cloned.1.call-done), kind=kOutput, calls=%fused_computation.51 | convolution fusion | flops 25769803776 | bytes 33554432 | tf_op jit(solution)/shard_map/dot_general | solution.py:95
  325.3 7.5 %select_add_fusion = f32[1024,2048]{1,0:T(8,128)} fusion(f32[1024,2048]{1,0:T(8,128)S(1)} %fusion.12, f32[2048]{0:T(1024)S(1)} %copy-done.4, s32[2048]{0:T(1024)S(1)} %iota_add_fusion, s32[1024]{0:T(1024)S(1)} %iota_add_fusion.1, f32[128,2048]{1,0:T(8,128)S(1)} %get-tuple-element.13, f32[128,2048]{1,0:T(8,128)S(1)} %get-tuple-element.12, ...), kind=kOutput, calls=%fused_computation.1 | convolution fusion | flops 3230400512 | bytes 19943424 | tf_op jit(solution)/shard_map/dot_general | solution.py:103
  (78 shorter events, 20.0 us)
Async XLA Ops:
  7.2 95.6 %copy-start = (f32[2048]{0:T(1024)S(1)}, f32[2048]{0:T(1024)}, u32[]{:S(2)}) copy-start(f32[2048]{0:T(1024)} %param.13) | copy-start | bytes 24580
  7.2 169.9 %all-gather.2.cloned.1.call-start = ((), (), s32[]{:S(2)}) async-start(), calls=%async_computation | async-start | bytes 17825792 | tf_op jit(solution)/shard_map/all_gather | solution.py:23
  13.7 88.9 %copy-start.1 = (f32[64,2048]{1,0:T(8,128)S(1)}, f32[64,2048]{1,0:T(8,128)}, u32[]{:S(2)}) copy-start(f32[64,2048]{1,0:T(8,128)} %param.11) | copy-start | bytes 1572868
  13.7 88.9 %copy-start.4 = (f32[2048]{0:T(1024)S(1)}, f32[2048]{0:T(1024)}, u32[]{:S(2)}) copy-start(f32[2048]{0:T(1024)} %param.10) | copy-start | bytes 24580
  14.7 2.0 collective-permute-start.1
  14.9 1.8 collective-permute-start
  22.1 75.3 %collective-permute-start.2 = (f32[128,1024]{1,0:T(8,128)S(1)}, f32[128,1024]{1,0:T(8,128)S(1)}, u32[]{:S(2)}, u32[]{:S(2)}) collective-permute-start(f32[128,1024]{1,0:T(8,128)S(1)} %get-tuple-element.11), channel_id=1, source_target_pairs={{0,2},{2,4},{4,6},{6,7},{7,5},{5,3},{3,1},{1,0},{8,10},{10,12},{12... | collective-permute-start | bytes 1572872 | tf_op jit(solution)/shard_map/ppermute | solution.py:56
  66.7 31.9 %collective-permute-start.3 = (f32[128,1024]{1,0:T(8,128)S(1)}, f32[128,1024]{1,0:T(8,128)S(1)}, u32[]{:S(2)}, u32[]{:S(2)}) collective-permute-start(f32[128,1024]{1,0:T(8,128)S(1)} %get-tuple-element.9), channel_id=1, source_target_pairs={{0,1},{2,0},{4,2},{6,4},{7,6},{5,7},{3,5},{1,3},{8,9},{10,8},{12,1... | collective-permute-start | bytes 1572872 | tf_op jit(solution)/shard_map/ppermute | solution.py:57
  97.4 26.5 %collective-permute-start.4 = (f32[128,1024]{1,0:T(8,128)S(1)}, f32[128,1024]{1,0:T(8,128)}, u32[]{:S(2)}, u32[]{:S(2)}) collective-permute-start(f32[128,1024]{1,0:T(8,128)S(1)} %collective-permute-done.2), channel_id=1, source_target_pairs={{0,2},{2,4},{4,6},{6,7},{7,5},{5,3},{3,1},{1,0},{8,10},{10,12},{12... | collective-permute-start | bytes 1572872 | tf_op jit(solution)/shard_map/ppermute | solution.py:56
  98.5 78.6 %copy-start.2 = (f32[128,1024]{1,0:T(8,128)}, f32[128,1024]{1,0:T(8,128)S(1)}, u32[]{:S(2)}) copy-start(f32[128,1024]{1,0:T(8,128)S(1)} %collective-permute-done.3) | copy-start | bytes 1572868
  98.5 26.8 %collective-permute-start.5 = (f32[128,1024]{1,0:T(8,128)S(1)}, f32[128,1024]{1,0:T(8,128)S(1)}, u32[]{:S(2)}, u32[]{:S(2)}) collective-permute-start(f32[128,1024]{1,0:T(8,128)S(1)} %collective-permute-done.3), channel_id=1, source_target_pairs={{0,1},{2,0},{4,2},{6,4},{7,6},{5,7},{3,5},{1,3},{8,9},{10,8},{12,1... | collective-permute-start | bytes 1572872 | tf_op jit(solution)/shard_map/ppermute | solution.py:57
  103.4 85.2 %copy-start.5 = (s32[512]{0:T(512)S(1)}, s32[512]{0:T(512)}, u32[]{:S(2)}) copy-start(s32[512]{0:T(512)} %param.12) | copy-start | bytes 6148
  103.4 107.1 %copy-start.6 = (s32[8]{0:T(128)S(1)}, s32[8]{0:T(128)}, u32[]{:S(2)}) copy-start(s32[8]{0:T(128)} %constant.194.clone) | copy-start | bytes 100
  103.4 117.0 %copy-start.3 = (s32[8]{0:T(128)S(1)}, s32[8]{0:T(128)}, u32[]{:S(2)}) copy-start(s32[8]{0:T(128)} %constant.193.clone) | copy-start | bytes 100
  123.9 64.7 %collective-permute-start.6 = (f32[128,1024]{1,0:T(8,128)}, f32[128,1024]{1,0:T(8,128)S(1)}, u32[]{:S(2)}, u32[]{:S(2)}) collective-permute-start(f32[128,1024]{1,0:T(8,128)} %collective-permute-done.4), channel_id=1, source_target_pairs={{0,2},{2,4},{4,6},{6,7},{7,5},{5,3},{3,1},{1,0},{8,10},{10,12},{12... | collective-permute-start | bytes 1572872 | tf_op jit(solution)/shard_map/ppermute | solution.py:56
  125.4 71.6 %collective-permute-start.7 = (f32[128,1024]{1,0:T(8,128)S(1)}, f32[128,1024]{1,0:T(8,128)}, u32[]{:S(2)}, u32[]{:S(2)}) collective-permute-start(f32[128,1024]{1,0:T(8,128)S(1)} %collective-permute-done.5), channel_id=1, source_target_pairs={{0,1},{2,0},{4,2},{6,4},{7,6},{5,7},{3,5},{1,3},{8,9},{10,8},{12,1... | collective-permute-start | bytes 1572872 | tf_op jit(solution)/shard_map/ppermute | solution.py:57
  188.5 17.0 %collective-permute-start.14 = (f32[2050,64]{0,1:T(8,128)S(1)}, f32[2050,64]{0,1:T(8,128)S(1)}, u32[]{:S(2)}, u32[]{:S(2)}) collective-permute-start(f32[2050,64]{0,1:T(8,128)S(1)} %concatenate.33), channel_id=1, source_target_pairs={{0,4},{1,5},{2,6},{3,7},{4,0},{5,1},{6,2},{7,3},{8,12},{9,13},{10,... | collective-permute-start | bytes 1574408 | tf_op jit(solution)/shard_map/ppermute | solution.py:77
  188.6 45.8 %collective-permute-start.8 = (f32[128,1024]{1,0:T(8,128)S(1)}, f32[128,1024]{1,0:T(8,128)}, u32[]{:S(2)}, u32[]{:S(2)}) collective-permute-start(f32[128,1024]{1,0:T(8,128)S(1)} %collective-permute-done.6), channel_id=1, source_target_pairs={{0,2},{2,4},{4,6},{6,7},{7,5},{5,3},{3,1},{1,0},{8,10},{10,12},{12... | collective-permute-start | bytes 1572872 | tf_op jit(solution)/shard_map/ppermute | solution.py:56
  196.9 37.5 %collective-permute-start.9 = (f32[128,1024]{1,0:T(8,128)}, f32[128,1024]{1,0:T(8,128)}, u32[]{:S(2)}, u32[]{:S(2)}) collective-permute-start(f32[128,1024]{1,0:T(8,128)} %collective-permute-done.7), channel_id=1, source_target_pairs={{0,1},{2,0},{4,2},{6,4},{7,6},{5,7},{3,5},{1,3},{8,9},{10,8},{12,1... | collective-permute-start | bytes 1572872 | tf_op jit(solution)/shard_map/ppermute | solution.py:57
  205.6 33.2 %collective-permute-start.15 = (f32[2050,64]{0,1:T(8,128)S(1)}, f32[2050,64]{0,1:T(8,128)S(1)}, u32[]{:S(2)}, u32[]{:S(2)}) collective-permute-start(f32[2050,64]{0,1:T(8,128)S(1)} %add.411), channel_id=1, source_target_pairs={{0,2},{1,3},{2,0},{3,1},{4,6},{5,7},{6,4},{7,5},{8,10},{9,11},{10,... | collective-permute-start | bytes 1574408 | tf_op jit(solution)/shard_map/ppermute | solution.py:77
  234.4 16.6 %collective-permute-start.10 = (f32[128,1024]{1,0:T(8,128)}, f32[128,1024]{1,0:T(8,128)S(1)}, u32[]{:S(2)}, u32[]{:S(2)}) collective-permute-start(f32[128,1024]{1,0:T(8,128)} %collective-permute-done.8), channel_id=1, source_target_pairs={{0,2},{2,4},{4,6},{6,7},{7,5},{5,3},{3,1},{1,0},{8,10},{10,12},{12... | collective-permute-start | bytes 1572872 | tf_op jit(solution)/shard_map/ppermute | solution.py:56
  234.4 16.5 %collective-permute-start.11 = (f32[128,1024]{1,0:T(8,128)}, f32[128,1024]{1,0:T(8,128)S(1)}, u32[]{:S(2)}, u32[]{:S(2)}) collective-permute-start(f32[128,1024]{1,0:T(8,128)} %collective-permute-done.9), channel_id=1, source_target_pairs={{0,1},{2,0},{4,2},{6,4},{7,6},{5,7},{3,5},{1,3},{8,9},{10,8},{12,1... | collective-permute-start | bytes 1572872 | tf_op jit(solution)/shard_map/ppermute | solution.py:57
  238.8 24.1 %collective-permute-start.16 = (f32[2050,64]{0,1:T(8,128)S(1)}, f32[2050,64]{0,1:T(8,128)S(1)}, u32[]{:S(2)}, u32[]{:S(2)}) collective-permute-start(f32[2050,64]{0,1:T(8,128)S(1)} %add.412), channel_id=1, source_target_pairs={{0,1},{1,0},{2,3},{3,2},{4,5},{5,4},{6,7},{7,6},{8,9},{9,8},{10,11... | collective-permute-start | bytes 1574408 | tf_op jit(solution)/shard_map/ppermute | solution.py:77
  251.0 24.6 %collective-permute-start.12 = (f32[128,1024]{1,0:T(8,128)S(1)}, f32[128,1024]{1,0:T(8,128)}, u32[]{:S(2)}, u32[]{:S(2)}) collective-permute-start(f32[128,1024]{1,0:T(8,128)S(1)} %collective-permute-done.10), channel_id=1, source_target_pairs={{0,2},{2,4},{4,6},{6,7},{7,5},{5,3},{3,1},{1,0},{8,10},{10,12},{12... | collective-permute-start | bytes 1572872 | tf_op jit(solution)/shard_map/ppermute | solution.py:56
  251.0 20.5 %collective-permute-start.13 = (f32[128,1024]{1,0:T(8,128)S(1)}, f32[128,1024]{1,0:T(8,128)}, u32[]{:S(2)}, u32[]{:S(2)}) collective-permute-start(f32[128,1024]{1,0:T(8,128)S(1)} %collective-permute-done.11), channel_id=1, source_target_pairs={{0,1},{2,0},{4,2},{6,4},{7,6},{5,7},{3,5},{1,3},{8,9},{10,8},{12,1... | collective-permute-start | bytes 1572872 | tf_op jit(solution)/shard_map/ppermute | solution.py:57
  263.3 12.3 %collective-permute-start.17 = (f32[64]{0:T(128)S(1)}, f32[64]{0:T(128)S(1)}, u32[]{:S(2)}, u32[]{:S(2)}) collective-permute-start(f32[64]{0:T(128)S(1)} %sqrt_add_fusion), channel_id=1, source_target_pairs={{0,8},{8,0},{16,24},{24,16},{32,40},{40,32},{48,56},{56,48},{64,72... | collective-permute-start | bytes 776 | tf_op jit(solution)/shard_map/ppermute | solution.py:88
  271.5 53.7 %collective-permute-start.22 = (f32[128,1024]{1,0:T(8,128)}, f32[128,1024]{1,0:T(8,128)S(1)}, u32[]{:S(2)}, u32[]{:S(2)}) collective-permute-start(f32[128,1024]{1,0:T(8,128)} %collective-permute-done.13), channel_id=1, source_target_pairs={{0,1},{2,0},{4,2},{6,4},{7,6},{5,7},{3,5},{1,3},{8,9},{10,8},{12,1... | collective-permute-start | bytes 1572872 | tf_op jit(solution)/shard_map/ppermute | solution.py:57
  275.6 49.6 %collective-permute-start.21 = (f32[128,1024]{1,0:T(8,128)}, f32[128,1024]{1,0:T(8,128)S(1)}, u32[]{:S(2)}, u32[]{:S(2)}) collective-permute-start(f32[128,1024]{1,0:T(8,128)} %collective-permute-done.12), channel_id=1, source_target_pairs={{0,2},{2,4},{4,6},{6,7},{7,5},{5,3},{3,1},{1,0},{8,10},{10,12},{12... | collective-permute-start | bytes 1572872 | tf_op jit(solution)/shard_map/ppermute | solution.py:56
  275.7 3.6 %collective-permute-start.18 = (f32[128]{0:T(128)S(1)}, f32[128]{0:T(128)S(1)}, u32[]{:S(2)}, u32[]{:S(2)}) collective-permute-start(f32[128]{0:T(128)S(1)} %broadcast_select_fusion.1), channel_id=1, source_target_pairs={{0,16},{8,24},{16,0},{24,8},{32,48},{40,56},{48,32},{56,40},{64,80... | collective-permute-start | bytes 1544 | tf_op jit(solution)/shard_map/ppermute | solution.py:88
  279.3 5.1 %collective-permute-start.19 = (f32[256]{0:T(256)S(1)}, f32[256]{0:T(256)S(1)}, u32[]{:S(2)}, u32[]{:S(2)}) collective-permute-start(f32[256]{0:T(256)S(1)} %maximum_select_fusion.2), channel_id=1, source_target_pairs={{0,32},{8,40},{16,48},{24,56},{32,0},{40,8},{48,16},{56,24},{64,96... | collective-permute-start | bytes 3080 | tf_op jit(solution)/shard_map/ppermute | solution.py:88
  284.4 3.6 %collective-permute-start.20 = (f32[512]{0:T(512)S(1)}, f32[512]{0:T(512)S(1)}, u32[]{:S(2)}, u32[]{:S(2)}) collective-permute-start(f32[512]{0:T(512)S(1)} %maximum_select_fusion.1), channel_id=1, source_target_pairs={{0,64},{8,72},{16,80},{24,88},{32,96},{40,104},{48,112},{56,120},{... | collective-permute-start | bytes 6152 | tf_op jit(solution)/shard_map/ppermute | solution.py:88
Sparse Core Ops, SparseCore 0:
  11.6 165.4 all-gather.1

commit v16 on v13

--- a/solution.py
+++ b/solution.py
@@ -42,25 +42,22 @@
     n_y = n_col // 2
     ring = [y * 2 for y in range(n_y)] + [y * 2 + 1 for y in reversed(range(n_y))]
     where_in_ring = [ring.index(c) for c in range(n_col)]
-    forward = [(ring[p], ring[(p + 1) % n_col]) for p in range(n_col)]
-    backward = [(ring[p], ring[(p - 1) % n_col]) for p in range(n_col)]
+    pairs = []
+    for r in range(n_row):
+        way = 1 if r % 2 == 0 else -1
+        for p in range(n_col):
+            pairs.append((r * n_col + ring[p], r * n_col + ring[(p + way) % n_col]))
     block_rows = row_block.shape[0]
-    half_rows = block_rows // 2
     ring_tab = jnp.array(ring, jnp.int32)
     me = jnp.array(where_in_ring, jnp.int32)[col_pos]
+    way = 1 - 2 * (row_pos % 2)
     row_all = jnp.zeros((n_col * block_rows, width_row), jnp.float32)
-    ahead, behind = row_block[:half_rows], row_block[half_rows:]
-    row_all = lax.dynamic_update_slice_in_dim(row_all, ahead, col_pos * block_rows, 0)
-    row_all = lax.dynamic_update_slice_in_dim(row_all, behind, col_pos * block_rows + half_rows, 0)
+    row_all = lax.dynamic_update_slice_in_dim(row_all, row_block, col_pos * block_rows, 0)
+    held = row_block
     for k in range(1, n_col):
-        ahead = lax.ppermute(ahead, "col", forward)
-        behind = lax.ppermute(behind, "col", backward)
-        from_ahead = ring_tab[(me - k) % n_col]
-        from_behind = ring_tab[(me + k) % n_col]
-        row_all = lax.dynamic_update_slice_in_dim(row_all, ahead, from_ahead * block_rows, 0)
-        row_all = lax.dynamic_update_slice_in_dim(
-            row_all, behind, from_behind * block_rows + half_rows, 0
-        )
+        held = lax.ppermute(held, ("row", "col"), pairs)
+        came_from = ring_tab[(me - k * way) % n_col]
+        row_all = lax.dynamic_update_slice_in_dim(row_all, held, came_from * block_rows, 0)
 
     z_part = lax.dot_general(
         col_all, items, (((1,), (1,)), ((), ())), precision=high,

time: 321 us -> 319 us (level)
  between operations: 32.5 us -> 23.5 us
  starting transfers between devices: 78.7 us -> 85.7 us
  local copies, waits for them, and re-layouts: 31.1 us -> 26.5 us
    ppermute x14 -> x7, waiting for transfers between devices: 59.7 us -> 109 us  [body(): held = lax.ppermute(held, ('row', 'col'), pairs)]
    all_gather x1, waiting for transfers between devices: 32.5 us -> 0.01 us  [body(): col_all = lax.all_gather(masked, 'row', axis=0, tiled=True)]
    ppermute x14 -> x7, starting transfers between devices: 72.8 us -> 49.9 us  [body(): held = lax.ppermute(held, ('row', 'col'), pairs)]
    ppermute x3, starting transfers between devices: 5 us -> 22.3 us  [body(): packed = packed + lax.ppermute(packed, 'col', pairs)]
    ppermute x4, starting transfers between devices: 0.11 us -> 12.7 us  [body(): other = lax.ppermute(held, 'row', pairs)]
    ppermute x3, waiting for transfers between devices: 27.1 us -> 16.4 us  [body(): packed = packed + lax.ppermute(packed, 'col', pairs)]
    dynamic_update_slice x14 -> x7, local copies, waits for them, and re-layouts: 17.1 us -> 12.7 us  [body(): lax.dynamic_update_slice_in_dim(row_all, held, came_from * block_rows, 0)]
  transfers between devices with their start and end apart: 24 -> 17, of which waited for: 18 -> 12; matrix products, arithmetic and copies ran while one was open for 13% -> 11% of each run, Pallas kernels for 0% -> 0%
where the time goes in v16:
time: 319 us; the launch traced here: 317 us
  waiting for transfers between devices  130 us (41%)
  starting transfers between devices  85.7 us (27%)
  matrix products  45.6 us (14%)
  local copies, waits for them, and re-layouts  26.5 us (8%)
  between operations  23.5 us (7%)
  other arithmetic  5.01 us (2%)
    ppermute x7, waiting for transfers between devices, body(): held = lax.ppermute(held, ('row', 'col'), pairs)  109 us
    ppermute x7, starting transfers between devices, body(): held = lax.ppermute(held, ('row', 'col'), pairs)  49.9 us
    dot_general x1, matrix products, body(): lax.dot_general(row_all, col_all, contract, precision=high, preferred_ele...  33.8 us
    ppermute x3, starting transfers between devices, body(): packed = packed + lax.ppermute(packed, 'col', pairs)  22.3 us
    ppermute x3, waiting for transfers between devices, body(): packed = packed + lax.ppermute(packed, 'col', pairs)  16.4 us
    ppermute x4, starting transfers between devices, body(): other = lax.ppermute(held, 'row', pairs)  12.7 us
    dynamic_update_slice x7, local copies, waits for them, and re-layouts, body(): lax.dynamic_update_slice_in_dim(row_all, held, came_from * block_rows, 0)  12.7 us
    dot_general x1, matrix products, body(): lax.dot_general(col_all, items, (((1,), (1,)), ((), ())), precision=high,...  11.3 us
  transfers between devices with their start and end apart: 17, of which 12 were waited for; matrix products, arithmetic and copies ran while one was open for 11% of the time, Pallas kernels for 0%

profile of v16, /device:TPU:0, one launch (start us, length us, event | category | flops | bytes accessed | tf_op | source)
XLA Modules:
  0.0 316.5 jit_solution(3214981056480927641)
XLA Ops:
  7.2 1.2 dynamic_slice.33
  9.1 2.3 broadcast_select_fusion
  11.5 2.1 reshape.26
  15.6 1.1 collective-permute-done.1
  16.8 4.3 %broadcast_in_dim.46 = f32[2048,1024]{1,0:T(8,128)} broadcast(f32[]{:T(128)} %constant.82.clone.1), dimensions={} | broadcast | bytes 8388612 | tf_op jit(solution)/shard_map/broadcast_in_dim | solution.py:54
  21.1 1.3 pad_maximum_fusion
  22.4 43.7 %collective-permute-start.2 = (f32[256,1024]{1,0:T(8,128)S(1)}, f32[256,1024]{1,0:T(8,128)S(1)}, u32[]{:S(2)}, u32[]{:S(2)}) collective-permute-start(f32[256,1024]{1,0:T(8,128)S(1)} %get-tuple-element.8), channel_id=1, source_target_pairs={{0,2},{2,4},{4,6},{6,7},{7,5},{5,3},{3,1},{1,0},{8,9},{10,8},{12,1... | collective-permute-start | bytes 3145736 | tf_op jit(solution)/shard_map/ppermute | solution.py:58
  66.1 34.7 %collective-permute-done.2 = f32[256,1024]{1,0:T(8,128)S(1)} collective-permute-done((f32[256,1024]{1,0:T(8,128)S(1)}, f32[256,1024]{1,0:T(8,128)S(1)}, u32[]{:S(2)}, u32[]{:S(2)}) %collective-permute-start.2) | collective-permute-done | bytes 1048608 | tf_op jit(solution)/shard_map/ppermute | solution.py:58
  100.9 38.7 %collective-permute-done.3 = f32[256,1024]{1,0:T(8,128)S(1)} collective-permute-done((f32[256,1024]{1,0:T(8,128)S(1)}, f32[256,1024]{1,0:T(8,128)S(1)}, u32[]{:S(2)}, u32[]{:S(2)}) %collective-permute-start.3) | collective-permute-done | bytes 1048608 | tf_op jit(solution)/shard_map/ppermute | solution.py:58
  139.6 17.9 %collective-permute-done.4 = f32[256,1024]{1,0:T(8,128)} collective-permute-done((f32[256,1024]{1,0:T(8,128)S(1)}, f32[256,1024]{1,0:T(8,128)}, u32[]{:S(2)}, u32[]{:S(2)}) %collective-permute-start.4) | collective-permute-done | bytes 1048608 | tf_op jit(solution)/shard_map/ppermute | solution.py:58
  158.4 15.7 %collective-permute-done.5 = f32[256,1024]{1,0:T(8,128)} collective-permute-done((f32[256,1024]{1,0:T(8,128)}, f32[256,1024]{1,0:T(8,128)}, u32[]{:S(2)}, u32[]{:S(2)}) %collective-permute-start.5) | collective-permute-done | bytes 1048608 | tf_op jit(solution)/shard_map/ppermute | solution.py:58
  174.1 3.6 %collective-permute-start.6 = (f32[256,1024]{1,0:T(8,128)}, f32[256,1024]{1,0:T(8,128)S(1)}, u32[]{:S(2)}, u32[]{:S(2)}) collective-permute-start(f32[256,1024]{1,0:T(8,128)} %collective-permute-done.5), channel_id=1, source_target_pairs={{0,2},{2,4},{4,6},{6,7},{7,5},{5,3},{3,1},{1,0},{8,9},{10,8},{12,1... | collective-permute-start | bytes 3145736 | tf_op jit(solution)/shard_map/ppermute | solution.py:58
  177.7 11.3 %fusion.3 = f32[2048,64]{0,1:T(8,128)S(1)} fusion(f32[2048,2048]{1,0:T(8,128)} %all-gather.2.cloned.1.call-done, f32[64,2048]{1,0:T(8,128)S(1)} %copy-done.1), kind=kOutput, calls=%fused_computation.35 | convolution fusion | flops 1610612736 | bytes 17825792 | tf_op jit(solution)/shard_map/dot_general | solution.py:62
  189.1 15.7 %collective-permute-start.9 = (f32[2050,64]{0,1:T(8,128)S(1)}, f32[2050,64]{0,1:T(8,128)S(1)}, u32[]{:S(2)}, u32[]{:S(2)}) collective-permute-start(f32[2050,64]{0,1:T(8,128)S(1)} %concatenate.31), channel_id=1, source_target_pairs={{0,4},{1,5},{2,6},{3,7},{4,0},{5,1},{6,2},{7,3},{8,12},{9,13},{10,... | collective-permute-start | bytes 1574408 | tf_op jit(solution)/shard_map/ppermute | solution.py:72
  204.7 10.9 %collective-permute-done.9 = f32[2050,64]{0,1:T(8,128)S(1)} collective-permute-done((f32[2050,64]{0,1:T(8,128)S(1)}, f32[2050,64]{0,1:T(8,128)S(1)}, u32[]{:S(2)}, u32[]{:S(2)}) %collective-permute-start.9) | collective-permute-done | bytes 524832 | tf_op jit(solution)/shard_map/ppermute | solution.py:72
  215.7 5.8 %collective-permute-start.10 = (f32[2050,64]{0,1:T(8,128)S(1)}, f32[2050,64]{0,1:T(8,128)S(1)}, u32[]{:S(2)}, u32[]{:S(2)}) collective-permute-start(f32[2050,64]{0,1:T(8,128)S(1)} %add.158), channel_id=1, source_target_pairs={{0,2},{1,3},{2,0},{3,1},{4,6},{5,7},{6,4},{7,5},{8,10},{9,11},{10,... | collective-permute-start | bytes 1574408 | tf_op jit(solution)/shard_map/ppermute | solution.py:72
  232.2 2.7 collective-permute-done.10
  235.8 2.3 constant_dynamic-update-slice_fusion.6
  238.1 2.3 constant_dynamic-update-slice_fusion.5
  240.4 2.3 constant_dynamic-update-slice_fusion.4
  242.8 2.1 collective-permute-done.7
  244.9 2.5 collective-permute-start.8
  247.4 2.8 collective-permute-done.11
  250.9 2.4 constant_dynamic-update-slice_fusion.3
  253.4 1.1 constant_dynamic-update-slice_fusion.2
  254.5 2.4 collective-permute-done.13
  256.9 9.0 %collective-permute-start.14 = (f32[256]{0:T(256)S(1)}, f32[256]{0:T(256)S(1)}, u32[]{:S(2)}, u32[]{:S(2)}) collective-permute-start(f32[256]{0:T(256)S(1)} %maximum_select_fusion.2), channel_id=1, source_target_pairs={{0,32},{8,40},{16,48},{24,56},{32,0},{40,8},{48,16},{56,24},{64,96... | collective-permute-start | bytes 3080 | tf_op jit(solution)/shard_map/ppermute | solution.py:83
  265.9 1.1 constant_dynamic-update-slice_fusion.1
  267.4 3.4 %collective-permute-start.15 = (f32[512]{0:T(512)S(1)}, f32[512]{0:T(512)S(1)}, u32[]{:S(2)}, u32[]{:S(2)}) collective-permute-start(f32[512]{0:T(512)S(1)} %maximum_select_fusion.1), channel_id=1, source_target_pairs={{0,64},{8,72},{16,80},{24,88},{32,96},{40,104},{48,112},{56,120},{... | collective-permute-start | bytes 6152 | tf_op jit(solution)/shard_map/ppermute | solution.py:83
  270.9 1.1 constant_dynamic-update-slice_fusion
  272.4 3.4 %gather_fusion = f32[512]{0:T(512)} fusion(f32[1024]{0:T(1024)S(1)} %maximum_select_fusion, s32[1024]{0:T(1024)S(1)} %pad_clamp_fusion), kind=kCustom, calls=%fused_computation | custom fusion | bytes 6144 | tf_op jit(solution)/shard_map/gather | solution.py:87
  275.8 33.8 %select_add_fusion = f32[1024,2048]{1,0:T(8,128)} fusion(f32[2048]{0:T(1024)S(1)} %copy-done.5, s32[2048]{0:T(1024)S(1)} %iota_add_fusion, s32[1024]{0:T(1024)S(1)} %iota_add_fusion.1, f32[2048,1024]{1,0:T(8,128)} %constant_dynamic-update-slice_fusion, f32[2048,2048]{1,0:T(8,128)} %all-gather.2.cloned.1.call-done), kind=kOutput, calls=%fused_computation.1 | convolution fusion | flops 25776095232 | bytes 33574912 | tf_op jit(solution)/shard_map/dot_general | solution.py:90
  (59 shorter events, 7.7 us)
Async XLA Ops:
  7.2 150.6 %copy-start = (f32[2048]{0:T(1024)S(1)}, f32[2048]{0:T(1024)}, u32[]{:S(2)}) copy-start(f32[2048]{0:T(1024)} %param.13) | copy-start | bytes 24580
  7.2 170.6 %all-gather.2.cloned.1.call-start = ((), (), s32[]{:S(2)}) async-start(), calls=%async_computation | async-start | bytes 17825792 | tf_op jit(solution)/shard_map/all_gather | solution.py:23
  14.5 143.0 %copy-start.1 = (f32[64,2048]{1,0:T(8,128)S(1)}, f32[64,2048]{1,0:T(8,128)}, u32[]{:S(2)}) copy-start(f32[64,2048]{1,0:T(8,128)} %param.11) | copy-start | bytes 1572868
  14.5 143.0 %copy-start.5 = (f32[2048]{0:T(1024)S(1)}, f32[2048]{0:T(1024)}, u32[]{:S(2)}) copy-start(f32[2048]{0:T(1024)} %param.10) | copy-start | bytes 24580
  14.7 2.0 collective-permute-start.1
  14.9 1.8 collective-permute-start
  22.4 78.5 %collective-permute-start.2 = (f32[256,1024]{1,0:T(8,128)S(1)}, f32[256,1024]{1,0:T(8,128)S(1)}, u32[]{:S(2)}, u32[]{:S(2)}) collective-permute-start(f32[256,1024]{1,0:T(8,128)S(1)} %get-tuple-element.8), channel_id=1, source_target_pairs={{0,2},{2,4},{4,6},{6,7},{7,5},{5,3},{3,1},{1,0},{8,9},{10,8},{12,1... | collective-permute-start | bytes 3145736 | tf_op jit(solution)/shard_map/ppermute | solution.py:58
  100.9 57.5 %copy-start.2 = (f32[256,1024]{1,0:T(8,128)}, f32[256,1024]{1,0:T(8,128)S(1)}, u32[]{:S(2)}) copy-start(f32[256,1024]{1,0:T(8,128)S(1)} %collective-permute-done.2) | copy-start | bytes 3145732
  100.9 38.7 %collective-permute-start.3 = (f32[256,1024]{1,0:T(8,128)S(1)}, f32[256,1024]{1,0:T(8,128)S(1)}, u32[]{:S(2)}, u32[]{:S(2)}) collective-permute-start(f32[256,1024]{1,0:T(8,128)S(1)} %collective-permute-done.2), channel_id=1, source_target_pairs={{0,2},{2,4},{4,6},{6,7},{7,5},{5,3},{3,1},{1,0},{8,9},{10,8},{12,1... | collective-permute-start | bytes 3145736 | tf_op jit(solution)/shard_map/ppermute | solution.py:58
  139.6 38.1 %copy-start.3 = (f32[256,1024]{1,0:T(8,128)}, f32[256,1024]{1,0:T(8,128)S(1)}, u32[]{:S(2)}) copy-start(f32[256,1024]{1,0:T(8,128)S(1)} %collective-permute-done.3) | copy-start | bytes 3145732
  139.6 17.9 %collective-permute-start.4 = (f32[256,1024]{1,0:T(8,128)S(1)}, f32[256,1024]{1,0:T(8,128)}, u32[]{:S(2)}, u32[]{:S(2)}) collective-permute-start(f32[256,1024]{1,0:T(8,128)S(1)} %collective-permute-done.3), channel_id=1, source_target_pairs={{0,2},{2,4},{4,6},{6,7},{7,5},{5,3},{3,1},{1,0},{8,9},{10,8},{12,1... | collective-permute-start | bytes 3145736 | tf_op jit(solution)/shard_map/ppermute | solution.py:58
  157.5 16.6 %collective-permute-start.5 = (f32[256,1024]{1,0:T(8,128)}, f32[256,1024]{1,0:T(8,128)}, u32[]{:S(2)}, u32[]{:S(2)}) collective-permute-start(f32[256,1024]{1,0:T(8,128)} %collective-permute-done.4), channel_id=1, source_target_pairs={{0,2},{2,4},{4,6},{6,7},{7,5},{5,3},{3,1},{1,0},{8,9},{10,8},{12,1... | collective-permute-start | bytes 3145736 | tf_op jit(solution)/shard_map/ppermute | solution.py:58
  158.4 63.3 %copy-start.7 = (s32[8]{0:T(128)S(1)}, s32[8]{0:T(128)}, u32[]{:S(2)}) copy-start(s32[8]{0:T(128)} %constant.102.clone) | copy-start | bytes 100
  158.4 68.5 %copy-start.4 = (s32[8]{0:T(128)S(1)}, s32[8]{0:T(128)}, u32[]{:S(2)}) copy-start(s32[8]{0:T(128)} %constant.101.clone) | copy-start | bytes 100
  158.4 73.8 %copy-start.6 = (s32[512]{0:T(512)S(1)}, s32[512]{0:T(512)}, u32[]{:S(2)}) copy-start(s32[512]{0:T(512)} %param.12) | copy-start | bytes 6148
  174.1 47.4 %collective-permute-start.6 = (f32[256,1024]{1,0:T(8,128)}, f32[256,1024]{1,0:T(8,128)S(1)}, u32[]{:S(2)}, u32[]{:S(2)}) collective-permute-start(f32[256,1024]{1,0:T(8,128)} %collective-permute-done.5), channel_id=1, source_target_pairs={{0,2},{2,4},{4,6},{6,7},{7,5},{5,3},{3,1},{1,0},{8,9},{10,8},{12,1... | collective-permute-start | bytes 3145736 | tf_op jit(solution)/shard_map/ppermute | solution.py:58
  189.1 26.6 %collective-permute-start.9 = (f32[2050,64]{0,1:T(8,128)S(1)}, f32[2050,64]{0,1:T(8,128)S(1)}, u32[]{:S(2)}, u32[]{:S(2)}) collective-permute-start(f32[2050,64]{0,1:T(8,128)S(1)} %concatenate.31), channel_id=1, source_target_pairs={{0,4},{1,5},{2,6},{3,7},{4,0},{5,1},{6,2},{7,3},{8,12},{9,13},{10,... | collective-permute-start | bytes 1574408 | tf_op jit(solution)/shard_map/ppermute | solution.py:72
  215.7 19.2 %collective-permute-start.10 = (f32[2050,64]{0,1:T(8,128)S(1)}, f32[2050,64]{0,1:T(8,128)S(1)}, u32[]{:S(2)}, u32[]{:S(2)}) collective-permute-start(f32[2050,64]{0,1:T(8,128)S(1)} %add.158), channel_id=1, source_target_pairs={{0,2},{1,3},{2,0},{3,1},{4,6},{5,7},{6,4},{7,5},{8,10},{9,11},{10,... | collective-permute-start | bytes 1574408 | tf_op jit(solution)/shard_map/ppermute | solution.py:72
  221.5 23.4 %collective-permute-start.7 = (f32[256,1024]{1,0:T(8,128)S(1)}, f32[256,1024]{1,0:T(8,128)S(1)}, u32[]{:S(2)}, u32[]{:S(2)}) collective-permute-start(f32[256,1024]{1,0:T(8,128)S(1)} %collective-permute-done.6), channel_id=1, source_target_pairs={{0,2},{2,4},{4,6},{6,7},{7,5},{5,3},{3,1},{1,0},{8,9},{10,8},{12,1... | collective-permute-start | bytes 3145736 | tf_op jit(solution)/shard_map/ppermute | solution.py:58
  235.0 15.2 %collective-permute-start.11 = (f32[2050,64]{0,1:T(8,128)S(1)}, f32[2050,64]{0,1:T(8,128)S(1)}, u32[]{:S(2)}, u32[]{:S(2)}) collective-permute-start(f32[2050,64]{0,1:T(8,128)S(1)} %add.159), channel_id=1, source_target_pairs={{0,1},{1,0},{2,3},{3,2},{4,5},{5,4},{6,7},{7,6},{8,9},{9,8},{10,11... | collective-permute-start | bytes 1574408 | tf_op jit(solution)/shard_map/ppermute | solution.py:72
  244.9 25.9 %collective-permute-start.8 = (f32[256,1024]{1,0:T(8,128)S(1)}, f32[256,1024]{1,0:T(8,128)S(1)}, u32[]{:S(2)}, u32[]{:S(2)}) collective-permute-start(f32[256,1024]{1,0:T(8,128)S(1)} %collective-permute-done.7), channel_id=1, source_target_pairs={{0,2},{2,4},{4,6},{6,7},{7,5},{5,3},{3,1},{1,0},{8,9},{10,8},{12,1... | collective-permute-start | bytes 3145736 | tf_op jit(solution)/shard_map/ppermute | solution.py:58
  250.6 2.7 collective-permute-start.12
  253.3 3.6 %collective-permute-start.13 = (f32[128]{0:T(128)S(1)}, f32[128]{0:T(128)S(1)}, u32[]{:S(2)}, u32[]{:S(2)}) collective-permute-start(f32[128]{0:T(128)S(1)} %broadcast_select_fusion.1), channel_id=1, source_target_pairs={{0,16},{8,24},{16,0},{24,8},{32,48},{40,56},{48,32},{56,40},{64,80... | collective-permute-start | bytes 1544 | tf_op jit(solution)/shard_map/ppermute | solution.py:83
  256.9 10.5 %collective-permute-start.14 = (f32[256]{0:T(256)S(1)}, f32[256]{0:T(256)S(1)}, u32[]{:S(2)}, u32[]{:S(2)}) collective-permute-start(f32[256]{0:T(256)S(1)} %maximum_select_fusion.2), channel_id=1, source_target_pairs={{0,32},{8,40},{16,48},{24,56},{32,0},{40,8},{48,16},{56,24},{64,96... | collective-permute-start | bytes 3080 | tf_op jit(solution)/shard_map/ppermute | solution.py:83
  267.4 5.0 %collective-permute-start.15 = (f32[512]{0:T(512)S(1)}, f32[512]{0:T(512)S(1)}, u32[]{:S(2)}, u32[]{:S(2)}) collective-permute-start(f32[512]{0:T(512)S(1)} %maximum_select_fusion.1), channel_id=1, source_target_pairs={{0,64},{8,72},{16,80},{24,88},{32,96},{40,104},{48,112},{56,120},{... | collective-permute-start | bytes 6152 | tf_op jit(solution)/shard_map/ppermute | solution.py:83
Sparse Core Ops, SparseCore 0:
  11.6 162.0 all-gather.1

commit v17 on v16

--- a/solution.py
+++ b/solution.py
@@ -51,11 +51,14 @@
     ring_tab = jnp.array(ring, jnp.int32)
     me = jnp.array(where_in_ring, jnp.int32)[col_pos]
     way = 1 - 2 * (row_pos % 2)
-    row_all = jnp.zeros((n_col * block_rows, width_row), jnp.float32)
-    row_all = lax.dynamic_update_slice_in_dim(row_all, row_block, col_pos * block_rows, 0)
     held = row_block
     for k in range(1, n_col):
         held = lax.ppermute(held, ("row", "col"), pairs)
+        if k == 1:
+            row_all, held = lax.optimization_barrier(
+                (jnp.zeros((n_col * block_rows, width_row), jnp.float32), held)
+            )
+            row_all = lax.dynamic_update_slice_in_dim(row_all, row_block, col_pos * block_rows, 0)
         came_from = ring_tab[(me - k * way) % n_col]
         row_all = lax.dynamic_update_slice_in_dim(row_all, held, came_from * block_rows, 0)
 

time: 319 us -> 318 us (level)
  waiting for transfers between devices: 130 us -> 144 us
  starting transfers between devices: 85.7 us -> 79 us
  local copies, waits for them, and re-layouts: 26.5 us -> 20.2 us
    ppermute x3, waiting for transfers between devices: 16.4 us -> 27.3 us  [body(): packed = packed + lax.ppermute(packed, 'col', pairs)]
    ppermute x4, starting transfers between devices: 12.7 us -> 2.21 us  [body(): other = lax.ppermute(held, 'row', pairs)]
    dynamic_update_slice x7, local copies, waits for them, and re-layouts: 12.7 us -> 4.33 us  [body(): lax.dynamic_update_slice_in_dim(row_all, held, came_from * block_rows, 0)]
    unnamed x18 -> x28, local copies, waits for them, and re-layouts: 0.24 us -> 5.47 us
    ppermute x3, starting transfers between devices: 22.3 us -> 25.5 us  [body(): packed = packed + lax.ppermute(packed, 'col', pairs)]
    broadcast_in_dim x1, local copies, waits for them, and re-layouts: 4.31 us -> 1.05 us  [body(): jnp.zeros((n_col * block_rows, width_row), jnp.float32)]
  transfers between devices with their start and end apart: 17 -> 17, of which waited for: 12 -> 11; matrix products, arithmetic and copies ran while one was open for 11% -> 8% of each run, Pallas kernels for 0% -> 0%
where the time goes in v17:
time: 318 us; the launch traced here: 317 us
  waiting for transfers between devices  144 us (45%)
  starting transfers between devices  79 us (25%)
  matrix products  45.7 us (14%)
  between operations  23.6 us (7%)
  local copies, waits for them, and re-layouts  20.2 us (6%)
  other arithmetic  4.99 us (2%)
    ppermute x7, waiting for transfers between devices, body(): held = lax.ppermute(held, ('row', 'col'), pairs)  108 us
    ppermute x7, starting transfers between devices, body(): held = lax.ppermute(held, ('row', 'col'), pairs)  50.4 us
    dot_general x1, matrix products, body(): lax.dot_general(row_all, col_all, contract, precision=high, preferred_ele...  33.8 us
    ppermute x3, waiting for transfers between devices, body(): packed = packed + lax.ppermute(packed, 'col', pairs)  27.3 us
    ppermute x3, starting transfers between devices, body(): packed = packed + lax.ppermute(packed, 'col', pairs)  25.5 us
    dot_general x1, matrix products, body(): lax.dot_general(col_all, items, (((1,), (1,)), ((), ())), precision=high,...  11.3 us
  transfers between devices with their start and end apart: 17, of which 11 were waited for; matrix products, arithmetic and copies ran while one was open for 8% of the time, Pallas kernels for 0%

profile of v17, /device:TPU:0, one launch (start us, length us, event | category | flops | bytes accessed | tf_op | source)
XLA Modules:
  0.0 317.2 jit_solution(11280223385281742680)
XLA Ops:
  7.3 1.3 dynamic_slice.33
  9.2 2.3 broadcast_select_fusion
  11.6 2.1 reshape.26
  15.6 1.1 collective-permute-done.1
  16.9 43.8 %collective-permute-start.2 = (f32[256,1024]{1,0:T(8,128)S(1)}, f32[256,1024]{1,0:T(8,128)S(1)}, u32[]{:S(2)}, u32[]{:S(2)}) collective-permute-start(f32[256,1024]{1,0:T(8,128)S(1)} %pad_maximum_fusion), channel_id=1, source_target_pairs={{0,2},{2,4},{4,6},{6,7},{7,5},{5,3},{3,1},{1,0},{8,9},{10,8},{12,1... | collective-permute-start | bytes 3145736 | tf_op jit(solution)/shard_map/ppermute | solution.py:56
  60.7 31.5 %collective-permute-done.2 = f32[256,1024]{1,0:T(8,128)S(1)} collective-permute-done((f32[256,1024]{1,0:T(8,128)S(1)}, f32[256,1024]{1,0:T(8,128)S(1)}, u32[]{:S(2)}, u32[]{:S(2)}) %collective-permute-start.2) | collective-permute-done | bytes 1048608 | tf_op jit(solution)/shard_map/ppermute | solution.py:56
  92.2 1.0 copy-done.3
  93.2 38.5 %collective-permute-done.3 = f32[256,1024]{1,0:T(8,128)S(1)} collective-permute-done((f32[256,1024]{1,0:T(8,128)S(1)}, f32[256,1024]{1,0:T(8,128)S(1)}, u32[]{:S(2)}, u32[]{:S(2)}) %collective-permute-start.3) | collective-permute-done | bytes 1048608 | tf_op jit(solution)/shard_map/ppermute | solution.py:56
  131.7 1.0 copy-done.5
  132.7 22.1 %collective-permute-done.4 = f32[256,1024]{1,0:T(8,128)S(1)} collective-permute-done((f32[256,1024]{1,0:T(8,128)S(1)}, f32[256,1024]{1,0:T(8,128)S(1)}, u32[]{:S(2)}, u32[]{:S(2)}) %collective-permute-start.4) | collective-permute-done | bytes 1048608 | tf_op jit(solution)/shard_map/ppermute | solution.py:56
  155.7 15.5 %collective-permute-done.5 = f32[256,1024]{1,0:T(8,128)} collective-permute-done((f32[256,1024]{1,0:T(8,128)S(1)}, f32[256,1024]{1,0:T(8,128)}, u32[]{:S(2)}, u32[]{:S(2)}) %collective-permute-start.5) | collective-permute-done | bytes 1048608 | tf_op jit(solution)/shard_map/ppermute | solution.py:56
  171.2 2.2 collective-permute-start.6
  173.5 2.0 all-gather.2.cloned.1.call-done
  175.5 11.3 %fusion.3 = f32[2048,64]{0,1:T(8,128)S(1)} fusion(f32[2048,2048]{1,0:T(8,128)} %all-gather.2.cloned.1.call-done, f32[64,2048]{1,0:T(8,128)S(1)} %copy-done.2), kind=kOutput, calls=%fused_computation.35 | convolution fusion | flops 1610612736 | bytes 17825792 | tf_op jit(solution)/shard_map/dot_general | solution.py:65
  186.8 17.6 %collective-permute-start.9 = (f32[2050,64]{0,1:T(8,128)S(1)}, f32[2050,64]{0,1:T(8,128)}, u32[]{:S(2)}, u32[]{:S(2)}) collective-permute-start(f32[2050,64]{0,1:T(8,128)S(1)} %concatenate.31), channel_id=1, source_target_pairs={{0,4},{1,5},{2,6},{3,7},{4,0},{5,1},{6,2},{7,3},{8,12},{9,13},{10,... | collective-permute-start | bytes 1574408 | tf_op jit(solution)/shard_map/ppermute | solution.py:75
  204.4 3.5 %collective-permute-start.7 = (f32[256,1024]{1,0:T(8,128)}, f32[256,1024]{1,0:T(8,128)}, u32[]{:S(2)}, u32[]{:S(2)}) collective-permute-start(f32[256,1024]{1,0:T(8,128)} %collective-permute-done.6), channel_id=1, source_target_pairs={{0,2},{2,4},{4,6},{6,7},{7,5},{5,3},{3,1},{1,0},{8,9},{10,8},{12,1... | collective-permute-start | bytes 3145736 | tf_op jit(solution)/shard_map/ppermute | solution.py:56
  207.9 7.3 %collective-permute-done.9 = f32[2050,64]{0,1:T(8,128)} collective-permute-done((f32[2050,64]{0,1:T(8,128)S(1)}, f32[2050,64]{0,1:T(8,128)}, u32[]{:S(2)}, u32[]{:S(2)}) %collective-permute-start.9) | collective-permute-done | bytes 524832 | tf_op jit(solution)/shard_map/ppermute | solution.py:75
  215.2 1.2 add.158
  216.4 6.3 %collective-permute-start.10 = (f32[2050,64]{0,1:T(8,128)S(1)}, f32[2050,64]{0,1:T(8,128)S(1)}, u32[]{:S(2)}, u32[]{:S(2)}) collective-permute-start(f32[2050,64]{0,1:T(8,128)S(1)} %add.158), channel_id=1, source_target_pairs={{0,2},{1,3},{2,0},{3,1},{4,6},{5,7},{6,4},{7,5},{8,10},{9,11},{10,... | collective-permute-start | bytes 1574408 | tf_op jit(solution)/shard_map/ppermute | solution.py:75
  233.2 7.4 %collective-permute-done.10 = f32[2050,64]{0,1:T(8,128)S(1)} collective-permute-done((f32[2050,64]{0,1:T(8,128)S(1)}, f32[2050,64]{0,1:T(8,128)S(1)}, u32[]{:S(2)}, u32[]{:S(2)}) %collective-permute-start.10) | collective-permute-done | bytes 524832 | tf_op jit(solution)/shard_map/ppermute | solution.py:75
  240.7 1.7 collective-permute-start.11
  242.4 1.1 broadcast_in_dim.46
  244.9 12.5 %collective-permute-done.11 = f32[2050,64]{0,1:T(8,128)S(1)} collective-permute-done((f32[2050,64]{0,1:T(8,128)S(1)}, f32[2050,64]{0,1:T(8,128)S(1)}, u32[]{:S(2)}, u32[]{:S(2)}) %collective-permute-start.11) | collective-permute-done | bytes 524832 | tf_op jit(solution)/shard_map/ppermute | solution.py:75
  258.1 1.3 constant_dynamic-update-slice_fusion.3
  259.5 1.3 constant_dynamic-update-slice_fusion.2
  260.8 2.2 collective-permute-done.13
  263.4 1.3 constant_dynamic-update-slice_fusion.1
  264.7 3.4 %collective-permute-done.14 = f32[256]{0:T(256)S(1)} collective-permute-done((f32[256]{0:T(256)S(1)}, f32[256]{0:T(256)S(1)}, u32[]{:S(2)}, u32[]{:S(2)}) %collective-permute-start.14) | collective-permute-done | bytes 1056 | tf_op jit(solution)/shard_map/ppermute | solution.py:86
  268.1 1.6 collective-permute-start.15
  269.8 3.2 %copy-done.1 = f32[2048,1024]{1,0:T(8,128)} copy-done((f32[2048,1024]{1,0:T(8,128)}, f32[2048,1024]{1,0:T(8,128)S(1)}, u32[]{:S(2)}) %copy-start.1) | copy-done | bytes 8388632
  273.0 3.4 %gather_fusion = f32[512]{0:T(512)} fusion(f32[1024]{0:T(1024)S(1)} %maximum_select_fusion, s32[1024]{0:T(1024)S(1)} %pad_clamp_fusion), kind=kCustom, calls=%fused_computation | custom fusion | bytes 6144 | tf_op jit(solution)/shard_map/gather | solution.py:90
  276.5 33.8 %select_add_fusion = f32[1024,2048]{1,0:T(8,128)} fusion(f32[2048]{0:T(1024)S(1)} %copy-done.10, s32[2048]{0:T(1024)S(1)} %iota_add_fusion, s32[1024]{0:T(1024)S(1)} %iota_add_fusion.1, f32[2048,1024]{1,0:T(8,128)} %copy-done.1, f32[2048,2048]{1,0:T(8,128)} %all-gather.2.cloned.1.call-done), kind=kOutput, calls=%fused_computation.1 | convolution fusion | flops 25776095232 | bytes 33574912 | tf_op jit(solution)/shard_map/dot_general | solution.py:93
  (70 shorter events, 7.7 us)
Async XLA Ops:
  7.2 147.9 %copy-start = (f32[2048]{0:T(1024)S(1)}, f32[2048]{0:T(1024)}, u32[]{:S(2)}) copy-start(f32[2048]{0:T(1024)} %param.13) | copy-start | bytes 24580
  7.2 147.7 %copy-start.10 = (f32[2048]{0:T(1024)S(1)}, f32[2048]{0:T(1024)}, u32[]{:S(2)}) copy-start(f32[2048]{0:T(1024)} %param.10) | copy-start | bytes 24580
  7.2 147.7 %copy-start.2 = (f32[64,2048]{1,0:T(8,128)S(1)}, f32[64,2048]{1,0:T(8,128)}, u32[]{:S(2)}) copy-start(f32[64,2048]{1,0:T(8,128)} %param.11) | copy-start | bytes 1572868
  7.2 168.3 %all-gather.2.cloned.1.call-start = ((), (), s32[]{:S(2)}) async-start(), calls=%async_computation | async-start | bytes 17825792 | tf_op jit(solution)/shard_map/all_gather | solution.py:23
  14.7 2.0 collective-permute-start.1
  14.9 1.8 collective-permute-start
  16.9 75.3 %collective-permute-start.2 = (f32[256,1024]{1,0:T(8,128)S(1)}, f32[256,1024]{1,0:T(8,128)S(1)}, u32[]{:S(2)}, u32[]{:S(2)}) collective-permute-start(f32[256,1024]{1,0:T(8,128)S(1)} %pad_maximum_fusion), channel_id=1, source_target_pairs={{0,2},{2,4},{4,6},{6,7},{7,5},{5,3},{3,1},{1,0},{8,9},{10,8},{12,1... | collective-permute-start | bytes 3145736 | tf_op jit(solution)/shard_map/ppermute | solution.py:56
  92.2 1.0 copy-start.3
  93.2 38.5 %collective-permute-start.3 = (f32[256,1024]{1,0:T(8,128)S(1)}, f32[256,1024]{1,0:T(8,128)S(1)}, u32[]{:S(2)}, u32[]{:S(2)}) collective-permute-start(f32[256,1024]{1,0:T(8,128)S(1)} %collective-permute-done.2), channel_id=1, source_target_pairs={{0,2},{2,4},{4,6},{6,7},{7,5},{5,3},{3,1},{1,0},{8,9},{10,8},{12,1... | collective-permute-start | bytes 3145736 | tf_op jit(solution)/shard_map/ppermute | solution.py:56
  131.7 1.0 copy-start.5
  132.7 22.1 %collective-permute-start.4 = (f32[256,1024]{1,0:T(8,128)S(1)}, f32[256,1024]{1,0:T(8,128)S(1)}, u32[]{:S(2)}, u32[]{:S(2)}) collective-permute-start(f32[256,1024]{1,0:T(8,128)S(1)} %collective-permute-done.3), channel_id=1, source_target_pairs={{0,2},{2,4},{4,6},{6,7},{7,5},{5,3},{3,1},{1,0},{8,9},{10,8},{12,1... | collective-permute-start | bytes 3145736 | tf_op jit(solution)/shard_map/ppermute | solution.py:56
  154.8 18.6 %copy-start.7 = (f32[256,1024]{1,0:T(8,128)}, f32[256,1024]{1,0:T(8,128)S(1)}, u32[]{:S(2)}) copy-start(f32[256,1024]{1,0:T(8,128)S(1)} %collective-permute-done.4) | copy-start | bytes 3145732
  154.8 16.4 %collective-permute-start.5 = (f32[256,1024]{1,0:T(8,128)S(1)}, f32[256,1024]{1,0:T(8,128)}, u32[]{:S(2)}, u32[]{:S(2)}) collective-permute-start(f32[256,1024]{1,0:T(8,128)S(1)} %collective-permute-done.4), channel_id=1, source_target_pairs={{0,2},{2,4},{4,6},{6,7},{7,5},{5,3},{3,1},{1,0},{8,9},{10,8},{12,1... | collective-permute-start | bytes 3145736 | tf_op jit(solution)/shard_map/ppermute | solution.py:56
  155.7 67.0 %copy-start.12 = (s32[8]{0:T(128)S(1)}, s32[8]{0:T(128)}, u32[]{:S(2)}) copy-start(s32[8]{0:T(128)} %constant.102.clone) | copy-start | bytes 100
  155.7 72.2 %copy-start.9 = (s32[8]{0:T(128)S(1)}, s32[8]{0:T(128)}, u32[]{:S(2)}) copy-start(s32[8]{0:T(128)} %constant.101.clone) | copy-start | bytes 100
  155.7 77.4 %copy-start.11 = (s32[512]{0:T(512)S(1)}, s32[512]{0:T(512)}, u32[]{:S(2)}) copy-start(s32[512]{0:T(512)} %param.12) | copy-start | bytes 6148
  171.2 33.1 %collective-permute-start.6 = (f32[256,1024]{1,0:T(8,128)}, f32[256,1024]{1,0:T(8,128)}, u32[]{:S(2)}, u32[]{:S(2)}) collective-permute-start(f32[256,1024]{1,0:T(8,128)} %collective-permute-done.5), channel_id=1, source_target_pairs={{0,2},{2,4},{4,6},{6,7},{7,5},{5,3},{3,1},{1,0},{8,9},{10,8},{12,1... | collective-permute-start | bytes 3145736 | tf_op jit(solution)/shard_map/ppermute | solution.py:56
  186.8 56.7 %copy-start.4 = (f32[256,1024]{1,0:T(8,128)S(1)}, f32[256,1024]{1,0:T(8,128)}, u32[]{:S(2)}) copy-start(f32[256,1024]{1,0:T(8,128)} %copy-done.3) | copy-start | bytes 3145732
  186.8 28.4 %collective-permute-start.9 = (f32[2050,64]{0,1:T(8,128)S(1)}, f32[2050,64]{0,1:T(8,128)}, u32[]{:S(2)}, u32[]{:S(2)}) collective-permute-start(f32[2050,64]{0,1:T(8,128)S(1)} %concatenate.31), channel_id=1, source_target_pairs={{0,4},{1,5},{2,6},{3,7},{4,0},{5,1},{6,2},{7,3},{8,12},{9,13},{10,... | collective-permute-start | bytes 1574408 | tf_op jit(solution)/shard_map/ppermute | solution.py:75
  204.4 39.6 %collective-permute-start.7 = (f32[256,1024]{1,0:T(8,128)}, f32[256,1024]{1,0:T(8,128)}, u32[]{:S(2)}, u32[]{:S(2)}) collective-permute-start(f32[256,1024]{1,0:T(8,128)} %collective-permute-done.6), channel_id=1, source_target_pairs={{0,2},{2,4},{4,6},{6,7},{7,5},{5,3},{3,1},{1,0},{8,9},{10,8},{12,1... | collective-permute-start | bytes 3145736 | tf_op jit(solution)/shard_map/ppermute | solution.py:56
  216.4 24.2 %collective-permute-start.10 = (f32[2050,64]{0,1:T(8,128)S(1)}, f32[2050,64]{0,1:T(8,128)S(1)}, u32[]{:S(2)}, u32[]{:S(2)}) collective-permute-start(f32[2050,64]{0,1:T(8,128)S(1)} %add.158), channel_id=1, source_target_pairs={{0,2},{1,3},{2,0},{3,1},{4,6},{5,7},{6,4},{7,5},{8,10},{9,11},{10,... | collective-permute-start | bytes 1574408 | tf_op jit(solution)/shard_map/ppermute | solution.py:75
  233.1 10.6 %copy-start.6 = (f32[256,1024]{1,0:T(8,128)S(1)}, f32[256,1024]{1,0:T(8,128)}, u32[]{:S(2)}) copy-start(f32[256,1024]{1,0:T(8,128)} %copy-done.5) | copy-start | bytes 3145732
  233.1 10.7 %copy-start.8 = (f32[256,1024]{1,0:T(8,128)S(1)}, f32[256,1024]{1,0:T(8,128)}, u32[]{:S(2)}) copy-start(f32[256,1024]{1,0:T(8,128)} %copy-done.7) | copy-start | bytes 3145732
  240.7 16.7 %collective-permute-start.11 = (f32[2050,64]{0,1:T(8,128)S(1)}, f32[2050,64]{0,1:T(8,128)S(1)}, u32[]{:S(2)}, u32[]{:S(2)}) collective-permute-start(f32[2050,64]{0,1:T(8,128)S(1)} %add.159), channel_id=1, source_target_pairs={{0,1},{1,0},{2,3},{3,2},{4,5},{5,4},{6,7},{7,6},{8,9},{9,8},{10,11... | collective-permute-start | bytes 1574408 | tf_op jit(solution)/shard_map/ppermute | solution.py:75
  244.0 25.7 %collective-permute-start.8 = (f32[256,1024]{1,0:T(8,128)}, f32[256,1024]{1,0:T(8,128)S(1)}, u32[]{:S(2)}, u32[]{:S(2)}) collective-permute-start(f32[256,1024]{1,0:T(8,128)} %collective-permute-done.7), channel_id=1, source_target_pairs={{0,2},{2,4},{4,6},{6,7},{7,5},{5,3},{3,1},{1,0},{8,9},{10,8},{12,1... | collective-permute-start | bytes 3145736 | tf_op jit(solution)/shard_map/ppermute | solution.py:56
  257.8 1.6 collective-permute-start.12
  259.5 3.6 %collective-permute-start.13 = (f32[128]{0:T(128)S(1)}, f32[128]{0:T(128)S(1)}, u32[]{:S(2)}, u32[]{:S(2)}) collective-permute-start(f32[128]{0:T(128)S(1)} %broadcast_select_fusion.1), channel_id=1, source_target_pairs={{0,16},{8,24},{16,0},{24,8},{32,48},{40,56},{48,32},{56,40},{64,80... | collective-permute-start | bytes 1544 | tf_op jit(solution)/shard_map/ppermute | solution.py:86
  263.1 5.1 %collective-permute-start.14 = (f32[256]{0:T(256)S(1)}, f32[256]{0:T(256)S(1)}, u32[]{:S(2)}, u32[]{:S(2)}) collective-permute-start(f32[256]{0:T(256)S(1)} %maximum_select_fusion.2), channel_id=1, source_target_pairs={{0,32},{8,40},{16,48},{24,56},{32,0},{40,8},{48,16},{56,24},{64,96... | collective-permute-start | bytes 3080 | tf_op jit(solution)/shard_map/ppermute | solution.py:86
  268.1 4.9 %collective-permute-start.15 = (f32[512]{0:T(512)S(1)}, f32[512]{0:T(512)S(1)}, u32[]{:S(2)}, u32[]{:S(2)}) collective-permute-start(f32[512]{0:T(512)S(1)} %maximum_select_fusion.1), channel_id=1, source_target_pairs={{0,64},{8,72},{16,80},{24,88},{32,96},{40,104},{48,112},{56,120},{... | collective-permute-start | bytes 6152 | tf_op jit(solution)/shard_map/ppermute | solution.py:86
  269.8 3.2 %copy-start.1 = (f32[2048,1024]{1,0:T(8,128)}, f32[2048,1024]{1,0:T(8,128)S(1)}, u32[]{:S(2)}) copy-start(f32[2048,1024]{1,0:T(8,128)S(1)} %constant_dynamic-update-slice_fusion) | copy-start | bytes 25165828
Sparse Core Ops, SparseCore 0:
  11.7 163.7 all-gather.1

commit v18 on v17

--- a/solution.py
+++ b/solution.py
@@ -87,7 +87,8 @@
         low = (row_pos & step) == 0
         held = jnp.where(low, jnp.concatenate([held, other]), jnp.concatenate([other, held]))
         step *= 2
-    scores = held[cand_ids]
+    pick = cand_ids[:, None] == lax.broadcasted_iota(jnp.int32, (cand_ids.shape[0], held.shape[0]), 1)
+    scores = jnp.sum(jnp.where(pick, held[None, :], jnp.float32(0.0)), axis=1)
     row_all, scores = lax.optimization_barrier((row_all, scores))
     contract = (((0,), (0,)), ((), ()))
     tile = lax.dot_general(

time: 318 us -> 314 us (0.987)
  local copies, waits for them, and re-layouts: 20.2 us -> 12.4 us
  starting transfers between devices: 79 us -> 86.7 us
  waiting for transfers between devices: 144 us -> 140 us
    ppermute x4, starting transfers between devices: 2.21 us -> 12.6 us  [body(): other = lax.ppermute(held, 'row', pairs)]
    ppermute x3, waiting for transfers between devices: 27.3 us -> 17.6 us  [body(): packed = packed + lax.ppermute(packed, 'col', pairs)]
    ppermute x7, waiting for transfers between devices: 108 us -> 114 us  [body(): held = lax.ppermute(held, ('row', 'col'), pairs)]
    gather x1 -> x0, local copies, waits for them, and re-layouts: 3.42 us -> none  [body(): scores = held[cand_ids]]
    unnamed x28 -> x26, local copies, waits for them, and re-layouts: 5.47 us -> 2.21 us
  transfers between devices with their start and end apart: 17 -> 17, of which waited for: 11 -> 13; matrix products, arithmetic and copies ran while one was open for 8% -> 7% of each run, Pallas kernels for 0% -> 0%
where the time goes in v18:
time: 314 us; the launch traced here: 312 us
  waiting for transfers between devices  140 us (45%)
  starting transfers between devices  86.7 us (28%)
  matrix products  43.8 us (14%)
  between operations  23.7 us (8%)
  local copies, waits for them, and re-layouts  12.4 us (4%)
  other arithmetic  6.01 us (2%)
    ppermute x7, waiting for transfers between devices, body(): held = lax.ppermute(held, ('row', 'col'), pairs)  114 us
    ppermute x7, starting transfers between devices, body(): held = lax.ppermute(held, ('row', 'col'), pairs)  48.8 us
    dot_general x1, matrix products, body(): lax.dot_general(row_all, col_all, contract, precision=high, preferred_ele...  32 us
    ppermute x3, starting transfers between devices, body(): packed = packed + lax.ppermute(packed, 'col', pairs)  24.5 us
    ppermute x3, waiting for transfers between devices, body(): packed = packed + lax.ppermute(packed, 'col', pairs)  17.6 us
    ppermute x4, starting transfers between devices, body(): other = lax.ppermute(held, 'row', pairs)  12.6 us
    dot_general x1, matrix products, body(): lax.dot_general(col_all, items, (((1,), (1,)), ((), ())), precision=high,...  11.3 us
  transfers between devices with their start and end apart: 17, of which 13 were waited for; matrix products, arithmetic and copies ran while one was open for 7% of the time, Pallas kernels for 0%

profile of v18, /device:TPU:0, one launch (start us, length us, event | category | flops | bytes accessed | tf_op | source)
XLA Modules:
  0.0 312.0 jit_solution(4480240077801488830)
XLA Ops:
  7.3 1.3 dynamic_slice.33
  9.2 2.3 broadcast_select_fusion
  11.6 2.1 reshape.72
  15.6 1.1 collective-permute-done.1
  17.0 43.8 %collective-permute-start.2 = (f32[256,1024]{1,0:T(8,128)S(1)}, f32[256,1024]{1,0:T(8,128)S(1)}, u32[]{:S(2)}, u32[]{:S(2)}) collective-permute-start(f32[256,1024]{1,0:T(8,128)S(1)} %pad_maximum_fusion), channel_id=1, source_target_pairs={{0,2},{2,4},{4,6},{6,7},{7,5},{5,3},{3,1},{1,0},{8,9},{10,8},{12,1... | collective-permute-start | bytes 3145736 | tf_op jit(solution)/shard_map/ppermute | solution.py:56
  60.8 31.4 %collective-permute-done.2 = f32[256,1024]{1,0:T(8,128)S(1)} collective-permute-done((f32[256,1024]{1,0:T(8,128)S(1)}, f32[256,1024]{1,0:T(8,128)S(1)}, u32[]{:S(2)}, u32[]{:S(2)}) %collective-permute-start.2) | collective-permute-done | bytes 1048608 | tf_op jit(solution)/shard_map/ppermute | solution.py:56
  92.2 1.0 copy-done.2
  93.2 38.5 %collective-permute-done.3 = f32[256,1024]{1,0:T(8,128)S(1)} collective-permute-done((f32[256,1024]{1,0:T(8,128)S(1)}, f32[256,1024]{1,0:T(8,128)S(1)}, u32[]{:S(2)}, u32[]{:S(2)}) %collective-permute-start.3) | collective-permute-done | bytes 1048608 | tf_op jit(solution)/shard_map/ppermute | solution.py:56
  131.7 1.0 copy-done.4
  132.7 22.1 %collective-permute-done.4 = f32[256,1024]{1,0:T(8,128)S(1)} collective-permute-done((f32[256,1024]{1,0:T(8,128)S(1)}, f32[256,1024]{1,0:T(8,128)S(1)}, u32[]{:S(2)}, u32[]{:S(2)}) %collective-permute-start.4) | collective-permute-done | bytes 1048608 | tf_op jit(solution)/shard_map/ppermute | solution.py:56
  155.7 15.5 %collective-permute-done.5 = f32[256,1024]{1,0:T(8,128)} collective-permute-done((f32[256,1024]{1,0:T(8,128)S(1)}, f32[256,1024]{1,0:T(8,128)}, u32[]{:S(2)}, u32[]{:S(2)}) %collective-permute-start.5) | collective-permute-done | bytes 1048608 | tf_op jit(solution)/shard_map/ppermute | solution.py:56
  171.2 2.5 collective-permute-start.6
  173.7 1.7 all-gather.2.cloned.1.call-done
  175.4 11.3 %fusion.3 = f32[2048,64]{0,1:T(8,128)S(1)} fusion(f32[2048,2048]{1,0:T(8,128)} %all-gather.2.cloned.1.call-done, f32[64,2048]{1,0:T(8,128)S(1)} %copy-done.1), kind=kOutput, calls=%fused_computation.34 | convolution fusion | flops 1610612736 | bytes 17825792 | tf_op jit(solution)/shard_map/dot_general | solution.py:65
  186.8 17.6 %collective-permute-start.9 = (f32[2050,64]{0,1:T(8,128)S(1)}, f32[2050,64]{0,1:T(8,128)S(1)}, u32[]{:S(2)}, u32[]{:S(2)}) collective-permute-start(f32[2050,64]{0,1:T(8,128)S(1)} %concatenate.45), channel_id=1, source_target_pairs={{0,4},{1,5},{2,6},{3,7},{4,0},{5,1},{6,2},{7,3},{8,12},{9,13},{10,... | collective-permute-start | bytes 1574408 | tf_op jit(solution)/shard_map/ppermute | solution.py:75
  204.4 10.8 %collective-permute-done.9 = f32[2050,64]{0,1:T(8,128)S(1)} collective-permute-done((f32[2050,64]{0,1:T(8,128)S(1)}, f32[2050,64]{0,1:T(8,128)S(1)}, u32[]{:S(2)}, u32[]{:S(2)}) %collective-permute-start.9) | collective-permute-done | bytes 524832 | tf_op jit(solution)/shard_map/ppermute | solution.py:75
  215.2 6.1 %collective-permute-start.10 = (f32[2050,64]{0,1:T(8,128)S(1)}, f32[2050,64]{0,1:T(8,128)}, u32[]{:S(2)}, u32[]{:S(2)}) collective-permute-start(f32[2050,64]{0,1:T(8,128)S(1)} %add.152), channel_id=1, source_target_pairs={{0,2},{1,3},{2,0},{3,1},{4,6},{5,7},{6,4},{7,5},{8,10},{9,11},{10,... | collective-permute-start | bytes 1574408 | tf_op jit(solution)/shard_map/ppermute | solution.py:75
  232.0 2.8 collective-permute-done.10
  234.9 1.2 add.153
  236.9 1.1 broadcast_in_dim.57
  238.5 6.4 %collective-permute-done.7 = f32[256,1024]{1,0:T(8,128)S(1)} collective-permute-done((f32[256,1024]{1,0:T(8,128)}, f32[256,1024]{1,0:T(8,128)S(1)}, u32[]{:S(2)}, u32[]{:S(2)}) %collective-permute-start.7) | collective-permute-done | bytes 1048608 | tf_op jit(solution)/shard_map/ppermute | solution.py:56
  244.9 2.4 collective-permute-start.8
  247.2 4.0 %collective-permute-done.11 = f32[2050,64]{0,1:T(8,128)S(1)} collective-permute-done((f32[2050,64]{0,1:T(8,128)S(1)}, f32[2050,64]{0,1:T(8,128)S(1)}, u32[]{:S(2)}, u32[]{:S(2)}) %collective-permute-start.11) | collective-permute-done | bytes 524832 | tf_op jit(solution)/shard_map/ppermute | solution.py:75
  251.9 1.3 constant_dynamic-update-slice_fusion.3
  253.3 1.3 constant_dynamic-update-slice_fusion.2
  254.7 2.2 collective-permute-done.13
  256.9 8.8 %collective-permute-start.14 = (f32[256]{0:T(256)S(1)}, f32[256]{0:T(256)S(1)}, u32[]{:S(2)}, u32[]{:S(2)}) collective-permute-start(f32[256]{0:T(256)S(1)} %maximum_select_fusion.2), channel_id=1, source_target_pairs={{0,32},{8,40},{16,48},{24,56},{32,0},{40,8},{48,16},{56,24},{64,96... | collective-permute-start | bytes 3080 | tf_op jit(solution)/shard_map/ppermute | solution.py:86
  265.8 1.4 collective-permute-done.14
  267.2 3.5 %collective-permute-start.15 = (f32[512]{0:T(512)S(1)}, f32[512]{0:T(512)S(1)}, u32[]{:S(2)}, u32[]{:S(2)}) collective-permute-start(f32[512]{0:T(512)S(1)} %maximum_select_fusion.1), channel_id=1, source_target_pairs={{0,64},{8,72},{16,80},{24,88},{32,96},{40,104},{48,112},{56,120},{... | collective-permute-start | bytes 6152 | tf_op jit(solution)/shard_map/ppermute | solution.py:86
  270.9 1.4 collective-permute-done.15
  272.3 0.9 select_reduce_fusion
  273.2 32.0 %select_add_fusion = f32[1024,2048]{1,0:T(8,128)} fusion(f32[2048]{0:T(1024)S(1)} %copy-done.9, s32[2048]{0:T(1024)S(1)} %iota_add_fusion, s32[1024]{0:T(1024)S(1)} %iota_add_fusion.1, f32[2048,1024]{1,0:T(8,128)S(1)} %constant_dynamic-update-slice_fusion, f32[2048,2048]{1,0:T(8,128)} %all-gather.2.cloned.1.call-done), kind=kOutput, calls=%fused_computation | convolution fusion | flops 25776095232 | bytes 33574912 | tf_op jit(solution)/shard_map/dot_general | solution.py:94
  (66 shorter events, 7.6 us)
Async XLA Ops:
  7.2 147.9 %copy-start = (f32[2048]{0:T(1024)S(1)}, f32[2048]{0:T(1024)}, u32[]{:S(2)}) copy-start(f32[2048]{0:T(1024)} %param.13) | copy-start | bytes 24580
  7.2 147.7 %copy-start.9 = (f32[2048]{0:T(1024)S(1)}, f32[2048]{0:T(1024)}, u32[]{:S(2)}) copy-start(f32[2048]{0:T(1024)} %param.10) | copy-start | bytes 24580
  7.2 147.7 %copy-start.1 = (f32[64,2048]{1,0:T(8,128)S(1)}, f32[64,2048]{1,0:T(8,128)}, u32[]{:S(2)}) copy-start(f32[64,2048]{1,0:T(8,128)} %param.11) | copy-start | bytes 1572868
  7.2 168.2 %all-gather.2.cloned.1.call-start = ((), (), s32[]{:S(2)}) async-start(), calls=%async_computation | async-start | bytes 17825792 | tf_op jit(solution)/shard_map/all_gather | solution.py:23
  14.7 2.0 collective-permute-start.1
  14.9 1.8 collective-permute-start
  17.0 75.2 %collective-permute-start.2 = (f32[256,1024]{1,0:T(8,128)S(1)}, f32[256,1024]{1,0:T(8,128)S(1)}, u32[]{:S(2)}, u32[]{:S(2)}) collective-permute-start(f32[256,1024]{1,0:T(8,128)S(1)} %pad_maximum_fusion), channel_id=1, source_target_pairs={{0,2},{2,4},{4,6},{6,7},{7,5},{5,3},{3,1},{1,0},{8,9},{10,8},{12,1... | collective-permute-start | bytes 3145736 | tf_op jit(solution)/shard_map/ppermute | solution.py:56
  92.2 1.0 copy-start.2
  93.2 38.5 %collective-permute-start.3 = (f32[256,1024]{1,0:T(8,128)S(1)}, f32[256,1024]{1,0:T(8,128)S(1)}, u32[]{:S(2)}, u32[]{:S(2)}) collective-permute-start(f32[256,1024]{1,0:T(8,128)S(1)} %collective-permute-done.2), channel_id=1, source_target_pairs={{0,2},{2,4},{4,6},{6,7},{7,5},{5,3},{3,1},{1,0},{8,9},{10,8},{12,1... | collective-permute-start | bytes 3145736 | tf_op jit(solution)/shard_map/ppermute | solution.py:56
  131.7 1.0 copy-start.4
  132.7 22.1 %collective-permute-start.4 = (f32[256,1024]{1,0:T(8,128)S(1)}, f32[256,1024]{1,0:T(8,128)S(1)}, u32[]{:S(2)}, u32[]{:S(2)}) collective-permute-start(f32[256,1024]{1,0:T(8,128)S(1)} %collective-permute-done.3), channel_id=1, source_target_pairs={{0,2},{2,4},{4,6},{6,7},{7,5},{5,3},{3,1},{1,0},{8,9},{10,8},{12,1... | collective-permute-start | bytes 3145736 | tf_op jit(solution)/shard_map/ppermute | solution.py:56
  154.8 18.9 %copy-start.6 = (f32[256,1024]{1,0:T(8,128)}, f32[256,1024]{1,0:T(8,128)S(1)}, u32[]{:S(2)}) copy-start(f32[256,1024]{1,0:T(8,128)S(1)} %collective-permute-done.4) | copy-start | bytes 3145732
  154.8 16.4 %collective-permute-start.5 = (f32[256,1024]{1,0:T(8,128)S(1)}, f32[256,1024]{1,0:T(8,128)}, u32[]{:S(2)}, u32[]{:S(2)}) collective-permute-start(f32[256,1024]{1,0:T(8,128)S(1)} %collective-permute-done.4), channel_id=1, source_target_pairs={{0,2},{2,4},{4,6},{6,7},{7,5},{5,3},{3,1},{1,0},{8,9},{10,8},{12,1... | collective-permute-start | bytes 3145736 | tf_op jit(solution)/shard_map/ppermute | solution.py:56
  155.7 65.8 %copy-start.11 = (s32[8]{0:T(128)S(1)}, s32[8]{0:T(128)}, u32[]{:S(2)}) copy-start(s32[8]{0:T(128)} %constant.100.clone) | copy-start | bytes 100
  155.7 71.0 %copy-start.8 = (s32[8]{0:T(128)S(1)}, s32[8]{0:T(128)}, u32[]{:S(2)}) copy-start(s32[8]{0:T(128)} %constant.99.clone) | copy-start | bytes 100
  171.2 50.1 %collective-permute-start.6 = (f32[256,1024]{1,0:T(8,128)}, f32[256,1024]{1,0:T(8,128)}, u32[]{:S(2)}, u32[]{:S(2)}) collective-permute-start(f32[256,1024]{1,0:T(8,128)} %collective-permute-done.5), channel_id=1, source_target_pairs={{0,2},{2,4},{4,6},{6,7},{7,5},{5,3},{3,1},{1,0},{8,9},{10,8},{12,1... | collective-permute-start | bytes 3145736 | tf_op jit(solution)/shard_map/ppermute | solution.py:56
  186.8 28.4 %collective-permute-start.9 = (f32[2050,64]{0,1:T(8,128)S(1)}, f32[2050,64]{0,1:T(8,128)S(1)}, u32[]{:S(2)}, u32[]{:S(2)}) collective-permute-start(f32[2050,64]{0,1:T(8,128)S(1)} %concatenate.45), channel_id=1, source_target_pairs={{0,4},{1,5},{2,6},{3,7},{4,0},{5,1},{6,2},{7,3},{8,12},{9,13},{10,... | collective-permute-start | bytes 1574408 | tf_op jit(solution)/shard_map/ppermute | solution.py:75
  215.2 19.6 %collective-permute-start.10 = (f32[2050,64]{0,1:T(8,128)S(1)}, f32[2050,64]{0,1:T(8,128)}, u32[]{:S(2)}, u32[]{:S(2)}) collective-permute-start(f32[2050,64]{0,1:T(8,128)S(1)} %add.152), channel_id=1, source_target_pairs={{0,2},{1,3},{2,0},{3,1},{4,6},{5,7},{6,4},{7,5},{8,10},{9,11},{10,... | collective-permute-start | bytes 1574408 | tf_op jit(solution)/shard_map/ppermute | solution.py:75
  221.4 23.5 %collective-permute-start.7 = (f32[256,1024]{1,0:T(8,128)}, f32[256,1024]{1,0:T(8,128)S(1)}, u32[]{:S(2)}, u32[]{:S(2)}) collective-permute-start(f32[256,1024]{1,0:T(8,128)} %collective-permute-done.6), channel_id=1, source_target_pairs={{0,2},{2,4},{4,6},{6,7},{7,5},{5,3},{3,1},{1,0},{8,9},{10,8},{12,1... | collective-permute-start | bytes 3145736 | tf_op jit(solution)/shard_map/ppermute | solution.py:56
  232.0 6.1 %copy-start.3 = (f32[256,1024]{1,0:T(8,128)S(1)}, f32[256,1024]{1,0:T(8,128)}, u32[]{:S(2)}) copy-start(f32[256,1024]{1,0:T(8,128)} %copy-done.2) | copy-start | bytes 3145732
  232.0 6.2 %copy-start.5 = (f32[256,1024]{1,0:T(8,128)S(1)}, f32[256,1024]{1,0:T(8,128)}, u32[]{:S(2)}) copy-start(f32[256,1024]{1,0:T(8,128)} %copy-done.4) | copy-start | bytes 3145732
  232.0 6.3 %copy-start.7 = (f32[256,1024]{1,0:T(8,128)S(1)}, f32[256,1024]{1,0:T(8,128)}, u32[]{:S(2)}) copy-start(f32[256,1024]{1,0:T(8,128)} %copy-done.6) | copy-start | bytes 3145732
  236.0 15.2 %collective-permute-start.11 = (f32[2050,64]{0,1:T(8,128)S(1)}, f32[2050,64]{0,1:T(8,128)S(1)}, u32[]{:S(2)}, u32[]{:S(2)}) collective-permute-start(f32[2050,64]{0,1:T(8,128)S(1)} %add.153), channel_id=1, source_target_pairs={{0,1},{1,0},{2,3},{3,2},{4,5},{5,4},{6,7},{7,6},{8,9},{9,8},{10,11... | collective-permute-start | bytes 1574408 | tf_op jit(solution)/shard_map/ppermute | solution.py:75
  238.1 34.3 %copy-start.10 = (s32[512]{0:T(512)S(1)}, s32[512]{0:T(512)}, u32[]{:S(2)}) copy-start(s32[512]{0:T(512)} %param.12) | copy-start | bytes 6148
  244.9 25.9 %collective-permute-start.8 = (f32[256,1024]{1,0:T(8,128)S(1)}, f32[256,1024]{1,0:T(8,128)S(1)}, u32[]{:S(2)}, u32[]{:S(2)}) collective-permute-start(f32[256,1024]{1,0:T(8,128)S(1)} %collective-permute-done.7), channel_id=1, source_target_pairs={{0,2},{2,4},{4,6},{6,7},{7,5},{5,3},{3,1},{1,0},{8,9},{10,8},{12,1... | collective-permute-start | bytes 3145736 | tf_op jit(solution)/shard_map/ppermute | solution.py:56
  251.6 1.6 collective-permute-start.12
  253.3 3.6 %collective-permute-start.13 = (f32[128]{0:T(128)S(1)}, f32[128]{0:T(128)S(1)}, u32[]{:S(2)}, u32[]{:S(2)}) collective-permute-start(f32[128]{0:T(128)S(1)} %broadcast_select_fusion.1), channel_id=1, source_target_pairs={{0,16},{8,24},{16,0},{24,8},{32,48},{40,56},{48,32},{56,40},{64,80... | collective-permute-start | bytes 1544 | tf_op jit(solution)/shard_map/ppermute | solution.py:86
  256.9 10.3 %collective-permute-start.14 = (f32[256]{0:T(256)S(1)}, f32[256]{0:T(256)S(1)}, u32[]{:S(2)}, u32[]{:S(2)}) collective-permute-start(f32[256]{0:T(256)S(1)} %maximum_select_fusion.2), channel_id=1, source_target_pairs={{0,32},{8,40},{16,48},{24,56},{32,0},{40,8},{48,16},{56,24},{64,96... | collective-permute-start | bytes 3080 | tf_op jit(solution)/shard_map/ppermute | solution.py:86
  267.2 5.1 %collective-permute-start.15 = (f32[512]{0:T(512)S(1)}, f32[512]{0:T(512)S(1)}, u32[]{:S(2)}, u32[]{:S(2)}) collective-permute-start(f32[512]{0:T(512)S(1)} %maximum_select_fusion.1), channel_id=1, source_target_pairs={{0,64},{8,72},{16,80},{24,88},{32,96},{40,104},{48,112},{56,120},{... | collective-permute-start | bytes 6152 | tf_op jit(solution)/shard_map/ppermute | solution.py:86
Sparse Core Ops, SparseCore 0:
  11.7 163.7 all-gather.1

commit v19 on v18

--- a/solution.py
+++ b/solution.py
@@ -22,7 +22,6 @@
 
     col_all = lax.all_gather(masked, "row", axis=0, tiled=True)
 
-    halves = masked.reshape(ev_slots, ratio, width_row)
     received = []
     for t in range(ratio):
         perm = []
@@ -30,7 +29,7 @@
             for c in range(n_col):
                 b = (s % ratio) ^ t
                 perm.append((s * n_col + c, (ratio * c + b) * n_col + s // ratio))
-        piece = halves[:, (row_pos % ratio) ^ t, :]
+        piece = lax.dynamic_slice_in_dim(masked, ((row_pos % ratio) ^ t) * width_row, width_row, 1)
         received.append(lax.ppermute(piece, ("row", "col"), perm))
     parity = row_pos % ratio
     ordered = [

time: 314 us -> 312 us (level)
  no operation moved by 1% of the time
where the time goes in v19:
time: 312 us; the launch traced here: 310 us
  waiting for transfers between devices  141 us (45%)
  starting transfers between devices  84.7 us (27%)
  matrix products  43.8 us (14%)
  between operations  23.6 us (8%)
  local copies, waits for them, and re-layouts  10.4 us (3%)
  other arithmetic  6.02 us (2%)
    ppermute x7, waiting for transfers between devices, body(): held = lax.ppermute(held, ('row', 'col'), pairs)  116 us
    ppermute x7, starting transfers between devices, body(): held = lax.ppermute(held, ('row', 'col'), pairs)  46.9 us
    dot_general x1, matrix products, body(): lax.dot_general(row_all, col_all, contract, precision=high, preferred_ele...  32 us
    ppermute x3, starting transfers between devices, body(): packed = packed + lax.ppermute(packed, 'col', pairs)  24.6 us
    ppermute x3, waiting for transfers between devices, body(): packed = packed + lax.ppermute(packed, 'col', pairs)  17.6 us
    ppermute x4, starting transfers between devices, body(): other = lax.ppermute(held, 'row', pairs)  12.4 us
    dot_general x1, matrix products, body(): lax.dot_general(col_all, items, (((1,), (1,)), ((), ())), precision=high,...  11.3 us
  transfers between devices with their start and end apart: 17, of which 13 were waited for; matrix products, arithmetic and copies ran while one was open for 7% of the time, Pallas kernels for 0%

profile of v19, /device:TPU:0, one launch (start us, length us, event | category | flops | bytes accessed | tf_op | source)
XLA Modules:
  0.0 310.0 jit_solution(15945255922241294652)
XLA Ops:
  7.3 1.3 dynamic_slice.33
  9.2 2.3 broadcast_select_fusion
  11.6 1.3 constant_dynamic-slice_fusion.1
  13.7 1.2 collective-permute-done.1
  15.1 41.9 %collective-permute-start.2 = (f32[256,1024]{1,0:T(8,128)S(1)}, f32[256,1024]{1,0:T(8,128)S(1)}, u32[]{:S(2)}, u32[]{:S(2)}) collective-permute-start(f32[256,1024]{1,0:T(8,128)S(1)} %pad_maximum_fusion), channel_id=1, source_target_pairs={{0,2},{2,4},{4,6},{6,7},{7,5},{5,3},{3,1},{1,0},{8,9},{10,8},{12,1... | collective-permute-start | bytes 3145736 | tf_op jit(solution)/shard_map/ppermute | solution.py:55
  57.1 33.9 %collective-permute-done.2 = f32[256,1024]{1,0:T(8,128)S(1)} collective-permute-done((f32[256,1024]{1,0:T(8,128)S(1)}, f32[256,1024]{1,0:T(8,128)S(1)}, u32[]{:S(2)}, u32[]{:S(2)}) %collective-permute-start.2) | collective-permute-done | bytes 1048608 | tf_op jit(solution)/shard_map/ppermute | solution.py:55
  91.0 1.0 copy-done.2
  92.0 38.3 %collective-permute-done.3 = f32[256,1024]{1,0:T(8,128)S(1)} collective-permute-done((f32[256,1024]{1,0:T(8,128)S(1)}, f32[256,1024]{1,0:T(8,128)S(1)}, u32[]{:S(2)}, u32[]{:S(2)}) %collective-permute-start.3) | collective-permute-done | bytes 1048608 | tf_op jit(solution)/shard_map/ppermute | solution.py:55
  130.2 1.0 copy-done.4
  131.2 21.7 %collective-permute-done.4 = f32[256,1024]{1,0:T(8,128)S(1)} collective-permute-done((f32[256,1024]{1,0:T(8,128)S(1)}, f32[256,1024]{1,0:T(8,128)S(1)}, u32[]{:S(2)}, u32[]{:S(2)}) %collective-permute-start.4) | collective-permute-done | bytes 1048608 | tf_op jit(solution)/shard_map/ppermute | solution.py:55
  153.8 15.5 %collective-permute-done.5 = f32[256,1024]{1,0:T(8,128)} collective-permute-done((f32[256,1024]{1,0:T(8,128)S(1)}, f32[256,1024]{1,0:T(8,128)}, u32[]{:S(2)}, u32[]{:S(2)}) %collective-permute-start.5) | collective-permute-done | bytes 1048608 | tf_op jit(solution)/shard_map/ppermute | solution.py:55
  169.4 2.5 collective-permute-start.6
  171.9 1.6 all-gather.2.cloned.1.call-done
  173.5 11.3 %fusion.3 = f32[2048,64]{0,1:T(8,128)S(1)} fusion(f32[2048,2048]{1,0:T(8,128)} %all-gather.2.cloned.1.call-done, f32[64,2048]{1,0:T(8,128)S(1)} %copy-done.1), kind=kOutput, calls=%fused_computation.32 | convolution fusion | flops 1610612736 | bytes 17825792 | tf_op jit(solution)/shard_map/dot_general | solution.py:64
  184.9 17.6 %collective-permute-start.9 = (f32[2050,64]{0,1:T(8,128)S(1)}, f32[2050,64]{0,1:T(8,128)S(1)}, u32[]{:S(2)}, u32[]{:S(2)}) collective-permute-start(f32[2050,64]{0,1:T(8,128)S(1)} %concatenate.45), channel_id=1, source_target_pairs={{0,4},{1,5},{2,6},{3,7},{4,0},{5,1},{6,2},{7,3},{8,12},{9,13},{10,... | collective-permute-start | bytes 1574408 | tf_op jit(solution)/shard_map/ppermute | solution.py:74
  202.5 10.8 %collective-permute-done.9 = f32[2050,64]{0,1:T(8,128)S(1)} collective-permute-done((f32[2050,64]{0,1:T(8,128)S(1)}, f32[2050,64]{0,1:T(8,128)S(1)}, u32[]{:S(2)}, u32[]{:S(2)}) %collective-permute-start.9) | collective-permute-done | bytes 524832 | tf_op jit(solution)/shard_map/ppermute | solution.py:74
  213.4 6.1 %collective-permute-start.10 = (f32[2050,64]{0,1:T(8,128)S(1)}, f32[2050,64]{0,1:T(8,128)}, u32[]{:S(2)}, u32[]{:S(2)}) collective-permute-start(f32[2050,64]{0,1:T(8,128)S(1)} %add.152), channel_id=1, source_target_pairs={{0,2},{1,3},{2,0},{3,1},{4,6},{5,7},{6,4},{7,5},{8,10},{9,11},{10,... | collective-permute-start | bytes 1574408 | tf_op jit(solution)/shard_map/ppermute | solution.py:74
  230.2 2.8 collective-permute-done.10
  233.0 1.2 add.153
  235.0 1.1 broadcast_in_dim.57
  236.6 6.4 %collective-permute-done.7 = f32[256,1024]{1,0:T(8,128)S(1)} collective-permute-done((f32[256,1024]{1,0:T(8,128)}, f32[256,1024]{1,0:T(8,128)S(1)}, u32[]{:S(2)}, u32[]{:S(2)}) %collective-permute-start.7) | collective-permute-done | bytes 1048608 | tf_op jit(solution)/shard_map/ppermute | solution.py:55
  243.0 2.4 collective-permute-start.8
  245.4 4.0 %collective-permute-done.11 = f32[2050,64]{0,1:T(8,128)S(1)} collective-permute-done((f32[2050,64]{0,1:T(8,128)S(1)}, f32[2050,64]{0,1:T(8,128)S(1)}, u32[]{:S(2)}, u32[]{:S(2)}) %collective-permute-start.11) | collective-permute-done | bytes 524832 | tf_op jit(solution)/shard_map/ppermute | solution.py:74
  249.9 1.3 constant_dynamic-update-slice_fusion.3
  251.3 1.3 constant_dynamic-update-slice_fusion.2
  252.6 2.2 collective-permute-done.13
  254.9 8.8 %collective-permute-start.14 = (f32[256]{0:T(256)S(1)}, f32[256]{0:T(256)S(1)}, u32[]{:S(2)}, u32[]{:S(2)}) collective-permute-start(f32[256]{0:T(256)S(1)} %maximum_select_fusion.2), channel_id=1, source_target_pairs={{0,32},{8,40},{16,48},{24,56},{32,0},{40,8},{48,16},{56,24},{64,96... | collective-permute-start | bytes 3080 | tf_op jit(solution)/shard_map/ppermute | solution.py:85
  263.7 1.4 collective-permute-done.14
  265.2 3.5 %collective-permute-start.15 = (f32[512]{0:T(512)S(1)}, f32[512]{0:T(512)S(1)}, u32[]{:S(2)}, u32[]{:S(2)}) collective-permute-start(f32[512]{0:T(512)S(1)} %maximum_select_fusion.1), channel_id=1, source_target_pairs={{0,64},{8,72},{16,80},{24,88},{32,96},{40,104},{48,112},{56,120},{... | collective-permute-start | bytes 6152 | tf_op jit(solution)/shard_map/ppermute | solution.py:85
  268.8 1.4 collective-permute-done.15
  270.3 0.9 select_reduce_fusion
  271.2 32.0 %select_add_fusion = f32[1024,2048]{1,0:T(8,128)} fusion(f32[2048]{0:T(1024)S(1)} %copy-done.9, s32[2048]{0:T(1024)S(1)} %iota_add_fusion, s32[1024]{0:T(1024)S(1)} %iota_add_fusion.1, f32[2048,1024]{1,0:T(8,128)S(1)} %constant_dynamic-update-slice_fusion, f32[2048,2048]{1,0:T(8,128)} %all-gather.2.cloned.1.call-done), kind=kOutput, calls=%fused_computation | convolution fusion | flops 25776095232 | bytes 33574912 | tf_op jit(solution)/shard_map/dot_general | solution.py:93
  (63 shorter events, 6.3 us)
Async XLA Ops:
  7.2 146.1 %copy-start = (f32[2048]{0:T(1024)S(1)}, f32[2048]{0:T(1024)}, u32[]{:S(2)}) copy-start(f32[2048]{0:T(1024)} %param.13) | copy-start | bytes 24580
  7.2 145.8 %copy-start.9 = (f32[2048]{0:T(1024)S(1)}, f32[2048]{0:T(1024)}, u32[]{:S(2)}) copy-start(f32[2048]{0:T(1024)} %param.10) | copy-start | bytes 24580
  7.2 145.8 %copy-start.1 = (f32[64,2048]{1,0:T(8,128)S(1)}, f32[64,2048]{1,0:T(8,128)}, u32[]{:S(2)}) copy-start(f32[64,2048]{1,0:T(8,128)} %param.11) | copy-start | bytes 1572868
  7.2 166.3 %all-gather.2.cloned.1.call-start = ((), (), s32[]{:S(2)}) async-start(), calls=%async_computation | async-start | bytes 17825792 | tf_op jit(solution)/shard_map/all_gather | solution.py:23
  12.9 2.0 collective-permute-start.1
  13.0 1.9 collective-permute-start
  15.1 75.9 %collective-permute-start.2 = (f32[256,1024]{1,0:T(8,128)S(1)}, f32[256,1024]{1,0:T(8,128)S(1)}, u32[]{:S(2)}, u32[]{:S(2)}) collective-permute-start(f32[256,1024]{1,0:T(8,128)S(1)} %pad_maximum_fusion), channel_id=1, source_target_pairs={{0,2},{2,4},{4,6},{6,7},{7,5},{5,3},{3,1},{1,0},{8,9},{10,8},{12,1... | collective-permute-start | bytes 3145736 | tf_op jit(solution)/shard_map/ppermute | solution.py:55
  91.0 1.0 copy-start.2
  92.0 38.3 %collective-permute-start.3 = (f32[256,1024]{1,0:T(8,128)S(1)}, f32[256,1024]{1,0:T(8,128)S(1)}, u32[]{:S(2)}, u32[]{:S(2)}) collective-permute-start(f32[256,1024]{1,0:T(8,128)S(1)} %collective-permute-done.2), channel_id=1, source_target_pairs={{0,2},{2,4},{4,6},{6,7},{7,5},{5,3},{3,1},{1,0},{8,9},{10,8},{12,1... | collective-permute-start | bytes 3145736 | tf_op jit(solution)/shard_map/ppermute | solution.py:55
  130.2 1.0 copy-start.4
  131.2 21.8 %collective-permute-start.4 = (f32[256,1024]{1,0:T(8,128)S(1)}, f32[256,1024]{1,0:T(8,128)S(1)}, u32[]{:S(2)}, u32[]{:S(2)}) collective-permute-start(f32[256,1024]{1,0:T(8,128)S(1)} %collective-permute-done.3), channel_id=1, source_target_pairs={{0,2},{2,4},{4,6},{6,7},{7,5},{5,3},{3,1},{1,0},{8,9},{10,8},{12,1... | collective-permute-start | bytes 3145736 | tf_op jit(solution)/shard_map/ppermute | solution.py:55
  153.0 18.9 %copy-start.6 = (f32[256,1024]{1,0:T(8,128)}, f32[256,1024]{1,0:T(8,128)S(1)}, u32[]{:S(2)}) copy-start(f32[256,1024]{1,0:T(8,128)S(1)} %collective-permute-done.4) | copy-start | bytes 3145732
  153.0 16.4 %collective-permute-start.5 = (f32[256,1024]{1,0:T(8,128)S(1)}, f32[256,1024]{1,0:T(8,128)}, u32[]{:S(2)}, u32[]{:S(2)}) collective-permute-start(f32[256,1024]{1,0:T(8,128)S(1)} %collective-permute-done.4), channel_id=1, source_target_pairs={{0,2},{2,4},{4,6},{6,7},{7,5},{5,3},{3,1},{1,0},{8,9},{10,8},{12,1... | collective-permute-start | bytes 3145736 | tf_op jit(solution)/shard_map/ppermute | solution.py:55
  153.8 65.8 %copy-start.11 = (s32[8]{0:T(128)S(1)}, s32[8]{0:T(128)}, u32[]{:S(2)}) copy-start(s32[8]{0:T(128)} %constant.100.clone) | copy-start | bytes 100
  153.8 71.0 %copy-start.8 = (s32[8]{0:T(128)S(1)}, s32[8]{0:T(128)}, u32[]{:S(2)}) copy-start(s32[8]{0:T(128)} %constant.99.clone) | copy-start | bytes 100
  169.4 50.1 %collective-permute-start.6 = (f32[256,1024]{1,0:T(8,128)}, f32[256,1024]{1,0:T(8,128)}, u32[]{:S(2)}, u32[]{:S(2)}) collective-permute-start(f32[256,1024]{1,0:T(8,128)} %collective-permute-done.5), channel_id=1, source_target_pairs={{0,2},{2,4},{4,6},{6,7},{7,5},{5,3},{3,1},{1,0},{8,9},{10,8},{12,1... | collective-permute-start | bytes 3145736 | tf_op jit(solution)/shard_map/ppermute | solution.py:55
  184.9 28.4 %collective-permute-start.9 = (f32[2050,64]{0,1:T(8,128)S(1)}, f32[2050,64]{0,1:T(8,128)S(1)}, u32[]{:S(2)}, u32[]{:S(2)}) collective-permute-start(f32[2050,64]{0,1:T(8,128)S(1)} %concatenate.45), channel_id=1, source_target_pairs={{0,4},{1,5},{2,6},{3,7},{4,0},{5,1},{6,2},{7,3},{8,12},{9,13},{10,... | collective-permute-start | bytes 1574408 | tf_op jit(solution)/shard_map/ppermute | solution.py:74
  213.4 19.6 %collective-permute-start.10 = (f32[2050,64]{0,1:T(8,128)S(1)}, f32[2050,64]{0,1:T(8,128)}, u32[]{:S(2)}, u32[]{:S(2)}) collective-permute-start(f32[2050,64]{0,1:T(8,128)S(1)} %add.152), channel_id=1, source_target_pairs={{0,2},{1,3},{2,0},{3,1},{4,6},{5,7},{6,4},{7,5},{8,10},{9,11},{10,... | collective-permute-start | bytes 1574408 | tf_op jit(solution)/shard_map/ppermute | solution.py:74
  219.5 23.5 %collective-permute-start.7 = (f32[256,1024]{1,0:T(8,128)}, f32[256,1024]{1,0:T(8,128)S(1)}, u32[]{:S(2)}, u32[]{:S(2)}) collective-permute-start(f32[256,1024]{1,0:T(8,128)} %collective-permute-done.6), channel_id=1, source_target_pairs={{0,2},{2,4},{4,6},{6,7},{7,5},{5,3},{3,1},{1,0},{8,9},{10,8},{12,1... | collective-permute-start | bytes 3145736 | tf_op jit(solution)/shard_map/ppermute | solution.py:55
  230.1 6.1 %copy-start.3 = (f32[256,1024]{1,0:T(8,128)S(1)}, f32[256,1024]{1,0:T(8,128)}, u32[]{:S(2)}) copy-start(f32[256,1024]{1,0:T(8,128)} %copy-done.2) | copy-start | bytes 3145732
  230.1 6.2 %copy-start.5 = (f32[256,1024]{1,0:T(8,128)S(1)}, f32[256,1024]{1,0:T(8,128)}, u32[]{:S(2)}) copy-start(f32[256,1024]{1,0:T(8,128)} %copy-done.4) | copy-start | bytes 3145732
  230.2 6.3 %copy-start.7 = (f32[256,1024]{1,0:T(8,128)S(1)}, f32[256,1024]{1,0:T(8,128)}, u32[]{:S(2)}) copy-start(f32[256,1024]{1,0:T(8,128)} %copy-done.6) | copy-start | bytes 3145732
  234.2 15.2 %collective-permute-start.11 = (f32[2050,64]{0,1:T(8,128)S(1)}, f32[2050,64]{0,1:T(8,128)S(1)}, u32[]{:S(2)}, u32[]{:S(2)}) collective-permute-start(f32[2050,64]{0,1:T(8,128)S(1)} %add.153), channel_id=1, source_target_pairs={{0,1},{1,0},{2,3},{3,2},{4,5},{5,4},{6,7},{7,6},{8,9},{9,8},{10,11... | collective-permute-start | bytes 1574408 | tf_op jit(solution)/shard_map/ppermute | solution.py:74
  236.2 34.1 %copy-start.10 = (s32[512]{0:T(512)S(1)}, s32[512]{0:T(512)}, u32[]{:S(2)}) copy-start(s32[512]{0:T(512)} %param.12) | copy-start | bytes 6148
  243.0 25.7 %collective-permute-start.8 = (f32[256,1024]{1,0:T(8,128)S(1)}, f32[256,1024]{1,0:T(8,128)S(1)}, u32[]{:S(2)}, u32[]{:S(2)}) collective-permute-start(f32[256,1024]{1,0:T(8,128)S(1)} %collective-permute-done.7), channel_id=1, source_target_pairs={{0,2},{2,4},{4,6},{6,7},{7,5},{5,3},{3,1},{1,0},{8,9},{10,8},{12,1... | collective-permute-start | bytes 3145736 | tf_op jit(solution)/shard_map/ppermute | solution.py:55
  249.8 1.4 collective-permute-start.12
  251.3 3.6 %collective-permute-start.13 = (f32[128]{0:T(128)S(1)}, f32[128]{0:T(128)S(1)}, u32[]{:S(2)}, u32[]{:S(2)}) collective-permute-start(f32[128]{0:T(128)S(1)} %broadcast_select_fusion.1), channel_id=1, source_target_pairs={{0,16},{8,24},{16,0},{24,8},{32,48},{40,56},{48,32},{56,40},{64,80... | collective-permute-start | bytes 1544 | tf_op jit(solution)/shard_map/ppermute | solution.py:85
  254.9 10.3 %collective-permute-start.14 = (f32[256]{0:T(256)S(1)}, f32[256]{0:T(256)S(1)}, u32[]{:S(2)}, u32[]{:S(2)}) collective-permute-start(f32[256]{0:T(256)S(1)} %maximum_select_fusion.2), channel_id=1, source_target_pairs={{0,32},{8,40},{16,48},{24,56},{32,0},{40,8},{48,16},{56,24},{64,96... | collective-permute-start | bytes 3080 | tf_op jit(solution)/shard_map/ppermute | solution.py:85
  265.2 5.1 %collective-permute-start.15 = (f32[512]{0:T(512)S(1)}, f32[512]{0:T(512)S(1)}, u32[]{:S(2)}, u32[]{:S(2)}) collective-permute-start(f32[512]{0:T(512)S(1)} %maximum_select_fusion.1), channel_id=1, source_target_pairs={{0,64},{8,72},{16,80},{24,88},{32,96},{40,104},{48,112},{56,120},{... | collective-permute-start | bytes 6152 | tf_op jit(solution)/shard_map/ppermute | solution.py:85
Sparse Core Ops, SparseCore 0:
  11.7 161.8 all-gather.1

commit v20 on v19

--- a/solution.py
+++ b/solution.py
@@ -32,11 +32,11 @@
         piece = lax.dynamic_slice_in_dim(masked, ((row_pos % ratio) ^ t) * width_row, width_row, 1)
         received.append(lax.ppermute(piece, ("row", "col"), perm))
     parity = row_pos % ratio
-    ordered = [
-        sum(jnp.where(parity ^ t == a, received[t], 0.0) for t in range(ratio))
-        for a in range(ratio)
-    ]
-    row_block = jnp.concatenate(ordered, axis=0)
+    row_block = jnp.where(
+        parity == 0,
+        jnp.concatenate([received[0], received[1]], axis=0),
+        jnp.concatenate([received[1], received[0]], axis=0),
+    )
 
     n_y = n_col // 2
     ring = [y * 2 for y in range(n_y)] + [y * 2 + 1 for y in reversed(range(n_y))]

time: 312 us -> 312 us (level)
  transfers between devices with their start and end apart: 17 -> 17, of which waited for: 13 -> 13; matrix products, arithmetic and copies ran while one was open for 7% -> 8% of each run, Pallas kernels for 0% -> 0%
where the time goes in v20:
time: 312 us; the launch traced here: 310 us
  waiting for transfers between devices  140 us (45%)
  starting transfers between devices  84.1 us (27%)
  matrix products  44.8 us (14%)
  between operations  23.5 us (8%)
  local copies, waits for them, and re-layouts  10.5 us (3%)
  other arithmetic  7.17 us (2%)
    ppermute x7, waiting for transfers between devices, body(): held = lax.ppermute(held, ('row', 'col'), pairs)  114 us
    ppermute x7, starting transfers between devices, body(): held = lax.ppermute(held, ('row', 'col'), pairs)  46.5 us
    dot_general x1, matrix products, body(): lax.dot_general(row_all, col_all, contract, precision=high, preferred_ele...  32 us
    ppermute x3, starting transfers between devices, body(): packed = packed + lax.ppermute(packed, 'col', pairs)  24.3 us
    ppermute x3, waiting for transfers between devices, body(): packed = packed + lax.ppermute(packed, 'col', pairs)  17.8 us
    ppermute x4, starting transfers between devices, body(): other = lax.ppermute(held, 'row', pairs)  12.4 us
    dot_general x1, matrix products, body(): lax.dot_general(col_all, items, (((1,), (1,)), ((), ())), precision=high,...  11.3 us
  transfers between devices with their start and end apart: 17, of which 13 were waited for; matrix products, arithmetic and copies ran while one was open for 8% of the time, Pallas kernels for 0%

profile of v20, /device:TPU:0, one launch (start us, length us, event | category | flops | bytes accessed | tf_op | source)
XLA Modules:
  0.0 310.0 jit_solution(13447102680665323043)
XLA Ops:
  7.2 1.3 dynamic_slice.33
  9.2 2.3 broadcast_select_fusion
  11.6 1.3 constant_dynamic-slice_fusion.1
  13.6 1.2 collective-permute-done.1
  15.0 41.9 %collective-permute-start.2 = (f32[256,1024]{1,0:T(8,128)S(1)}, f32[256,1024]{1,0:T(8,128)S(1)}, u32[]{:S(2)}, u32[]{:S(2)}) collective-permute-start(f32[256,1024]{1,0:T(8,128)S(1)} %maximum_select_fusion), channel_id=1, source_target_pairs={{0,2},{2,4},{4,6},{6,7},{7,5},{5,3},{3,1},{1,0},{8,9},{10,8},{12,1... | collective-permute-start | bytes 3145736 | tf_op jit(solution)/shard_map/ppermute | solution.py:55
  56.9 34.1 %collective-permute-done.2 = f32[256,1024]{1,0:T(8,128)S(1)} collective-permute-done((f32[256,1024]{1,0:T(8,128)S(1)}, f32[256,1024]{1,0:T(8,128)S(1)}, u32[]{:S(2)}, u32[]{:S(2)}) %collective-permute-start.2) | collective-permute-done | bytes 1048608 | tf_op jit(solution)/shard_map/ppermute | solution.py:55
  92.0 38.2 %collective-permute-done.3 = f32[256,1024]{1,0:T(8,128)S(1)} collective-permute-done((f32[256,1024]{1,0:T(8,128)S(1)}, f32[256,1024]{1,0:T(8,128)S(1)}, u32[]{:S(2)}, u32[]{:S(2)}) %collective-permute-start.3) | collective-permute-done | bytes 1048608 | tf_op jit(solution)/shard_map/ppermute | solution.py:55
  130.2 1.0 copy-done.4
  131.2 21.8 %collective-permute-done.4 = f32[256,1024]{1,0:T(8,128)S(1)} collective-permute-done((f32[256,1024]{1,0:T(8,128)S(1)}, f32[256,1024]{1,0:T(8,128)S(1)}, u32[]{:S(2)}, u32[]{:S(2)}) %collective-permute-start.4) | collective-permute-done | bytes 1048608 | tf_op jit(solution)/shard_map/ppermute | solution.py:55
  153.0 1.6 fusion
  154.7 1.6 fusion.4
  156.3 13.1 %collective-permute-done.5 = f32[256,1024]{1,0:T(8,128)} collective-permute-done((f32[256,1024]{1,0:T(8,128)S(1)}, f32[256,1024]{1,0:T(8,128)}, u32[]{:S(2)}, u32[]{:S(2)}) %collective-permute-start.5) | collective-permute-done | bytes 1048608 | tf_op jit(solution)/shard_map/ppermute | solution.py:55
  169.4 2.1 collective-permute-start.6
  171.5 2.1 all-gather.2.cloned.1.call-done
  173.6 11.3 %fusion.3 = f32[2048,64]{0,1:T(8,128)S(1)} fusion(f32[2048,2048]{1,0:T(8,128)} %all-gather.2.cloned.1.call-done, f32[64,2048]{1,0:T(8,128)S(1)} %copy-done.1), kind=kOutput, calls=%fused_computation.30 | convolution fusion | flops 1610612736 | bytes 17825792 | tf_op jit(solution)/shard_map/dot_general | solution.py:64
  185.0 17.5 %collective-permute-start.9 = (f32[2050,64]{0,1:T(8,128)S(1)}, f32[2050,64]{0,1:T(8,128)S(1)}, u32[]{:S(2)}, u32[]{:S(2)}) collective-permute-start(f32[2050,64]{0,1:T(8,128)S(1)} %concatenate.49), channel_id=1, source_target_pairs={{0,4},{1,5},{2,6},{3,7},{4,0},{5,1},{6,2},{7,3},{8,12},{9,13},{10,... | collective-permute-start | bytes 1574408 | tf_op jit(solution)/shard_map/ppermute | solution.py:74
  202.5 10.8 %collective-permute-done.9 = f32[2050,64]{0,1:T(8,128)S(1)} collective-permute-done((f32[2050,64]{0,1:T(8,128)S(1)}, f32[2050,64]{0,1:T(8,128)S(1)}, u32[]{:S(2)}, u32[]{:S(2)}) %collective-permute-start.9) | collective-permute-done | bytes 524832 | tf_op jit(solution)/shard_map/ppermute | solution.py:74
  213.4 6.1 %collective-permute-start.10 = (f32[2050,64]{0,1:T(8,128)S(1)}, f32[2050,64]{0,1:T(8,128)}, u32[]{:S(2)}, u32[]{:S(2)}) collective-permute-start(f32[2050,64]{0,1:T(8,128)S(1)} %add.144), channel_id=1, source_target_pairs={{0,2},{1,3},{2,0},{3,1},{4,6},{5,7},{6,4},{7,5},{8,10},{9,11},{10,... | collective-permute-start | bytes 1574408 | tf_op jit(solution)/shard_map/ppermute | solution.py:74
  230.0 3.0 collective-permute-done.10
  233.0 1.2 add.145
  234.9 1.1 broadcast_in_dim.50
  236.5 6.5 %collective-permute-done.7 = f32[256,1024]{1,0:T(8,128)S(1)} collective-permute-done((f32[256,1024]{1,0:T(8,128)}, f32[256,1024]{1,0:T(8,128)S(1)}, u32[]{:S(2)}, u32[]{:S(2)}) %collective-permute-start.7) | collective-permute-done | bytes 1048608 | tf_op jit(solution)/shard_map/ppermute | solution.py:55
  243.0 2.4 collective-permute-start.8
  245.4 4.0 %collective-permute-done.11 = f32[2050,64]{0,1:T(8,128)S(1)} collective-permute-done((f32[2050,64]{0,1:T(8,128)S(1)}, f32[2050,64]{0,1:T(8,128)S(1)}, u32[]{:S(2)}, u32[]{:S(2)}) %collective-permute-start.11) | collective-permute-done | bytes 524832 | tf_op jit(solution)/shard_map/ppermute | solution.py:74
  249.9 1.3 constant_dynamic-update-slice_fusion.3
  251.3 1.3 constant_dynamic-update-slice_fusion.2
  252.6 2.2 collective-permute-done.13
  254.8 8.8 %collective-permute-start.14 = (f32[256]{0:T(256)S(1)}, f32[256]{0:T(256)S(1)}, u32[]{:S(2)}, u32[]{:S(2)}) collective-permute-start(f32[256]{0:T(256)S(1)} %maximum_select_fusion.3), channel_id=1, source_target_pairs={{0,32},{8,40},{16,48},{24,56},{32,0},{40,8},{48,16},{56,24},{64,96... | collective-permute-start | bytes 3080 | tf_op jit(solution)/shard_map/ppermute | solution.py:85
  263.7 1.4 collective-permute-done.14
  265.2 3.5 %collective-permute-start.15 = (f32[512]{0:T(512)S(1)}, f32[512]{0:T(512)S(1)}, u32[]{:S(2)}, u32[]{:S(2)}) collective-permute-start(f32[512]{0:T(512)S(1)} %maximum_select_fusion.2), channel_id=1, source_target_pairs={{0,64},{8,72},{16,80},{24,88},{32,96},{40,104},{48,112},{56,120},{... | collective-permute-start | bytes 6152 | tf_op jit(solution)/shard_map/ppermute | solution.py:85
  268.8 1.4 collective-permute-done.15
  271.2 32.0 %select_add_fusion = f32[1024,2048]{1,0:T(8,128)} fusion(f32[2048]{0:T(1024)S(1)} %copy-done.9, s32[2048]{0:T(1024)S(1)} %iota_add_fusion, s32[1024]{0:T(1024)S(1)} %iota_add_fusion.1, f32[2048,1024]{1,0:T(8,128)S(1)} %constant_dynamic-update-slice_fusion, f32[2048,2048]{1,0:T(8,128)} %all-gather.2.cloned.1.call-done), kind=kOutput, calls=%fused_computation | convolution fusion | flops 25776095232 | bytes 33574912 | tf_op jit(solution)/shard_map/dot_general | solution.py:93
  (62 shorter events, 7.2 us)
Async XLA Ops:
  7.2 147.5 %copy-start = (f32[2048]{0:T(1024)S(1)}, f32[2048]{0:T(1024)}, u32[]{:S(2)}) copy-start(f32[2048]{0:T(1024)} %param.13) | copy-start | bytes 24580
  7.2 166.5 %copy-start.1 = (f32[64,2048]{1,0:T(8,128)S(1)}, f32[64,2048]{1,0:T(8,128)}, u32[]{:S(2)}) copy-start(f32[64,2048]{1,0:T(8,128)} %param.11) | copy-start | bytes 1572868
  7.2 166.4 %all-gather.2.cloned.1.call-start = ((), (), s32[]{:S(2)}) async-start(), calls=%async_computation | async-start | bytes 17825792 | tf_op jit(solution)/shard_map/all_gather | solution.py:23
  12.8 2.0 collective-permute-start.1
  12.9 1.9 collective-permute-start
  15.0 76.0 %collective-permute-start.2 = (f32[256,1024]{1,0:T(8,128)S(1)}, f32[256,1024]{1,0:T(8,128)S(1)}, u32[]{:S(2)}, u32[]{:S(2)}) collective-permute-start(f32[256,1024]{1,0:T(8,128)S(1)} %maximum_select_fusion), channel_id=1, source_target_pairs={{0,2},{2,4},{4,6},{6,7},{7,5},{5,3},{3,1},{1,0},{8,9},{10,8},{12,1... | collective-permute-start | bytes 3145736 | tf_op jit(solution)/shard_map/ppermute | solution.py:55
  91.0 1.0 copy-start.2
  92.0 38.3 %collective-permute-start.3 = (f32[256,1024]{1,0:T(8,128)S(1)}, f32[256,1024]{1,0:T(8,128)S(1)}, u32[]{:S(2)}, u32[]{:S(2)}) collective-permute-start(f32[256,1024]{1,0:T(8,128)S(1)} %collective-permute-done.2), channel_id=1, source_target_pairs={{0,2},{2,4},{4,6},{6,7},{7,5},{5,3},{3,1},{1,0},{8,9},{10,8},{12,1... | collective-permute-start | bytes 3145736 | tf_op jit(solution)/shard_map/ppermute | solution.py:55
  130.2 1.0 copy-start.4
  131.2 21.8 %collective-permute-start.4 = (f32[256,1024]{1,0:T(8,128)S(1)}, f32[256,1024]{1,0:T(8,128)S(1)}, u32[]{:S(2)}, u32[]{:S(2)}) collective-permute-start(f32[256,1024]{1,0:T(8,128)S(1)} %collective-permute-done.3), channel_id=1, source_target_pairs={{0,2},{2,4},{4,6},{6,7},{7,5},{5,3},{3,1},{1,0},{8,9},{10,8},{12,1... | collective-permute-start | bytes 3145736 | tf_op jit(solution)/shard_map/ppermute | solution.py:55
  153.0 18.5 %copy-start.6 = (f32[256,1024]{1,0:T(8,128)}, f32[256,1024]{1,0:T(8,128)S(1)}, u32[]{:S(2)}) copy-start(f32[256,1024]{1,0:T(8,128)S(1)} %collective-permute-done.4) | copy-start | bytes 3145732
  153.0 16.4 %collective-permute-start.5 = (f32[256,1024]{1,0:T(8,128)S(1)}, f32[256,1024]{1,0:T(8,128)}, u32[]{:S(2)}, u32[]{:S(2)}) collective-permute-start(f32[256,1024]{1,0:T(8,128)S(1)} %collective-permute-done.4), channel_id=1, source_target_pairs={{0,2},{2,4},{4,6},{6,7},{7,5},{5,3},{3,1},{1,0},{8,9},{10,8},{12,1... | collective-permute-start | bytes 3145736 | tf_op jit(solution)/shard_map/ppermute | solution.py:55
  156.3 63.3 %copy-start.11 = (s32[8]{0:T(128)S(1)}, s32[8]{0:T(128)}, u32[]{:S(2)}) copy-start(s32[8]{0:T(128)} %constant.100.clone) | copy-start | bytes 100
  156.3 68.6 %copy-start.8 = (s32[8]{0:T(128)S(1)}, s32[8]{0:T(128)}, u32[]{:S(2)}) copy-start(s32[8]{0:T(128)} %constant.99.clone) | copy-start | bytes 100
  169.4 50.1 %collective-permute-start.6 = (f32[256,1024]{1,0:T(8,128)}, f32[256,1024]{1,0:T(8,128)}, u32[]{:S(2)}, u32[]{:S(2)}) collective-permute-start(f32[256,1024]{1,0:T(8,128)} %collective-permute-done.5), channel_id=1, source_target_pairs={{0,2},{2,4},{4,6},{6,7},{7,5},{5,3},{3,1},{1,0},{8,9},{10,8},{12,1... | collective-permute-start | bytes 3145736 | tf_op jit(solution)/shard_map/ppermute | solution.py:55
  185.0 28.3 %collective-permute-start.9 = (f32[2050,64]{0,1:T(8,128)S(1)}, f32[2050,64]{0,1:T(8,128)S(1)}, u32[]{:S(2)}, u32[]{:S(2)}) collective-permute-start(f32[2050,64]{0,1:T(8,128)S(1)} %concatenate.49), channel_id=1, source_target_pairs={{0,4},{1,5},{2,6},{3,7},{4,0},{5,1},{6,2},{7,3},{8,12},{9,13},{10,... | collective-permute-start | bytes 1574408 | tf_op jit(solution)/shard_map/ppermute | solution.py:74
  213.4 19.6 %collective-permute-start.10 = (f32[2050,64]{0,1:T(8,128)S(1)}, f32[2050,64]{0,1:T(8,128)}, u32[]{:S(2)}, u32[]{:S(2)}) collective-permute-start(f32[2050,64]{0,1:T(8,128)S(1)} %add.144), channel_id=1, source_target_pairs={{0,2},{1,3},{2,0},{3,1},{4,6},{5,7},{6,4},{7,5},{8,10},{9,11},{10,... | collective-permute-start | bytes 1574408 | tf_op jit(solution)/shard_map/ppermute | solution.py:74
  219.5 23.5 %collective-permute-start.7 = (f32[256,1024]{1,0:T(8,128)}, f32[256,1024]{1,0:T(8,128)S(1)}, u32[]{:S(2)}, u32[]{:S(2)}) collective-permute-start(f32[256,1024]{1,0:T(8,128)} %collective-permute-done.6), channel_id=1, source_target_pairs={{0,2},{2,4},{4,6},{6,7},{7,5},{5,3},{3,1},{1,0},{8,9},{10,8},{12,1... | collective-permute-start | bytes 3145736 | tf_op jit(solution)/shard_map/ppermute | solution.py:55
  230.0 6.1 %copy-start.3 = (f32[256,1024]{1,0:T(8,128)S(1)}, f32[256,1024]{1,0:T(8,128)}, u32[]{:S(2)}) copy-start(f32[256,1024]{1,0:T(8,128)} %copy-done.2) | copy-start | bytes 3145732
  230.0 6.2 %copy-start.5 = (f32[256,1024]{1,0:T(8,128)S(1)}, f32[256,1024]{1,0:T(8,128)}, u32[]{:S(2)}) copy-start(f32[256,1024]{1,0:T(8,128)} %copy-done.4) | copy-start | bytes 3145732
  230.0 6.3 %copy-start.7 = (f32[256,1024]{1,0:T(8,128)S(1)}, f32[256,1024]{1,0:T(8,128)}, u32[]{:S(2)}) copy-start(f32[256,1024]{1,0:T(8,128)} %copy-done.6) | copy-start | bytes 3145732
  234.2 15.2 %collective-permute-start.11 = (f32[2050,64]{0,1:T(8,128)S(1)}, f32[2050,64]{0,1:T(8,128)S(1)}, u32[]{:S(2)}, u32[]{:S(2)}) collective-permute-start(f32[2050,64]{0,1:T(8,128)S(1)} %add.145), channel_id=1, source_target_pairs={{0,1},{1,0},{2,3},{3,2},{4,5},{5,4},{6,7},{7,6},{8,9},{9,8},{10,11... | collective-permute-start | bytes 1574408 | tf_op jit(solution)/shard_map/ppermute | solution.py:74
  236.0 34.2 %copy-start.10 = (s32[512]{0:T(512)S(1)}, s32[512]{0:T(512)}, u32[]{:S(2)}) copy-start(s32[512]{0:T(512)} %param.12) | copy-start | bytes 6148
  236.1 35.2 %copy-start.9 = (f32[2048]{0:T(1024)S(1)}, f32[2048]{0:T(1024)}, u32[]{:S(2)}) copy-start(f32[2048]{0:T(1024)} %param.10) | copy-start | bytes 24580
  243.0 25.7 %collective-permute-start.8 = (f32[256,1024]{1,0:T(8,128)S(1)}, f32[256,1024]{1,0:T(8,128)S(1)}, u32[]{:S(2)}, u32[]{:S(2)}) collective-permute-start(f32[256,1024]{1,0:T(8,128)S(1)} %collective-permute-done.7), channel_id=1, source_target_pairs={{0,2},{2,4},{4,6},{6,7},{7,5},{5,3},{3,1},{1,0},{8,9},{10,8},{12,1... | collective-permute-start | bytes 3145736 | tf_op jit(solution)/shard_map/ppermute | solution.py:55
  249.8 1.4 collective-permute-start.12
  251.3 3.6 %collective-permute-start.13 = (f32[128]{0:T(128)S(1)}, f32[128]{0:T(128)S(1)}, u32[]{:S(2)}, u32[]{:S(2)}) collective-permute-start(f32[128]{0:T(128)S(1)} %broadcast_select_fusion.1), channel_id=1, source_target_pairs={{0,16},{8,24},{16,0},{24,8},{32,48},{40,56},{48,32},{56,40},{64,80... | collective-permute-start | bytes 1544 | tf_op jit(solution)/shard_map/ppermute | solution.py:85
  254.8 10.3 %collective-permute-start.14 = (f32[256]{0:T(256)S(1)}, f32[256]{0:T(256)S(1)}, u32[]{:S(2)}, u32[]{:S(2)}) collective-permute-start(f32[256]{0:T(256)S(1)} %maximum_select_fusion.3), channel_id=1, source_target_pairs={{0,32},{8,40},{16,48},{24,56},{32,0},{40,8},{48,16},{56,24},{64,96... | collective-permute-start | bytes 3080 | tf_op jit(solution)/shard_map/ppermute | solution.py:85
  265.2 5.1 %collective-permute-start.15 = (f32[512]{0:T(512)S(1)}, f32[512]{0:T(512)S(1)}, u32[]{:S(2)}, u32[]{:S(2)}) collective-permute-start(f32[512]{0:T(512)S(1)} %maximum_select_fusion.2), channel_id=1, source_target_pairs={{0,64},{8,72},{16,80},{24,88},{32,96},{40,104},{48,112},{56,120},{... | collective-permute-start | bytes 6152 | tf_op jit(solution)/shard_map/ppermute | solution.py:85
Sparse Core Ops, SparseCore 0:
  11.7 161.9 all-gather.1
